TPU v7x, 256 devices: a whole 4x4x8 slice. The times are simulated.
256 devices in a mesh: resp: 32 (over y, x, core), head: 8 (over z).
Axes of the slice: x: 4, y: 4, z: 8, core: 2. Of those that a mesh axis runs over, the one named last changes fastest.
Arguments:
- queries: bfloat16 [32, 512, 8192], P('resp', None, 'head'), may hold values from -18 to 18
- key_states: bfloat16 [32, 512, 1024], P('resp', None, 'head'), may hold values from -6 to 6
- value_states: bfloat16 [32, 512, 1024], P('resp', None, 'head'), may hold values from -30 to 30
- partners: int32 [32, 3], P('resp'), may hold values from 0 to 31, as said below
- counts: int32 [32], P('resp'), may hold values from 1 to 3, as said below
- norm_gain: float32 [8192], P('head'), may hold values from 0.25 to 1.75
- out_grad: bfloat16 [32, 512, 8192], P('resp', None, 'head'), may hold values from -6 to 6
Outputs:
- normed_out: bfloat16 [32, 512, 8192], P('resp', None, 'head')
- query_grads: bfloat16 [32, 512, 8192], P('resp', None, 'head')
- key_grads: bfloat16 [32, 512, 1024], P('resp', None, 'head')
- value_grads: bfloat16 [32, 512, 1024], P('resp', None, 'head')
Inputs may be any that keep to these rules, and one draw needn't show every extreme that they name: Row r lists 3 different partners, all in the aligned block of 8 responses that holds r, none equal to r; the first counts[r] of them are live, the rest unused. Live partnership is symmetric: b is a live partner of a exactly when a is a live partner of b. `counts`: some response has 3 live partners.
All inputs are finite; a program needn't handle non-finite values.
Results may differ from a plain program's by a relative error of at most 0.015.
Values may be sent and summed in bfloat16 or wider, within the bound.
No kernel may reach another device: no remote copies, remote signals or barrier semaphores. Data moves between devices by JAX's collectives and lax.ppermute only.
A program may use at most 64 MiB of HBM per device.

v0:
```python
import jax
import jax.numpy as jnp
from jax import lax
from jax.sharding import PartitionSpec as P

HD = 128
D = 8192
GROUP = 8


EPSILON = 1e-05
NEG_FLOOR = -1e30


def partner(block, axis, apart):
    count = lax.axis_size(axis)
    route = []
    for low in range(count):
        high = low | 1 << apart
        if high != low and high < count:
            route += [(low, high), (high, low)]
    return lax.ppermute(block, axis, route)


def add_row(buffer, addend, row_index):
    current = lax.dynamic_index_in_dim(buffer, row_index, 0, keepdims=False)
    return lax.dynamic_update_index_in_dim(buffer, current + addend, row_index, 0)


def body(queries, key_states, value_states, partners, counts, norm_gain, out_grad):
    my_index = lax.axis_index("resp")
    my_place = my_index % GROUP
    group_first = my_index - my_place
    seq_len = queries.shape[1]
    kv_cols = key_states.shape[2]
    kv_heads = kv_cols // HD
    per_group = queries.shape[2] // kv_cols
    levels = GROUP.bit_length() - 1
    fetch_bits = list(range(levels))
    cluster_key_rows, group_values = (key_states, value_states)
    for bit_number in fetch_bits:
        other_keys, other_values = partner((cluster_key_rows, group_values), "resp", bit_number)
        is_upper = my_index >> bit_number & 1 == 1
        cluster_key_rows = jnp.where(
            is_upper,
            jnp.concatenate([other_keys, cluster_key_rows], 0),
            jnp.concatenate([cluster_key_rows, other_keys], 0),
        )
        group_values = jnp.where(
            is_upper,
            jnp.concatenate([other_values, group_values], 0),
            jnp.concatenate([group_values, other_values], 0),
        )
    query_heads = queries[0].reshape(seq_len, kv_heads, per_group, HD)
    score_scale = HD ** (-0.5)
    mate_rows = partners[0] - group_first
    live_count = counts[0]

    def partner_block_tile(slot_index):
        mate_row = mate_rows[slot_index]
        mate_keys = lax.dynamic_index_in_dim(cluster_key_rows, mate_row, 0, keepdims=False).reshape(
            seq_len, kv_heads, HD
        )
        mate_values = lax.dynamic_index_in_dim(group_values, mate_row, 0, keepdims=False).reshape(
            seq_len, kv_heads, HD
        )
        return (mate_keys, mate_values)

    def score_block(mate_keys):
        return (
            jnp.einsum("qhgd,khd->qhgk", query_heads, mate_keys, preferred_element_type=jnp.float32)
            * score_scale
        )

    def forward_step(slot_index, running):
        running_max, denominator, weighted = running
        mate_keys, mate_values = partner_block_tile(slot_index)
        scores = score_block(mate_keys)
        new_max = jnp.maximum(running_max, jnp.max(scores, -1))
        rescale = jnp.exp(running_max - new_max)
        weights = jnp.exp(scores - new_max[..., None])
        denominator = denominator * rescale + jnp.sum(weights, -1)
        weighted = weighted * rescale[..., None] + jnp.einsum(
            "qhgk,khd->qhgd",
            weights.astype(jnp.bfloat16),
            mate_values,
            preferred_element_type=jnp.float32,
        )
        return (new_max, denominator, weighted)

    stat_shape = (seq_len, kv_heads, per_group)
    start_state = (
        jnp.full(stat_shape, NEG_FLOOR, jnp.float32),
        jnp.zeros(stat_shape, jnp.float32),
        jnp.zeros(stat_shape + (HD,), jnp.float32),
    )
    running_max, denominator, weighted = lax.fori_loop(0, live_count, forward_step, start_state)
    attention = (weighted / denominator[..., None]).astype(jnp.bfloat16)
    log_total = running_max + jnp.log(denominator)
    attention_flat = attention.reshape(seq_len, -1).astype(jnp.float32)
    square_sums = lax.psum(jnp.sum(attention_flat * attention_flat, -1), "head")
    inverse_rms = lax.rsqrt(square_sums / D + EPSILON)
    normed_out = (attention_flat * inverse_rms[:, None] * norm_gain).astype(jnp.bfloat16)[None]
    scaled_grad = out_grad[0].astype(jnp.float32) * norm_gain
    dot_sums = lax.psum(jnp.sum(attention_flat * scaled_grad, -1), "head")
    attention_grad = (
        inverse_rms[:, None] * scaled_grad
        - attention_flat * (inverse_rms**3 * dot_sums / D)[:, None]
    )
    attention_grad = attention_grad.astype(jnp.bfloat16).reshape(seq_len, kv_heads, per_group, HD)
    row_delta = jnp.sum(attention_grad.astype(jnp.float32) * attention.astype(jnp.float32), -1)

    def backward_step(slot_index, running):
        query_grad, key_buffer, value_storage = running
        mate_keys, mate_values = partner_block_tile(slot_index)
        back_probs = jnp.exp(score_block(mate_keys) - log_total[..., None])
        value_term = jnp.einsum(
            "qhgk,qhgd->khd",
            back_probs.astype(jnp.bfloat16),
            attention_grad,
            preferred_element_type=jnp.float32,
        )
        prob_grad = jnp.einsum(
            "qhgd,khd->qhgk", attention_grad, mate_values, preferred_element_type=jnp.float32
        )
        score_grad = (back_probs * (prob_grad - row_delta[..., None])).astype(jnp.bfloat16)
        query_grad = query_grad + score_scale * jnp.einsum(
            "qhgk,khd->qhgd", score_grad, mate_keys, preferred_element_type=jnp.float32
        )
        key_term = score_scale * jnp.einsum(
            "qhgk,qhgd->khd", score_grad, query_heads, preferred_element_type=jnp.float32
        )
        mate_row = mate_rows[slot_index]
        key_buffer = add_row(key_buffer, key_term.reshape(seq_len, kv_cols), mate_row)
        value_storage = add_row(value_storage, value_term.reshape(seq_len, kv_cols), mate_row)
        return (query_grad, key_buffer, value_storage)

    zero_buffer = jnp.zeros((GROUP, seq_len, kv_cols), jnp.float32)
    query_grad, key_buffer, value_storage = lax.fori_loop(
        0,
        live_count,
        backward_step,
        (jnp.zeros(stat_shape + (HD,), jnp.float32), zero_buffer, zero_buffer),
    )
    query_grads = query_grad.reshape(seq_len, -1).astype(jnp.bfloat16)[None]
    return_bits = list(reversed(range(levels)))
    key_total, value_total = (key_buffer, value_storage)
    for bit_number in return_bits:
        half_rows = key_total.shape[0] // 2
        is_upper = my_index >> bit_number & 1 == 1
        key_low, key_high = (key_total[:half_rows], key_total[half_rows:])
        value_low, value_high = (value_total[:half_rows], value_total[half_rows:])
        keep_keys = jnp.where(is_upper, key_high, key_low)
        give_keys = jnp.where(is_upper, key_low, key_high)
        keep_values = jnp.where(is_upper, value_high, value_low)
        give_values = jnp.where(is_upper, value_low, value_high)
        got_keys, got_values = (
            partner(give_keys.astype(jnp.bfloat16), "resp", bit_number).astype(give_keys.dtype),
            partner(give_values.astype(jnp.bfloat16), "resp", bit_number).astype(give_values.dtype),
        )
        key_total = keep_keys + got_keys
        value_total = keep_values + got_values
    return (
        normed_out,
        query_grads,
        key_total.astype(jnp.bfloat16),
        value_total.astype(jnp.bfloat16),
    )


def solution(mesh):
    placed = (
        P("resp", None, "head"),
        P("resp", None, "head"),
        P("resp", None, "head"),
        P("resp", None),
        P("resp"),
        P("head"),
        P("resp", None, "head"),
    )
    return jax.shard_map(
        body,
        mesh=mesh,
        in_specs=placed,
        out_specs=(
            P("resp", None, "head"),
            P("resp", None, "head"),
            P("resp", None, "head"),
            P("resp", None, "head"),
        ),
        check_vma=False,
    )
```

profile of v0, /device:TPU:1, one launch (start us, length us, event | category | flops | bytes accessed | tf_op | source)
XLA Modules:
  0.0 195.4 jit_solution(12113924337441914545)
XLA Ops:
  0.6 3.3 %collective-permute-start = (bf16[1,512,128]{2,1,0:T(8,128)(2,1)}, bf16[1,512,128]{2,1,0:T(8,128)(2,1)S(1)}, u32[]{:S(2)}, u32[]{:S(2)}) collective-permute-start(bf16[1,512,128]{2,1,0:T(8,128)(2,1)} %param.12), channel_id=1, source_target_pairs={{0,8},{8,0},{16,24},{24,16},{32,40},{40,32},{48,56},{56,48},{64,72... | collective-permute-start | bytes 393224 | tf_op jit(solution)/shard_map/ppermute | solution.py:22
  4.1 1.1 collective-permute-done
  5.2 1.0 maximum_select_fusion.4
  6.3 1.0 maximum_select_fusion.5
  7.3 1.5 collective-permute-start.4
  8.8 5.0 %collective-permute-done.1 = bf16[2,512,128]{2,1,0:T(8,128)(2,1)S(1)} collective-permute-done((bf16[2,512,128]{2,1,0:T(8,128)(2,1)S(1)}, bf16[2,512,128]{2,1,0:T(8,128)(2,1)S(1)}, u32[]{:S(2)}, u32[]{:S(2)}) %collective-permute-start.1) | collective-permute-done | bytes 262176 | tf_op jit(solution)/shard_map/ppermute | solution.py:22
  13.9 1.1 collective-permute-start.2
  15.0 4.4 %collective-permute-done.4 = bf16[2,512,128]{2,1,0:T(8,128)(2,1)S(1)} collective-permute-done((bf16[2,512,128]{2,1,0:T(8,128)(2,1)S(1)}, bf16[2,512,128]{2,1,0:T(8,128)(2,1)S(1)}, u32[]{:S(2)}, u32[]{:S(2)}) %collective-permute-start.4) | collective-permute-done | bytes 262176 | tf_op jit(solution)/shard_map/ppermute | solution.py:22
  19.5 1.1 collective-permute-start.5
  20.6 1.3 copy.25
  21.9 1.5 copy.21
  23.4 0.7 copy.22
  24.1 7.1 %collective-permute-done.2 = bf16[4,512,128]{2,1,0:T(8,128)(2,1)} collective-permute-done((bf16[4,512,128]{2,1,0:T(8,128)(2,1)S(1)}, bf16[4,512,128]{2,1,0:T(8,128)(2,1)}, u32[]{:S(2)}, u32[]{:S(2)}) %collective-permute-start.2) | collective-permute-done | bytes 524320 | tf_op jit(solution)/shard_map/ppermute | solution.py:22
  31.2 2.4 %maximum_select_fusion = bf16[8,512,128]{2,1,0:T(8,128)(2,1)} fusion(bf16[4,512,128]{2,1,0:T(8,128)(2,1)S(1)} %maximum_select_fusion.2, bf16[4,512,128]{2,1,0:T(8,128)(2,1)} %collective-permute-done.2, pred[]{:T(512)S(6)} %eq.14), kind=kLoop, calls=%fused_computation.69 | loop fusion | flops 1572864 | bytes 2097153 | tf_op jit(solution)/shard_map/jit(_where)/select_n | solution.py:44
  33.6 8.9 %collective-permute-done.5 = bf16[4,512,128]{2,1,0:T(8,128)(2,1)} collective-permute-done((bf16[4,512,128]{2,1,0:T(8,128)(2,1)S(1)}, bf16[4,512,128]{2,1,0:T(8,128)(2,1)}, u32[]{:S(2)}, u32[]{:S(2)}) %collective-permute-start.5) | collective-permute-done | bytes 524320 | tf_op jit(solution)/shard_map/ppermute | solution.py:22
  42.5 2.4 %maximum_select_fusion.1 = bf16[8,512,128]{2,1,0:T(8,128)(2,1)} fusion(bf16[4,512,128]{2,1,0:T(8,128)(2,1)S(1)} %maximum_select_fusion.3, bf16[4,512,128]{2,1,0:T(8,128)(2,1)} %collective-permute-done.5, pred[]{:T(512)S(6)} %eq.14), kind=kLoop, calls=%fused_computation.70 | loop fusion | flops 1572864 | bytes 2097153 | tf_op jit(solution)/shard_map/jit(_where)/select_n | solution.py:49
  45.2 20.3 %while.28 = (s32[]{:T(128)}, f32[512,1,8]{0,2,1:T(8,128)S(1)}, f32[512,1,8]{0,2,1:T(8,128)S(1)}, f32[512,1,8,128]{0,3,2,1:T(8,128)S(1)}, s32[]{:T(128)}, /*index...) while((s32[]{:T(128)}, f32[512,1,8]{0,2,1:T(8,128)S(1)}, ...), condition=%wide.region_3.4_spmd, body=%wide.region_0.3_spmd.sunk | while | flops 1091579904 | bytes 30933212 | solution.py:97
  45.8 0.7 dynamic_slice.62
  48.3 2.2 %bitcast_reduce_fusion.2 = (f32[512,8]{0,1:T(8,128)S(1)}, f32[512,512,8]{1,0,2:T(8,128)S(1)}) fusion(bf16[512,1,8,128]{3,0,2,1:T(8,128)(2,1)S(1)} %get-tuple-element.379, bf16[8,512,128]{2,1,0:T(8,128)(2,1)} %get-tuple-element.378, s32[]{:T(128)S(6)} %select_n.191), kind=kOutput, calls=%fused_computation.1.clone.1 | convolution fusion | flops 541061120 | bytes 9584644 | tf_op jit(solution)/shard_map/while/body/qhgd,khd->qhgk/dot_general | solution.py:71
  50.5 1.4 fusion.88
  51.9 3.0 %bitcast_add_fusion.7 = f32[512,1,8,128]{0,3,2,1:T(8,128)S(1)} fusion(f32[512,1,8,128]{0,3,2,1:T(8,128)S(1)} %get-tuple-element.362, f32[512,512,8]{1,0,2:T(8,128)S(1)} %get-tuple-element.332, f32[512,8]{0,1:T(8,128)S(1)} %bitcast.240, f32[512,8]{0,1:T(8,128)S(1)} %get-tuple-element.333, bf16[8,512,128]{2,1,0:T(8,128)(2,1)} %get-tuple-element.380, ...), kind=kOutput, calls=%fused_computation.9.clone.1 | convolution fusion | flops 544210944 | bytes 12746756 | tf_op jit(solution)/shard_map/while/body/qhgk,khd->qhgd/dot_general | solution.py:83
  55.6 0.7 dynamic_slice.62
  58.2 2.2 %bitcast_reduce_fusion.2 = (f32[512,8]{0,1:T(8,128)S(1)}, f32[512,512,8]{1,0,2:T(8,128)S(1)}) fusion(bf16[512,1,8,128]{3,0,2,1:T(8,128)(2,1)S(1)} %get-tuple-element.379, bf16[8,512,128]{2,1,0:T(8,128)(2,1)} %get-tuple-element.378, s32[]{:T(128)S(6)} %select_n.191), kind=kOutput, calls=%fused_computation.1.clone.1 | convolution fusion | flops 541061120 | bytes 9584644 | tf_op jit(solution)/shard_map/while/body/qhgd,khd->qhgk/dot_general | solution.py:71
  60.4 1.4 fusion.88
  61.8 3.0 %bitcast_add_fusion.7 = f32[512,1,8,128]{0,3,2,1:T(8,128)S(1)} fusion(f32[512,1,8,128]{0,3,2,1:T(8,128)S(1)} %get-tuple-element.362, f32[512,512,8]{1,0,2:T(8,128)S(1)} %get-tuple-element.332, f32[512,8]{0,1:T(8,128)S(1)} %bitcast.240, f32[512,8]{0,1:T(8,128)S(1)} %get-tuple-element.333, bf16[8,512,128]{2,1,0:T(8,128)(2,1)} %get-tuple-element.380, ...), kind=kOutput, calls=%fused_computation.9.clone.1 | convolution fusion | flops 544210944 | bytes 12746756 | tf_op jit(solution)/shard_map/while/body/qhgk,khd->qhgd/dot_general | solution.py:83
  65.5 2.7 %fusion.60 = (f32[512]{0:T(512)S(1)}, f32[512]{0:T(512)S(1)}, bf16[512,1,8,128]{0,3,2,1:T(8,128)(2,1)}) fusion(bf16[512,1,8,128]{0,3,2,1:T(8,128)(2,1)} %bitcast.241, f32[8,128]{1,0:T(8,128)S(1)} %bitcast.249, f32[512,1,8,128]{0,3,2,1:T(8,128)S(1)} %get-tuple-element.119, f32[512,8]{0,1:T(8,128)S(1)} %bitcast.246), kind=kLoop, calls=%fused_computation.61 | loop fusion | flops 4717568 | bytes 4218880 | tf_op jit(solution)/shard_map/reduce_sum | solution.py:105
  68.2 16.5 %all-reduce = (f32[512]{0:T(512)S(1)}, f32[512]{0:T(512)S(1)}) all-reduce(f32[512]{0:T(512)S(1)} %get-tuple-element.156, f32[512]{0:T(512)S(1)} %get-tuple-element.155), channel_id=1, replica_groups=mesh['resp'=32,'head'=8] {'head'}, use_global_device_ids=true, to_apply=%region_5.6 | all-reduce | flops 1024 | bytes 8192 | tf_op jit(solution)/shard_map/psum | solution.py:101
  84.8 2.0 %fusion.59 = bf16[512,1,8,128]{0,3,2,1:T(8,128)(2,1)S(1)} fusion(bf16[512,1,8,128]{0,3,2,1:T(8,128)(2,1)} %get-tuple-element.203, f32[512]{0:T(512)S(1)} %get-tuple-element.206, f32[8,128]{1,0:T(8,128)S(1)} %bitcast.250, f32[512]{0:T(512)S(1)} %get-tuple-element.207, bf16[1,512,1024]{1,2,0:T(8,128)(2,1)} %copy.25), kind=kLoop, calls=%fused_computation.60 | loop fusion | flops 3670016 | bytes 3153920 | tf_op jit(solution)/shard_map/convert_element_type | solution.py:110
  86.8 1.0 copy-done.5
  87.8 0.3 fusion.62
  88.1 1.6 copy.27
  89.7 1.6 copy.24
  91.3 1.5 broadcast_in_dim.12.clone
  92.8 1.5 broadcast_in_dim.12
  94.3 1.6 broadcast.131
  95.9 36.8 %while.29 = (s32[]{:T(128)}, f32[512,1,8,128]{0,3,2,1:T(8,128)}, f32[8,512,128]{2,1,0:T(8,128)}, f32[8,512,128]{2,1,0:T(8,128)}, s32[]{:T(128)}, /*index=5*/s32[...) while((s32[]{:T(128)}, f32[512,1,8,128]{0,3,2,1:T(8,128)}, ...), condition=%wide.region_10.11_spmd, body=%wide.region_9.10_spmd.sunk | while | flops 2702376960 | bytes 64405816 | solution.py:139
  96.6 0.6 dynamic_slice.68
  99.1 2.2 %fusion.99 = f32[512,512,8]{1,0,2:T(8,128)S(1)} fusion(bf16[512,1,8,128]{3,0,2,1:T(8,128)(2,1)S(1)} %get-tuple-element.424, bf16[8,512,128]{2,1,0:T(8,128)(2,1)} %get-tuple-element.423, s32[]{:T(128)S(6)} %select_n.193), kind=kOutput, calls=%fused_computation.44.clone.1 | convolution fusion | flops 536870912 | bytes 9568260 | tf_op jit(solution)/shard_map/while/body/qhgd,khd->qhgk/dot_general | solution.py:71
  101.3 3.2 %fusion.102 = f32[8,512,128]{2,1,0:T(8,128)} fusion(f32[8,512,128]{2,1,0:T(8,128)} %get-tuple-element.404, s32[]{:T(128)S(6)} %select_n.193, f32[512,512,8]{1,0,2:T(8,128)S(1)} %fusion.99, f32[512,8]{0,1:T(8,128)S(1)} %bitcast.242, bf16[512,1,8,128]{3,0,2,1:T(8,128)(2,1)S(1)} %get-tuple-element.427), kind=kOutput, calls=%fused_computation.38.clone.1 | convolution fusion | flops 543227904 | bytes 9977860 | tf_op jit(solution)/shard_map/while/body/qhgk,qhgd->khd/dot_general | solution.py:117
  104.5 3.1 %fusion.100 = bf16[512,8,512]{0,2,1:T(8,128)(2,1)S(1)} fusion(f32[512,512,8]{1,0,2:T(8,128)S(1)} %fusion.99, f32[512,8]{0,1:T(8,128)S(1)} %bitcast.248, f32[512,8]{0,1:T(8,128)S(1)} %bitcast.243, bf16[512,1,8,128]{3,0,2,1:T(8,128)(2,1)S(1)} %get-tuple-element.427, bf16[8,512,128]{2,1,0:T(8,128)(2,1)} %get-tuple-element.426, s32[]{:T(128)S(6)} %select_n.193), kind=kOutput, calls=%fused_computation.30.clone.1 | convolution fusion | flops 547356672 | bytes 13795332 | tf_op jit(solution)/shard_map/while/body/qhgd,khd->qhgk/dot_general | solution.py:123
  107.6 3.1 %fusion.101 = f32[8,512,128]{2,1,0:T(8,128)} fusion(f32[8,512,128]{2,1,0:T(8,128)} %get-tuple-element.403, s32[]{:T(128)S(6)} %select_n.193, bf16[512,8,512]{0,2,1:T(8,128)(2,1)S(1)} %fusion.100, bf16[512,1,8,128]{3,0,2,1:T(8,128)(2,1)S(1)} %get-tuple-element.424), kind=kOutput, calls=%fused_computation.40.clone.1 | convolution fusion | flops 537001984 | bytes 5767172 | tf_op jit(solution)/shard_map/while/body/qhgk,qhgd->khd/dot_general | solution.py:130
  110.7 2.0 %bitcast_add_fusion.8 = f32[512,1,8,128]{0,3,2,1:T(8,128)S(1)} fusion(f32[512,1,8,128]{0,3,2,1:T(8,128)S(1)} %copy-done, bf16[512,8,512]{0,2,1:T(8,128)(2,1)S(1)} %fusion.100, bf16[8,512,128]{2,1,0:T(8,128)(2,1)} %get-tuple-element.423, s32[]{:T(128)S(6)} %select_n.193), kind=kOutput, calls=%fused_computation.32.clone.1 | convolution fusion | flops 537919488 | bytes 8519684 | tf_op jit(solution)/shard_map/while/body/qhgk,khd->qhgd/dot_general | solution.py:127
  112.7 1.3 copy-done.1
  114.7 0.6 dynamic_slice.68
  117.2 2.2 %fusion.99 = f32[512,512,8]{1,0,2:T(8,128)S(1)} fusion(bf16[512,1,8,128]{3,0,2,1:T(8,128)(2,1)S(1)} %get-tuple-element.424, bf16[8,512,128]{2,1,0:T(8,128)(2,1)} %get-tuple-element.423, s32[]{:T(128)S(6)} %select_n.193), kind=kOutput, calls=%fused_computation.44.clone.1 | convolution fusion | flops 536870912 | bytes 9568260 | tf_op jit(solution)/shard_map/while/body/qhgd,khd->qhgk/dot_general | solution.py:71
  119.4 3.3 %fusion.102 = f32[8,512,128]{2,1,0:T(8,128)} fusion(f32[8,512,128]{2,1,0:T(8,128)} %get-tuple-element.404, s32[]{:T(128)S(6)} %select_n.193, f32[512,512,8]{1,0,2:T(8,128)S(1)} %fusion.99, f32[512,8]{0,1:T(8,128)S(1)} %bitcast.242, bf16[512,1,8,128]{3,0,2,1:T(8,128)(2,1)S(1)} %get-tuple-element.427), kind=kOutput, calls=%fused_computation.38.clone.1 | convolution fusion | flops 543227904 | bytes 9977860 | tf_op jit(solution)/shard_map/while/body/qhgk,qhgd->khd/dot_general | solution.py:117
  122.6 3.1 %fusion.100 = bf16[512,8,512]{0,2,1:T(8,128)(2,1)S(1)} fusion(f32[512,512,8]{1,0,2:T(8,128)S(1)} %fusion.99, f32[512,8]{0,1:T(8,128)S(1)} %bitcast.248, f32[512,8]{0,1:T(8,128)S(1)} %bitcast.243, bf16[512,1,8,128]{3,0,2,1:T(8,128)(2,1)S(1)} %get-tuple-element.427, bf16[8,512,128]{2,1,0:T(8,128)(2,1)} %get-tuple-element.426, s32[]{:T(128)S(6)} %select_n.193), kind=kOutput, calls=%fused_computation.30.clone.1 | convolution fusion | flops 547356672 | bytes 13795332 | tf_op jit(solution)/shard_map/while/body/qhgd,khd->qhgk/dot_general | solution.py:123
  125.7 3.1 %fusion.101 = f32[8,512,128]{2,1,0:T(8,128)} fusion(f32[8,512,128]{2,1,0:T(8,128)} %get-tuple-element.403, s32[]{:T(128)S(6)} %select_n.193, bf16[512,8,512]{0,2,1:T(8,128)(2,1)S(1)} %fusion.100, bf16[512,1,8,128]{3,0,2,1:T(8,128)(2,1)S(1)} %get-tuple-element.424), kind=kOutput, calls=%fused_computation.40.clone.1 | convolution fusion | flops 537001984 | bytes 5767172 | tf_op jit(solution)/shard_map/while/body/qhgk,qhgd->khd/dot_general | solution.py:130
  128.8 2.0 %bitcast_add_fusion.8 = f32[512,1,8,128]{0,3,2,1:T(8,128)S(1)} fusion(f32[512,1,8,128]{0,3,2,1:T(8,128)S(1)} %copy-done, bf16[512,8,512]{0,2,1:T(8,128)(2,1)S(1)} %fusion.100, bf16[8,512,128]{2,1,0:T(8,128)(2,1)} %get-tuple-element.423, s32[]{:T(128)S(6)} %select_n.193), kind=kOutput, calls=%fused_computation.32.clone.1 | convolution fusion | flops 537919488 | bytes 8519684 | tf_op jit(solution)/shard_map/while/body/qhgk,khd->qhgd/dot_general | solution.py:127
  130.8 1.3 copy-done.1
  132.8 1.7 convert_element_type.138
  134.5 1.3 copy.33
  135.8 1.8 select_convert_fusion.1
  137.6 0.6 collective-permute-start.6
  138.3 2.5 %collective-permute-start.9 = (bf16[4,512,128]{2,1,0:T(8,128)(2,1)S(1)}, bf16[4,512,128]{2,1,0:T(8,128)(2,1)S(1)}, u32[]{:S(2)}, u32[]{:S(2)}) collective-permute-start(bf16[4,512,128]{2,1,0:T(8,128)(2,1)S(1)} %select_convert_fusion), channel_id=1, source_target_pairs={{0,32},{32,0},{8,40},{40,8},{16,48},{48,16},{24,56},{56,24},{64,96... | collective-permute-start | bytes 1572872 | tf_op jit(solution)/shard_map/ppermute | solution.py:22
  140.8 1.2 multiply_convert_fusion
  142.1 5.2 %collective-permute-done.6 = bf16[4,512,128]{2,1,0:T(8,128)(2,1)S(1)} collective-permute-done((bf16[4,512,128]{2,1,0:T(8,128)(2,1)S(1)}, bf16[4,512,128]{2,1,0:T(8,128)(2,1)S(1)}, u32[]{:S(2)}, u32[]{:S(2)}) %collective-permute-start.6) | collective-permute-done | bytes 524320 | tf_op jit(solution)/shard_map/ppermute | solution.py:22
  147.5 5.3 %collective-permute-done.9 = bf16[4,512,128]{2,1,0:T(8,128)(2,1)S(1)} collective-permute-done((bf16[4,512,128]{2,1,0:T(8,128)(2,1)S(1)}, bf16[4,512,128]{2,1,0:T(8,128)(2,1)S(1)}, u32[]{:S(2)}, u32[]{:S(2)}) %collective-permute-start.9) | collective-permute-done | bytes 524320 | tf_op jit(solution)/shard_map/ppermute | solution.py:22
  153.2 0.3 collective-permute-done.7
  153.6 34.5 %collective-permute-start.8 = (bf16[1,512,128]{2,1,0:T(8,128)(2,1)S(1)}, bf16[1,512,128]{2,1,0:T(8,128)(2,1)S(1)}, u32[]{:S(2)}, u32[]{:S(2)}) collective-permute-start(bf16[1,512,128]{2,1,0:T(8,128)(2,1)S(1)} %select_convert_fusion.5), channel_id=1, source_target_pairs={{0,8},{8,0},{16,24},{24,16},{32,40},{40,32},{48,56},{56,48},{64,72... | collective-permute-start | bytes 393224 | tf_op jit(solution)/shard_map/ppermute | solution.py:22
  188.2 5.5 %collective-permute-start.11 = (bf16[1,512,128]{2,1,0:T(8,128)(2,1)S(1)}, bf16[1,512,128]{2,1,0:T(8,128)(2,1)S(1)}, u32[]{:S(2)}, u32[]{:S(2)}) collective-permute-start(bf16[1,512,128]{2,1,0:T(8,128)(2,1)S(1)} %select_convert_fusion.4), channel_id=1, source_target_pairs={{0,8},{8,0},{16,24},{24,16},{32,40},{40,32},{48,56},{56,48},{64,72... | collective-permute-start | bytes 393224 | tf_op jit(solution)/shard_map/ppermute | solution.py:22
  193.8 0.7 add_convert_fusion.1
  194.5 0.3 collective-permute-done.11
  194.7 0.7 add_convert_fusion
  (51 shorter events, 1.6 us)
Async XLA Ops:
  0.6 20.0 %copy-start.7 = (bf16[1,512,1024]{2,1,0:T(8,128)(2,1)S(1)}, bf16[1,512,1024]{2,1,0:T(8,128)(2,1)}, u32[]{:S(2)}) copy-start(bf16[1,512,1024]{2,1,0:T(8,128)(2,1)} %param.17) | copy-start | bytes 3145732
  0.6 4.5 %collective-permute-start = (bf16[1,512,128]{2,1,0:T(8,128)(2,1)}, bf16[1,512,128]{2,1,0:T(8,128)(2,1)S(1)}, u32[]{:S(2)}, u32[]{:S(2)}) collective-permute-start(bf16[1,512,128]{2,1,0:T(8,128)(2,1)} %param.12), channel_id=1, source_target_pairs={{0,8},{8,0},{16,24},{24,16},{32,40},{40,32},{48,56},{56,48},{64,72... | collective-permute-start | bytes 393224 | tf_op jit(solution)/shard_map/ppermute | solution.py:22
  4.0 2.3 %collective-permute-start.3 = (bf16[1,512,128]{2,1,0:T(8,128)(2,1)}, bf16[1,512,128]{2,1,0:T(8,128)(2,1)S(1)}, u32[]{:S(2)}, u32[]{:S(2)}) collective-permute-start(bf16[1,512,128]{2,1,0:T(8,128)(2,1)} %param.13), channel_id=1, source_target_pairs={{0,8},{8,0},{16,24},{24,16},{32,40},{40,32},{48,56},{56,48},{64,72... | collective-permute-start | bytes 393224 | tf_op jit(solution)/shard_map/ppermute | solution.py:22
  6.2 7.6 %collective-permute-start.1 = (bf16[2,512,128]{2,1,0:T(8,128)(2,1)S(1)}, bf16[2,512,128]{2,1,0:T(8,128)(2,1)S(1)}, u32[]{:S(2)}, u32[]{:S(2)}) collective-permute-start(bf16[2,512,128]{2,1,0:T(8,128)(2,1)S(1)} %maximum_select_fusion.4), channel_id=1, source_target_pairs={{0,16},{16,0},{8,24},{24,8},{32,48},{48,32},{40,56},{56,40},{64,80... | collective-permute-start | bytes 786440 | tf_op jit(solution)/shard_map/ppermute | solution.py:22
  7.3 12.1 %collective-permute-start.4 = (bf16[2,512,128]{2,1,0:T(8,128)(2,1)S(1)}, bf16[2,512,128]{2,1,0:T(8,128)(2,1)S(1)}, u32[]{:S(2)}, u32[]{:S(2)}) collective-permute-start(bf16[2,512,128]{2,1,0:T(8,128)(2,1)S(1)} %maximum_select_fusion.5), channel_id=1, source_target_pairs={{0,16},{16,0},{8,24},{24,8},{32,48},{48,32},{40,56},{56,40},{64,80... | collective-permute-start | bytes 786440 | tf_op jit(solution)/shard_map/ppermute | solution.py:22
  13.9 17.3 %collective-permute-start.2 = (bf16[4,512,128]{2,1,0:T(8,128)(2,1)S(1)}, bf16[4,512,128]{2,1,0:T(8,128)(2,1)}, u32[]{:S(2)}, u32[]{:S(2)}) collective-permute-start(bf16[4,512,128]{2,1,0:T(8,128)(2,1)S(1)} %maximum_select_fusion.2), channel_id=1, source_target_pairs={{0,32},{32,0},{8,40},{40,8},{16,48},{48,16},{24,56},{56,24},{64,96... | collective-permute-start | bytes 1572872 | tf_op jit(solution)/shard_map/ppermute | solution.py:22
  19.5 22.9 %collective-permute-start.5 = (bf16[4,512,128]{2,1,0:T(8,128)(2,1)S(1)}, bf16[4,512,128]{2,1,0:T(8,128)(2,1)}, u32[]{:S(2)}, u32[]{:S(2)}) collective-permute-start(bf16[4,512,128]{2,1,0:T(8,128)(2,1)S(1)} %maximum_select_fusion.3), channel_id=1, source_target_pairs={{0,32},{32,0},{8,40},{40,8},{16,48},{48,16},{24,56},{56,24},{64,96... | collective-permute-start | bytes 1572872 | tf_op jit(solution)/shard_map/ppermute | solution.py:22
  21.9 2.2 %copy-start.9 = (s32[1,3]{1,0:T(1,128)S(1)}, s32[1,3]{1,0:T(1,128)}, u32[]{:S(2)}) copy-start(s32[1,3]{1,0:T(1,128)} %param.14) | copy-start | bytes 40
  45.1 20.3 %copy-start.8 = (f32[1024]{0:T(1024)S(1)}, f32[1024]{0:T(1024)}, u32[]{:S(2)}) copy-start(f32[1024]{0:T(1024)} %param.16) | copy-start | bytes 12292
  68.2 19.6 %copy-start.4 = (bf16[512,1,8,128]{0,3,2,1:T(8,128)(2,1)S(1)}, bf16[512,1,8,128]{0,3,2,1:T(8,128)(2,1)}, u32[]{:S(2)}) copy-start(bf16[512,1,8,128]{0,3,2,1:T(8,128)(2,1)} %get-tuple-element.203) | copy-start | bytes 3145732
  86.8 1.0 copy-start.5
  107.6 3.1 %copy-start = (f32[512,1,8,128]{0,3,2,1:T(8,128)S(1)}, f32[512,1,8,128]{0,3,2,1:T(8,128)}, u32[]{:S(2)}) copy-start(f32[512,1,8,128]{0,3,2,1:T(8,128)} %get-tuple-element.402) | copy-start | bytes 6291460 | tf_op jit(solution)/shard_map/while
  112.7 1.3 copy-start.1
  125.7 3.1 %copy-start = (f32[512,1,8,128]{0,3,2,1:T(8,128)S(1)}, f32[512,1,8,128]{0,3,2,1:T(8,128)}, u32[]{:S(2)}) copy-start(f32[512,1,8,128]{0,3,2,1:T(8,128)} %get-tuple-element.402) | copy-start | bytes 6291460 | tf_op jit(solution)/shard_map/while
  130.8 1.3 copy-start.1
  134.5 3.7 %copy-start.2 = (f32[8,512,128]{2,1,0:T(8,128)S(1)}, f32[8,512,128]{2,1,0:T(8,128)}, u32[]{:S(2)}) copy-start(f32[8,512,128]{2,1,0:T(8,128)} %get-tuple-element.124) | copy-start | bytes 6291460
  135.8 5.0 %copy-start.6 = (f32[1,512,1024]{2,1,0:T(8,128)S(1)}, f32[1,512,1024]{2,1,0:T(8,128)}, u32[]{:S(2)}) copy-start(f32[1,512,1024]{2,1,0:T(8,128)} %copy.24) | copy-start | bytes 6291460
  137.6 9.6 %collective-permute-start.6 = (bf16[4,512,128]{2,1,0:T(8,128)(2,1)S(1)}, bf16[4,512,128]{2,1,0:T(8,128)(2,1)S(1)}, u32[]{:S(2)}, u32[]{:S(2)}) collective-permute-start(bf16[4,512,128]{2,1,0:T(8,128)(2,1)S(1)} %select_convert_fusion.1), channel_id=1, source_target_pairs={{0,32},{32,0},{8,40},{40,8},{16,48},{48,16},{24,56},{56,24},{64,96... | collective-permute-start | bytes 1572872 | tf_op jit(solution)/shard_map/ppermute | solution.py:22
  138.2 9.0 %copy-start.3 = (f32[8,512,128]{2,1,0:T(8,128)S(1)}, f32[8,512,128]{2,1,0:T(8,128)}, u32[]{:S(2)}) copy-start(f32[8,512,128]{2,1,0:T(8,128)} %get-tuple-element.123) | copy-start | bytes 6291460
  138.3 14.5 %collective-permute-start.9 = (bf16[4,512,128]{2,1,0:T(8,128)(2,1)S(1)}, bf16[4,512,128]{2,1,0:T(8,128)(2,1)S(1)}, u32[]{:S(2)}, u32[]{:S(2)}) collective-permute-start(bf16[4,512,128]{2,1,0:T(8,128)(2,1)S(1)} %select_convert_fusion), channel_id=1, source_target_pairs={{0,32},{32,0},{8,40},{40,8},{16,48},{48,16},{24,56},{56,24},{64,96... | collective-permute-start | bytes 1572872 | tf_op jit(solution)/shard_map/ppermute | solution.py:22
  147.4 6.1 %collective-permute-start.7 = (bf16[2,512,128]{2,1,0:T(8,128)(2,1)S(1)}, bf16[2,512,128]{2,1,0:T(8,128)(2,1)S(1)}, u32[]{:S(2)}, u32[]{:S(2)}) collective-permute-start(bf16[2,512,128]{2,1,0:T(8,128)(2,1)S(1)} %select_convert_fusion.3), channel_id=1, source_target_pairs={{0,16},{16,0},{8,24},{24,8},{32,48},{48,32},{40,56},{56,40},{64,80... | collective-permute-start | bytes 786440 | tf_op jit(solution)/shard_map/ppermute | solution.py:22
  153.1 35.1 %collective-permute-start.10 = (bf16[2,512,128]{2,1,0:T(8,128)(2,1)S(1)}, bf16[2,512,128]{2,1,0:T(8,128)(2,1)S(1)}, u32[]{:S(2)}, u32[]{:S(2)}) collective-permute-start(bf16[2,512,128]{2,1,0:T(8,128)(2,1)S(1)} %select_convert_fusion.2), channel_id=1, source_target_pairs={{0,16},{16,0},{8,24},{24,8},{32,48},{48,32},{40,56},{56,40},{64,80... | collective-permute-start | bytes 786440 | tf_op jit(solution)/shard_map/ppermute | solution.py:22
  153.6 40.2 %collective-permute-start.8 = (bf16[1,512,128]{2,1,0:T(8,128)(2,1)S(1)}, bf16[1,512,128]{2,1,0:T(8,128)(2,1)S(1)}, u32[]{:S(2)}, u32[]{:S(2)}) collective-permute-start(bf16[1,512,128]{2,1,0:T(8,128)(2,1)S(1)} %select_convert_fusion.5), channel_id=1, source_target_pairs={{0,8},{8,0},{16,24},{24,16},{32,40},{40,32},{48,56},{56,48},{64,72... | collective-permute-start | bytes 393224 | tf_op jit(solution)/shard_map/ppermute | solution.py:22
  188.2 6.5 %collective-permute-start.11 = (bf16[1,512,128]{2,1,0:T(8,128)(2,1)S(1)}, bf16[1,512,128]{2,1,0:T(8,128)(2,1)S(1)}, u32[]{:S(2)}, u32[]{:S(2)}) collective-permute-start(bf16[1,512,128]{2,1,0:T(8,128)(2,1)S(1)} %select_convert_fusion.4), channel_id=1, source_target_pairs={{0,8},{8,0},{16,24},{24,16},{32,40},{40,32},{48,56},{56,48},{64,72... | collective-permute-start | bytes 393224 | tf_op jit(solution)/shard_map/ppermute | solution.py:22
where the time goes:
time: 196 us; the launch traced here: 195 us
  starting transfers between devices  50.6 us (26%)
  waiting for transfers between devices  37.6 us (19%)
  matrix products  37.4 us (19%)
  other arithmetic  21.7 us (11%)
  local copies, waits for them, and re-layouts  19 us (10%)
  blocking collectives  16.5 us (8%)
  loops' own time  11.8 us (6%)
    ppermute x12, starting transfers between devices, partner(): return lax.ppermute(block, axis, route)  50.6 us
    ppermute x12, waiting for transfers between devices, partner(): return lax.ppermute(block, axis, route)  37.6 us
    psum x1, blocking collectives, body(): square_sums = lax.psum(jnp.sum(attention_flat * attention_flat, -1), 'head')  16.5 us
    dot_general x4, matrix products, score_block(): jnp.einsum('qhgd,khd->qhgk', query_heads, mate_keys, preferred_element_ty...  8.65 us
    dot_general x2, matrix products, backward_step(): jnp.einsum('qhgk,qhgd->khd', back_probs.astype(jnp.bfloat16), attention_g...  6.51 us
    dot_general x2, matrix products, backward_step(): jnp.einsum('qhgd,khd->qhgk', attention_grad, mate_values, preferred_eleme...  6.19 us
    dot_general x2, matrix products, backward_step(): jnp.einsum('qhgk,qhgd->khd', score_grad, query_heads, preferred_element_t...  6.11 us
    dot_general x2, matrix products, forward_step(): jnp.einsum('qhgk,khd->qhgd', weights.astype(jnp.bfloat16), mate_values, p...  6.02 us
  transfers between devices with their start and end apart: 12, of which 9 were waited for; matrix products, arithmetic and copies ran while one was open for 5% of the time, Pallas kernels for 0%

commit v1 on v0

--- a/solution.py
+++ b/solution.py
@@ -12,16 +12,6 @@
 NEG_FLOOR = -1e30
 
 
-def partner(block, axis, apart):
-    count = lax.axis_size(axis)
-    route = []
-    for low in range(count):
-        high = low | 1 << apart
-        if high != low and high < count:
-            route += [(low, high), (high, low)]
-    return lax.ppermute(block, axis, route)
-
-
 def add_row(buffer, addend, row_index):
     current = lax.dynamic_index_in_dim(buffer, row_index, 0, keepdims=False)
     return lax.dynamic_update_index_in_dim(buffer, current + addend, row_index, 0)
@@ -29,31 +19,24 @@
 
 def body(queries, key_states, value_states, partners, counts, norm_gain, out_grad):
     my_index = lax.axis_index("resp")
-    my_place = my_index % GROUP
-    group_first = my_index - my_place
     seq_len = queries.shape[1]
     kv_cols = key_states.shape[2]
     kv_heads = kv_cols // HD
     per_group = queries.shape[2] // kv_cols
-    levels = GROUP.bit_length() - 1
-    fetch_bits = list(range(levels))
-    cluster_key_rows, group_values = (key_states, value_states)
-    for bit_number in fetch_bits:
-        other_keys, other_values = partner((cluster_key_rows, group_values), "resp", bit_number)
-        is_upper = my_index >> bit_number & 1 == 1
-        cluster_key_rows = jnp.where(
-            is_upper,
-            jnp.concatenate([other_keys, cluster_key_rows], 0),
-            jnp.concatenate([cluster_key_rows, other_keys], 0),
-        )
-        group_values = jnp.where(
-            is_upper,
-            jnp.concatenate([other_values, group_values], 0),
-            jnp.concatenate([group_values, other_values], 0),
-        )
+    resp_count = lax.axis_size("resp")
+
+    def by_distance(block):
+        rows = [block]
+        for distance in range(1, GROUP):
+            route = [(low, low ^ distance) for low in range(resp_count)]
+            rows.append(lax.ppermute(block, "resp", route))
+        return jnp.concatenate(rows, 0)
+
+    cluster_key_rows = by_distance(key_states)
+    group_values = by_distance(value_states)
     query_heads = queries[0].reshape(seq_len, kv_heads, per_group, HD)
     score_scale = HD ** (-0.5)
-    mate_rows = partners[0] - group_first
+    mate_rows = jnp.bitwise_xor(partners[0], my_index)
     live_count = counts[0]
 
     def partner_block_tile(slot_index):
@@ -143,23 +126,16 @@
         (jnp.zeros(stat_shape + (HD,), jnp.float32), zero_buffer, zero_buffer),
     )
     query_grads = query_grad.reshape(seq_len, -1).astype(jnp.bfloat16)[None]
-    return_bits = list(reversed(range(levels)))
-    key_total, value_total = (key_buffer, value_storage)
-    for bit_number in return_bits:
-        half_rows = key_total.shape[0] // 2
-        is_upper = my_index >> bit_number & 1 == 1
-        key_low, key_high = (key_total[:half_rows], key_total[half_rows:])
-        value_low, value_high = (value_total[:half_rows], value_total[half_rows:])
-        keep_keys = jnp.where(is_upper, key_high, key_low)
-        give_keys = jnp.where(is_upper, key_low, key_high)
-        keep_values = jnp.where(is_upper, value_high, value_low)
-        give_values = jnp.where(is_upper, value_low, value_high)
-        got_keys, got_values = (
-            partner(give_keys.astype(jnp.bfloat16), "resp", bit_number).astype(give_keys.dtype),
-            partner(give_values.astype(jnp.bfloat16), "resp", bit_number).astype(give_values.dtype),
-        )
-        key_total = keep_keys + got_keys
-        value_total = keep_values + got_values
+    def to_owners(buffer):
+        total = jnp.zeros(buffer.shape[1:], jnp.float32)
+        for distance in range(1, GROUP):
+            route = [(low, low ^ distance) for low in range(resp_count)]
+            sent = buffer[distance].astype(jnp.bfloat16)
+            total = total + lax.ppermute(sent, "resp", route).astype(jnp.float32)
+        return total[None]
+
+    key_total = to_owners(key_buffer)
+    value_total = to_owners(value_storage)
     return (
         normed_out,
         query_grads,

time: 196 us -> 201 us (1.026)
  matrix products: 37.4 us -> 56.2 us
  waiting for transfers between devices: 37.6 us -> 19.8 us
  local copies, waits for them, and re-layouts: 19 us -> 32.7 us
  starting transfers between devices: 50.6 us -> 41.3 us
  other arithmetic: 21.7 us -> 14.9 us
  loops' own time: 11.8 us -> 18 us
    ppermute x12 -> x28, waiting for transfers between devices: 37.6 us -> 19.8 us  [the longest x14 15 us: to_owners(): total = total + lax.ppermute(sent, 'resp', route).astype(jnp.float32)]
    unnamed x18 -> x36, local copies, waits for them, and re-layouts: 3.82 us -> 14 us
    ppermute x12 -> x28, starting transfers between devices: 50.6 us -> 41.3 us  [the longest x14 21.2 us: by_distance(): rows.append(lax.ppermute(block, 'resp', route))]
    select_n x6 -> x0, other arithmetic: 6.98 us -> none  [the longest x3 3.53 us: body(): jnp.where(is_upper, jnp.concatenate([other_values, group_values], 0), jnp...]
    dot_general x4 -> x6, matrix products: 8.65 us -> 13 us  [score_block(): jnp.einsum('qhgd,khd->qhgk', query_heads, mate_keys, preferred_element_ty...]
    another operation x1, loops' own time: 5.81 us -> 9.19 us  [body(): lax.fori_loop(0, live_count, forward_step, start_state)]
    dot_general x2 -> x3, matrix products: 6.51 us -> 9.79 us  [backward_step(): jnp.einsum('qhgk,qhgd->khd', back_probs.astype(jnp.bfloat16), attention_g...]
    dot_general x2 -> x3, matrix products: 6.19 us -> 9.3 us  [backward_step(): jnp.einsum('qhgd,khd->qhgk', attention_grad, mate_values, preferred_eleme...]
  transfers between devices with their start and end apart: 12 -> 28, of which waited for: 9 -> 9; matrix products, arithmetic and copies ran while one was open for 5% -> 9% of each run, Pallas kernels for 0% -> 0%
where the time goes in v1:
time: 201 us; the launch traced here: 200 us
  matrix products  56.2 us (28%)
  starting transfers between devices  41.3 us (21%)
  local copies, waits for them, and re-layouts  32.7 us (16%)
  waiting for transfers between devices  19.8 us (10%)
  loops' own time  18 us (9%)
  blocking collectives  15.9 us (8%)
  other arithmetic  14.9 us (7%)
    ppermute x14, starting transfers between devices, by_distance(): rows.append(lax.ppermute(block, 'resp', route))  21.2 us
    ppermute x14, starting transfers between devices, to_owners(): total = total + lax.ppermute(sent, 'resp', route).astype(jnp.float32)  20.2 us
    psum x1, blocking collectives, body(): square_sums = lax.psum(jnp.sum(attention_flat * attention_flat, -1), 'head')  15.9 us
    ppermute x14, waiting for transfers between devices, to_owners(): total = total + lax.ppermute(sent, 'resp', route).astype(jnp.float32)  15 us
    unnamed x36, local copies, waits for them, and re-layouts  14 us
    dot_general x6, matrix products, score_block(): jnp.einsum('qhgd,khd->qhgk', query_heads, mate_keys, preferred_element_ty...  13 us
    dot_general x3, matrix products, backward_step(): jnp.einsum('qhgk,qhgd->khd', back_probs.astype(jnp.bfloat16), attention_g...  9.79 us
    dot_general x3, matrix products, backward_step(): jnp.einsum('qhgd,khd->qhgk', attention_grad, mate_values, preferred_eleme...  9.3 us
  transfers between devices with their start and end apart: 28, of which 9 were waited for; matrix products, arithmetic and copies ran while one was open for 9% of the time, Pallas kernels for 0%

profile of v1, /device:TPU:1, one launch (start us, length us, event | category | flops | bytes accessed | tf_op | source)
XLA Modules:
  0.0 199.8 jit_solution(2755921004239567861)
XLA Ops:
  0.6 3.4 %collective-permute-start.5 = (bf16[1,512,128]{2,1,0:T(8,128)(2,1)}, bf16[1,512,128]{2,1,0:T(8,128)(2,1)S(1)}, u32[]{:S(2)}, u32[]{:S(2)}) collective-permute-start(bf16[1,512,128]{2,1,0:T(8,128)(2,1)} %param.12), channel_id=1, source_target_pairs={{0,48},{8,56},{16,32},{24,40},{32,16},{40,24},{48,0},{56,8},{64,11... | collective-permute-start | bytes 393224 | tf_op jit(solution)/shard_map/ppermute | solution.py:32
  4.0 1.4 collective-permute-start.4
  5.4 2.5 %collective-permute-start.3 = (bf16[1,512,128]{2,1,0:T(8,128)(2,1)}, bf16[1,512,128]{2,1,0:T(8,128)(2,1)}, u32[]{:S(2)}, u32[]{:S(2)}) collective-permute-start(bf16[1,512,128]{2,1,0:T(8,128)(2,1)} %param.12), channel_id=1, source_target_pairs={{0,32},{8,40},{16,48},{24,56},{32,0},{40,8},{48,16},{56,24},{64,96... | collective-permute-start | bytes 393224 | tf_op jit(solution)/shard_map/ppermute | solution.py:32
  9.7 1.6 constant_dynamic-update-slice_fusion.15
  11.2 2.3 %copy.25 = bf16[1,512,1024]{1,2,0:T(8,128)(2,1)} copy(bf16[1,512,1024]{2,1,0:T(8,128)(2,1)} %param.17) | data formatting | bytes 2097152 | tf_op args[6]
  14.8 1.7 collective-permute-start.2
  17.4 1.9 collective-permute-start.6
  20.3 1.9 collective-permute-start.12
  22.2 2.0 collective-permute-start.11
  25.1 1.7 collective-permute-start.10
  28.0 1.2 collective-permute-start.8
  31.0 3.2 %collective-permute-done.8 = bf16[1,512,128]{2,1,0:T(8,128)(2,1)S(1)} collective-permute-done((bf16[1,512,128]{2,1,0:T(8,128)(2,1)S(1)}, bf16[1,512,128]{2,1,0:T(8,128)(2,1)S(1)}, u32[]{:S(2)}, u32[]{:S(2)}) %collective-permute-start.8) | collective-permute-done | bytes 131104 | tf_op jit(solution)/shard_map/ppermute | solution.py:32
  34.3 2.0 %collective-permute-start.13 = (bf16[1,512,128]{2,1,0:T(8,128)(2,1)S(1)}, bf16[1,512,128]{2,1,0:T(8,128)(2,1)S(1)}, u32[]{:S(2)}, u32[]{:S(2)}) collective-permute-start(bf16[1,512,128]{2,1,0:T(8,128)(2,1)S(1)} %copy-done.10), channel_id=1, source_target_pairs={{0,56},{8,48},{16,40},{24,32},{32,24},{40,16},{48,8},{56,0},{64,12... | collective-permute-start | bytes 393224 | tf_op jit(solution)/shard_map/ppermute | solution.py:32
  39.8 1.3 collective-permute-done.13
  42.0 31.0 %while.28 = (s32[]{:T(128)}, f32[512,1,8]{0,2,1:T(8,128)S(1)}, f32[512,1,8]{0,2,1:T(8,128)S(1)}, f32[512,1,8,128]{0,3,2,1:T(8,128)S(1)}, s32[]{:T(128)}, /*index...) while((s32[]{:T(128)}, f32[512,1,8]{0,2,1:T(8,128)S(1)}, ...), condition=%wide.region_3.4_spmd, body=%wide.region_0.3_spmd.sunk | while | flops 1091579904 | bytes 30933212 | solution.py:80
  45.6 2.2 %bitcast_reduce_fusion.2 = (f32[512,8]{0,1:T(8,128)S(1)}, f32[512,512,8]{1,0,2:T(8,128)S(1)}) fusion(bf16[512,1,8,128]{3,0,2,1:T(8,128)(2,1)S(1)} %get-tuple-element.393, bf16[8,512,128]{2,1,0:T(8,128)(2,1)} %get-tuple-element.392, s32[]{:T(128)S(6)} %select_n.27), kind=kOutput, calls=%fused_computation.1.clone.1 | convolution fusion | flops 541061120 | bytes 9584644 | tf_op jit(solution)/shard_map/while/body/qhgd,khd->qhgk/dot_general | solution.py:54
  47.8 1.4 fusion.90
  49.2 3.0 %bitcast_add_fusion.7 = f32[512,1,8,128]{0,3,2,1:T(8,128)S(1)} fusion(f32[512,1,8,128]{0,3,2,1:T(8,128)S(1)} %get-tuple-element.376, f32[512,512,8]{1,0,2:T(8,128)S(1)} %get-tuple-element.346, f32[512,8]{0,1:T(8,128)S(1)} %bitcast.272, f32[512,8]{0,1:T(8,128)S(1)} %get-tuple-element.347, bf16[8,512,128]{2,1,0:T(8,128)(2,1)} %get-tuple-element.394, ...), kind=kOutput, calls=%fused_computation.9.clone.1 | convolution fusion | flops 544210944 | bytes 12746756 | tf_op jit(solution)/shard_map/while/body/qhgk,khd->qhgd/dot_general | solution.py:66
  55.7 2.2 %bitcast_reduce_fusion.2 = (f32[512,8]{0,1:T(8,128)S(1)}, f32[512,512,8]{1,0,2:T(8,128)S(1)}) fusion(bf16[512,1,8,128]{3,0,2,1:T(8,128)(2,1)S(1)} %get-tuple-element.393, bf16[8,512,128]{2,1,0:T(8,128)(2,1)} %get-tuple-element.392, s32[]{:T(128)S(6)} %select_n.27), kind=kOutput, calls=%fused_computation.1.clone.1 | convolution fusion | flops 541061120 | bytes 9584644 | tf_op jit(solution)/shard_map/while/body/qhgd,khd->qhgk/dot_general | solution.py:54
  57.9 1.4 fusion.90
  59.3 3.0 %bitcast_add_fusion.7 = f32[512,1,8,128]{0,3,2,1:T(8,128)S(1)} fusion(f32[512,1,8,128]{0,3,2,1:T(8,128)S(1)} %get-tuple-element.376, f32[512,512,8]{1,0,2:T(8,128)S(1)} %get-tuple-element.346, f32[512,8]{0,1:T(8,128)S(1)} %bitcast.272, f32[512,8]{0,1:T(8,128)S(1)} %get-tuple-element.347, bf16[8,512,128]{2,1,0:T(8,128)(2,1)} %get-tuple-element.394, ...), kind=kOutput, calls=%fused_computation.9.clone.1 | convolution fusion | flops 544210944 | bytes 12746756 | tf_op jit(solution)/shard_map/while/body/qhgk,khd->qhgd/dot_general | solution.py:66
  65.7 2.2 %bitcast_reduce_fusion.2 = (f32[512,8]{0,1:T(8,128)S(1)}, f32[512,512,8]{1,0,2:T(8,128)S(1)}) fusion(bf16[512,1,8,128]{3,0,2,1:T(8,128)(2,1)S(1)} %get-tuple-element.393, bf16[8,512,128]{2,1,0:T(8,128)(2,1)} %get-tuple-element.392, s32[]{:T(128)S(6)} %select_n.27), kind=kOutput, calls=%fused_computation.1.clone.1 | convolution fusion | flops 541061120 | bytes 9584644 | tf_op jit(solution)/shard_map/while/body/qhgd,khd->qhgk/dot_general | solution.py:54
  67.9 1.4 fusion.90
  69.3 3.0 %bitcast_add_fusion.7 = f32[512,1,8,128]{0,3,2,1:T(8,128)S(1)} fusion(f32[512,1,8,128]{0,3,2,1:T(8,128)S(1)} %get-tuple-element.376, f32[512,512,8]{1,0,2:T(8,128)S(1)} %get-tuple-element.346, f32[512,8]{0,1:T(8,128)S(1)} %bitcast.272, f32[512,8]{0,1:T(8,128)S(1)} %get-tuple-element.347, bf16[8,512,128]{2,1,0:T(8,128)(2,1)} %get-tuple-element.394, ...), kind=kOutput, calls=%fused_computation.9.clone.1 | convolution fusion | flops 544210944 | bytes 12746756 | tf_op jit(solution)/shard_map/while/body/qhgk,khd->qhgd/dot_general | solution.py:66
  73.0 2.8 %fusion.60 = (f32[512]{0:T(512)S(1)}, f32[512]{0:T(512)S(1)}, bf16[512,1,8,128]{0,3,2,1:T(8,128)(2,1)}) fusion(bf16[512,1,8,128]{0,3,2,1:T(8,128)(2,1)} %bitcast.273, f32[8,128]{1,0:T(8,128)S(1)} %bitcast.281, f32[512,1,8,128]{0,3,2,1:T(8,128)S(1)} %get-tuple-element.119, f32[512,8]{0,1:T(8,128)S(1)} %bitcast.278), kind=kLoop, calls=%fused_computation.61 | loop fusion | flops 4717568 | bytes 4218880 | tf_op jit(solution)/shard_map/reduce_sum | solution.py:88
  75.8 15.9 %all-reduce = (f32[512]{0:T(512)S(1)}, f32[512]{0:T(512)S(1)}) all-reduce(f32[512]{0:T(512)S(1)} %get-tuple-element.156, f32[512]{0:T(512)S(1)} %get-tuple-element.155), channel_id=1, replica_groups=mesh['resp'=32,'head'=8] {'head'}, use_global_device_ids=true, to_apply=%region_5.6 | all-reduce | flops 1024 | bytes 8192 | tf_op jit(solution)/shard_map/psum | solution.py:84
  91.7 2.0 %fusion.59 = bf16[512,1,8,128]{0,3,2,1:T(8,128)(2,1)S(1)} fusion(bf16[512,1,8,128]{0,3,2,1:T(8,128)(2,1)} %get-tuple-element.203, f32[512]{0:T(512)S(1)} %get-tuple-element.220, f32[8,128]{1,0:T(8,128)S(1)} %bitcast.282, f32[512]{0:T(512)S(1)} %get-tuple-element.221, bf16[1,512,1024]{1,2,0:T(8,128)(2,1)} %copy.25), kind=kLoop, calls=%fused_computation.60 | loop fusion | flops 3670016 | bytes 3153920 | tf_op jit(solution)/shard_map/convert_element_type | solution.py:93
  95.0 1.6 copy.27
  96.6 1.6 copy.24
  98.3 1.6 broadcast_in_dim.12.clone
  99.8 1.5 broadcast_in_dim.12
  101.4 1.6 broadcast.130
  102.9 55.2 %while.29 = (s32[]{:T(128)}, f32[512,1,8,128]{0,3,2,1:T(8,128)}, f32[8,512,128]{2,1,0:T(8,128)}, f32[8,512,128]{2,1,0:T(8,128)}, s32[]{:T(128)}, /*index=5*/s32[...) while((s32[]{:T(128)}, f32[512,1,8,128]{0,3,2,1:T(8,128)}, ...), condition=%wide.region_10.11_spmd, body=%wide.region_9.10_spmd.sunk | while | flops 2702376960 | bytes 64405816 | solution.py:122
  106.4 2.2 %fusion.101 = f32[512,512,8]{1,0,2:T(8,128)S(1)} fusion(bf16[512,1,8,128]{3,0,2,1:T(8,128)(2,1)S(1)} %get-tuple-element.438, bf16[8,512,128]{2,1,0:T(8,128)(2,1)} %get-tuple-element.437, s32[]{:T(128)S(6)} %select_n.29), kind=kOutput, calls=%fused_computation.44.clone.1 | convolution fusion | flops 536870912 | bytes 9568260 | tf_op jit(solution)/shard_map/while/body/qhgd,khd->qhgk/dot_general | solution.py:54
  108.5 3.2 %fusion.104 = f32[8,512,128]{2,1,0:T(8,128)} fusion(f32[8,512,128]{2,1,0:T(8,128)} %get-tuple-element.418, s32[]{:T(128)S(6)} %select_n.29, f32[512,512,8]{1,0,2:T(8,128)S(1)} %fusion.101, f32[512,8]{0,1:T(8,128)S(1)} %bitcast.274, bf16[512,1,8,128]{3,0,2,1:T(8,128)(2,1)S(1)} %get-tuple-element.441), kind=kOutput, calls=%fused_computation.38.clone.1 | convolution fusion | flops 543227904 | bytes 9977860 | tf_op jit(solution)/shard_map/while/body/qhgk,qhgd->khd/dot_general | solution.py:100
  111.8 3.1 %fusion.102 = bf16[512,8,512]{0,2,1:T(8,128)(2,1)S(1)} fusion(f32[512,512,8]{1,0,2:T(8,128)S(1)} %fusion.101, f32[512,8]{0,1:T(8,128)S(1)} %bitcast.280, f32[512,8]{0,1:T(8,128)S(1)} %bitcast.275, bf16[512,1,8,128]{3,0,2,1:T(8,128)(2,1)S(1)} %get-tuple-element.441, bf16[8,512,128]{2,1,0:T(8,128)(2,1)} %get-tuple-element.440, s32[]{:T(128)S(6)} %select_n.29), kind=kOutput, calls=%fused_computation.30.clone.1 | convolution fusion | flops 547356672 | bytes 13795332 | tf_op jit(solution)/shard_map/while/body/qhgd,khd->qhgk/dot_general | solution.py:106
  114.9 3.1 %fusion.103 = f32[8,512,128]{2,1,0:T(8,128)} fusion(f32[8,512,128]{2,1,0:T(8,128)} %get-tuple-element.417, s32[]{:T(128)S(6)} %select_n.29, bf16[512,8,512]{0,2,1:T(8,128)(2,1)S(1)} %fusion.102, bf16[512,1,8,128]{3,0,2,1:T(8,128)(2,1)S(1)} %get-tuple-element.438), kind=kOutput, calls=%fused_computation.40.clone.1 | convolution fusion | flops 537001984 | bytes 5767172 | tf_op jit(solution)/shard_map/while/body/qhgk,qhgd->khd/dot_general | solution.py:113
  118.0 2.0 bitcast_add_fusion.8
  120.0 1.3 copy-done.1
  124.5 2.2 %fusion.101 = f32[512,512,8]{1,0,2:T(8,128)S(1)} fusion(bf16[512,1,8,128]{3,0,2,1:T(8,128)(2,1)S(1)} %get-tuple-element.438, bf16[8,512,128]{2,1,0:T(8,128)(2,1)} %get-tuple-element.437, s32[]{:T(128)S(6)} %select_n.29), kind=kOutput, calls=%fused_computation.44.clone.1 | convolution fusion | flops 536870912 | bytes 9568260 | tf_op jit(solution)/shard_map/while/body/qhgd,khd->qhgk/dot_general | solution.py:54
  126.6 3.3 %fusion.104 = f32[8,512,128]{2,1,0:T(8,128)} fusion(f32[8,512,128]{2,1,0:T(8,128)} %get-tuple-element.418, s32[]{:T(128)S(6)} %select_n.29, f32[512,512,8]{1,0,2:T(8,128)S(1)} %fusion.101, f32[512,8]{0,1:T(8,128)S(1)} %bitcast.274, bf16[512,1,8,128]{3,0,2,1:T(8,128)(2,1)S(1)} %get-tuple-element.441), kind=kOutput, calls=%fused_computation.38.clone.1 | convolution fusion | flops 543227904 | bytes 9977860 | tf_op jit(solution)/shard_map/while/body/qhgk,qhgd->khd/dot_general | solution.py:100
  129.9 3.1 %fusion.102 = bf16[512,8,512]{0,2,1:T(8,128)(2,1)S(1)} fusion(f32[512,512,8]{1,0,2:T(8,128)S(1)} %fusion.101, f32[512,8]{0,1:T(8,128)S(1)} %bitcast.280, f32[512,8]{0,1:T(8,128)S(1)} %bitcast.275, bf16[512,1,8,128]{3,0,2,1:T(8,128)(2,1)S(1)} %get-tuple-element.441, bf16[8,512,128]{2,1,0:T(8,128)(2,1)} %get-tuple-element.440, s32[]{:T(128)S(6)} %select_n.29), kind=kOutput, calls=%fused_computation.30.clone.1 | convolution fusion | flops 547356672 | bytes 13795332 | tf_op jit(solution)/shard_map/while/body/qhgd,khd->qhgk/dot_general | solution.py:106
  133.0 3.1 %fusion.103 = f32[8,512,128]{2,1,0:T(8,128)} fusion(f32[8,512,128]{2,1,0:T(8,128)} %get-tuple-element.417, s32[]{:T(128)S(6)} %select_n.29, bf16[512,8,512]{0,2,1:T(8,128)(2,1)S(1)} %fusion.102, bf16[512,1,8,128]{3,0,2,1:T(8,128)(2,1)S(1)} %get-tuple-element.438), kind=kOutput, calls=%fused_computation.40.clone.1 | convolution fusion | flops 537001984 | bytes 5767172 | tf_op jit(solution)/shard_map/while/body/qhgk,qhgd->khd/dot_general | solution.py:113
  136.1 2.0 bitcast_add_fusion.8
  138.1 1.3 copy-done.1
  142.6 2.2 %fusion.101 = f32[512,512,8]{1,0,2:T(8,128)S(1)} fusion(bf16[512,1,8,128]{3,0,2,1:T(8,128)(2,1)S(1)} %get-tuple-element.438, bf16[8,512,128]{2,1,0:T(8,128)(2,1)} %get-tuple-element.437, s32[]{:T(128)S(6)} %select_n.29), kind=kOutput, calls=%fused_computation.44.clone.1 | convolution fusion | flops 536870912 | bytes 9568260 | tf_op jit(solution)/shard_map/while/body/qhgd,khd->qhgk/dot_general | solution.py:54
  144.7 3.3 %fusion.104 = f32[8,512,128]{2,1,0:T(8,128)} fusion(f32[8,512,128]{2,1,0:T(8,128)} %get-tuple-element.418, s32[]{:T(128)S(6)} %select_n.29, f32[512,512,8]{1,0,2:T(8,128)S(1)} %fusion.101, f32[512,8]{0,1:T(8,128)S(1)} %bitcast.274, bf16[512,1,8,128]{3,0,2,1:T(8,128)(2,1)S(1)} %get-tuple-element.441), kind=kOutput, calls=%fused_computation.38.clone.1 | convolution fusion | flops 543227904 | bytes 9977860 | tf_op jit(solution)/shard_map/while/body/qhgk,qhgd->khd/dot_general | solution.py:100
  148.0 3.1 %fusion.102 = bf16[512,8,512]{0,2,1:T(8,128)(2,1)S(1)} fusion(f32[512,512,8]{1,0,2:T(8,128)S(1)} %fusion.101, f32[512,8]{0,1:T(8,128)S(1)} %bitcast.280, f32[512,8]{0,1:T(8,128)S(1)} %bitcast.275, bf16[512,1,8,128]{3,0,2,1:T(8,128)(2,1)S(1)} %get-tuple-element.441, bf16[8,512,128]{2,1,0:T(8,128)(2,1)} %get-tuple-element.440, s32[]{:T(128)S(6)} %select_n.29), kind=kOutput, calls=%fused_computation.30.clone.1 | convolution fusion | flops 547356672 | bytes 13795332 | tf_op jit(solution)/shard_map/while/body/qhgd,khd->qhgk/dot_general | solution.py:106
  151.1 3.1 %fusion.103 = f32[8,512,128]{2,1,0:T(8,128)} fusion(f32[8,512,128]{2,1,0:T(8,128)} %get-tuple-element.417, s32[]{:T(128)S(6)} %select_n.29, bf16[512,8,512]{0,2,1:T(8,128)(2,1)S(1)} %fusion.102, bf16[512,1,8,128]{3,0,2,1:T(8,128)(2,1)S(1)} %get-tuple-element.438), kind=kOutput, calls=%fused_computation.40.clone.1 | convolution fusion | flops 537001984 | bytes 5767172 | tf_op jit(solution)/shard_map/while/body/qhgk,qhgd->khd/dot_general | solution.py:113
  154.2 2.0 bitcast_add_fusion.8
  156.2 1.3 copy-done.1
  158.2 1.9 convert.24
  160.1 4.3 %collective-permute-start.21 = (bf16[512,128]{1,0:T(8,128)(2,1)S(1)}, bf16[512,128]{1,0:T(8,128)(2,1)S(1)}, u32[]{:S(2)}, u32[]{:S(2)}) collective-permute-start(bf16[512,128]{1,0:T(8,128)(2,1)S(1)} %get-tuple-element.206), channel_id=1, source_target_pairs={{0,8},{8,0},{16,24},{24,16},{32,40},{40,32},{48,56},{56,48},{64,72... | collective-permute-start | bytes 393224 | tf_op jit(solution)/shard_map/ppermute | solution.py:134
  164.4 2.7 %collective-permute-start.26 = (bf16[512,128]{1,0:T(8,128)(2,1)S(1)}, bf16[512,128]{1,0:T(8,128)(2,1)S(1)}, u32[]{:S(2)}, u32[]{:S(2)}) collective-permute-start(bf16[512,128]{1,0:T(8,128)(2,1)S(1)} %get-tuple-element.208), channel_id=1, source_target_pairs={{0,48},{8,56},{16,32},{24,40},{32,16},{40,24},{48,0},{56,8},{64,11... | collective-permute-start | bytes 393224 | tf_op jit(solution)/shard_map/ppermute | solution.py:134
  167.2 3.5 %collective-permute-start.24 = (bf16[512,128]{1,0:T(8,128)(2,1)S(1)}, bf16[512,128]{1,0:T(8,128)(2,1)S(1)}, u32[]{:S(2)}, u32[]{:S(2)}) collective-permute-start(bf16[512,128]{1,0:T(8,128)(2,1)S(1)} %get-tuple-element.210), channel_id=1, source_target_pairs={{0,32},{8,40},{16,48},{24,56},{32,0},{40,8},{48,16},{56,24},{64,96... | collective-permute-start | bytes 393224 | tf_op jit(solution)/shard_map/ppermute | solution.py:134
  172.4 6.6 %collective-permute-done.26 = bf16[512,128]{1,0:T(8,128)(2,1)S(1)} collective-permute-done((bf16[512,128]{1,0:T(8,128)(2,1)S(1)}, bf16[512,128]{1,0:T(8,128)(2,1)S(1)}, u32[]{:S(2)}, u32[]{:S(2)}) %collective-permute-start.26) | collective-permute-done | bytes 131104 | tf_op jit(solution)/shard_map/ppermute | solution.py:134
  180.0 1.2 multiply_convert_fusion
  181.3 1.3 copy.33
  182.6 2.6 %collective-permute-start.19 = (bf16[512,128]{1,0:T(8,128)(2,1)S(1)}, bf16[512,128]{1,0:T(8,128)(2,1)S(1)}, u32[]{:S(2)}, u32[]{:S(2)}) collective-permute-start(bf16[512,128]{1,0:T(8,128)(2,1)S(1)} %get-tuple-element.215), channel_id=1, source_target_pairs={{0,48},{8,56},{16,32},{24,40},{32,16},{40,24},{48,0},{56,8},{64,11... | collective-permute-start | bytes 393224 | tf_op jit(solution)/shard_map/ppermute | solution.py:134
  185.2 3.6 %collective-permute-start.17 = (bf16[512,128]{1,0:T(8,128)(2,1)S(1)}, bf16[512,128]{1,0:T(8,128)(2,1)S(1)}, u32[]{:S(2)}, u32[]{:S(2)}) collective-permute-start(bf16[512,128]{1,0:T(8,128)(2,1)S(1)} %get-tuple-element.217), channel_id=1, source_target_pairs={{0,32},{8,40},{16,48},{24,56},{32,0},{40,8},{48,16},{56,24},{64,96... | collective-permute-start | bytes 393224 | tf_op jit(solution)/shard_map/ppermute | solution.py:134
  188.9 1.4 collective-permute-start.15
  191.0 2.0 %collective-permute-done.19 = bf16[512,128]{1,0:T(8,128)(2,1)S(1)} collective-permute-done((bf16[512,128]{1,0:T(8,128)(2,1)S(1)}, bf16[512,128]{1,0:T(8,128)(2,1)S(1)}, u32[]{:S(2)}, u32[]{:S(2)}) %collective-permute-start.19) | collective-permute-done | bytes 131104 | tf_op jit(solution)/shard_map/ppermute | solution.py:134
  193.0 2.5 %collective-permute-done.17 = bf16[512,128]{1,0:T(8,128)(2,1)S(1)} collective-permute-done((bf16[512,128]{1,0:T(8,128)(2,1)S(1)}, bf16[512,128]{1,0:T(8,128)(2,1)S(1)}, u32[]{:S(2)}, u32[]{:S(2)}) %collective-permute-start.17) | collective-permute-done | bytes 131104 | tf_op jit(solution)/shard_map/ppermute | solution.py:134
  196.2 2.8 %collective-permute-done.15 = bf16[512,128]{1,0:T(8,128)(2,1)S(1)} collective-permute-done((bf16[512,128]{1,0:T(8,128)(2,1)S(1)}, bf16[512,128]{1,0:T(8,128)(2,1)S(1)}, u32[]{:S(2)}, u32[]{:S(2)}) %collective-permute-start.15) | collective-permute-done | bytes 131104 | tf_op jit(solution)/shard_map/ppermute | solution.py:134
  (108 shorter events, 23.6 us)
Async XLA Ops:
  0.6 12.9 %copy-start.8 = (bf16[1,512,1024]{2,1,0:T(8,128)(2,1)S(1)}, bf16[1,512,1024]{2,1,0:T(8,128)(2,1)}, u32[]{:S(2)}) copy-start(bf16[1,512,1024]{2,1,0:T(8,128)(2,1)} %param.11) | copy-start | bytes 3145732
  0.6 27.1 %collective-permute-start.5 = (bf16[1,512,128]{2,1,0:T(8,128)(2,1)}, bf16[1,512,128]{2,1,0:T(8,128)(2,1)S(1)}, u32[]{:S(2)}, u32[]{:S(2)}) collective-permute-start(bf16[1,512,128]{2,1,0:T(8,128)(2,1)} %param.12), channel_id=1, source_target_pairs={{0,48},{8,56},{16,32},{24,40},{32,16},{40,24},{48,0},{56,8},{64,11... | collective-permute-start | bytes 393224 | tf_op jit(solution)/shard_map/ppermute | solution.py:32
  4.0 21.0 %collective-permute-start.4 = (bf16[1,512,128]{2,1,0:T(8,128)(2,1)}, bf16[1,512,128]{2,1,0:T(8,128)(2,1)}, u32[]{:S(2)}, u32[]{:S(2)}) collective-permute-start(bf16[1,512,128]{2,1,0:T(8,128)(2,1)} %param.12), channel_id=1, source_target_pairs={{0,40},{8,32},{16,56},{24,48},{32,8},{40,0},{48,24},{56,16},{64,10... | collective-permute-start | bytes 393224 | tf_op jit(solution)/shard_map/ppermute | solution.py:32
  5.4 16.8 %collective-permute-start.3 = (bf16[1,512,128]{2,1,0:T(8,128)(2,1)}, bf16[1,512,128]{2,1,0:T(8,128)(2,1)}, u32[]{:S(2)}, u32[]{:S(2)}) collective-permute-start(bf16[1,512,128]{2,1,0:T(8,128)(2,1)} %param.12), channel_id=1, source_target_pairs={{0,32},{8,40},{16,48},{24,56},{32,0},{40,8},{48,16},{56,24},{64,96... | collective-permute-start | bytes 393224 | tf_op jit(solution)/shard_map/ppermute | solution.py:32
  7.8 9.5 %collective-permute-start.1 = (bf16[1,512,128]{2,1,0:T(8,128)(2,1)}, bf16[1,512,128]{2,1,0:T(8,128)(2,1)}, u32[]{:S(2)}, u32[]{:S(2)}) collective-permute-start(bf16[1,512,128]{2,1,0:T(8,128)(2,1)} %param.12), channel_id=1, source_target_pairs={{0,16},{8,24},{16,0},{24,8},{32,48},{40,56},{48,32},{56,40},{64,80... | collective-permute-start | bytes 393224 | tf_op jit(solution)/shard_map/ppermute | solution.py:32
  7.8 6.9 %collective-permute-start = (bf16[1,512,128]{2,1,0:T(8,128)(2,1)}, bf16[1,512,128]{2,1,0:T(8,128)(2,1)}, u32[]{:S(2)}, u32[]{:S(2)}) collective-permute-start(bf16[1,512,128]{2,1,0:T(8,128)(2,1)} %param.12), channel_id=1, source_target_pairs={{0,8},{8,0},{16,24},{24,16},{32,40},{40,32},{48,56},{56,48},{64,72... | collective-permute-start | bytes 393224 | tf_op jit(solution)/shard_map/ppermute | solution.py:32
  13.5 1.2 copy-start.9
  13.5 6.7 %copy-start.10 = (bf16[1,512,128]{2,1,0:T(8,128)(2,1)S(1)}, bf16[1,512,128]{2,1,0:T(8,128)(2,1)}, u32[]{:S(2)}) copy-start(bf16[1,512,128]{2,1,0:T(8,128)(2,1)} %param.13) | copy-start | bytes 393220
  14.8 5.5 %collective-permute-start.2 = (bf16[1,512,128]{2,1,0:T(8,128)(2,1)S(1)}, bf16[1,512,128]{2,1,0:T(8,128)(2,1)S(1)}, u32[]{:S(2)}, u32[]{:S(2)}) collective-permute-start(bf16[1,512,128]{2,1,0:T(8,128)(2,1)S(1)} %copy-done.9), channel_id=1, source_target_pairs={{0,24},{8,16},{16,8},{24,0},{32,56},{40,48},{48,40},{56,32},{64,88... | collective-permute-start | bytes 393224 | tf_op jit(solution)/shard_map/ppermute | solution.py:32
  17.4 10.6 %collective-permute-start.6 = (bf16[1,512,128]{2,1,0:T(8,128)(2,1)S(1)}, bf16[1,512,128]{2,1,0:T(8,128)(2,1)S(1)}, u32[]{:S(2)}, u32[]{:S(2)}) collective-permute-start(bf16[1,512,128]{2,1,0:T(8,128)(2,1)S(1)} %copy-done.9), channel_id=1, source_target_pairs={{0,56},{8,48},{16,40},{24,32},{32,24},{40,16},{48,8},{56,0},{64,12... | collective-permute-start | bytes 393224 | tf_op jit(solution)/shard_map/ppermute | solution.py:32
  20.3 18.9 %collective-permute-start.12 = (bf16[1,512,128]{2,1,0:T(8,128)(2,1)S(1)}, bf16[1,512,128]{2,1,0:T(8,128)(2,1)S(1)}, u32[]{:S(2)}, u32[]{:S(2)}) collective-permute-start(bf16[1,512,128]{2,1,0:T(8,128)(2,1)S(1)} %copy-done.10), channel_id=1, source_target_pairs={{0,48},{8,56},{16,32},{24,40},{32,16},{40,24},{48,0},{56,8},{64,11... | collective-permute-start | bytes 393224 | tf_op jit(solution)/shard_map/ppermute | solution.py:32
  22.2 16.3 %collective-permute-start.11 = (bf16[1,512,128]{2,1,0:T(8,128)(2,1)S(1)}, bf16[1,512,128]{2,1,0:T(8,128)(2,1)S(1)}, u32[]{:S(2)}, u32[]{:S(2)}) collective-permute-start(bf16[1,512,128]{2,1,0:T(8,128)(2,1)S(1)} %copy-done.10), channel_id=1, source_target_pairs={{0,40},{8,32},{16,56},{24,48},{32,8},{40,0},{48,24},{56,16},{64,10... | collective-permute-start | bytes 393224 | tf_op jit(solution)/shard_map/ppermute | solution.py:32
  25.1 12.8 %collective-permute-start.10 = (bf16[1,512,128]{2,1,0:T(8,128)(2,1)S(1)}, bf16[1,512,128]{2,1,0:T(8,128)(2,1)S(1)}, u32[]{:S(2)}, u32[]{:S(2)}) collective-permute-start(bf16[1,512,128]{2,1,0:T(8,128)(2,1)S(1)} %copy-done.10), channel_id=1, source_target_pairs={{0,32},{8,40},{16,48},{24,56},{32,0},{40,8},{48,16},{56,24},{64,96... | collective-permute-start | bytes 393224 | tf_op jit(solution)/shard_map/ppermute | solution.py:32
  27.8 1.5 collective-permute-start.7
  28.0 6.3 %collective-permute-start.8 = (bf16[1,512,128]{2,1,0:T(8,128)(2,1)S(1)}, bf16[1,512,128]{2,1,0:T(8,128)(2,1)S(1)}, u32[]{:S(2)}, u32[]{:S(2)}) collective-permute-start(bf16[1,512,128]{2,1,0:T(8,128)(2,1)S(1)} %copy-done.10), channel_id=1, source_target_pairs={{0,16},{8,24},{16,0},{24,8},{32,48},{40,56},{48,32},{56,40},{64,80... | collective-permute-start | bytes 393224 | tf_op jit(solution)/shard_map/ppermute | solution.py:32
  29.3 12.5 %copy-start.7 = (bf16[8,512,128]{2,1,0:T(8,128)(2,1)}, bf16[8,512,128]{2,1,0:T(8,128)(2,1)S(1)}, u32[]{:S(2)}) copy-start(bf16[8,512,128]{2,1,0:T(8,128)(2,1)S(1)} %constant_dynamic-update-slice_fusion) | copy-start | bytes 3145732
  29.3 7.9 %collective-permute-start.9 = (bf16[1,512,128]{2,1,0:T(8,128)(2,1)S(1)}, bf16[1,512,128]{2,1,0:T(8,128)(2,1)S(1)}, u32[]{:S(2)}, u32[]{:S(2)}) collective-permute-start(bf16[1,512,128]{2,1,0:T(8,128)(2,1)S(1)} %copy-done.10), channel_id=1, source_target_pairs={{0,24},{8,16},{16,8},{24,0},{32,56},{40,48},{48,40},{56,32},{64,88... | collective-permute-start | bytes 393224 | tf_op jit(solution)/shard_map/ppermute | solution.py:32
  34.3 6.9 %collective-permute-start.13 = (bf16[1,512,128]{2,1,0:T(8,128)(2,1)S(1)}, bf16[1,512,128]{2,1,0:T(8,128)(2,1)S(1)}, u32[]{:S(2)}, u32[]{:S(2)}) collective-permute-start(bf16[1,512,128]{2,1,0:T(8,128)(2,1)S(1)} %copy-done.10), channel_id=1, source_target_pairs={{0,56},{8,48},{16,40},{24,32},{32,24},{40,16},{48,8},{56,0},{64,12... | collective-permute-start | bytes 393224 | tf_op jit(solution)/shard_map/ppermute | solution.py:32
  42.0 31.0 %copy-start.11 = (f32[1024]{0:T(1024)S(1)}, f32[1024]{0:T(1024)}, u32[]{:S(2)}) copy-start(f32[1024]{0:T(1024)} %param.16) | copy-start | bytes 12292
  75.8 18.9 %copy-start.3 = (bf16[512,1,8,128]{0,3,2,1:T(8,128)(2,1)S(1)}, bf16[512,1,8,128]{0,3,2,1:T(8,128)(2,1)}, u32[]{:S(2)}) copy-start(bf16[512,1,8,128]{0,3,2,1:T(8,128)(2,1)} %get-tuple-element.203) | copy-start | bytes 3145732
  93.7 1.0 copy-start.5
  114.9 3.1 %copy-start = (f32[512,1,8,128]{0,3,2,1:T(8,128)S(1)}, f32[512,1,8,128]{0,3,2,1:T(8,128)}, u32[]{:S(2)}) copy-start(f32[512,1,8,128]{0,3,2,1:T(8,128)} %get-tuple-element.416) | copy-start | bytes 6291460 | tf_op jit(solution)/shard_map/while
  120.0 1.3 copy-start.1
  133.0 3.1 %copy-start = (f32[512,1,8,128]{0,3,2,1:T(8,128)S(1)}, f32[512,1,8,128]{0,3,2,1:T(8,128)}, u32[]{:S(2)}) copy-start(f32[512,1,8,128]{0,3,2,1:T(8,128)} %get-tuple-element.416) | copy-start | bytes 6291460 | tf_op jit(solution)/shard_map/while
  138.0 1.3 copy-start.1
  151.1 3.1 %copy-start = (f32[512,1,8,128]{0,3,2,1:T(8,128)S(1)}, f32[512,1,8,128]{0,3,2,1:T(8,128)}, u32[]{:S(2)}) copy-start(f32[512,1,8,128]{0,3,2,1:T(8,128)} %get-tuple-element.416) | copy-start | bytes 6291460 | tf_op jit(solution)/shard_map/while
  156.2 1.3 copy-start.1
  158.1 12.5 %copy-start.4 = (f32[8,512,128]{2,1,0:T(8,128)S(1)}, f32[8,512,128]{2,1,0:T(8,128)}, u32[]{:S(2)}) copy-start(f32[8,512,128]{2,1,0:T(8,128)} %get-tuple-element.123) | copy-start | bytes 6291460
  160.1 10.8 %collective-permute-start.21 = (bf16[512,128]{1,0:T(8,128)(2,1)S(1)}, bf16[512,128]{1,0:T(8,128)(2,1)S(1)}, u32[]{:S(2)}, u32[]{:S(2)}) collective-permute-start(bf16[512,128]{1,0:T(8,128)(2,1)S(1)} %get-tuple-element.206), channel_id=1, source_target_pairs={{0,8},{8,0},{16,24},{24,16},{32,40},{40,32},{48,56},{56,48},{64,72... | collective-permute-start | bytes 393224 | tf_op jit(solution)/shard_map/ppermute | solution.py:134
  164.4 7.0 %collective-permute-start.27 = (bf16[512,128]{1,0:T(8,128)(2,1)S(1)}, bf16[512,128]{1,0:T(8,128)(2,1)S(1)}, u32[]{:S(2)}, u32[]{:S(2)}) collective-permute-start(bf16[512,128]{1,0:T(8,128)(2,1)S(1)} %get-tuple-element.207), channel_id=1, source_target_pairs={{0,56},{8,48},{16,40},{24,32},{32,24},{40,16},{48,8},{56,0},{64,12... | collective-permute-start | bytes 393224 | tf_op jit(solution)/shard_map/ppermute | solution.py:134
  164.4 14.6 %collective-permute-start.26 = (bf16[512,128]{1,0:T(8,128)(2,1)S(1)}, bf16[512,128]{1,0:T(8,128)(2,1)S(1)}, u32[]{:S(2)}, u32[]{:S(2)}) collective-permute-start(bf16[512,128]{1,0:T(8,128)(2,1)S(1)} %get-tuple-element.208), channel_id=1, source_target_pairs={{0,48},{8,56},{16,32},{24,40},{32,16},{40,24},{48,0},{56,8},{64,11... | collective-permute-start | bytes 393224 | tf_op jit(solution)/shard_map/ppermute | solution.py:134
  167.1 12.9 %collective-permute-start.25 = (bf16[512,128]{1,0:T(8,128)(2,1)S(1)}, bf16[512,128]{1,0:T(8,128)(2,1)S(1)}, u32[]{:S(2)}, u32[]{:S(2)}) collective-permute-start(bf16[512,128]{1,0:T(8,128)(2,1)S(1)} %get-tuple-element.209), channel_id=1, source_target_pairs={{0,40},{8,32},{16,56},{24,48},{32,8},{40,0},{48,24},{56,16},{64,10... | collective-permute-start | bytes 393224 | tf_op jit(solution)/shard_map/ppermute | solution.py:134
  167.2 15.5 %collective-permute-start.24 = (bf16[512,128]{1,0:T(8,128)(2,1)S(1)}, bf16[512,128]{1,0:T(8,128)(2,1)S(1)}, u32[]{:S(2)}, u32[]{:S(2)}) collective-permute-start(bf16[512,128]{1,0:T(8,128)(2,1)S(1)} %get-tuple-element.210), channel_id=1, source_target_pairs={{0,32},{8,40},{16,48},{24,56},{32,0},{40,8},{48,16},{56,24},{64,96... | collective-permute-start | bytes 393224 | tf_op jit(solution)/shard_map/ppermute | solution.py:134
  170.6 9.3 %copy-start.6 = (f32[1,512,1024]{2,1,0:T(8,128)S(1)}, f32[1,512,1024]{2,1,0:T(8,128)}, u32[]{:S(2)}) copy-start(f32[1,512,1024]{2,1,0:T(8,128)} %copy.24) | copy-start | bytes 6291460
  170.8 10.4 %copy-start.2 = (f32[512,1,8,128]{0,3,2,1:T(8,128)S(1)}, f32[512,1,8,128]{0,3,2,1:T(8,128)}, u32[]{:S(2)}) copy-start(f32[512,1,8,128]{0,3,2,1:T(8,128)} %get-tuple-element.122) | copy-start | bytes 6291460
  170.9 14.3 %collective-permute-start.23 = (bf16[512,128]{1,0:T(8,128)(2,1)S(1)}, bf16[512,128]{1,0:T(8,128)(2,1)S(1)}, u32[]{:S(2)}, u32[]{:S(2)}) collective-permute-start(bf16[512,128]{1,0:T(8,128)(2,1)S(1)} %get-tuple-element.211), channel_id=1, source_target_pairs={{0,24},{8,16},{16,8},{24,0},{32,56},{40,48},{48,40},{56,32},{64,88... | collective-permute-start | bytes 393224 | tf_op jit(solution)/shard_map/ppermute | solution.py:134
  171.4 13.8 %collective-permute-start.22 = (bf16[512,128]{1,0:T(8,128)(2,1)S(1)}, bf16[512,128]{1,0:T(8,128)(2,1)S(1)}, u32[]{:S(2)}, u32[]{:S(2)}) collective-permute-start(bf16[512,128]{1,0:T(8,128)(2,1)S(1)} %get-tuple-element.212), channel_id=1, source_target_pairs={{0,16},{8,24},{16,0},{24,8},{32,48},{40,56},{48,32},{56,40},{64,80... | collective-permute-start | bytes 393224 | tf_op jit(solution)/shard_map/ppermute | solution.py:134
  179.0 9.9 %collective-permute-start.14 = (bf16[512,128]{1,0:T(8,128)(2,1)S(1)}, bf16[512,128]{1,0:T(8,128)(2,1)S(1)}, u32[]{:S(2)}, u32[]{:S(2)}) collective-permute-start(bf16[512,128]{1,0:T(8,128)(2,1)S(1)} %get-tuple-element.213), channel_id=1, source_target_pairs={{0,8},{8,0},{16,24},{24,16},{32,40},{40,32},{48,56},{56,48},{64,72... | collective-permute-start | bytes 393224 | tf_op jit(solution)/shard_map/ppermute | solution.py:134
  180.0 8.9 %collective-permute-start.20 = (bf16[512,128]{1,0:T(8,128)(2,1)S(1)}, bf16[512,128]{1,0:T(8,128)(2,1)S(1)}, u32[]{:S(2)}, u32[]{:S(2)}) collective-permute-start(bf16[512,128]{1,0:T(8,128)(2,1)S(1)} %get-tuple-element.214), channel_id=1, source_target_pairs={{0,56},{8,48},{16,40},{24,32},{32,24},{40,16},{48,8},{56,0},{64,12... | collective-permute-start | bytes 393224 | tf_op jit(solution)/shard_map/ppermute | solution.py:134
  182.6 10.4 %collective-permute-start.19 = (bf16[512,128]{1,0:T(8,128)(2,1)S(1)}, bf16[512,128]{1,0:T(8,128)(2,1)S(1)}, u32[]{:S(2)}, u32[]{:S(2)}) collective-permute-start(bf16[512,128]{1,0:T(8,128)(2,1)S(1)} %get-tuple-element.215), channel_id=1, source_target_pairs={{0,48},{8,56},{16,32},{24,40},{32,16},{40,24},{48,0},{56,8},{64,11... | collective-permute-start | bytes 393224 | tf_op jit(solution)/shard_map/ppermute | solution.py:134
  185.2 7.8 %collective-permute-start.18 = (bf16[512,128]{1,0:T(8,128)(2,1)S(1)}, bf16[512,128]{1,0:T(8,128)(2,1)S(1)}, u32[]{:S(2)}, u32[]{:S(2)}) collective-permute-start(bf16[512,128]{1,0:T(8,128)(2,1)S(1)} %get-tuple-element.216), channel_id=1, source_target_pairs={{0,40},{8,32},{16,56},{24,48},{32,8},{40,0},{48,24},{56,16},{64,10... | collective-permute-start | bytes 393224 | tf_op jit(solution)/shard_map/ppermute | solution.py:134
  185.2 10.3 %collective-permute-start.17 = (bf16[512,128]{1,0:T(8,128)(2,1)S(1)}, bf16[512,128]{1,0:T(8,128)(2,1)S(1)}, u32[]{:S(2)}, u32[]{:S(2)}) collective-permute-start(bf16[512,128]{1,0:T(8,128)(2,1)S(1)} %get-tuple-element.217), channel_id=1, source_target_pairs={{0,32},{8,40},{16,48},{24,56},{32,0},{40,8},{48,16},{56,24},{64,96... | collective-permute-start | bytes 393224 | tf_op jit(solution)/shard_map/ppermute | solution.py:134
  188.9 7.3 %collective-permute-start.16 = (bf16[512,128]{1,0:T(8,128)(2,1)S(1)}, bf16[512,128]{1,0:T(8,128)(2,1)S(1)}, u32[]{:S(2)}, u32[]{:S(2)}) collective-permute-start(bf16[512,128]{1,0:T(8,128)(2,1)S(1)} %get-tuple-element.218), channel_id=1, source_target_pairs={{0,24},{8,16},{16,8},{24,0},{32,56},{40,48},{48,40},{56,32},{64,88... | collective-permute-start | bytes 393224 | tf_op jit(solution)/shard_map/ppermute | solution.py:134
  188.9 10.1 %collective-permute-start.15 = (bf16[512,128]{1,0:T(8,128)(2,1)S(1)}, bf16[512,128]{1,0:T(8,128)(2,1)S(1)}, u32[]{:S(2)}, u32[]{:S(2)}) collective-permute-start(bf16[512,128]{1,0:T(8,128)(2,1)S(1)} %get-tuple-element.219), channel_id=1, source_target_pairs={{0,16},{8,24},{16,0},{24,8},{32,48},{40,56},{48,32},{56,40},{64,80... | collective-permute-start | bytes 393224 | tf_op jit(solution)/shard_map/ppermute | solution.py:134

commit v2 on v1

--- a/solution.py
+++ b/solution.py
@@ -17,26 +17,24 @@
     return lax.dynamic_update_index_in_dim(buffer, current + addend, row_index, 0)
 
 
+def head_sum(row_part):
+    return jnp.sum(lax.all_gather(row_part, "head"), 0)
+
+
 def body(queries, key_states, value_states, partners, counts, norm_gain, out_grad):
-    my_index = lax.axis_index("resp")
     seq_len = queries.shape[1]
     kv_cols = key_states.shape[2]
     kv_heads = kv_cols // HD
     per_group = queries.shape[2] // kv_cols
-    resp_count = lax.axis_size("resp")
-
-    def by_distance(block):
-        rows = [block]
-        for distance in range(1, GROUP):
-            route = [(low, low ^ distance) for low in range(resp_count)]
-            rows.append(lax.ppermute(block, "resp", route))
-        return jnp.concatenate(rows, 0)
-
-    cluster_key_rows = by_distance(key_states)
-    group_values = by_distance(value_states)
+    group_size = lax.axis_size("grp")
+    my_place = lax.axis_index("grp")
+    both_states = jnp.concatenate([key_states[0], value_states[0]], -1)
+    group_states = lax.all_gather(both_states, "grp")
+    cluster_key_rows = group_states[..., :kv_cols]
+    group_values = group_states[..., kv_cols:]
     query_heads = queries[0].reshape(seq_len, kv_heads, per_group, HD)
     score_scale = HD ** (-0.5)
-    mate_rows = jnp.bitwise_xor(partners[0], my_index)
+    mate_rows = partners[0] % group_size
     live_count = counts[0]
 
     def partner_block_tile(slot_index):
@@ -81,11 +79,11 @@
     attention = (weighted / denominator[..., None]).astype(jnp.bfloat16)
     log_total = running_max + jnp.log(denominator)
     attention_flat = attention.reshape(seq_len, -1).astype(jnp.float32)
-    square_sums = lax.psum(jnp.sum(attention_flat * attention_flat, -1), "head")
+    square_sums = head_sum(jnp.sum(attention_flat * attention_flat, -1))
     inverse_rms = lax.rsqrt(square_sums / D + EPSILON)
     normed_out = (attention_flat * inverse_rms[:, None] * norm_gain).astype(jnp.bfloat16)[None]
     scaled_grad = out_grad[0].astype(jnp.float32) * norm_gain
-    dot_sums = lax.psum(jnp.sum(attention_flat * scaled_grad, -1), "head")
+    dot_sums = head_sum(jnp.sum(attention_flat * scaled_grad, -1))
     attention_grad = (
         inverse_rms[:, None] * scaled_grad
         - attention_flat * (inverse_rms**3 * dot_sums / D)[:, None]
@@ -126,16 +124,10 @@
         (jnp.zeros(stat_shape + (HD,), jnp.float32), zero_buffer, zero_buffer),
     )
     query_grads = query_grad.reshape(seq_len, -1).astype(jnp.bfloat16)[None]
-    def to_owners(buffer):
-        total = jnp.zeros(buffer.shape[1:], jnp.float32)
-        for distance in range(1, GROUP):
-            route = [(low, low ^ distance) for low in range(resp_count)]
-            sent = buffer[distance].astype(jnp.bfloat16)
-            total = total + lax.ppermute(sent, "resp", route).astype(jnp.float32)
-        return total[None]
-
-    key_total = to_owners(key_buffer)
-    value_total = to_owners(value_storage)
+    both_terms = jnp.concatenate([key_buffer, value_storage], -1).astype(jnp.bfloat16)
+    both_totals = lax.psum_scatter(both_terms, "grp", scatter_dimension=0, tiled=True)
+    key_total = both_totals[..., :kv_cols]
+    value_total = both_totals[..., kv_cols:]
     return (
         normed_out,
         query_grads,
@@ -154,15 +146,22 @@
         P("head"),
         P("resp", None, "head"),
     )
+    group_count = mesh.shape["resp"] // GROUP
+    grouped = jax.sharding.Mesh(
+        mesh.devices.reshape(group_count, GROUP, mesh.shape["head"]), ("blk", "grp", "head")
+    )
+    placed = jax.tree.map(
+        lambda spec: P(*[("blk", "grp") if name == "resp" else name for name in spec]), placed
+    )
     return jax.shard_map(
         body,
-        mesh=mesh,
+        mesh=grouped,
         in_specs=placed,
         out_specs=(
-            P("resp", None, "head"),
-            P("resp", None, "head"),
-            P("resp", None, "head"),
-            P("resp", None, "head"),
+            P(("blk", "grp"), None, "head"),
+            P(("blk", "grp"), None, "head"),
+            P(("blk", "grp"), None, "head"),
+            P(("blk", "grp"), None, "head"),
         ),
         check_vma=False,
     )

time: 201 us -> 234 us (1.16)
  waiting for transfers between devices: 19.8 us -> 94.2 us
  starting transfers between devices: 41.3 us -> 0.08 us
  matrix products: 56.2 us -> 37.5 us
  blocking collectives: 15.9 us -> 33.7 us
  between operations: 0.96 us -> 14.2 us
  local copies, waits for them, and re-layouts: 32.7 us -> 25.3 us
  loops' own time: 18 us -> 11.6 us
    reduce_scatter x0 -> x1, waiting for transfers between devices: none -> 64.4 us  [body(): lax.psum_scatter(both_terms, 'grp', scatter_dimension=0, tiled=True)]
    ppermute x28 -> x0, starting transfers between devices: 41.3 us -> none  [the longest x14 21.2 us: by_distance(): rows.append(lax.ppermute(block, 'resp', route))]
    all_gather x0 -> x2, blocking collectives: none -> 33.7 us  [head_sum(): return jnp.sum(lax.all_gather(row_part, 'head'), 0)]
    all_gather x0 -> x1, waiting for transfers between devices: none -> 29.8 us  [body(): group_states = lax.all_gather(both_states, 'grp')]
    ppermute x28 -> x0, waiting for transfers between devices: 19.8 us -> none  [the longest x14 15 us: to_owners(): total = total + lax.ppermute(sent, 'resp', route).astype(jnp.float32)]
    psum x1 -> x0, blocking collectives: 15.9 us -> none  [body(): square_sums = lax.psum(jnp.sum(attention_flat * attention_flat, -1), 'head')]
    unnamed x36 -> x18, local copies, waits for them, and re-layouts: 14 us -> 5.46 us
    slice x0 -> x2, local copies, waits for them, and re-layouts: none -> 4.77 us  [the longest x1 3.09 us: body(): group_values = group_states[..., kv_cols:]]
  transfers between devices with their start and end apart: 28 -> 2, of which waited for: 9 -> 2; matrix products, arithmetic and copies ran while one was open for 9% -> 3% of each run, Pallas kernels for 0% -> 0%
where the time goes in v2:
time: 234 us; the launch traced here: 231 us
  waiting for transfers between devices  94.2 us (40%)
  matrix products  37.5 us (16%)
  blocking collectives  33.7 us (14%)
  local copies, waits for them, and re-layouts  25.3 us (11%)
  other arithmetic  14.7 us (6%)
  between operations  14.2 us (6%)
  loops' own time  11.6 us (5%)
    reduce_scatter x1, waiting for transfers between devices, body(): lax.psum_scatter(both_terms, 'grp', scatter_dimension=0, tiled=True)  64.4 us
    all_gather x2, blocking collectives, head_sum(): return jnp.sum(lax.all_gather(row_part, 'head'), 0)  33.7 us
    all_gather x1, waiting for transfers between devices, body(): group_states = lax.all_gather(both_states, 'grp')  29.8 us
    dot_general x4, matrix products, score_block(): jnp.einsum('qhgd,khd->qhgk', query_heads, mate_keys, preferred_element_ty...  8.65 us
    dot_general x2, matrix products, backward_step(): jnp.einsum('qhgk,qhgd->khd', back_probs.astype(jnp.bfloat16), attention_g...  6.53 us
    dot_general x2, matrix products, backward_step(): jnp.einsum('qhgd,khd->qhgk', attention_grad, mate_values, preferred_eleme...  6.19 us
    dot_general x2, matrix products, backward_step(): jnp.einsum('qhgk,qhgd->khd', score_grad, query_heads, preferred_element_t...  6.16 us
    another operation x1, loops' own time, body(): lax.fori_loop(0, live_count, backward_step, (jnp.zeros(stat_shape + (HD,)...  6.12 us
  transfers between devices with their start and end apart: 2, of which 2 were waited for; matrix products, arithmetic and copies ran while one was open for 3% of the time, Pallas kernels for 0%

profile of v2, /device:TPU:1, one launch (start us, length us, event | category | flops | bytes accessed | tf_op | source)
XLA Modules:
  0.0 231.3 jit_solution(17958019627231627273)
XLA Ops:
  7.2 0.0 copy-start.7
  7.2 0.0 all-gather.7.cloned.1.call-start
  7.2 1.8 pad_maximum_fusion.1
  9.0 0.0 all-gather.7.cloned.1.call-update
  9.0 0.0 reduce-scatter.2.cloned.1.call-start
  9.1 2.3 copy.36
  11.4 0.0 copy-done.7
  11.4 0.5 copy.32
  11.9 0.7 copy.33
  12.6 0.0 copy-done.9
  12.6 29.8 %all-gather.7.cloned.1.call-done = bf16[4096,256]{1,0:T(8,128)(2,1)} async-done(((bf16[512,256]{1,0:T(8,128)(2,1)}), bf16[4096,256]{1,0:T(8,128)(2,1)}) %all-gather.7.cloned.1.call-update) | async-done | bytes 2097168 | tf_op jit(solution)/shard_map/all_gather | solution.py:32
  42.4 3.1 %fusion.66 = (bf16[8,512,128]{2,1,0:T(8,128)(2,1)}, bf16[8,512,128]{2,1,0:T(8,128)(2,1)}) fusion(bf16[8,512,256]{2,1,0:T(8,128)(2,1)} %bitcast.251), kind=kLoop, calls=%fused_computation.80 | loop fusion | bytes 4194304 | tf_op jit(solution)/shard_map/slice | solution.py:34
  45.5 0.2 broadcast.152.clone
  45.7 0.0 copy-start.8
  45.7 19.8 %while.28 = (s32[]{:T(128)}, f32[512,1,8]{0,2,1:T(8,128)S(1)}, f32[512,1,8]{0,2,1:T(8,128)S(1)}, f32[512,1,8,128]{0,3,2,1:T(8,128)S(1)}, s32[]{:T(128)}, /*index...) while((s32[]{:T(128)}, f32[512,1,8]{0,2,1:T(8,128)S(1)}, ...), condition=%wide.region_3.4_spmd, body=%wide.region_0.3_spmd.sunk | while | flops 1091579904 | bytes 30933212 | solution.py:78
  46.4 0.6 dynamic_slice.62
  48.7 2.2 bitcast_reduce_fusion.2
  50.9 1.4 fusion.91
  52.3 3.0 %bitcast_add_fusion.7 = f32[512,1,8,128]{0,3,2,1:T(8,128)S(1)} fusion(f32[512,1,8,128]{0,3,2,1:T(8,128)S(1)} %get-tuple-element.385, f32[512,512,8]{1,0,2:T(8,128)S(1)} %get-tuple-element.355, f32[512,8]{0,1:T(8,128)S(1)} %bitcast.245, f32[512,8]{0,1:T(8,128)S(1)} %get-tuple-element.356, bf16[8,512,128]{2,1,0:T(8,128)(2,1)} %get-tuple-element.403, ...), kind=kOutput, calls=%fused_computation.9.clone.1 | convolution fusion | flops 544210944 | bytes 12746756 | tf_op jit(solution)/shard_map/while/body/qhgk,khd->qhgd/dot_general | solution.py:64
  56.0 0.6 dynamic_slice.62
  58.2 2.2 bitcast_reduce_fusion.2
  60.4 1.4 fusion.91
  61.8 3.0 %bitcast_add_fusion.7 = f32[512,1,8,128]{0,3,2,1:T(8,128)S(1)} fusion(f32[512,1,8,128]{0,3,2,1:T(8,128)S(1)} %get-tuple-element.385, f32[512,512,8]{1,0,2:T(8,128)S(1)} %get-tuple-element.355, f32[512,8]{0,1:T(8,128)S(1)} %bitcast.245, f32[512,8]{0,1:T(8,128)S(1)} %get-tuple-element.356, bf16[8,512,128]{2,1,0:T(8,128)(2,1)} %get-tuple-element.403, ...), kind=kOutput, calls=%fused_computation.9.clone.1 | convolution fusion | flops 544210944 | bytes 12746756 | tf_op jit(solution)/shard_map/while/body/qhgk,khd->qhgd/dot_general | solution.py:64
  65.5 0.0 copy-done.8
  65.5 2.8 %fusion.60 = (f32[512]{0:T(512)S(1)}, f32[512]{0:T(512)S(1)}, bf16[512,1,8,128]{0,3,2,1:T(8,128)(2,1)}) fusion(bf16[512,1,8,128]{0,3,2,1:T(8,128)(2,1)} %bitcast.246, f32[8,128]{1,0:T(8,128)S(1)} %bitcast.257, f32[512,1,8,128]{0,3,2,1:T(8,128)S(1)} %get-tuple-element.119, f32[512,8]{0,1:T(8,128)S(1)} %bitcast.252), kind=kLoop, calls=%fused_computation.62 | loop fusion | flops 4717568 | bytes 4218880 | tf_op jit(solution)/shard_map/reduce_sum | solution.py:86
  68.3 18.3 %all-gather.3 = f32[8,1,512]{2,1,0:T(1,128)S(1)} all-gather(f32[1,1,512]{2,1,0:T(1,128)S(1)} %bitcast.260), channel_id=3, replica_groups=mesh['blk'=4,'grp'=8,'head'=8] {'head'}, dimensions={0}, use_global_device_ids=true | all-gather | bytes 18432 | tf_op jit(solution)/shard_map/all_gather | solution.py:21
  86.6 15.4 %all-gather.4 = f32[8,1,512]{2,1,0:T(1,128)S(1)} all-gather(f32[1,1,512]{2,1,0:T(1,128)S(1)} %bitcast.259), channel_id=4, replica_groups=mesh['blk'=4,'grp'=8,'head'=8] {'head'}, dimensions={0}, use_global_device_ids=true | all-gather | bytes 18432 | tf_op jit(solution)/shard_map/all_gather | solution.py:21
  102.1 2.0 fusion.59
  104.1 0.0 copy-start.5
  104.1 1.0 copy-done.5
  105.1 0.3 fusion.62
  105.4 1.6 copy.38
  107.0 1.5 broadcast_in_dim.12.clone
  108.5 1.5 broadcast_in_dim.12
  110.0 1.6 broadcast.152
  111.6 37.1 %while.29 = (s32[]{:T(128)}, f32[512,1,8,128]{0,3,2,1:T(8,128)}, f32[8,512,128]{2,1,0:T(8,128)}, f32[8,512,128]{2,1,0:T(8,128)}, s32[]{:T(128)}, /*index=5*/s32[...) while((s32[]{:T(128)}, f32[512,1,8,128]{0,3,2,1:T(8,128)}, ...), condition=%wide.region_10.11_spmd, body=%wide.region_9.10_spmd.sunk | while | flops 2702376960 | bytes 64405816 | solution.py:120
  112.5 0.6 dynamic_slice.68
  115.0 2.2 fusion.102
  117.2 3.3 %fusion.105 = f32[8,512,128]{2,1,0:T(8,128)} fusion(f32[8,512,128]{2,1,0:T(8,128)} %get-tuple-element.427, s32[]{:T(128)S(6)} %select_n.38, f32[512,512,8]{1,0,2:T(8,128)S(1)} %fusion.102, f32[512,8]{0,1:T(8,128)S(1)} %bitcast.247, bf16[512,1,8,128]{3,0,2,1:T(8,128)(2,1)S(1)} %get-tuple-element.450), kind=kOutput, calls=%fused_computation.38.clone.1 | convolution fusion | flops 543227904 | bytes 9977860 | tf_op jit(solution)/shard_map/while/body/qhgk,qhgd->khd/dot_general | solution.py:98
  120.4 3.1 %fusion.103 = bf16[512,8,512]{0,2,1:T(8,128)(2,1)S(1)} fusion(f32[512,512,8]{1,0,2:T(8,128)S(1)} %fusion.102, f32[512,8]{0,1:T(8,128)S(1)} %bitcast.254, f32[512,8]{0,1:T(8,128)S(1)} %bitcast.248, bf16[512,1,8,128]{3,0,2,1:T(8,128)(2,1)S(1)} %get-tuple-element.450, bf16[8,512,128]{2,1,0:T(8,128)(2,1)} %get-tuple-element.449, s32[]{:T(128)S(6)} %select_n.38), kind=kOutput, calls=%fused_computation.30.clone.1 | convolution fusion | flops 547356672 | bytes 13795332 | tf_op jit(solution)/shard_map/while/body/qhgd,khd->qhgk/dot_general | solution.py:104
  123.5 3.1 %fusion.104 = f32[8,512,128]{2,1,0:T(8,128)} fusion(f32[8,512,128]{2,1,0:T(8,128)} %get-tuple-element.426, s32[]{:T(128)S(6)} %select_n.38, bf16[512,8,512]{0,2,1:T(8,128)(2,1)S(1)} %fusion.103, bf16[512,1,8,128]{3,0,2,1:T(8,128)(2,1)S(1)} %get-tuple-element.447), kind=kOutput, calls=%fused_computation.40.clone.1 | convolution fusion | flops 537001984 | bytes 5767172 | tf_op jit(solution)/shard_map/while/body/qhgk,qhgd->khd/dot_general | solution.py:111
  126.6 2.0 bitcast_add_fusion.8
  128.6 1.3 copy-done.1
  130.6 0.6 dynamic_slice.68
  133.2 2.2 fusion.102
  135.3 3.3 %fusion.105 = f32[8,512,128]{2,1,0:T(8,128)} fusion(f32[8,512,128]{2,1,0:T(8,128)} %get-tuple-element.427, s32[]{:T(128)S(6)} %select_n.38, f32[512,512,8]{1,0,2:T(8,128)S(1)} %fusion.102, f32[512,8]{0,1:T(8,128)S(1)} %bitcast.247, bf16[512,1,8,128]{3,0,2,1:T(8,128)(2,1)S(1)} %get-tuple-element.450), kind=kOutput, calls=%fused_computation.38.clone.1 | convolution fusion | flops 543227904 | bytes 9977860 | tf_op jit(solution)/shard_map/while/body/qhgk,qhgd->khd/dot_general | solution.py:98
  138.6 3.1 %fusion.103 = bf16[512,8,512]{0,2,1:T(8,128)(2,1)S(1)} fusion(f32[512,512,8]{1,0,2:T(8,128)S(1)} %fusion.102, f32[512,8]{0,1:T(8,128)S(1)} %bitcast.254, f32[512,8]{0,1:T(8,128)S(1)} %bitcast.248, bf16[512,1,8,128]{3,0,2,1:T(8,128)(2,1)S(1)} %get-tuple-element.450, bf16[8,512,128]{2,1,0:T(8,128)(2,1)} %get-tuple-element.449, s32[]{:T(128)S(6)} %select_n.38), kind=kOutput, calls=%fused_computation.30.clone.1 | convolution fusion | flops 547356672 | bytes 13795332 | tf_op jit(solution)/shard_map/while/body/qhgd,khd->qhgk/dot_general | solution.py:104
  141.7 3.1 %fusion.104 = f32[8,512,128]{2,1,0:T(8,128)} fusion(f32[8,512,128]{2,1,0:T(8,128)} %get-tuple-element.426, s32[]{:T(128)S(6)} %select_n.38, bf16[512,8,512]{0,2,1:T(8,128)(2,1)S(1)} %fusion.103, bf16[512,1,8,128]{3,0,2,1:T(8,128)(2,1)S(1)} %get-tuple-element.447), kind=kOutput, calls=%fused_computation.40.clone.1 | convolution fusion | flops 537001984 | bytes 5767172 | tf_op jit(solution)/shard_map/while/body/qhgk,qhgd->khd/dot_general | solution.py:111
  144.8 2.0 bitcast_add_fusion.8
  146.8 0.0 copy-start.1
  146.8 1.3 copy-done.1
  148.8 1.9 convert.12
  150.7 0.3 copy-done.4
  151.0 0.2 convert.11
  151.2 1.5 pad_maximum_fusion
  152.7 0.0 reduce-scatter.2.cloned.1.call-update
  152.7 1.6 copy.35
  154.4 0.7 copy-done.2
  155.1 0.1 convert_element_type.97
  155.2 1.3 copy.44
  156.5 0.6 copy-done.6
  157.2 1.2 multiply_convert_fusion
  158.4 64.4 %reduce-scatter.2.cloned.1.call-done = bf16[1,512,256]{2,1,0:T(8,128)(2,1)} async-done(((bf16[8,512,256]{2,1,0:T(8,128)(2,1)}), bf16[1,512,256]{2,1,0:T(8,128)(2,1)}) %reduce-scatter.2.cloned.1.call-update) | async-done | bytes 262160 | tf_op jit(solution)/shard_map/reduce_scatter | solution.py:128
  222.8 1.7 fusion.67
  (24 shorter events, 0.2 us)
Async XLA Ops:
  7.2 4.2 %copy-start.7 = (bf16[1,512,1024]{2,1,0:T(8,128)(2,1)S(1)}, bf16[1,512,1024]{2,1,0:T(8,128)(2,1)}, u32[]{:S(2)}) copy-start(bf16[1,512,1024]{2,1,0:T(8,128)(2,1)} %param.11) | copy-start | bytes 3145732
  7.2 35.2 %all-gather.7.cloned.1.call-start = ((), (), s32[]{:S(2)}) async-start(), calls=%async_computation.2 | async-start | bytes 2359296 | tf_op jit(solution)/shard_map/all_gather | solution.py:32
  9.0 213.7 %reduce-scatter.2.cloned.1.call-start = ((), (), s32[]{:S(2)}) async-start(), calls=%async_computation.1 | async-start | bytes 2359296 | tf_op jit(solution)/shard_map/reduce_scatter | solution.py:128
  11.4 1.2 copy-start.9
  45.7 19.8 %copy-start.8 = (f32[1024]{0:T(1024)S(1)}, f32[1024]{0:T(1024)}, u32[]{:S(2)}) copy-start(f32[1024]{0:T(1024)} %param.16) | copy-start | bytes 12292
  68.3 36.8 %copy-start.3 = (bf16[512,1,8,128]{0,3,2,1:T(8,128)(2,1)S(1)}, bf16[512,1,8,128]{0,3,2,1:T(8,128)(2,1)}, u32[]{:S(2)}) copy-start(bf16[512,1,8,128]{0,3,2,1:T(8,128)(2,1)} %get-tuple-element.222) | copy-start | bytes 3145732
  104.1 1.0 copy-start.5
  123.5 3.1 %copy-start = (f32[512,1,8,128]{0,3,2,1:T(8,128)S(1)}, f32[512,1,8,128]{0,3,2,1:T(8,128)}, u32[]{:S(2)}) copy-start(f32[512,1,8,128]{0,3,2,1:T(8,128)} %get-tuple-element.425) | copy-start | bytes 6291460 | tf_op jit(solution)/shard_map/while
  128.6 1.3 copy-start.1
  141.7 3.1 %copy-start = (f32[512,1,8,128]{0,3,2,1:T(8,128)S(1)}, f32[512,1,8,128]{0,3,2,1:T(8,128)}, u32[]{:S(2)}) copy-start(f32[512,1,8,128]{0,3,2,1:T(8,128)} %get-tuple-element.425) | copy-start | bytes 6291460 | tf_op jit(solution)/shard_map/while
  146.8 1.3 copy-start.1
  148.8 2.2 copy-start.4
  152.7 2.3 %copy-start.2 = (f32[512,1,8,128]{0,3,2,1:T(8,128)S(1)}, f32[512,1,8,128]{0,3,2,1:T(8,128)}, u32[]{:S(2)}) copy-start(f32[512,1,8,128]{0,3,2,1:T(8,128)} %get-tuple-element.122) | copy-start | bytes 6291460
  155.2 2.0 copy-start.6
Sparse Core Ops, SparseCore 0:
  10.4 31.8 all-gather.6
  152.9 69.8 reduce-scatter.1

commit v3 on v1

--- a/solution.py
+++ b/solution.py
@@ -25,15 +25,15 @@
     per_group = queries.shape[2] // kv_cols
     resp_count = lax.axis_size("resp")
 
-    def by_distance(block):
-        rows = [block]
-        for distance in range(1, GROUP):
-            route = [(low, low ^ distance) for low in range(resp_count)]
-            rows.append(lax.ppermute(block, "resp", route))
-        return jnp.concatenate(rows, 0)
+    def exchange(block, axis, bit):
+        route = [(low, low ^ (1 << bit)) for low in range(lax.axis_size(axis))]
+        return lax.ppermute(block, axis, route)
 
-    cluster_key_rows = by_distance(key_states)
-    group_values = by_distance(value_states)
+    group_states = jnp.concatenate([key_states, value_states], -1)
+    for bit in range(GROUP.bit_length() - 1):
+        group_states = jnp.concatenate([group_states, exchange(group_states, "resp", bit)], 0)
+    cluster_key_rows = group_states[..., :kv_cols]
+    group_values = group_states[..., kv_cols:]
     query_heads = queries[0].reshape(seq_len, kv_heads, per_group, HD)
     score_scale = HD ** (-0.5)
     mate_rows = jnp.bitwise_xor(partners[0], my_index)
@@ -81,11 +81,15 @@
     attention = (weighted / denominator[..., None]).astype(jnp.bfloat16)
     log_total = running_max + jnp.log(denominator)
     attention_flat = attention.reshape(seq_len, -1).astype(jnp.float32)
-    square_sums = lax.psum(jnp.sum(attention_flat * attention_flat, -1), "head")
+    scaled_grad = out_grad[0].astype(jnp.float32) * norm_gain
+    row_sums = jnp.stack(
+        [jnp.sum(attention_flat * attention_flat, -1), jnp.sum(attention_flat * scaled_grad, -1)]
+    )
+    for bit in range(lax.axis_size("head").bit_length() - 1):
+        row_sums = row_sums + exchange(row_sums, "head", bit)
+    square_sums, dot_sums = row_sums[0], row_sums[1]
     inverse_rms = lax.rsqrt(square_sums / D + EPSILON)
     normed_out = (attention_flat * inverse_rms[:, None] * norm_gain).astype(jnp.bfloat16)[None]
-    scaled_grad = out_grad[0].astype(jnp.float32) * norm_gain
-    dot_sums = lax.psum(jnp.sum(attention_flat * scaled_grad, -1), "head")
     attention_grad = (
         inverse_rms[:, None] * scaled_grad
         - attention_flat * (inverse_rms**3 * dot_sums / D)[:, None]
@@ -126,16 +130,13 @@
         (jnp.zeros(stat_shape + (HD,), jnp.float32), zero_buffer, zero_buffer),
     )
     query_grads = query_grad.reshape(seq_len, -1).astype(jnp.bfloat16)[None]
-    def to_owners(buffer):
-        total = jnp.zeros(buffer.shape[1:], jnp.float32)
-        for distance in range(1, GROUP):
-            route = [(low, low ^ distance) for low in range(resp_count)]
-            sent = buffer[distance].astype(jnp.bfloat16)
-            total = total + lax.ppermute(sent, "resp", route).astype(jnp.float32)
-        return total[None]
-
-    key_total = to_owners(key_buffer)
-    value_total = to_owners(value_storage)
+    both_terms = jnp.concatenate([key_buffer, value_storage], -1)
+    for bit in reversed(range(GROUP.bit_length() - 1)):
+        half = 1 << bit
+        sent = both_terms[half : 2 * half].astype(jnp.bfloat16)
+        both_terms = both_terms[:half] + exchange(sent, "resp", bit).astype(jnp.float32)
+    key_total = both_terms[..., :kv_cols]
+    value_total = both_terms[..., kv_cols:]
     return (
         normed_out,
         query_grads,

time: 201 us -> 206 us (1.025)
  waiting for transfers between devices: 19.8 us -> 63.9 us
  starting transfers between devices: 41.3 us -> 22.5 us
  blocking collectives: 15.9 us -> 0 us
  local copies, waits for them, and re-layouts: 32.7 us -> 28.7 us
    ppermute x28 -> x9, waiting for transfers between devices: 19.8 us -> 63.9 us  [exchange(): return lax.ppermute(block, axis, route)]
    ppermute x28 -> x9, starting transfers between devices: 41.3 us -> 22.5 us  [exchange(): return lax.ppermute(block, axis, route)]
    psum x1 -> x0, blocking collectives: 15.9 us -> none  [body(): square_sums = lax.psum(jnp.sum(attention_flat * attention_flat, -1), 'head')]
    unnamed x36 -> x22, local copies, waits for them, and re-layouts: 14 us -> 7.37 us
    slice x0 -> x5, local copies, waits for them, and re-layouts: none -> 3.59 us  [the longest x1 1.9 us: body(): group_values = group_states[..., kv_cols:]]
    concatenate x0 -> x3, other arithmetic: none -> 2.55 us  [body(): jnp.concatenate([group_states, exchange(group_states, 'resp', bit)], 0)]
  transfers between devices with their start and end apart: 28 -> 9, of which waited for: 9 -> 8; matrix products, arithmetic and copies ran while one was open for 9% -> 4% of each run, Pallas kernels for 0% -> 0%
where the time goes in v3:
time: 206 us; the launch traced here: 204 us
  waiting for transfers between devices  63.9 us (31%)
  matrix products  56.2 us (27%)
  local copies, waits for them, and re-layouts  28.7 us (14%)
  starting transfers between devices  22.5 us (11%)
  loops' own time  17.2 us (8%)
  other arithmetic  15 us (7%)
    ppermute x9, waiting for transfers between devices, exchange(): return lax.ppermute(block, axis, route)  63.9 us
    ppermute x9, starting transfers between devices, exchange(): return lax.ppermute(block, axis, route)  22.5 us
    dot_general x6, matrix products, score_block(): jnp.einsum('qhgd,khd->qhgk', query_heads, mate_keys, preferred_element_ty...  13 us
    dot_general x3, matrix products, backward_step(): jnp.einsum('qhgk,qhgd->khd', back_probs.astype(jnp.bfloat16), attention_g...  9.81 us
    dot_general x3, matrix products, backward_step(): jnp.einsum('qhgd,khd->qhgk', attention_grad, mate_values, preferred_eleme...  9.3 us
    dot_general x3, matrix products, backward_step(): jnp.einsum('qhgk,qhgd->khd', score_grad, query_heads, preferred_element_t...  9.14 us
    dot_general x3, matrix products, forward_step(): jnp.einsum('qhgk,khd->qhgd', weights.astype(jnp.bfloat16), mate_values, p...  9.03 us
    another operation x1, loops' own time, body(): lax.fori_loop(0, live_count, forward_step, start_state)  8.61 us
  transfers between devices with their start and end apart: 9, of which 8 were waited for; matrix products, arithmetic and copies ran while one was open for 4% of the time, Pallas kernels for 0%

profile of v3, /device:TPU:1, one launch (start us, length us, event | category | flops | bytes accessed | tf_op | source)
XLA Modules:
  0.0 204.3 jit_solution(4613406764459742127)
XLA Ops:
  0.6 1.0 constant_dynamic-update-slice_fusion.1
  1.7 0.9 constant_dynamic-update-slice_fusion
  2.6 3.3 %collective-permute-start = (bf16[1,512,256]{2,1,0:T(8,128)(2,1)S(1)}, bf16[1,512,256]{2,1,0:T(8,128)(2,1)S(1)}, u32[]{:S(2)}, u32[]{:S(2)}) collective-permute-start(bf16[1,512,256]{2,1,0:T(8,128)(2,1)S(1)} %constant_dynamic-update-slice_fusion), channel_id=1, source_target_pairs={{0,8},{8,0},{16,24},{24,16},{32,40},{40,32},{48,56},{56,48},{64,72... | collective-permute-start | bytes 786440 | tf_op jit(solution)/shard_map/ppermute | solution.py:30
  5.9 1.2 collective-permute-done
  7.2 13.1 %collective-permute-done.1 = bf16[2,512,256]{2,1,0:T(8,128)(2,1)S(1)} collective-permute-done((bf16[2,512,256]{2,1,0:T(8,128)(2,1)S(1)}, bf16[2,512,256]{2,1,0:T(8,128)(2,1)S(1)}, u32[]{:S(2)}, u32[]{:S(2)}) %collective-permute-start.1) | collective-permute-done | bytes 524320 | tf_op jit(solution)/shard_map/ppermute | solution.py:30
  20.4 1.1 pad_maximum_fusion.1
  21.4 1.0 collective-permute-start.2
  22.5 1.3 copy.24
  23.8 1.5 copy.21
  25.3 0.7 copy.22
  26.0 20.7 %collective-permute-done.2 = bf16[4,512,256]{2,1,0:T(8,128)(2,1)} collective-permute-done((bf16[4,512,256]{2,1,0:T(8,128)(2,1)}, bf16[4,512,256]{2,1,0:T(8,128)(2,1)}, u32[]{:S(2)}, u32[]{:S(2)}) %collective-permute-start.2) | collective-permute-done | bytes 1048608 | tf_op jit(solution)/shard_map/ppermute | solution.py:30
  46.7 1.4 pad_maximum_fusion
  48.1 1.9 fusion.69
  50.3 30.1 %while.28 = (s32[]{:T(128)}, f32[512,1,8]{0,2,1:T(8,128)S(1)}, f32[512,1,8]{0,2,1:T(8,128)S(1)}, f32[512,1,8,128]{0,3,2,1:T(8,128)S(1)}, s32[]{:T(128)}, /*index...) while((s32[]{:T(128)}, f32[512,1,8]{0,2,1:T(8,128)S(1)}, ...), condition=%wide.region_3.4_spmd, body=%wide.region_0.3_spmd.sunk | while | flops 1091579904 | bytes 30933212 | solution.py:80
  53.5 2.2 %bitcast_reduce_fusion.2 = (f32[512,8]{0,1:T(8,128)S(1)}, f32[512,512,8]{1,0,2:T(8,128)S(1)}) fusion(bf16[512,1,8,128]{3,0,2,1:T(8,128)(2,1)S(1)} %get-tuple-element.381, bf16[8,512,128]{2,1,0:T(8,128)(2,1)} %get-tuple-element.380, s32[]{:T(128)S(6)} %select_n.27), kind=kOutput, calls=%fused_computation.1.clone.1 | convolution fusion | flops 541061120 | bytes 9584644 | tf_op jit(solution)/shard_map/while/body/qhgd,khd->qhgk/dot_general | solution.py:54
  55.7 1.4 fusion.96
  57.1 3.0 %bitcast_add_fusion.7 = f32[512,1,8,128]{0,3,2,1:T(8,128)S(1)} fusion(f32[512,1,8,128]{0,3,2,1:T(8,128)S(1)} %get-tuple-element.364, f32[512,512,8]{1,0,2:T(8,128)S(1)} %get-tuple-element.334, f32[512,8]{0,1:T(8,128)S(1)} %bitcast.244, f32[512,8]{0,1:T(8,128)S(1)} %get-tuple-element.335, bf16[8,512,128]{2,1,0:T(8,128)(2,1)} %get-tuple-element.382, ...), kind=kOutput, calls=%fused_computation.9.clone.1 | convolution fusion | flops 544210944 | bytes 12746756 | tf_op jit(solution)/shard_map/while/body/qhgk,khd->qhgd/dot_general | solution.py:66
  63.4 2.2 %bitcast_reduce_fusion.2 = (f32[512,8]{0,1:T(8,128)S(1)}, f32[512,512,8]{1,0,2:T(8,128)S(1)}) fusion(bf16[512,1,8,128]{3,0,2,1:T(8,128)(2,1)S(1)} %get-tuple-element.381, bf16[8,512,128]{2,1,0:T(8,128)(2,1)} %get-tuple-element.380, s32[]{:T(128)S(6)} %select_n.27), kind=kOutput, calls=%fused_computation.1.clone.1 | convolution fusion | flops 541061120 | bytes 9584644 | tf_op jit(solution)/shard_map/while/body/qhgd,khd->qhgk/dot_general | solution.py:54
  65.5 1.4 fusion.96
  66.9 3.0 %bitcast_add_fusion.7 = f32[512,1,8,128]{0,3,2,1:T(8,128)S(1)} fusion(f32[512,1,8,128]{0,3,2,1:T(8,128)S(1)} %get-tuple-element.364, f32[512,512,8]{1,0,2:T(8,128)S(1)} %get-tuple-element.334, f32[512,8]{0,1:T(8,128)S(1)} %bitcast.244, f32[512,8]{0,1:T(8,128)S(1)} %get-tuple-element.335, bf16[8,512,128]{2,1,0:T(8,128)(2,1)} %get-tuple-element.382, ...), kind=kOutput, calls=%fused_computation.9.clone.1 | convolution fusion | flops 544210944 | bytes 12746756 | tf_op jit(solution)/shard_map/while/body/qhgk,khd->qhgd/dot_general | solution.py:66
  73.2 2.2 %bitcast_reduce_fusion.2 = (f32[512,8]{0,1:T(8,128)S(1)}, f32[512,512,8]{1,0,2:T(8,128)S(1)}) fusion(bf16[512,1,8,128]{3,0,2,1:T(8,128)(2,1)S(1)} %get-tuple-element.381, bf16[8,512,128]{2,1,0:T(8,128)(2,1)} %get-tuple-element.380, s32[]{:T(128)S(6)} %select_n.27), kind=kOutput, calls=%fused_computation.1.clone.1 | convolution fusion | flops 541061120 | bytes 9584644 | tf_op jit(solution)/shard_map/while/body/qhgd,khd->qhgk/dot_general | solution.py:54
  75.4 1.4 fusion.96
  76.8 3.0 %bitcast_add_fusion.7 = f32[512,1,8,128]{0,3,2,1:T(8,128)S(1)} fusion(f32[512,1,8,128]{0,3,2,1:T(8,128)S(1)} %get-tuple-element.364, f32[512,512,8]{1,0,2:T(8,128)S(1)} %get-tuple-element.334, f32[512,8]{0,1:T(8,128)S(1)} %bitcast.244, f32[512,8]{0,1:T(8,128)S(1)} %get-tuple-element.335, bf16[8,512,128]{2,1,0:T(8,128)(2,1)} %get-tuple-element.382, ...), kind=kOutput, calls=%fused_computation.9.clone.1 | convolution fusion | flops 544210944 | bytes 12746756 | tf_op jit(solution)/shard_map/while/body/qhgk,khd->qhgd/dot_general | solution.py:66
  80.5 2.8 %fusion.61 = (f32[512]{0:T(512)S(1)}, f32[512]{0:T(512)S(1)}, bf16[512,1,8,128]{0,3,2,1:T(8,128)(2,1)}) fusion(f32[8,128]{1,0:T(8,128)S(1)} %bitcast.253, bf16[512,1,8,128]{0,3,2,1:T(8,128)(2,1)} %bitcast.245, f32[512,1,8,128]{0,3,2,1:T(8,128)S(1)} %get-tuple-element.119, f32[512,8]{0,1:T(8,128)S(1)} %bitcast.250), kind=kLoop, calls=%fused_computation.68 | loop fusion | flops 4717568 | bytes 4218880 | tf_op jit(solution)/shard_map/reduce_sum | solution.py:86
  83.4 2.4 %collective-permute-done.3 = f32[2,512]{1,0:T(2,128)S(1)} collective-permute-done((f32[2,512]{1,0:T(2,128)S(1)}, f32[2,512]{1,0:T(2,128)S(1)}, u32[]{:S(2)}, u32[]{:S(2)}) %collective-permute-start.3) | collective-permute-done | bytes 4128 | tf_op jit(solution)/shard_map/ppermute | solution.py:30
  85.8 1.5 collective-permute-start.4
  87.3 1.9 collective-permute-done.4
  89.3 5.4 %collective-permute-start.5 = (f32[2,512]{1,0:T(2,128)S(1)}, f32[2,512]{1,0:T(2,128)S(1)}, u32[]{:S(2)}, u32[]{:S(2)}) collective-permute-start(f32[2,512]{1,0:T(2,128)S(1)} %fusion.74), channel_id=1, source_target_pairs={{0,4},{1,5},{2,6},{3,7},{4,0},{5,1},{6,2},{7,3},{8,12},{9,13},{10,... | collective-permute-start | bytes 12296 | tf_op jit(solution)/shard_map/ppermute | solution.py:30
  94.7 1.2 collective-permute-done.5
  95.9 2.0 fusion.60
  98.9 1.5 broadcast_in_dim.12.clone
  100.5 1.5 broadcast_in_dim.12
  101.9 1.6 broadcast.154
  103.5 55.0 %while.29 = (s32[]{:T(128)}, f32[512,1,8,128]{0,3,2,1:T(8,128)}, f32[8,512,128]{2,1,0:T(8,128)}, f32[8,512,128]{2,1,0:T(8,128)}, s32[]{:T(128)}, /*index=5*/s32[...) while((s32[]{:T(128)}, f32[512,1,8,128]{0,3,2,1:T(8,128)}, ...), condition=%wide.region_8.9_spmd, body=%wide.region_7.8_spmd.sunk | while | flops 2702376960 | bytes 64405816 | solution.py:126
  106.7 2.2 %fusion.107 = f32[512,512,8]{1,0,2:T(8,128)S(1)} fusion(bf16[512,1,8,128]{3,0,2,1:T(8,128)(2,1)S(1)} %get-tuple-element.426, bf16[8,512,128]{2,1,0:T(8,128)(2,1)} %get-tuple-element.425, s32[]{:T(128)S(6)} %select_n.29), kind=kOutput, calls=%fused_computation.44.clone.1 | convolution fusion | flops 536870912 | bytes 9568260 | tf_op jit(solution)/shard_map/while/body/qhgd,khd->qhgk/dot_general | solution.py:54
  108.9 3.3 %fusion.110 = f32[8,512,128]{2,1,0:T(8,128)} fusion(f32[8,512,128]{2,1,0:T(8,128)} %get-tuple-element.406, s32[]{:T(128)S(6)} %select_n.29, f32[512,512,8]{1,0,2:T(8,128)S(1)} %fusion.107, f32[512,8]{0,1:T(8,128)S(1)} %bitcast.246, bf16[512,1,8,128]{3,0,2,1:T(8,128)(2,1)S(1)} %get-tuple-element.429), kind=kOutput, calls=%fused_computation.38.clone.1 | convolution fusion | flops 543227904 | bytes 9977860 | tf_op jit(solution)/shard_map/while/body/qhgk,qhgd->khd/dot_general | solution.py:104
  112.1 3.1 %fusion.108 = bf16[512,8,512]{0,2,1:T(8,128)(2,1)S(1)} fusion(f32[512,512,8]{1,0,2:T(8,128)S(1)} %fusion.107, f32[512,8]{0,1:T(8,128)S(1)} %bitcast.252, f32[512,8]{0,1:T(8,128)S(1)} %bitcast.247, bf16[512,1,8,128]{3,0,2,1:T(8,128)(2,1)S(1)} %get-tuple-element.429, bf16[8,512,128]{2,1,0:T(8,128)(2,1)} %get-tuple-element.428, s32[]{:T(128)S(6)} %select_n.29), kind=kOutput, calls=%fused_computation.30.clone.1 | convolution fusion | flops 547356672 | bytes 13795332 | tf_op jit(solution)/shard_map/while/body/qhgd,khd->qhgk/dot_general | solution.py:110
  115.3 3.0 %fusion.109 = f32[8,512,128]{2,1,0:T(8,128)} fusion(f32[8,512,128]{2,1,0:T(8,128)} %get-tuple-element.405, s32[]{:T(128)S(6)} %select_n.29, bf16[512,8,512]{0,2,1:T(8,128)(2,1)S(1)} %fusion.108, bf16[512,1,8,128]{3,0,2,1:T(8,128)(2,1)S(1)} %get-tuple-element.426), kind=kOutput, calls=%fused_computation.40.clone.1 | convolution fusion | flops 537001984 | bytes 5767172 | tf_op jit(solution)/shard_map/while/body/qhgk,qhgd->khd/dot_general | solution.py:117
  118.3 2.0 bitcast_add_fusion.8
  120.3 1.3 copy-done.1
  124.8 2.2 %fusion.107 = f32[512,512,8]{1,0,2:T(8,128)S(1)} fusion(bf16[512,1,8,128]{3,0,2,1:T(8,128)(2,1)S(1)} %get-tuple-element.426, bf16[8,512,128]{2,1,0:T(8,128)(2,1)} %get-tuple-element.425, s32[]{:T(128)S(6)} %select_n.29), kind=kOutput, calls=%fused_computation.44.clone.1 | convolution fusion | flops 536870912 | bytes 9568260 | tf_op jit(solution)/shard_map/while/body/qhgd,khd->qhgk/dot_general | solution.py:54
  127.0 3.3 %fusion.110 = f32[8,512,128]{2,1,0:T(8,128)} fusion(f32[8,512,128]{2,1,0:T(8,128)} %get-tuple-element.406, s32[]{:T(128)S(6)} %select_n.29, f32[512,512,8]{1,0,2:T(8,128)S(1)} %fusion.107, f32[512,8]{0,1:T(8,128)S(1)} %bitcast.246, bf16[512,1,8,128]{3,0,2,1:T(8,128)(2,1)S(1)} %get-tuple-element.429), kind=kOutput, calls=%fused_computation.38.clone.1 | convolution fusion | flops 543227904 | bytes 9977860 | tf_op jit(solution)/shard_map/while/body/qhgk,qhgd->khd/dot_general | solution.py:104
  130.2 3.1 %fusion.108 = bf16[512,8,512]{0,2,1:T(8,128)(2,1)S(1)} fusion(f32[512,512,8]{1,0,2:T(8,128)S(1)} %fusion.107, f32[512,8]{0,1:T(8,128)S(1)} %bitcast.252, f32[512,8]{0,1:T(8,128)S(1)} %bitcast.247, bf16[512,1,8,128]{3,0,2,1:T(8,128)(2,1)S(1)} %get-tuple-element.429, bf16[8,512,128]{2,1,0:T(8,128)(2,1)} %get-tuple-element.428, s32[]{:T(128)S(6)} %select_n.29), kind=kOutput, calls=%fused_computation.30.clone.1 | convolution fusion | flops 547356672 | bytes 13795332 | tf_op jit(solution)/shard_map/while/body/qhgd,khd->qhgk/dot_general | solution.py:110
  133.4 3.1 %fusion.109 = f32[8,512,128]{2,1,0:T(8,128)} fusion(f32[8,512,128]{2,1,0:T(8,128)} %get-tuple-element.405, s32[]{:T(128)S(6)} %select_n.29, bf16[512,8,512]{0,2,1:T(8,128)(2,1)S(1)} %fusion.108, bf16[512,1,8,128]{3,0,2,1:T(8,128)(2,1)S(1)} %get-tuple-element.426), kind=kOutput, calls=%fused_computation.40.clone.1 | convolution fusion | flops 537001984 | bytes 5767172 | tf_op jit(solution)/shard_map/while/body/qhgk,qhgd->khd/dot_general | solution.py:117
  136.4 2.0 bitcast_add_fusion.8
  138.4 1.3 copy-done.1
  142.9 2.2 %fusion.107 = f32[512,512,8]{1,0,2:T(8,128)S(1)} fusion(bf16[512,1,8,128]{3,0,2,1:T(8,128)(2,1)S(1)} %get-tuple-element.426, bf16[8,512,128]{2,1,0:T(8,128)(2,1)} %get-tuple-element.425, s32[]{:T(128)S(6)} %select_n.29), kind=kOutput, calls=%fused_computation.44.clone.1 | convolution fusion | flops 536870912 | bytes 9568260 | tf_op jit(solution)/shard_map/while/body/qhgd,khd->qhgk/dot_general | solution.py:54
  145.1 3.3 %fusion.110 = f32[8,512,128]{2,1,0:T(8,128)} fusion(f32[8,512,128]{2,1,0:T(8,128)} %get-tuple-element.406, s32[]{:T(128)S(6)} %select_n.29, f32[512,512,8]{1,0,2:T(8,128)S(1)} %fusion.107, f32[512,8]{0,1:T(8,128)S(1)} %bitcast.246, bf16[512,1,8,128]{3,0,2,1:T(8,128)(2,1)S(1)} %get-tuple-element.429), kind=kOutput, calls=%fused_computation.38.clone.1 | convolution fusion | flops 543227904 | bytes 9977860 | tf_op jit(solution)/shard_map/while/body/qhgk,qhgd->khd/dot_general | solution.py:104
  148.3 3.1 %fusion.108 = bf16[512,8,512]{0,2,1:T(8,128)(2,1)S(1)} fusion(f32[512,512,8]{1,0,2:T(8,128)S(1)} %fusion.107, f32[512,8]{0,1:T(8,128)S(1)} %bitcast.252, f32[512,8]{0,1:T(8,128)S(1)} %bitcast.247, bf16[512,1,8,128]{3,0,2,1:T(8,128)(2,1)S(1)} %get-tuple-element.429, bf16[8,512,128]{2,1,0:T(8,128)(2,1)} %get-tuple-element.428, s32[]{:T(128)S(6)} %select_n.29), kind=kOutput, calls=%fused_computation.30.clone.1 | convolution fusion | flops 547356672 | bytes 13795332 | tf_op jit(solution)/shard_map/while/body/qhgd,khd->qhgk/dot_general | solution.py:110
  151.5 3.1 %fusion.109 = f32[8,512,128]{2,1,0:T(8,128)} fusion(f32[8,512,128]{2,1,0:T(8,128)} %get-tuple-element.405, s32[]{:T(128)S(6)} %select_n.29, bf16[512,8,512]{0,2,1:T(8,128)(2,1)S(1)} %fusion.108, bf16[512,1,8,128]{3,0,2,1:T(8,128)(2,1)S(1)} %get-tuple-element.426), kind=kOutput, calls=%fused_computation.40.clone.1 | convolution fusion | flops 537001984 | bytes 5767172 | tf_op jit(solution)/shard_map/while/body/qhgk,qhgd->khd/dot_general | solution.py:117
  154.5 2.0 bitcast_add_fusion.8
  156.5 1.3 copy-done.1
  158.5 1.9 constant_dynamic-update-slice_fusion.3
  161.0 2.6 %collective-permute-start.6 = (bf16[4,512,256]{2,1,0:T(8,128)(2,1)S(1)}, bf16[4,512,256]{2,1,0:T(8,128)(2,1)S(1)}, u32[]{:S(2)}, u32[]{:S(2)}) collective-permute-start(bf16[4,512,256]{2,1,0:T(8,128)(2,1)S(1)} %slice.78), channel_id=1, source_target_pairs={{0,32},{8,40},{16,48},{24,56},{32,0},{40,8},{48,16},{56,24},{64,96... | collective-permute-start | bytes 3145736 | tf_op jit(solution)/shard_map/ppermute | solution.py:30
  163.7 18.0 %collective-permute-done.6 = bf16[4,512,256]{2,1,0:T(8,128)(2,1)S(1)} collective-permute-done((bf16[4,512,256]{2,1,0:T(8,128)(2,1)S(1)}, bf16[4,512,256]{2,1,0:T(8,128)(2,1)S(1)}, u32[]{:S(2)}, u32[]{:S(2)}) %collective-permute-start.6) | collective-permute-done | bytes 1048608 | tf_op jit(solution)/shard_map/ppermute | solution.py:30
  181.9 1.3 copy-done.7
  183.2 0.8 slice.79
  184.1 1.6 copy.25
  185.9 1.3 copy.33
  187.2 5.2 %collective-permute-done.7 = bf16[2,512,256]{2,1,0:T(8,128)(2,1)} collective-permute-done((bf16[2,512,256]{2,1,0:T(8,128)(2,1)}, bf16[2,512,256]{2,1,0:T(8,128)(2,1)}, u32[]{:S(2)}, u32[]{:S(2)}) %collective-permute-start.7) | collective-permute-done | bytes 524320 | tf_op jit(solution)/shard_map/ppermute | solution.py:30
  192.4 1.5 slice_add_fusion.1
  193.9 8.4 %collective-permute-start.8 = (bf16[1,512,256]{2,1,0:T(8,128)(2,1)S(1)}, bf16[1,512,256]{2,1,0:T(8,128)(2,1)S(1)}, u32[]{:S(2)}, u32[]{:S(2)}) collective-permute-start(bf16[1,512,256]{2,1,0:T(8,128)(2,1)S(1)} %slice.80), channel_id=1, source_target_pairs={{0,8},{8,0},{16,24},{24,16},{32,40},{40,32},{48,56},{56,48},{64,72... | collective-permute-start | bytes 786440 | tf_op jit(solution)/shard_map/ppermute | solution.py:30
  202.3 1.2 multiply_convert_fusion
  203.6 0.7 fusion.70
  (65 shorter events, 6.2 us)
Async XLA Ops:
  0.6 21.8 %copy-start.8 = (bf16[1,512,1024]{2,1,0:T(8,128)(2,1)S(1)}, bf16[1,512,1024]{2,1,0:T(8,128)(2,1)}, u32[]{:S(2)}) copy-start(bf16[1,512,1024]{2,1,0:T(8,128)(2,1)} %param.17) | copy-start | bytes 3145732
  2.6 4.5 %collective-permute-start = (bf16[1,512,256]{2,1,0:T(8,128)(2,1)S(1)}, bf16[1,512,256]{2,1,0:T(8,128)(2,1)S(1)}, u32[]{:S(2)}, u32[]{:S(2)}) collective-permute-start(bf16[1,512,256]{2,1,0:T(8,128)(2,1)S(1)} %constant_dynamic-update-slice_fusion), channel_id=1, source_target_pairs={{0,8},{8,0},{16,24},{24,16},{32,40},{40,32},{48,56},{56,48},{64,72... | collective-permute-start | bytes 786440 | tf_op jit(solution)/shard_map/ppermute | solution.py:30
  7.1 13.2 %collective-permute-start.1 = (bf16[2,512,256]{2,1,0:T(8,128)(2,1)S(1)}, bf16[2,512,256]{2,1,0:T(8,128)(2,1)S(1)}, u32[]{:S(2)}, u32[]{:S(2)}) collective-permute-start(bf16[2,512,256]{2,1,0:T(8,128)(2,1)S(1)} %pad_maximum_fusion.2), channel_id=1, source_target_pairs={{0,16},{8,24},{16,0},{24,8},{32,48},{40,56},{48,32},{56,40},{64,80... | collective-permute-start | bytes 1572872 | tf_op jit(solution)/shard_map/ppermute | solution.py:30
  21.4 25.3 %collective-permute-start.2 = (bf16[4,512,256]{2,1,0:T(8,128)(2,1)}, bf16[4,512,256]{2,1,0:T(8,128)(2,1)}, u32[]{:S(2)}, u32[]{:S(2)}) collective-permute-start(bf16[4,512,256]{2,1,0:T(8,128)(2,1)} %pad_maximum_fusion.1), channel_id=1, source_target_pairs={{0,32},{8,40},{16,48},{24,56},{32,0},{40,8},{48,16},{56,24},{64,96... | collective-permute-start | bytes 3145736 | tf_op jit(solution)/shard_map/ppermute | solution.py:30
  23.8 2.2 %copy-start.10 = (s32[1,3]{1,0:T(1,128)S(1)}, s32[1,3]{1,0:T(1,128)}, u32[]{:S(2)}) copy-start(s32[1,3]{1,0:T(1,128)} %param.14) | copy-start | bytes 40
  50.3 30.2 %copy-start.9 = (f32[1024]{0:T(1024)S(1)}, f32[1024]{0:T(1024)}, u32[]{:S(2)}) copy-start(f32[1024]{0:T(1024)} %param.16) | copy-start | bytes 12292
  83.2 14.7 %copy-start.3 = (bf16[512,1,8,128]{0,3,2,1:T(8,128)(2,1)S(1)}, bf16[512,1,8,128]{0,3,2,1:T(8,128)(2,1)}, u32[]{:S(2)}) copy-start(bf16[512,1,8,128]{0,3,2,1:T(8,128)(2,1)} %get-tuple-element.201) | copy-start | bytes 3145732
  83.3 2.5 %collective-permute-start.3 = (f32[2,512]{1,0:T(2,128)S(1)}, f32[2,512]{1,0:T(2,128)S(1)}, u32[]{:S(2)}, u32[]{:S(2)}) collective-permute-start(f32[2,512]{1,0:T(2,128)S(1)} %pad_maximum_fusion.3), channel_id=1, source_target_pairs={{0,1},{1,0},{2,3},{3,2},{4,5},{5,4},{6,7},{7,6},{8,9},{9,8},{10,11... | collective-permute-start | bytes 12296 | tf_op jit(solution)/shard_map/ppermute | solution.py:30
  85.8 3.4 %collective-permute-start.4 = (f32[2,512]{1,0:T(2,128)S(1)}, f32[2,512]{1,0:T(2,128)S(1)}, u32[]{:S(2)}, u32[]{:S(2)}) collective-permute-start(f32[2,512]{1,0:T(2,128)S(1)} %fusion.68), channel_id=1, source_target_pairs={{0,2},{1,3},{2,0},{3,1},{4,6},{5,7},{6,4},{7,5},{8,10},{9,11},{10,... | collective-permute-start | bytes 12296 | tf_op jit(solution)/shard_map/ppermute | solution.py:30
  89.3 6.6 %collective-permute-start.5 = (f32[2,512]{1,0:T(2,128)S(1)}, f32[2,512]{1,0:T(2,128)S(1)}, u32[]{:S(2)}, u32[]{:S(2)}) collective-permute-start(f32[2,512]{1,0:T(2,128)S(1)} %fusion.74), channel_id=1, source_target_pairs={{0,4},{1,5},{2,6},{3,7},{4,0},{5,1},{6,2},{7,3},{8,12},{9,13},{10,... | collective-permute-start | bytes 12296 | tf_op jit(solution)/shard_map/ppermute | solution.py:30
  115.2 3.0 %copy-start = (f32[512,1,8,128]{0,3,2,1:T(8,128)S(1)}, f32[512,1,8,128]{0,3,2,1:T(8,128)}, u32[]{:S(2)}) copy-start(f32[512,1,8,128]{0,3,2,1:T(8,128)} %get-tuple-element.404) | copy-start | bytes 6291460 | tf_op jit(solution)/shard_map/while
  120.3 1.3 copy-start.1
  133.3 3.1 %copy-start = (f32[512,1,8,128]{0,3,2,1:T(8,128)S(1)}, f32[512,1,8,128]{0,3,2,1:T(8,128)}, u32[]{:S(2)}) copy-start(f32[512,1,8,128]{0,3,2,1:T(8,128)} %get-tuple-element.404) | copy-start | bytes 6291460 | tf_op jit(solution)/shard_map/while
  138.4 1.3 copy-start.1
  151.5 3.1 %copy-start = (f32[512,1,8,128]{0,3,2,1:T(8,128)S(1)}, f32[512,1,8,128]{0,3,2,1:T(8,128)}, u32[]{:S(2)}) copy-start(f32[512,1,8,128]{0,3,2,1:T(8,128)} %get-tuple-element.404) | copy-start | bytes 6291460 | tf_op jit(solution)/shard_map/while
  156.5 1.3 copy-start.1
  158.5 2.2 %copy-start.5 = (f32[8,512,128]{2,1,0:T(8,128)S(1)}, f32[8,512,128]{2,1,0:T(8,128)}, u32[]{:S(2)}) copy-start(f32[8,512,128]{2,1,0:T(8,128)} %get-tuple-element.124) | copy-start | bytes 6291460
  161.0 23.1 %copy-start.4 = (bf16[512,1,8,128]{0,3,2,1:T(8,128)(2,1)S(1)}, bf16[512,1,8,128]{0,3,2,1:T(8,128)(2,1)}, u32[]{:S(2)}) copy-start(bf16[512,1,8,128]{0,3,2,1:T(8,128)(2,1)} %get-tuple-element.201) | copy-start | bytes 3145732
  161.0 20.7 %collective-permute-start.6 = (bf16[4,512,256]{2,1,0:T(8,128)(2,1)S(1)}, bf16[4,512,256]{2,1,0:T(8,128)(2,1)S(1)}, u32[]{:S(2)}, u32[]{:S(2)}) collective-permute-start(bf16[4,512,256]{2,1,0:T(8,128)(2,1)S(1)} %slice.78), channel_id=1, source_target_pairs={{0,32},{8,40},{16,48},{24,56},{32,0},{40,8},{48,16},{56,24},{64,96... | collective-permute-start | bytes 3145736 | tf_op jit(solution)/shard_map/ppermute | solution.py:30
  181.9 1.3 copy-start.7
  183.2 2.5 %copy-start.2 = (f32[512,1,8,128]{0,3,2,1:T(8,128)S(1)}, f32[512,1,8,128]{0,3,2,1:T(8,128)}, u32[]{:S(2)}) copy-start(f32[512,1,8,128]{0,3,2,1:T(8,128)} %get-tuple-element.122) | copy-start | bytes 6291460
  184.1 8.3 %collective-permute-start.7 = (bf16[2,512,256]{2,1,0:T(8,128)(2,1)}, bf16[2,512,256]{2,1,0:T(8,128)(2,1)}, u32[]{:S(2)}, u32[]{:S(2)}) collective-permute-start(bf16[2,512,256]{2,1,0:T(8,128)(2,1)} %slice.79), channel_id=1, source_target_pairs={{0,16},{8,24},{16,0},{24,8},{32,48},{40,56},{48,32},{56,40},{64,80... | collective-permute-start | bytes 1572872 | tf_op jit(solution)/shard_map/ppermute | solution.py:30
  185.8 16.4 %copy-start.6 = (f32[1,512,1024]{2,1,0:T(8,128)S(1)}, f32[1,512,1024]{2,1,0:T(8,128)}, u32[]{:S(2)}) copy-start(f32[1,512,1024]{2,1,0:T(8,128)} %copy.25) | copy-start | bytes 6291460
  193.9 9.6 %collective-permute-start.8 = (bf16[1,512,256]{2,1,0:T(8,128)(2,1)S(1)}, bf16[1,512,256]{2,1,0:T(8,128)(2,1)S(1)}, u32[]{:S(2)}, u32[]{:S(2)}) collective-permute-start(bf16[1,512,256]{2,1,0:T(8,128)(2,1)S(1)} %slice.80), channel_id=1, source_target_pairs={{0,8},{8,0},{16,24},{24,16},{32,40},{40,32},{48,56},{56,48},{64,72... | collective-permute-start | bytes 786440 | tf_op jit(solution)/shard_map/ppermute | solution.py:30

commit v4 on v3

v4 whole, which is shorter than its diff:
```python
import functools

import jax
import jax.numpy as jnp
from jax import lax
from jax.experimental import pallas as pl
from jax.experimental.pallas import tpu as pltpu
from jax.sharding import PartitionSpec as P

HD = 128
D = 8192
GROUP = 8
SLOTS = 3


EPSILON = 1e-05
NEG_FLOOR = -1e30
SCORE_SCALE = HD ** (-0.5)

TRANS_B = (((1,), (1,)), ((), ()))
TRANS_A = (((0,), (0,)), ((), ()))


def slot_scores(count_ref, query_head, mate_keys, slot):
    scores = lax.dot_general(query_head, mate_keys, TRANS_B, preferred_element_type=jnp.float32)
    return jnp.where(slot < count_ref[0], scores * SCORE_SCALE, NEG_FLOOR)


def forward_kernel(count_ref, q_ref, k_ref, v_ref, out_ref, lse_ref):
    query_head = q_ref[...]
    scores = [slot_scores(count_ref, query_head, k_ref[slot], slot) for slot in range(SLOTS)]
    row_max = functools.reduce(
        jnp.maximum, [jnp.max(block, axis=1, keepdims=True) for block in scores]
    )
    exps = [jnp.exp(block - row_max) for block in scores]
    denominator = sum(jnp.sum(block, axis=1, keepdims=True) for block in exps)
    weighted = sum(
        jnp.dot(exps[slot].astype(jnp.bfloat16), v_ref[slot], preferred_element_type=jnp.float32)
        for slot in range(SLOTS)
    )
    out_ref[...] = (weighted / denominator).astype(out_ref.dtype)
    lse_ref[...] = jnp.broadcast_to(row_max + jnp.log(denominator), lse_ref.shape)


def backward_kernel(
    count_ref, q_ref, k_ref, v_ref, grad_ref, att_ref, lse_ref, dq_ref, dk_ref, dv_ref
):
    @pl.when(pl.program_id(0) == 0)
    def _():
        dk_ref[...] = jnp.zeros_like(dk_ref)
        dv_ref[...] = jnp.zeros_like(dv_ref)

    query_head = q_ref[...]
    grad_head = grad_ref[...]
    row_delta = jnp.sum(
        grad_head.astype(jnp.float32) * att_ref[...].astype(jnp.float32), axis=1, keepdims=True
    )
    log_total = lse_ref[:, :1]
    query_grad = jnp.zeros(dq_ref.shape, jnp.float32)
    for slot in range(SLOTS):
        mate_keys = k_ref[slot]
        back_probs = jnp.exp(slot_scores(count_ref, query_head, mate_keys, slot) - log_total)
        dv_ref[slot] += lax.dot_general(
            back_probs.astype(jnp.bfloat16), grad_head, TRANS_A, preferred_element_type=jnp.float32
        )
        prob_grad = lax.dot_general(
            grad_head, v_ref[slot], TRANS_B, preferred_element_type=jnp.float32
        )
        score_grad = (back_probs * (prob_grad - row_delta)).astype(jnp.bfloat16)
        query_grad = query_grad + jnp.dot(score_grad, mate_keys, preferred_element_type=jnp.float32)
        dk_ref[slot] += SCORE_SCALE * lax.dot_general(
            score_grad, query_head, TRANS_A, preferred_element_type=jnp.float32
        )
    dq_ref[...] = (SCORE_SCALE * query_grad).astype(dq_ref.dtype)


def attention_forward(count, queries, mate_keys, mate_values):
    seq_len, width = queries.shape
    heads = width // HD
    head_block = pl.BlockSpec((seq_len, HD), lambda h, c: (0, h))
    slot_block = pl.BlockSpec((SLOTS, seq_len, HD), lambda h, c: (0, 0, 0))
    return pl.pallas_call(
        forward_kernel,
        grid_spec=pltpu.PrefetchScalarGridSpec(
            num_scalar_prefetch=1,
            grid=(heads,),
            in_specs=[head_block, slot_block, slot_block],
            out_specs=[head_block, head_block],
        ),
        out_shape=[
            jax.ShapeDtypeStruct((seq_len, width), jnp.bfloat16),
            jax.ShapeDtypeStruct((seq_len, width), jnp.float32),
        ],
    )(count, queries, mate_keys, mate_values)


def attention_backward(count, queries, mate_keys, mate_values, attention_grad, attention, log_total):
    seq_len, width = queries.shape
    heads = width // HD
    head_block = pl.BlockSpec((seq_len, HD), lambda h, c: (0, h))
    slot_block = pl.BlockSpec((SLOTS, seq_len, HD), lambda h, c: (0, 0, 0))
    return pl.pallas_call(
        backward_kernel,
        grid_spec=pltpu.PrefetchScalarGridSpec(
            num_scalar_prefetch=1,
            grid=(heads,),
            in_specs=[head_block, slot_block, slot_block, head_block, head_block, head_block],
            out_specs=[head_block, slot_block, slot_block],
        ),
        out_shape=[
            jax.ShapeDtypeStruct((seq_len, width), jnp.bfloat16),
            jax.ShapeDtypeStruct((SLOTS, seq_len, HD), jnp.float32),
            jax.ShapeDtypeStruct((SLOTS, seq_len, HD), jnp.float32),
        ],
        compiler_params=pltpu.CompilerParams(dimension_semantics=("arbitrary",)),
    )(count, queries, mate_keys, mate_values, attention_grad, attention, log_total)


def exchange(block, axis, bit):
    route = [(low, low ^ (1 << bit)) for low in range(lax.axis_size(axis))]
    return lax.ppermute(block, axis, route)


def gather_group(block):
    for bit in range(GROUP.bit_length() - 1):
        block = jnp.concatenate([block, exchange(block, "resp", bit)], 0)
    return block


def return_group(terms):
    for bit in reversed(range(GROUP.bit_length() - 1)):
        half = 1 << bit
        sent = terms[half : 2 * half].astype(jnp.bfloat16)
        terms = terms[:half] + exchange(sent, "resp", bit).astype(jnp.float32)
    return terms


def body(queries, key_states, value_states, partners, counts, norm_gain, out_grad):
    my_index = lax.axis_index("resp")
    seq_len = queries.shape[1]
    mate_rows = jnp.bitwise_xor(partners[0], my_index)
    count = counts.astype(jnp.int32)
    mate_keys = jnp.take(gather_group(key_states), mate_rows, axis=0)
    mate_values = jnp.take(gather_group(value_states), mate_rows, axis=0)

    attention, log_total = attention_forward(count, queries[0], mate_keys, mate_values)
    attention_flat = attention.astype(jnp.float32)
    scaled_grad = out_grad[0].astype(jnp.float32) * norm_gain
    row_sums = jnp.stack(
        [jnp.sum(attention_flat * attention_flat, -1), jnp.sum(attention_flat * scaled_grad, -1)]
    )
    for bit in range(lax.axis_size("head").bit_length() - 1):
        row_sums = row_sums + exchange(row_sums, "head", bit)
    square_sums, dot_sums = row_sums[0], row_sums[1]
    inverse_rms = lax.rsqrt(square_sums / D + EPSILON)
    normed_out = (attention_flat * inverse_rms[:, None] * norm_gain).astype(jnp.bfloat16)[None]
    attention_grad = (
        inverse_rms[:, None] * scaled_grad
        - attention_flat * (inverse_rms**3 * dot_sums / D)[:, None]
    ).astype(jnp.bfloat16)

    query_grads, key_terms, value_terms = attention_backward(
        count, queries[0], mate_keys, mate_values, attention_grad, attention, log_total
    )
    zero_rows = jnp.zeros((GROUP,) + key_terms.shape[1:], jnp.float32)
    key_total = return_group(zero_rows.at[mate_rows].add(key_terms))
    value_total = return_group(zero_rows.at[mate_rows].add(value_terms))
    return (
        normed_out,
        query_grads[None],
        key_total.astype(jnp.bfloat16),
        value_total.astype(jnp.bfloat16),
    )


def solution(mesh):
    placed = (
        P("resp", None, "head"),
        P("resp", None, "head"),
        P("resp", None, "head"),
        P("resp", None),
        P("resp"),
        P("head"),
        P("resp", None, "head"),
    )
    return jax.shard_map(
        body,
        mesh=mesh,
        in_specs=placed,
        out_specs=(
            P("resp", None, "head"),
            P("resp", None, "head"),
            P("resp", None, "head"),
            P("resp", None, "head"),
        ),
        check_vma=False,
    )
```

time: 206 us -> 150 us (0.73)
  matrix products: 56.2 us -> 0 us
  Pallas kernels: 0 us -> 43.9 us
  local copies, waits for them, and re-layouts: 28.7 us -> 4.26 us
  loops' own time: 17.2 us -> 0 us
  waiting for transfers between devices: 63.9 us -> 51.5 us
  starting transfers between devices: 22.5 us -> 34.5 us
    dot_general x21 -> x0, matrix products: 56.2 us -> none  [the longest x6 13 us: score_block(): jnp.einsum('qhgd,khd->qhgk', query_heads, mate_keys, preferred_element_ty...]
    pallas_call x0 -> x2, Pallas kernels: none -> 43.9 us  [the longest x1 24.7 us: attention_backward(): pl.pallas_call(backward_kernel, grid_spec=pltpu.PrefetchScalarGridSpec(nu...]
    another operation x2 -> x0, loops' own time: 17.2 us -> none  [the longest x1 8.61 us: body(): lax.fori_loop(0, live_count, forward_step, start_state)]
    ppermute x9 -> x15, waiting for transfers between devices: 63.9 us -> 51.5 us  [exchange(): return lax.ppermute(block, axis, route)]
    ppermute x9 -> x15, starting transfers between devices: 22.5 us -> 34.5 us  [exchange(): return lax.ppermute(block, axis, route)]
    unnamed x22 -> x18, local copies, waits for them, and re-layouts: 7.37 us -> 1.7 us
    while x17 -> x0, local copies, waits for them, and re-layouts: 5.3 us -> none
    reduce_sum x4 -> x0, other arithmetic: 4.46 us -> none  [the longest x3 4.15 us: forward_step(): denominator = denominator * rescale + jnp.sum(weights, -1)]
  transfers between devices with their start and end apart: 9 -> 15, of which waited for: 8 -> 12; matrix products, arithmetic and copies ran while one was open for 4% -> 5% of each run, Pallas kernels for 0% -> 0%
where the time goes in v4:
time: 150 us
  waiting for transfers between devices  51.5 us (34%)
  Pallas kernels  43.9 us (29%)
  starting transfers between devices  34.5 us (23%)
  other arithmetic  13.9 us (9%)
  local copies, waits for them, and re-layouts  4.26 us (3%)
  between operations  1.57 us (1%)
    ppermute x15, waiting for transfers between devices, exchange(): return lax.ppermute(block, axis, route)  51.5 us
    ppermute x15, starting transfers between devices, exchange(): return lax.ppermute(block, axis, route)  34.5 us
    pallas_call x1, Pallas kernels, attention_backward(): pl.pallas_call(backward_kernel, grid_spec=pltpu.PrefetchScalarGridSpec(nu...  24.7 us
    pallas_call x1, Pallas kernels, attention_forward(): pl.pallas_call(forward_kernel, grid_spec=pltpu.PrefetchScalarGridSpec(num...  19.2 us
    concatenate x6, other arithmetic, gather_group(): block = jnp.concatenate([block, exchange(block, 'resp', bit)], 0)  4.12 us
  transfers between devices with their start and end apart: 15, of which 12 were waited for; matrix products, arithmetic and copies ran while one was open for 5% of the time, Pallas kernels for 0%

profile of v4, /device:TPU:1, one launch (start us, length us, event | category | flops | bytes accessed | tf_op | source)
XLA Modules:
  0.0 149.7 jit_solution(5339182338724819807)
XLA Ops:
  0.6 0.0 copy-start.3
  0.6 0.0 copy-start.4
  0.7 3.3 %collective-permute-start.3 = (bf16[1,512,128]{2,1,0:T(8,128)(2,1)}, bf16[1,512,128]{2,1,0:T(8,128)(2,1)S(1)}, u32[]{:S(2)}, u32[]{:S(2)}) collective-permute-start(bf16[1,512,128]{2,1,0:T(8,128)(2,1)} %param.11), channel_id=1, source_target_pairs={{0,8},{8,0},{16,24},{24,16},{32,40},{40,32},{48,56},{56,48},{64,72... | collective-permute-start | bytes 393224 | tf_op jit(solution)/shard_map/ppermute | solution.py:121
  4.0 0.1 collective-permute-start
  4.1 1.1 collective-permute-done.3
  5.2 0.9 pad_maximum_fusion.5
  6.1 0.1 collective-permute-start.4
  6.2 0.0 collective-permute-done
  6.2 0.9 pad_maximum_fusion.4
  7.2 1.5 %collective-permute-start.1 = (bf16[2,512,128]{2,1,0:T(8,128)(2,1)S(1)}, bf16[2,512,128]{2,1,0:T(8,128)(2,1)S(1)}, u32[]{:S(2)}, u32[]{:S(2)}) collective-permute-start(bf16[2,512,128]{2,1,0:T(8,128)(2,1)S(1)} %pad_maximum_fusion.4), channel_id=1, source_target_pairs={{0,16},{8,24},{16,0},{24,8},{32,48},{40,56},{48,32},{56,40},{64,80... | collective-permute-start | bytes 786440 | tf_op jit(solution)/shard_map/ppermute | solution.py:121
  8.7 5.0 %collective-permute-done.4 = bf16[2,512,128]{2,1,0:T(8,128)(2,1)S(1)} collective-permute-done((bf16[2,512,128]{2,1,0:T(8,128)(2,1)S(1)}, bf16[2,512,128]{2,1,0:T(8,128)(2,1)S(1)}, u32[]{:S(2)}, u32[]{:S(2)}) %collective-permute-start.4) | collective-permute-done | bytes 262176 | tf_op jit(solution)/shard_map/ppermute | solution.py:121
  13.7 1.0 pad_maximum_fusion.3
  14.7 1.1 collective-permute-start.5
  15.8 3.6 %collective-permute-done.1 = bf16[2,512,128]{2,1,0:T(8,128)(2,1)S(1)} collective-permute-done((bf16[2,512,128]{2,1,0:T(8,128)(2,1)S(1)}, bf16[2,512,128]{2,1,0:T(8,128)(2,1)S(1)}, u32[]{:S(2)}, u32[]{:S(2)}) %collective-permute-start.1) | collective-permute-done | bytes 262176 | tf_op jit(solution)/shard_map/ppermute | solution.py:121
  19.4 0.1 pad_maximum_fusion.2
  19.4 1.1 collective-permute-start.2
  21.2 9.9 %collective-permute-done.5 = bf16[4,512,128]{2,1,0:T(8,128)(2,1)} collective-permute-done((bf16[4,512,128]{2,1,0:T(8,128)(2,1)S(1)}, bf16[4,512,128]{2,1,0:T(8,128)(2,1)}, u32[]{:S(2)}, u32[]{:S(2)}) %collective-permute-start.5) | collective-permute-done | bytes 524320 | tf_op jit(solution)/shard_map/ppermute | solution.py:121
  31.1 1.1 pad_maximum_fusion.1
  32.2 0.6 gather_fusion.1
  32.8 9.3 %collective-permute-done.2 = bf16[4,512,128]{2,1,0:T(8,128)(2,1)S(1)} collective-permute-done((bf16[4,512,128]{2,1,0:T(8,128)(2,1)S(1)}, bf16[4,512,128]{2,1,0:T(8,128)(2,1)S(1)}, u32[]{:S(2)}, u32[]{:S(2)}) %collective-permute-start.2) | collective-permute-done | bytes 524320 | tf_op jit(solution)/shard_map/ppermute | solution.py:121
  42.2 0.1 pad_maximum_fusion
  42.3 0.0 copy-start.2
  42.3 0.0 copy-start.7
  42.3 0.6 gather_fusion
  43.0 1.0 broadcast_select_fusion
  44.0 19.2 %shard_map.102 = (bf16[512,1024]{1,0:T(8,128)(2,1)}, f32[512,1024]{1,0:T(8,128)}) custom-call(s32[1]{0:T(128)S(6)} %copy.13.count_ref, bf16[512,1024]{1,0:T(8,128)(2,1)} %bitcast.19, bf16[3,512,128]{2,1,0:T(8,128)(2,1)} %get-tuple-element.24.k_ref, bf16[3,512,128]{2,1,0:T(8,128)(2,1)} %get-tuple-element.23.v_ref), custom_call_target="tpu_custom_call" | custom-call | tf_op jit(solution)/shard_map/pallas_call | solution.py:82
  63.2 1.9 %fusion = (f32[512]{0:T(512)S(1)}, f32[512]{0:T(512)S(1)}) fusion(bf16[512,1024]{1,0:T(8,128)(2,1)} %get-tuple-element.10.att_ref, f32[1024]{0:T(1024)S(1)} %copy-done.7, bf16[1,512,1024]{2,1,0:T(8,128)(2,1)S(1)} %copy-done.2), kind=kLoop, calls=%fused_computation.8 | loop fusion | flops 3668992 | bytes 2105344 | tf_op jit(solution)/shard_map/reduce_sum | solution.py:150
  65.1 1.8 %collective-permute-start.6 = (f32[2,512]{1,0:T(2,128)S(1)}, f32[2,512]{1,0:T(2,128)S(1)}, u32[]{:S(2)}, u32[]{:S(2)}) collective-permute-start(f32[2,512]{1,0:T(2,128)S(1)} %pad_maximum_fusion.6), channel_id=1, source_target_pairs={{0,1},{1,0},{2,3},{3,2},{4,5},{5,4},{6,7},{7,6},{8,9},{9,8},{10,11... | collective-permute-start | bytes 12296 | tf_op jit(solution)/shard_map/ppermute | solution.py:121
  66.9 1.0 collective-permute-done.6
  67.9 3.1 %collective-permute-start.7 = (f32[2,512]{1,0:T(2,128)S(1)}, f32[2,512]{1,0:T(2,128)S(1)}, u32[]{:S(2)}, u32[]{:S(2)}) collective-permute-start(f32[2,512]{1,0:T(2,128)S(1)} %fusion.15), channel_id=1, source_target_pairs={{0,2},{1,3},{2,0},{3,1},{4,6},{5,7},{6,4},{7,5},{8,10},{9,11},{10,... | collective-permute-start | bytes 12296 | tf_op jit(solution)/shard_map/ppermute | solution.py:121
  71.0 1.0 collective-permute-done.7
  72.0 6.4 %collective-permute-start.8 = (f32[2,512]{1,0:T(2,128)S(1)}, f32[2,512]{1,0:T(2,128)S(1)}, u32[]{:S(2)}, u32[]{:S(2)}) collective-permute-start(f32[2,512]{1,0:T(2,128)S(1)} %fusion.17), channel_id=1, source_target_pairs={{0,4},{1,5},{2,6},{3,7},{4,0},{5,1},{6,2},{7,3},{8,12},{9,13},{10,... | collective-permute-start | bytes 12296 | tf_op jit(solution)/shard_map/ppermute | solution.py:121
  78.4 1.0 collective-permute-done.8
  79.4 0.0 copy-done.1
  79.4 2.0 %fusion.5 = (bf16[512,1024]{1,0:T(8,128)(2,1)}, bf16[1,512,1024]{2,1,0:T(8,128)(2,1)}) fusion(bf16[512,1024]{1,0:T(8,128)(2,1)S(1)} %copy-done.1, bf16[1,512,1024]{2,1,0:T(8,128)(2,1)S(1)} %copy-done.2, f32[512]{0:T(512)S(1)} %fusion.11, f32[512]{0:T(512)S(1)} %bitcast.28, f32[1024]{0:T(1024)S(1)} %copy-done.7), kind=kLoop, calls=%fused_computation.13 | loop fusion | flops 5242880 | bytes 4202496 | tf_op jit(solution)/shard_map/convert_element_type | solution.py:160
  81.4 24.7 %shard_map.103 = (bf16[512,1024]{1,0:T(8,128)(2,1)}, f32[3,512,128]{2,1,0:T(8,128)}, f32[3,512,128]{2,1,0:T(8,128)}) custom-call(s32[1]{0:T(128)S(6)} %copy.13.count_ref, bf16[512,1024]{1,0:T(8,128)(2,1)} %bitcast.20, bf16[3,512,128]{2,1,0:T(8,128)(2,1)} %get-tuple-element.24.k_ref, bf16[3,512,128]{2,1,0:T(8,128)(2,1)} %get-tuple-element.23.v_ref, ...), custom_call_target="tpu_custom_call" | custom-call | tf_op jit(solution)/shard_map/pallas_call | solution.py:102
  106.1 0.0 copy-start.6
  106.1 0.1 broadcast_in_dim.27.clone
  106.3 1.0 copy-done.6
  107.2 1.0 scatter_fusion
  108.2 0.0 copy-start
  108.3 0.0 copy-start.5
  108.3 0.9 slice.102
  109.1 0.0 collective-permute-start.9
  109.1 0.6 copy-done
  109.8 0.1 broadcast_in_dim.27.clone.1
  109.9 0.1 copy-done.5
  110.0 1.0 scatter_fusion.1
  111.0 0.1 slice.101
  111.0 2.4 %collective-permute-start.12 = (bf16[4,512,128]{2,1,0:T(8,128)(2,1)S(1)}, bf16[4,512,128]{2,1,0:T(8,128)(2,1)S(1)}, u32[]{:S(2)}, u32[]{:S(2)}) collective-permute-start(bf16[4,512,128]{2,1,0:T(8,128)(2,1)S(1)} %slice.101), channel_id=1, source_target_pairs={{0,32},{8,40},{16,48},{24,56},{32,0},{40,8},{48,16},{56,24},{64,96... | collective-permute-start | bytes 1572872 | tf_op jit(solution)/shard_map/ppermute | solution.py:121
  113.4 6.5 %collective-permute-done.9 = bf16[4,512,128]{2,1,0:T(8,128)(2,1)S(1)} collective-permute-done((bf16[4,512,128]{2,1,0:T(8,128)(2,1)}, bf16[4,512,128]{2,1,0:T(8,128)(2,1)S(1)}, u32[]{:S(2)}, u32[]{:S(2)}) %collective-permute-start.9) | collective-permute-done | bytes 524320 | tf_op jit(solution)/shard_map/ppermute | solution.py:121
  119.9 1.3 slice_add_fusion.1
  121.3 0.1 collective-permute-start.10
  121.4 9.8 %collective-permute-done.12 = bf16[4,512,128]{2,1,0:T(8,128)(2,1)S(1)} collective-permute-done((bf16[4,512,128]{2,1,0:T(8,128)(2,1)S(1)}, bf16[4,512,128]{2,1,0:T(8,128)(2,1)S(1)}, u32[]{:S(2)}, u32[]{:S(2)}) %collective-permute-start.12) | collective-permute-done | bytes 524320 | tf_op jit(solution)/shard_map/ppermute | solution.py:121
  131.1 0.1 slice_add_fusion
  131.3 0.1 collective-permute-start.13
  131.4 3.1 %collective-permute-done.10 = bf16[2,512,128]{2,1,0:T(8,128)(2,1)S(1)} collective-permute-done((bf16[2,512,128]{2,1,0:T(8,128)(2,1)S(1)}, bf16[2,512,128]{2,1,0:T(8,128)(2,1)S(1)}, u32[]{:S(2)}, u32[]{:S(2)}) %collective-permute-start.10) | collective-permute-done | bytes 262176 | tf_op jit(solution)/shard_map/ppermute | solution.py:121
  134.5 8.5 %collective-permute-start.11 = (bf16[1,512,128]{2,1,0:T(8,128)(2,1)S(1)}, bf16[1,512,128]{2,1,0:T(8,128)(2,1)S(1)}, u32[]{:S(2)}, u32[]{:S(2)}) collective-permute-start(bf16[1,512,128]{2,1,0:T(8,128)(2,1)S(1)} %slice.106), channel_id=1, source_target_pairs={{0,8},{8,0},{16,24},{24,16},{32,40},{40,32},{48,56},{56,48},{64,72... | collective-permute-start | bytes 393224 | tf_op jit(solution)/shard_map/ppermute | solution.py:121
  143.0 0.0 collective-permute-done.13
  143.1 5.0 %collective-permute-start.14 = (bf16[1,512,128]{2,1,0:T(8,128)(2,1)S(1)}, bf16[1,512,128]{2,1,0:T(8,128)(2,1)S(1)}, u32[]{:S(2)}, u32[]{:S(2)}) collective-permute-start(bf16[1,512,128]{2,1,0:T(8,128)(2,1)S(1)} %slice.105), channel_id=1, source_target_pairs={{0,8},{8,0},{16,24},{24,16},{32,40},{40,32},{48,56},{56,48},{64,72... | collective-permute-start | bytes 393224 | tf_op jit(solution)/shard_map/ppermute | solution.py:121
  148.1 0.0 collective-permute-done.11
  148.1 0.7 fusion.9
  148.8 0.3 collective-permute-done.14
  149.1 0.7 fusion.8
  (22 shorter events, 0.3 us)
Async XLA Ops:
  0.6 30.4 %copy-start.3 = (bf16[1,512,128]{2,1,0:T(8,128)(2,1)S(1)}, bf16[1,512,128]{2,1,0:T(8,128)(2,1)}, u32[]{:S(2)}) copy-start(bf16[1,512,128]{2,1,0:T(8,128)(2,1)} %param.11) | copy-start | bytes 393220
  0.6 18.7 %copy-start.4 = (bf16[1,512,128]{2,1,0:T(8,128)(2,1)S(1)}, bf16[1,512,128]{2,1,0:T(8,128)(2,1)}, u32[]{:S(2)}) copy-start(bf16[1,512,128]{2,1,0:T(8,128)(2,1)} %param.10) | copy-start | bytes 393220
  0.7 20.5 %copy-start.8 = (s32[1,3]{1,0:T(1,128)S(1)}, s32[1,3]{1,0:T(1,128)}, u32[]{:S(2)}) copy-start(s32[1,3]{1,0:T(1,128)} %param.12) | copy-start | bytes 40
  0.7 4.5 %collective-permute-start.3 = (bf16[1,512,128]{2,1,0:T(8,128)(2,1)}, bf16[1,512,128]{2,1,0:T(8,128)(2,1)S(1)}, u32[]{:S(2)}, u32[]{:S(2)}) collective-permute-start(bf16[1,512,128]{2,1,0:T(8,128)(2,1)} %param.11), channel_id=1, source_target_pairs={{0,8},{8,0},{16,24},{24,16},{32,40},{40,32},{48,56},{56,48},{64,72... | collective-permute-start | bytes 393224 | tf_op jit(solution)/shard_map/ppermute | solution.py:121
  4.0 2.2 %collective-permute-start = (bf16[1,512,128]{2,1,0:T(8,128)(2,1)}, bf16[1,512,128]{2,1,0:T(8,128)(2,1)S(1)}, u32[]{:S(2)}, u32[]{:S(2)}) collective-permute-start(bf16[1,512,128]{2,1,0:T(8,128)(2,1)} %param.10), channel_id=1, source_target_pairs={{0,8},{8,0},{16,24},{24,16},{32,40},{40,32},{48,56},{56,48},{64,72... | collective-permute-start | bytes 393224 | tf_op jit(solution)/shard_map/ppermute | solution.py:121
  6.1 7.6 %collective-permute-start.4 = (bf16[2,512,128]{2,1,0:T(8,128)(2,1)S(1)}, bf16[2,512,128]{2,1,0:T(8,128)(2,1)S(1)}, u32[]{:S(2)}, u32[]{:S(2)}) collective-permute-start(bf16[2,512,128]{2,1,0:T(8,128)(2,1)S(1)} %pad_maximum_fusion.5), channel_id=1, source_target_pairs={{0,16},{8,24},{16,0},{24,8},{32,48},{40,56},{48,32},{56,40},{64,80... | collective-permute-start | bytes 786440 | tf_op jit(solution)/shard_map/ppermute | solution.py:121
  7.2 12.2 %collective-permute-start.1 = (bf16[2,512,128]{2,1,0:T(8,128)(2,1)S(1)}, bf16[2,512,128]{2,1,0:T(8,128)(2,1)S(1)}, u32[]{:S(2)}, u32[]{:S(2)}) collective-permute-start(bf16[2,512,128]{2,1,0:T(8,128)(2,1)S(1)} %pad_maximum_fusion.4), channel_id=1, source_target_pairs={{0,16},{8,24},{16,0},{24,8},{32,48},{40,56},{48,32},{56,40},{64,80... | collective-permute-start | bytes 786440 | tf_op jit(solution)/shard_map/ppermute | solution.py:121
  14.7 16.4 %collective-permute-start.5 = (bf16[4,512,128]{2,1,0:T(8,128)(2,1)S(1)}, bf16[4,512,128]{2,1,0:T(8,128)(2,1)}, u32[]{:S(2)}, u32[]{:S(2)}) collective-permute-start(bf16[4,512,128]{2,1,0:T(8,128)(2,1)S(1)} %pad_maximum_fusion.3), channel_id=1, source_target_pairs={{0,32},{8,40},{16,48},{24,56},{32,0},{40,8},{48,16},{56,24},{64,96... | collective-permute-start | bytes 1572872 | tf_op jit(solution)/shard_map/ppermute | solution.py:121
  19.4 22.8 %collective-permute-start.2 = (bf16[4,512,128]{2,1,0:T(8,128)(2,1)S(1)}, bf16[4,512,128]{2,1,0:T(8,128)(2,1)S(1)}, u32[]{:S(2)}, u32[]{:S(2)}) collective-permute-start(bf16[4,512,128]{2,1,0:T(8,128)(2,1)S(1)} %pad_maximum_fusion.2), channel_id=1, source_target_pairs={{0,32},{8,40},{16,48},{24,56},{32,0},{40,8},{48,16},{56,24},{64,96... | collective-permute-start | bytes 1572872 | tf_op jit(solution)/shard_map/ppermute | solution.py:121
  42.3 20.9 %copy-start.2 = (bf16[1,512,1024]{2,1,0:T(8,128)(2,1)S(1)}, bf16[1,512,1024]{2,1,0:T(8,128)(2,1)}, u32[]{:S(2)}) copy-start(bf16[1,512,1024]{2,1,0:T(8,128)(2,1)} %param.15) | copy-start | bytes 3145732
  42.3 20.9 %copy-start.7 = (f32[1024]{0:T(1024)S(1)}, f32[1024]{0:T(1024)}, u32[]{:S(2)}) copy-start(f32[1024]{0:T(1024)} %param.14) | copy-start | bytes 12292
  63.2 16.2 %copy-start.1 = (bf16[512,1024]{1,0:T(8,128)(2,1)S(1)}, bf16[512,1024]{1,0:T(8,128)(2,1)}, u32[]{:S(2)}) copy-start(bf16[512,1024]{1,0:T(8,128)(2,1)} %get-tuple-element.10.att_ref) | copy-start | bytes 3145732
  65.1 2.8 %collective-permute-start.6 = (f32[2,512]{1,0:T(2,128)S(1)}, f32[2,512]{1,0:T(2,128)S(1)}, u32[]{:S(2)}, u32[]{:S(2)}) collective-permute-start(f32[2,512]{1,0:T(2,128)S(1)} %pad_maximum_fusion.6), channel_id=1, source_target_pairs={{0,1},{1,0},{2,3},{3,2},{4,5},{5,4},{6,7},{7,6},{8,9},{9,8},{10,11... | collective-permute-start | bytes 12296 | tf_op jit(solution)/shard_map/ppermute | solution.py:121
  67.9 4.1 %collective-permute-start.7 = (f32[2,512]{1,0:T(2,128)S(1)}, f32[2,512]{1,0:T(2,128)S(1)}, u32[]{:S(2)}, u32[]{:S(2)}) collective-permute-start(f32[2,512]{1,0:T(2,128)S(1)} %fusion.15), channel_id=1, source_target_pairs={{0,2},{1,3},{2,0},{3,1},{4,6},{5,7},{6,4},{7,5},{8,10},{9,11},{10,... | collective-permute-start | bytes 12296 | tf_op jit(solution)/shard_map/ppermute | solution.py:121
  72.0 7.4 %collective-permute-start.8 = (f32[2,512]{1,0:T(2,128)S(1)}, f32[2,512]{1,0:T(2,128)S(1)}, u32[]{:S(2)}, u32[]{:S(2)}) collective-permute-start(f32[2,512]{1,0:T(2,128)S(1)} %fusion.17), channel_id=1, source_target_pairs={{0,4},{1,5},{2,6},{3,7},{4,0},{5,1},{6,2},{7,3},{8,12},{9,13},{10,... | collective-permute-start | bytes 12296 | tf_op jit(solution)/shard_map/ppermute | solution.py:121
  106.1 1.1 copy-start.6
  108.2 1.5 %copy-start = (f32[8,512,128]{2,1,0:T(8,128)}, f32[8,512,128]{2,1,0:T(8,128)S(1)}, u32[]{:S(2)}) copy-start(f32[8,512,128]{2,1,0:T(8,128)S(1)} %scatter_fusion) | copy-start | bytes 6291460
  108.3 1.7 %copy-start.5 = (f32[3,512,128]{2,1,0:T(8,128)S(1)}, f32[3,512,128]{2,1,0:T(8,128)}, u32[]{:S(2)}) copy-start(f32[3,512,128]{2,1,0:T(8,128)} %get-tuple-element.14) | copy-start | bytes 2359300
  109.1 10.8 %collective-permute-start.9 = (bf16[4,512,128]{2,1,0:T(8,128)(2,1)}, bf16[4,512,128]{2,1,0:T(8,128)(2,1)S(1)}, u32[]{:S(2)}, u32[]{:S(2)}) collective-permute-start(bf16[4,512,128]{2,1,0:T(8,128)(2,1)} %slice.102), channel_id=1, source_target_pairs={{0,32},{8,40},{16,48},{24,56},{32,0},{40,8},{48,16},{56,24},{64,96... | collective-permute-start | bytes 1572872 | tf_op jit(solution)/shard_map/ppermute | solution.py:121
  111.0 20.1 %collective-permute-start.12 = (bf16[4,512,128]{2,1,0:T(8,128)(2,1)S(1)}, bf16[4,512,128]{2,1,0:T(8,128)(2,1)S(1)}, u32[]{:S(2)}, u32[]{:S(2)}) collective-permute-start(bf16[4,512,128]{2,1,0:T(8,128)(2,1)S(1)} %slice.101), channel_id=1, source_target_pairs={{0,32},{8,40},{16,48},{24,56},{32,0},{40,8},{48,16},{56,24},{64,96... | collective-permute-start | bytes 1572872 | tf_op jit(solution)/shard_map/ppermute | solution.py:121
  121.3 13.2 %collective-permute-start.10 = (bf16[2,512,128]{2,1,0:T(8,128)(2,1)S(1)}, bf16[2,512,128]{2,1,0:T(8,128)(2,1)S(1)}, u32[]{:S(2)}, u32[]{:S(2)}) collective-permute-start(bf16[2,512,128]{2,1,0:T(8,128)(2,1)S(1)} %slice.104), channel_id=1, source_target_pairs={{0,16},{8,24},{16,0},{24,8},{32,48},{40,56},{48,32},{56,40},{64,80... | collective-permute-start | bytes 786440 | tf_op jit(solution)/shard_map/ppermute | solution.py:121
  131.3 11.7 %collective-permute-start.13 = (bf16[2,512,128]{2,1,0:T(8,128)(2,1)S(1)}, bf16[2,512,128]{2,1,0:T(8,128)(2,1)S(1)}, u32[]{:S(2)}, u32[]{:S(2)}) collective-permute-start(bf16[2,512,128]{2,1,0:T(8,128)(2,1)S(1)} %slice.103), channel_id=1, source_target_pairs={{0,16},{8,24},{16,0},{24,8},{32,48},{40,56},{48,32},{56,40},{64,80... | collective-permute-start | bytes 786440 | tf_op jit(solution)/shard_map/ppermute | solution.py:121
  134.5 13.5 %collective-permute-start.11 = (bf16[1,512,128]{2,1,0:T(8,128)(2,1)S(1)}, bf16[1,512,128]{2,1,0:T(8,128)(2,1)S(1)}, u32[]{:S(2)}, u32[]{:S(2)}) collective-permute-start(bf16[1,512,128]{2,1,0:T(8,128)(2,1)S(1)} %slice.106), channel_id=1, source_target_pairs={{0,8},{8,0},{16,24},{24,16},{32,40},{40,32},{48,56},{56,48},{64,72... | collective-permute-start | bytes 393224 | tf_op jit(solution)/shard_map/ppermute | solution.py:121
  143.1 6.0 %collective-permute-start.14 = (bf16[1,512,128]{2,1,0:T(8,128)(2,1)S(1)}, bf16[1,512,128]{2,1,0:T(8,128)(2,1)S(1)}, u32[]{:S(2)}, u32[]{:S(2)}) collective-permute-start(bf16[1,512,128]{2,1,0:T(8,128)(2,1)S(1)} %slice.105), channel_id=1, source_target_pairs={{0,8},{8,0},{16,24},{24,16},{32,40},{40,32},{48,56},{56,48},{64,72... | collective-permute-start | bytes 393224 | tf_op jit(solution)/shard_map/ppermute | solution.py:121

commit v5 on v4

--- a/solution.py
+++ b/solution.py
@@ -121,24 +121,37 @@
     return lax.ppermute(block, axis, route)
 
 
+def bit_reversed(distance):
+    return ((distance & 1) << 2) | (distance & 2) | ((distance >> 2) & 1)
+
+
 def gather_group(block):
-    for bit in range(GROUP.bit_length() - 1):
+    for bit in reversed(range(GROUP.bit_length() - 1)):
         block = jnp.concatenate([block, exchange(block, "resp", bit)], 0)
     return block
 
 
 def return_group(terms):
-    for bit in reversed(range(GROUP.bit_length() - 1)):
-        half = 1 << bit
-        sent = terms[half : 2 * half].astype(jnp.bfloat16)
+    for bit in range(GROUP.bit_length() - 1):
+        half = terms.shape[0] // 2
+        sent = terms[half:].astype(jnp.bfloat16)
         terms = terms[:half] + exchange(sent, "resp", bit).astype(jnp.float32)
     return terms
+
+
+def head_sum(row_part):
+    heads = lax.axis_size("head")
+    total = row_part
+    for distance in range(1, heads):
+        route = [(low, low ^ distance) for low in range(heads)]
+        total = total + lax.ppermute(row_part, "head", route)
+    return total
 
 
 def body(queries, key_states, value_states, partners, counts, norm_gain, out_grad):
     my_index = lax.axis_index("resp")
     seq_len = queries.shape[1]
-    mate_rows = jnp.bitwise_xor(partners[0], my_index)
+    mate_rows = bit_reversed(jnp.bitwise_xor(partners[0], my_index))
     count = counts.astype(jnp.int32)
     mate_keys = jnp.take(gather_group(key_states), mate_rows, axis=0)
     mate_values = jnp.take(gather_group(value_states), mate_rows, axis=0)
@@ -149,8 +162,7 @@
     row_sums = jnp.stack(
         [jnp.sum(attention_flat * attention_flat, -1), jnp.sum(attention_flat * scaled_grad, -1)]
     )
-    for bit in range(lax.axis_size("head").bit_length() - 1):
-        row_sums = row_sums + exchange(row_sums, "head", bit)
+    row_sums = head_sum(row_sums)
     square_sums, dot_sums = row_sums[0], row_sums[1]
     inverse_rms = lax.rsqrt(square_sums / D + EPSILON)
     normed_out = (attention_flat * inverse_rms[:, None] * norm_gain).astype(jnp.bfloat16)[None]

time: 150 us -> 122 us (0.81)
  waiting for transfers between devices: 51.5 us -> 19.3 us
  starting transfers between devices: 34.5 us -> 39.4 us
    ppermute x15 -> x12, waiting for transfers between devices: 51.5 us -> 17.6 us  [exchange(): return lax.ppermute(block, axis, route)]
    ppermute x0 -> x7, starting transfers between devices: none -> 14.4 us  [head_sum(): total = total + lax.ppermute(row_part, 'head', route)]
    ppermute x15 -> x12, starting transfers between devices: 34.5 us -> 25 us  [exchange(): return lax.ppermute(block, axis, route)]
    ppermute x0 -> x7, waiting for transfers between devices: none -> 1.73 us  [head_sum(): total = total + lax.ppermute(row_part, 'head', route)]
  transfers between devices with their start and end apart: 15 -> 19, of which waited for: 12 -> 10; matrix products, arithmetic and copies ran while one was open for 5% -> 6% of each run, Pallas kernels for 0% -> 0%
where the time goes in v5:
time: 122 us; the launch traced here: 121 us
  Pallas kernels  43.9 us (36%)
  starting transfers between devices  39.4 us (32%)
  waiting for transfers between devices  19.3 us (16%)
  other arithmetic  13.6 us (11%)
  local copies, waits for them, and re-layouts  3.57 us (3%)
  between operations  1.57 us (1%)
    ppermute x12, starting transfers between devices, exchange(): return lax.ppermute(block, axis, route)  25 us
    pallas_call x1, Pallas kernels, attention_backward(): pl.pallas_call(backward_kernel, grid_spec=pltpu.PrefetchScalarGridSpec(nu...  24.7 us
    pallas_call x1, Pallas kernels, attention_forward(): pl.pallas_call(forward_kernel, grid_spec=pltpu.PrefetchScalarGridSpec(num...  19.2 us
    ppermute x12, waiting for transfers between devices, exchange(): return lax.ppermute(block, axis, route)  17.6 us
    ppermute x7, starting transfers between devices, head_sum(): total = total + lax.ppermute(row_part, 'head', route)  14.4 us
    concatenate x6, other arithmetic, gather_group(): block = jnp.concatenate([block, exchange(block, 'resp', bit)], 0)  3.08 us
  transfers between devices with their start and end apart: 19, of which 10 were waited for; matrix products, arithmetic and copies ran while one was open for 6% of the time, Pallas kernels for 0%

profile of v5, /device:TPU:1, one launch (start us, length us, event | category | flops | bytes accessed | tf_op | source)
XLA Modules:
  0.0 121.3 jit_solution(9692104489661402438)
XLA Ops:
  0.6 0.0 copy-start.3
  0.6 0.0 copy-start.4
  0.7 3.7 %collective-permute-start.3 = (bf16[1,512,128]{2,1,0:T(8,128)(2,1)}, bf16[1,512,128]{2,1,0:T(8,128)(2,1)S(1)}, u32[]{:S(2)}, u32[]{:S(2)}) collective-permute-start(bf16[1,512,128]{2,1,0:T(8,128)(2,1)} %param.11), channel_id=1, source_target_pairs={{0,32},{8,40},{16,48},{24,56},{32,0},{40,8},{48,16},{56,24},{64,96... | collective-permute-start | bytes 393224 | tf_op jit(solution)/shard_map/ppermute | solution.py:121
  4.3 0.1 collective-permute-start
  4.4 2.5 %collective-permute-done.3 = bf16[1,512,128]{2,1,0:T(8,128)(2,1)S(1)} collective-permute-done((bf16[1,512,128]{2,1,0:T(8,128)(2,1)}, bf16[1,512,128]{2,1,0:T(8,128)(2,1)S(1)}, u32[]{:S(2)}, u32[]{:S(2)}) %collective-permute-start.3) | collective-permute-done | bytes 131104 | tf_op jit(solution)/shard_map/ppermute | solution.py:121
  6.9 0.9 pad_maximum_fusion.5
  7.8 2.1 %collective-permute-start.4 = (bf16[2,512,128]{2,1,0:T(8,128)(2,1)S(1)}, bf16[2,512,128]{2,1,0:T(8,128)(2,1)S(1)}, u32[]{:S(2)}, u32[]{:S(2)}) collective-permute-start(bf16[2,512,128]{2,1,0:T(8,128)(2,1)S(1)} %pad_maximum_fusion.5), channel_id=1, source_target_pairs={{0,16},{8,24},{16,0},{24,8},{32,48},{40,56},{48,32},{56,40},{64,80... | collective-permute-start | bytes 786440 | tf_op jit(solution)/shard_map/ppermute | solution.py:121
  9.9 1.5 %collective-permute-done = bf16[1,512,128]{2,1,0:T(8,128)(2,1)S(1)} collective-permute-done((bf16[1,512,128]{2,1,0:T(8,128)(2,1)}, bf16[1,512,128]{2,1,0:T(8,128)(2,1)S(1)}, u32[]{:S(2)}, u32[]{:S(2)}) %collective-permute-start) | collective-permute-done | bytes 131104 | tf_op jit(solution)/shard_map/ppermute | solution.py:121
  11.4 0.9 pad_maximum_fusion.4
  12.3 0.5 collective-permute-start.1
  12.8 0.7 fusion.14
  13.5 0.7 collective-permute-done.4
  14.2 1.0 pad_maximum_fusion.3
  15.2 7.0 %collective-permute-start.5 = (bf16[4,512,128]{2,1,0:T(8,128)(2,1)S(1)}, bf16[4,512,128]{2,1,0:T(8,128)(2,1)S(1)}, u32[]{:S(2)}, u32[]{:S(2)}) collective-permute-start(bf16[4,512,128]{2,1,0:T(8,128)(2,1)S(1)} %pad_maximum_fusion.3), channel_id=1, source_target_pairs={{0,8},{8,0},{16,24},{24,16},{32,40},{40,32},{48,56},{56,48},{64,72... | collective-permute-start | bytes 1572872 | tf_op jit(solution)/shard_map/ppermute | solution.py:121
  22.2 0.0 collective-permute-done.1
  22.2 0.1 pad_maximum_fusion.2
  22.3 1.8 %collective-permute-start.2 = (bf16[4,512,128]{2,1,0:T(8,128)(2,1)S(1)}, bf16[4,512,128]{2,1,0:T(8,128)(2,1)S(1)}, u32[]{:S(2)}, u32[]{:S(2)}) collective-permute-start(bf16[4,512,128]{2,1,0:T(8,128)(2,1)S(1)} %pad_maximum_fusion.2), channel_id=1, source_target_pairs={{0,8},{8,0},{16,24},{24,16},{32,40},{40,32},{48,56},{56,48},{64,72... | collective-permute-start | bytes 1572872 | tf_op jit(solution)/shard_map/ppermute | solution.py:121
  24.8 0.0 collective-permute-done.5
  24.8 0.1 pad_maximum_fusion.1
  24.9 0.6 gather_fusion.1
  25.6 0.1 collective-permute-done.2
  25.6 0.1 pad_maximum_fusion
  25.8 0.0 copy-start.2
  25.8 0.0 copy-start.7
  25.8 0.6 gather_fusion
  26.4 1.0 broadcast_select_fusion
  27.4 19.2 %shard_map.102 = (bf16[512,1024]{1,0:T(8,128)(2,1)}, f32[512,1024]{1,0:T(8,128)}) custom-call(s32[1]{0:T(128)S(6)} %copy.13.count_ref, bf16[512,1024]{1,0:T(8,128)(2,1)} %bitcast.20, bf16[3,512,128]{2,1,0:T(8,128)(2,1)} %get-tuple-element.24.k_ref, bf16[3,512,128]{2,1,0:T(8,128)(2,1)} %get-tuple-element.23.v_ref), custom_call_target="tpu_custom_call" | custom-call | tf_op jit(solution)/shard_map/pallas_call | solution.py:82
  46.7 1.9 %fusion = (f32[512]{0:T(512)S(1)}, f32[512]{0:T(512)S(1)}) fusion(bf16[512,1024]{1,0:T(8,128)(2,1)} %get-tuple-element.10.att_ref, f32[1024]{0:T(1024)S(1)} %copy-done.7, bf16[1,512,1024]{2,1,0:T(8,128)(2,1)S(1)} %copy-done.2), kind=kLoop, calls=%fused_computation.8 | loop fusion | flops 3668992 | bytes 2105344 | tf_op jit(solution)/shard_map/reduce_sum | solution.py:163
  48.6 5.0 %collective-permute-start.12 = (f32[2,512]{1,0:T(2,128)S(1)}, f32[2,512]{1,0:T(2,128)S(1)}, u32[]{:S(2)}, u32[]{:S(2)}) collective-permute-start(f32[2,512]{1,0:T(2,128)S(1)} %pad_maximum_fusion.6), channel_id=1, source_target_pairs={{0,7},{1,6},{2,5},{3,4},{4,3},{5,2},{6,1},{7,0},{8,15},{9,14},{10,... | collective-permute-start | bytes 12296 | tf_op jit(solution)/shard_map/ppermute | solution.py:147
  53.6 0.5 collective-permute-start.11
  54.1 3.5 %collective-permute-start.10 = (f32[2,512]{1,0:T(2,128)S(1)}, f32[2,512]{1,0:T(2,128)S(1)}, u32[]{:S(2)}, u32[]{:S(2)}) collective-permute-start(f32[2,512]{1,0:T(2,128)S(1)} %pad_maximum_fusion.6), channel_id=1, source_target_pairs={{0,5},{1,4},{2,7},{3,6},{4,1},{5,0},{6,3},{7,2},{8,13},{9,12},{10,... | collective-permute-start | bytes 12296 | tf_op jit(solution)/shard_map/ppermute | solution.py:147
  57.6 1.8 %collective-permute-start.9 = (f32[2,512]{1,0:T(2,128)S(1)}, f32[2,512]{1,0:T(2,128)S(1)}, u32[]{:S(2)}, u32[]{:S(2)}) collective-permute-start(f32[2,512]{1,0:T(2,128)S(1)} %pad_maximum_fusion.6), channel_id=1, source_target_pairs={{0,4},{1,5},{2,6},{3,7},{4,0},{5,1},{6,2},{7,3},{8,12},{9,13},{10,... | collective-permute-start | bytes 12296 | tf_op jit(solution)/shard_map/ppermute | solution.py:147
  59.4 1.6 %collective-permute-start.8 = (f32[2,512]{1,0:T(2,128)S(1)}, f32[2,512]{1,0:T(2,128)S(1)}, u32[]{:S(2)}, u32[]{:S(2)}) collective-permute-start(f32[2,512]{1,0:T(2,128)S(1)} %pad_maximum_fusion.6), channel_id=1, source_target_pairs={{0,3},{1,2},{2,1},{3,0},{4,7},{5,6},{6,5},{7,4},{8,11},{9,10},{10,... | collective-permute-start | bytes 12296 | tf_op jit(solution)/shard_map/ppermute | solution.py:147
  61.0 0.0 collective-permute-start.7
  61.0 0.0 collective-permute-done.11
  61.0 1.9 %collective-permute-start.6 = (f32[2,512]{1,0:T(2,128)S(1)}, f32[2,512]{1,0:T(2,128)S(1)}, u32[]{:S(2)}, u32[]{:S(2)}) collective-permute-start(f32[2,512]{1,0:T(2,128)S(1)} %pad_maximum_fusion.6), channel_id=1, source_target_pairs={{0,1},{1,0},{2,3},{3,2},{4,5},{5,4},{6,7},{7,6},{8,9},{9,8},{10,11... | collective-permute-start | bytes 12296 | tf_op jit(solution)/shard_map/ppermute | solution.py:147
  63.0 0.0 collective-permute-done.10
  63.0 1.0 collective-permute-done.9
  64.0 0.0 collective-permute-done.8
  64.0 0.7 collective-permute-done.7
  64.7 0.0 collective-permute-done.6
  64.8 2.0 %fusion.5 = (bf16[512,1024]{1,0:T(8,128)(2,1)}, bf16[1,512,1024]{2,1,0:T(8,128)(2,1)}) fusion(bf16[512,1024]{1,0:T(8,128)(2,1)S(1)} %copy-done.1, bf16[1,512,1024]{2,1,0:T(8,128)(2,1)S(1)} %copy-done.2, f32[512]{0:T(512)S(1)} %fusion.11, f32[512]{0:T(512)S(1)} %bitcast.23, f32[1024]{0:T(1024)S(1)} %copy-done.7), kind=kLoop, calls=%fused_computation.13 | loop fusion | flops 5242880 | bytes 4202496 | tf_op jit(solution)/shard_map/convert_element_type | solution.py:172
  66.7 24.7 %shard_map.103 = (bf16[512,1024]{1,0:T(8,128)(2,1)}, f32[3,512,128]{2,1,0:T(8,128)}, f32[3,512,128]{2,1,0:T(8,128)}) custom-call(s32[1]{0:T(128)S(6)} %copy.13.count_ref, bf16[512,1024]{1,0:T(8,128)(2,1)} %bitcast.21, bf16[3,512,128]{2,1,0:T(8,128)(2,1)} %get-tuple-element.24.k_ref, bf16[3,512,128]{2,1,0:T(8,128)(2,1)} %get-tuple-element.23.v_ref, ...), custom_call_target="tpu_custom_call" | custom-call | tf_op jit(solution)/shard_map/pallas_call | solution.py:102
  91.4 0.1 broadcast_in_dim.27.clone
  91.5 1.0 copy-done.6
  92.5 1.0 scatter_fusion
  93.6 0.9 slice.102
  94.4 2.3 %collective-permute-start.13 = (bf16[4,512,128]{2,1,0:T(8,128)(2,1)}, bf16[4,512,128]{2,1,0:T(8,128)(2,1)S(1)}, u32[]{:S(2)}, u32[]{:S(2)}) collective-permute-start(bf16[4,512,128]{2,1,0:T(8,128)(2,1)} %slice.102), channel_id=1, source_target_pairs={{0,8},{8,0},{16,24},{24,16},{32,40},{40,32},{48,56},{56,48},{64,72... | collective-permute-start | bytes 1572872 | tf_op jit(solution)/shard_map/ppermute | solution.py:121
  96.8 0.1 broadcast_in_dim.27.clone.1
  96.9 1.0 scatter_fusion.1
  97.9 0.1 slice.101
  98.0 0.8 collective-permute-start.16
  98.8 1.3 %slice_add_fusion.1 = f32[4,512,128]{2,1,0:T(8,128)S(1)} fusion(f32[8,512,128]{2,1,0:T(8,128)} %copy-done, bf16[4,512,128]{2,1,0:T(8,128)(2,1)S(1)} %collective-permute-done.13), kind=kLoop, calls=%fused_computation.20 | loop fusion | flops 524288 | bytes 2621440 | tf_op jit(solution)/shard_map/add | solution.py:138
  100.1 1.3 %collective-permute-start.14 = (bf16[2,512,128]{2,1,0:T(8,128)(2,1)S(1)}, bf16[2,512,128]{2,1,0:T(8,128)(2,1)S(1)}, u32[]{:S(2)}, u32[]{:S(2)}) collective-permute-start(bf16[2,512,128]{2,1,0:T(8,128)(2,1)S(1)} %slice.104), channel_id=1, source_target_pairs={{0,16},{8,24},{16,0},{24,8},{32,48},{40,56},{48,32},{56,40},{64,80... | collective-permute-start | bytes 786440 | tf_op jit(solution)/shard_map/ppermute | solution.py:121
  101.4 0.1 slice_add_fusion
  101.5 0.4 collective-permute-start.17
  101.9 6.2 %collective-permute-done.14 = bf16[2,512,128]{2,1,0:T(8,128)(2,1)S(1)} collective-permute-done((bf16[2,512,128]{2,1,0:T(8,128)(2,1)S(1)}, bf16[2,512,128]{2,1,0:T(8,128)(2,1)S(1)}, u32[]{:S(2)}, u32[]{:S(2)}) %collective-permute-start.14) | collective-permute-done | bytes 262176 | tf_op jit(solution)/shard_map/ppermute | solution.py:121
  108.2 2.5 %collective-permute-start.15 = (bf16[1,512,128]{2,1,0:T(8,128)(2,1)S(1)}, bf16[1,512,128]{2,1,0:T(8,128)(2,1)S(1)}, u32[]{:S(2)}, u32[]{:S(2)}) collective-permute-start(bf16[1,512,128]{2,1,0:T(8,128)(2,1)S(1)} %slice.106), channel_id=1, source_target_pairs={{0,32},{8,40},{16,48},{24,56},{32,0},{40,8},{48,16},{56,24},{64,96... | collective-permute-start | bytes 393224 | tf_op jit(solution)/shard_map/ppermute | solution.py:121
  110.7 3.0 %collective-permute-done.17 = bf16[2,512,128]{2,1,0:T(8,128)(2,1)S(1)} collective-permute-done((bf16[2,512,128]{2,1,0:T(8,128)(2,1)S(1)}, bf16[2,512,128]{2,1,0:T(8,128)(2,1)S(1)}, u32[]{:S(2)}, u32[]{:S(2)}) %collective-permute-start.17) | collective-permute-done | bytes 262176 | tf_op jit(solution)/shard_map/ppermute | solution.py:121
  113.8 2.5 %collective-permute-start.18 = (bf16[1,512,128]{2,1,0:T(8,128)(2,1)S(1)}, bf16[1,512,128]{2,1,0:T(8,128)(2,1)S(1)}, u32[]{:S(2)}, u32[]{:S(2)}) collective-permute-start(bf16[1,512,128]{2,1,0:T(8,128)(2,1)S(1)} %slice.105), channel_id=1, source_target_pairs={{0,32},{8,40},{16,48},{24,56},{32,0},{40,8},{48,16},{56,24},{64,96... | collective-permute-start | bytes 393224 | tf_op jit(solution)/shard_map/ppermute | solution.py:121
  116.3 2.1 %collective-permute-done.15 = bf16[1,512,128]{2,1,0:T(8,128)(2,1)S(1)} collective-permute-done((bf16[1,512,128]{2,1,0:T(8,128)(2,1)S(1)}, bf16[1,512,128]{2,1,0:T(8,128)(2,1)S(1)}, u32[]{:S(2)}, u32[]{:S(2)}) %collective-permute-start.15) | collective-permute-done | bytes 131104 | tf_op jit(solution)/shard_map/ppermute | solution.py:121
  118.4 0.7 fusion.9
  119.1 1.5 %collective-permute-done.18 = bf16[1,512,128]{2,1,0:T(8,128)(2,1)S(1)} collective-permute-done((bf16[1,512,128]{2,1,0:T(8,128)(2,1)S(1)}, bf16[1,512,128]{2,1,0:T(8,128)(2,1)S(1)}, u32[]{:S(2)}, u32[]{:S(2)}) %collective-permute-start.18) | collective-permute-done | bytes 131104 | tf_op jit(solution)/shard_map/ppermute | solution.py:121
  120.6 0.7 fusion.8
  (27 shorter events, 0.3 us)
Async XLA Ops:
  0.6 24.2 %copy-start.3 = (bf16[1,512,128]{2,1,0:T(8,128)(2,1)S(1)}, bf16[1,512,128]{2,1,0:T(8,128)(2,1)}, u32[]{:S(2)}) copy-start(bf16[1,512,128]{2,1,0:T(8,128)(2,1)} %param.11) | copy-start | bytes 393220
  0.6 21.6 %copy-start.4 = (bf16[1,512,128]{2,1,0:T(8,128)(2,1)S(1)}, bf16[1,512,128]{2,1,0:T(8,128)(2,1)}, u32[]{:S(2)}) copy-start(bf16[1,512,128]{2,1,0:T(8,128)(2,1)} %param.10) | copy-start | bytes 393220
  0.7 6.2 %collective-permute-start.3 = (bf16[1,512,128]{2,1,0:T(8,128)(2,1)}, bf16[1,512,128]{2,1,0:T(8,128)(2,1)S(1)}, u32[]{:S(2)}, u32[]{:S(2)}) collective-permute-start(bf16[1,512,128]{2,1,0:T(8,128)(2,1)} %param.11), channel_id=1, source_target_pairs={{0,32},{8,40},{16,48},{24,56},{32,0},{40,8},{48,16},{56,24},{64,96... | collective-permute-start | bytes 393224 | tf_op jit(solution)/shard_map/ppermute | solution.py:121
  4.3 7.1 %collective-permute-start = (bf16[1,512,128]{2,1,0:T(8,128)(2,1)}, bf16[1,512,128]{2,1,0:T(8,128)(2,1)S(1)}, u32[]{:S(2)}, u32[]{:S(2)}) collective-permute-start(bf16[1,512,128]{2,1,0:T(8,128)(2,1)} %param.10), channel_id=1, source_target_pairs={{0,32},{8,40},{16,48},{24,56},{32,0},{40,8},{48,16},{56,24},{64,96... | collective-permute-start | bytes 393224 | tf_op jit(solution)/shard_map/ppermute | solution.py:121
  7.8 6.4 %collective-permute-start.4 = (bf16[2,512,128]{2,1,0:T(8,128)(2,1)S(1)}, bf16[2,512,128]{2,1,0:T(8,128)(2,1)S(1)}, u32[]{:S(2)}, u32[]{:S(2)}) collective-permute-start(bf16[2,512,128]{2,1,0:T(8,128)(2,1)S(1)} %pad_maximum_fusion.5), channel_id=1, source_target_pairs={{0,16},{8,24},{16,0},{24,8},{32,48},{40,56},{48,32},{56,40},{64,80... | collective-permute-start | bytes 786440 | tf_op jit(solution)/shard_map/ppermute | solution.py:121
  12.3 9.9 %collective-permute-start.1 = (bf16[2,512,128]{2,1,0:T(8,128)(2,1)S(1)}, bf16[2,512,128]{2,1,0:T(8,128)(2,1)S(1)}, u32[]{:S(2)}, u32[]{:S(2)}) collective-permute-start(bf16[2,512,128]{2,1,0:T(8,128)(2,1)S(1)} %pad_maximum_fusion.4), channel_id=1, source_target_pairs={{0,16},{8,24},{16,0},{24,8},{32,48},{40,56},{48,32},{56,40},{64,80... | collective-permute-start | bytes 786440 | tf_op jit(solution)/shard_map/ppermute | solution.py:121
  15.2 9.6 %collective-permute-start.5 = (bf16[4,512,128]{2,1,0:T(8,128)(2,1)S(1)}, bf16[4,512,128]{2,1,0:T(8,128)(2,1)S(1)}, u32[]{:S(2)}, u32[]{:S(2)}) collective-permute-start(bf16[4,512,128]{2,1,0:T(8,128)(2,1)S(1)} %pad_maximum_fusion.3), channel_id=1, source_target_pairs={{0,8},{8,0},{16,24},{24,16},{32,40},{40,32},{48,56},{56,48},{64,72... | collective-permute-start | bytes 1572872 | tf_op jit(solution)/shard_map/ppermute | solution.py:121
  22.3 3.4 %collective-permute-start.2 = (bf16[4,512,128]{2,1,0:T(8,128)(2,1)S(1)}, bf16[4,512,128]{2,1,0:T(8,128)(2,1)S(1)}, u32[]{:S(2)}, u32[]{:S(2)}) collective-permute-start(bf16[4,512,128]{2,1,0:T(8,128)(2,1)S(1)} %pad_maximum_fusion.2), channel_id=1, source_target_pairs={{0,8},{8,0},{16,24},{24,16},{32,40},{40,32},{48,56},{56,48},{64,72... | collective-permute-start | bytes 1572872 | tf_op jit(solution)/shard_map/ppermute | solution.py:121
  25.8 20.9 %copy-start.2 = (bf16[1,512,1024]{2,1,0:T(8,128)(2,1)S(1)}, bf16[1,512,1024]{2,1,0:T(8,128)(2,1)}, u32[]{:S(2)}) copy-start(bf16[1,512,1024]{2,1,0:T(8,128)(2,1)} %param.15) | copy-start | bytes 3145732
  25.8 20.9 %copy-start.7 = (f32[1024]{0:T(1024)S(1)}, f32[1024]{0:T(1024)}, u32[]{:S(2)}) copy-start(f32[1024]{0:T(1024)} %param.14) | copy-start | bytes 12292
  46.6 18.1 %copy-start.1 = (bf16[512,1024]{1,0:T(8,128)(2,1)S(1)}, bf16[512,1024]{1,0:T(8,128)(2,1)}, u32[]{:S(2)}) copy-start(bf16[512,1024]{1,0:T(8,128)(2,1)} %get-tuple-element.10.att_ref) | copy-start | bytes 3145732
  48.6 12.5 %collective-permute-start.12 = (f32[2,512]{1,0:T(2,128)S(1)}, f32[2,512]{1,0:T(2,128)S(1)}, u32[]{:S(2)}, u32[]{:S(2)}) collective-permute-start(f32[2,512]{1,0:T(2,128)S(1)} %pad_maximum_fusion.6), channel_id=1, source_target_pairs={{0,7},{1,6},{2,5},{3,4},{4,3},{5,2},{6,1},{7,0},{8,15},{9,14},{10,... | collective-permute-start | bytes 12296 | tf_op jit(solution)/shard_map/ppermute | solution.py:147
  53.6 7.5 %collective-permute-start.11 = (f32[2,512]{1,0:T(2,128)S(1)}, f32[2,512]{1,0:T(2,128)S(1)}, u32[]{:S(2)}, u32[]{:S(2)}) collective-permute-start(f32[2,512]{1,0:T(2,128)S(1)} %pad_maximum_fusion.6), channel_id=1, source_target_pairs={{0,6},{1,7},{2,4},{3,5},{4,2},{5,3},{6,0},{7,1},{8,14},{9,15},{10,... | collective-permute-start | bytes 12296 | tf_op jit(solution)/shard_map/ppermute | solution.py:147
  54.1 8.8 %collective-permute-start.10 = (f32[2,512]{1,0:T(2,128)S(1)}, f32[2,512]{1,0:T(2,128)S(1)}, u32[]{:S(2)}, u32[]{:S(2)}) collective-permute-start(f32[2,512]{1,0:T(2,128)S(1)} %pad_maximum_fusion.6), channel_id=1, source_target_pairs={{0,5},{1,4},{2,7},{3,6},{4,1},{5,0},{6,3},{7,2},{8,13},{9,12},{10,... | collective-permute-start | bytes 12296 | tf_op jit(solution)/shard_map/ppermute | solution.py:147
  57.6 6.4 %collective-permute-start.9 = (f32[2,512]{1,0:T(2,128)S(1)}, f32[2,512]{1,0:T(2,128)S(1)}, u32[]{:S(2)}, u32[]{:S(2)}) collective-permute-start(f32[2,512]{1,0:T(2,128)S(1)} %pad_maximum_fusion.6), channel_id=1, source_target_pairs={{0,4},{1,5},{2,6},{3,7},{4,0},{5,1},{6,2},{7,3},{8,12},{9,13},{10,... | collective-permute-start | bytes 12296 | tf_op jit(solution)/shard_map/ppermute | solution.py:147
  59.4 4.6 %collective-permute-start.8 = (f32[2,512]{1,0:T(2,128)S(1)}, f32[2,512]{1,0:T(2,128)S(1)}, u32[]{:S(2)}, u32[]{:S(2)}) collective-permute-start(f32[2,512]{1,0:T(2,128)S(1)} %pad_maximum_fusion.6), channel_id=1, source_target_pairs={{0,3},{1,2},{2,1},{3,0},{4,7},{5,6},{6,5},{7,4},{8,11},{9,10},{10,... | collective-permute-start | bytes 12296 | tf_op jit(solution)/shard_map/ppermute | solution.py:147
  61.0 3.7 %collective-permute-start.7 = (f32[2,512]{1,0:T(2,128)S(1)}, f32[2,512]{1,0:T(2,128)S(1)}, u32[]{:S(2)}, u32[]{:S(2)}) collective-permute-start(f32[2,512]{1,0:T(2,128)S(1)} %pad_maximum_fusion.6), channel_id=1, source_target_pairs={{0,2},{1,3},{2,0},{3,1},{4,6},{5,7},{6,4},{7,5},{8,10},{9,11},{10,... | collective-permute-start | bytes 12296 | tf_op jit(solution)/shard_map/ppermute | solution.py:147
  61.0 3.6 %collective-permute-start.6 = (f32[2,512]{1,0:T(2,128)S(1)}, f32[2,512]{1,0:T(2,128)S(1)}, u32[]{:S(2)}, u32[]{:S(2)}) collective-permute-start(f32[2,512]{1,0:T(2,128)S(1)} %pad_maximum_fusion.6), channel_id=1, source_target_pairs={{0,1},{1,0},{2,3},{3,2},{4,5},{5,4},{6,7},{7,6},{8,9},{9,8},{10,11... | collective-permute-start | bytes 12296 | tf_op jit(solution)/shard_map/ppermute | solution.py:147
  91.4 1.1 copy-start.6
  93.5 3.2 %copy-start = (f32[8,512,128]{2,1,0:T(8,128)}, f32[8,512,128]{2,1,0:T(8,128)S(1)}, u32[]{:S(2)}) copy-start(f32[8,512,128]{2,1,0:T(8,128)S(1)} %scatter_fusion) | copy-start | bytes 6291460
  93.5 3.4 %copy-start.5 = (f32[3,512,128]{2,1,0:T(8,128)S(1)}, f32[3,512,128]{2,1,0:T(8,128)}, u32[]{:S(2)}) copy-start(f32[3,512,128]{2,1,0:T(8,128)} %get-tuple-element.14) | copy-start | bytes 2359300
  94.4 4.4 %collective-permute-start.13 = (bf16[4,512,128]{2,1,0:T(8,128)(2,1)}, bf16[4,512,128]{2,1,0:T(8,128)(2,1)S(1)}, u32[]{:S(2)}, u32[]{:S(2)}) collective-permute-start(bf16[4,512,128]{2,1,0:T(8,128)(2,1)} %slice.102), channel_id=1, source_target_pairs={{0,8},{8,0},{16,24},{24,16},{32,40},{40,32},{48,56},{56,48},{64,72... | collective-permute-start | bytes 1572872 | tf_op jit(solution)/shard_map/ppermute | solution.py:121
  98.0 3.4 %collective-permute-start.16 = (bf16[4,512,128]{2,1,0:T(8,128)(2,1)S(1)}, bf16[4,512,128]{2,1,0:T(8,128)(2,1)S(1)}, u32[]{:S(2)}, u32[]{:S(2)}) collective-permute-start(bf16[4,512,128]{2,1,0:T(8,128)(2,1)S(1)} %slice.101), channel_id=1, source_target_pairs={{0,8},{8,0},{16,24},{24,16},{32,40},{40,32},{48,56},{56,48},{64,72... | collective-permute-start | bytes 1572872 | tf_op jit(solution)/shard_map/ppermute | solution.py:121
  100.1 8.0 %collective-permute-start.14 = (bf16[2,512,128]{2,1,0:T(8,128)(2,1)S(1)}, bf16[2,512,128]{2,1,0:T(8,128)(2,1)S(1)}, u32[]{:S(2)}, u32[]{:S(2)}) collective-permute-start(bf16[2,512,128]{2,1,0:T(8,128)(2,1)S(1)} %slice.104), channel_id=1, source_target_pairs={{0,16},{8,24},{16,0},{24,8},{32,48},{40,56},{48,32},{56,40},{64,80... | collective-permute-start | bytes 786440 | tf_op jit(solution)/shard_map/ppermute | solution.py:121
  101.5 12.2 %collective-permute-start.17 = (bf16[2,512,128]{2,1,0:T(8,128)(2,1)S(1)}, bf16[2,512,128]{2,1,0:T(8,128)(2,1)S(1)}, u32[]{:S(2)}, u32[]{:S(2)}) collective-permute-start(bf16[2,512,128]{2,1,0:T(8,128)(2,1)S(1)} %slice.103), channel_id=1, source_target_pairs={{0,16},{8,24},{16,0},{24,8},{32,48},{40,56},{48,32},{56,40},{64,80... | collective-permute-start | bytes 786440 | tf_op jit(solution)/shard_map/ppermute | solution.py:121
  108.2 10.2 %collective-permute-start.15 = (bf16[1,512,128]{2,1,0:T(8,128)(2,1)S(1)}, bf16[1,512,128]{2,1,0:T(8,128)(2,1)S(1)}, u32[]{:S(2)}, u32[]{:S(2)}) collective-permute-start(bf16[1,512,128]{2,1,0:T(8,128)(2,1)S(1)} %slice.106), channel_id=1, source_target_pairs={{0,32},{8,40},{16,48},{24,56},{32,0},{40,8},{48,16},{56,24},{64,96... | collective-permute-start | bytes 393224 | tf_op jit(solution)/shard_map/ppermute | solution.py:121
  113.8 6.8 %collective-permute-start.18 = (bf16[1,512,128]{2,1,0:T(8,128)(2,1)S(1)}, bf16[1,512,128]{2,1,0:T(8,128)(2,1)S(1)}, u32[]{:S(2)}, u32[]{:S(2)}) collective-permute-start(bf16[1,512,128]{2,1,0:T(8,128)(2,1)S(1)} %slice.105), channel_id=1, source_target_pairs={{0,32},{8,40},{16,48},{24,56},{32,0},{40,8},{48,16},{56,24},{64,96... | collective-permute-start | bytes 393224 | tf_op jit(solution)/shard_map/ppermute | solution.py:121

commit v6 on v5

--- a/solution.py
+++ b/solution.py
@@ -11,6 +11,7 @@
 D = 8192
 GROUP = 8
 SLOTS = 3
+CHUNKS = 2
 
 
 EPSILON = 1e-05
@@ -43,12 +44,12 @@
 
 
 def backward_kernel(
-    count_ref, q_ref, k_ref, v_ref, grad_ref, att_ref, lse_ref, dq_ref, dk_ref, dv_ref
+    count_ref, q_ref, k_ref, v_ref, grad_ref, att_ref, lse_ref, dk_in, dv_in, dq_ref, dk_ref, dv_ref
 ):
     @pl.when(pl.program_id(0) == 0)
     def _():
-        dk_ref[...] = jnp.zeros_like(dk_ref)
-        dv_ref[...] = jnp.zeros_like(dv_ref)
+        dk_ref[...] = dk_in[...]
+        dv_ref[...] = dv_in[...]
 
     query_head = q_ref[...]
     grad_head = grad_ref[...]
@@ -74,46 +75,52 @@
     dq_ref[...] = (SCORE_SCALE * query_grad).astype(dq_ref.dtype)
 
 
-def attention_forward(count, queries, mate_keys, mate_values):
+def attention_forward(count, queries, mate_keys, mate_values, chunk, rows):
     seq_len, width = queries.shape
     heads = width // HD
-    head_block = pl.BlockSpec((seq_len, HD), lambda h, c: (0, h))
+    query_block = pl.BlockSpec((rows, HD), lambda h, c: (chunk, h))
+    head_block = pl.BlockSpec((rows, HD), lambda h, c: (0, h))
     slot_block = pl.BlockSpec((SLOTS, seq_len, HD), lambda h, c: (0, 0, 0))
     return pl.pallas_call(
         forward_kernel,
         grid_spec=pltpu.PrefetchScalarGridSpec(
             num_scalar_prefetch=1,
             grid=(heads,),
-            in_specs=[head_block, slot_block, slot_block],
+            in_specs=[query_block, slot_block, slot_block],
             out_specs=[head_block, head_block],
         ),
         out_shape=[
-            jax.ShapeDtypeStruct((seq_len, width), jnp.bfloat16),
-            jax.ShapeDtypeStruct((seq_len, width), jnp.float32),
+            jax.ShapeDtypeStruct((rows, width), jnp.bfloat16),
+            jax.ShapeDtypeStruct((rows, width), jnp.float32),
         ],
     )(count, queries, mate_keys, mate_values)
 
 
-def attention_backward(count, queries, mate_keys, mate_values, attention_grad, attention, log_total):
+def attention_backward(
+    count, queries, mate_keys, mate_values, attention_grad, attention, log_total, key_part, value_part, chunk
+):
     seq_len, width = queries.shape
+    rows = attention.shape[0]
     heads = width // HD
-    head_block = pl.BlockSpec((seq_len, HD), lambda h, c: (0, h))
+    query_block = pl.BlockSpec((rows, HD), lambda h, c: (chunk, h))
+    head_block = pl.BlockSpec((rows, HD), lambda h, c: (0, h))
     slot_block = pl.BlockSpec((SLOTS, seq_len, HD), lambda h, c: (0, 0, 0))
     return pl.pallas_call(
         backward_kernel,
         grid_spec=pltpu.PrefetchScalarGridSpec(
             num_scalar_prefetch=1,
             grid=(heads,),
-            in_specs=[head_block, slot_block, slot_block, head_block, head_block, head_block],
+            in_specs=[query_block, slot_block, slot_block, head_block, head_block, head_block]
+            + [slot_block, slot_block],
             out_specs=[head_block, slot_block, slot_block],
         ),
         out_shape=[
-            jax.ShapeDtypeStruct((seq_len, width), jnp.bfloat16),
+            jax.ShapeDtypeStruct((rows, width), jnp.bfloat16),
             jax.ShapeDtypeStruct((SLOTS, seq_len, HD), jnp.float32),
             jax.ShapeDtypeStruct((SLOTS, seq_len, HD), jnp.float32),
         ],
         compiler_params=pltpu.CompilerParams(dimension_semantics=("arbitrary",)),
-    )(count, queries, mate_keys, mate_values, attention_grad, attention, log_total)
+    )(count, queries, mate_keys, mate_values, attention_grad, attention, log_total, key_part, value_part)
 
 
 def exchange(block, axis, bit):
@@ -156,24 +163,48 @@
     mate_keys = jnp.take(gather_group(key_states), mate_rows, axis=0)
     mate_values = jnp.take(gather_group(value_states), mate_rows, axis=0)
 
-    attention, log_total = attention_forward(count, queries[0], mate_keys, mate_values)
-    attention_flat = attention.astype(jnp.float32)
-    scaled_grad = out_grad[0].astype(jnp.float32) * norm_gain
-    row_sums = jnp.stack(
-        [jnp.sum(attention_flat * attention_flat, -1), jnp.sum(attention_flat * scaled_grad, -1)]
-    )
-    row_sums = head_sum(row_sums)
-    square_sums, dot_sums = row_sums[0], row_sums[1]
-    inverse_rms = lax.rsqrt(square_sums / D + EPSILON)
-    normed_out = (attention_flat * inverse_rms[:, None] * norm_gain).astype(jnp.bfloat16)[None]
-    attention_grad = (
-        inverse_rms[:, None] * scaled_grad
-        - attention_flat * (inverse_rms**3 * dot_sums / D)[:, None]
-    ).astype(jnp.bfloat16)
-
-    query_grads, key_terms, value_terms = attention_backward(
-        count, queries[0], mate_keys, mate_values, attention_grad, attention, log_total
-    )
+    rows = seq_len // CHUNKS
+    query_rows = queries[0]
+    forward_parts, partial_sums, scaled_parts = [], [], []
+    for chunk in range(CHUNKS):
+        attention, log_total = attention_forward(count, query_rows, mate_keys, mate_values, chunk, rows)
+        attention_flat = attention.astype(jnp.float32)
+        scaled_grad = out_grad[0, chunk * rows : (chunk + 1) * rows].astype(jnp.float32) * norm_gain
+        row_sums = jnp.stack(
+            [jnp.sum(attention_flat * attention_flat, -1), jnp.sum(attention_flat * scaled_grad, -1)]
+        )
+        row_sums, query_rows = lax.optimization_barrier((row_sums, query_rows))
+        forward_parts.append((attention, log_total))
+        partial_sums.append(row_sums)
+        scaled_parts.append(scaled_grad)
+    normed_parts, grad_parts = [], []
+    for chunk, (attention, log_total) in enumerate(forward_parts):
+        attention_flat = attention.astype(jnp.float32)
+        scaled_grad = scaled_parts[chunk]
+        row_sums = head_sum(partial_sums[chunk])
+        square_sums, dot_sums = row_sums[0], row_sums[1]
+        inverse_rms = lax.rsqrt(square_sums / D + EPSILON)
+        normed_parts.append((attention_flat * inverse_rms[:, None] * norm_gain).astype(jnp.bfloat16))
+        grad_parts.append(
+            (
+                inverse_rms[:, None] * scaled_grad
+                - attention_flat * (inverse_rms**3 * dot_sums / D)[:, None]
+            ).astype(jnp.bfloat16)
+        )
+    normed_out = jnp.concatenate(normed_parts, 0)[None]
+
+    key_terms = jnp.zeros(mate_keys.shape, jnp.float32)
+    value_terms = jnp.zeros(mate_values.shape, jnp.float32)
+    query_parts = []
+    for chunk, (attention, log_total) in enumerate(forward_parts):
+        if chunk + 1 < CHUNKS:
+            grad_parts[chunk], _ = lax.optimization_barrier((grad_parts[chunk], partial_sums[chunk + 1]))
+        query_part, key_terms, value_terms = attention_backward(
+            count, queries[0], mate_keys, mate_values, grad_parts[chunk], attention, log_total,
+            key_terms, value_terms, chunk,
+        )
+        query_parts.append(query_part)
+    query_grads = jnp.concatenate(query_parts, 0)
     zero_rows = jnp.zeros((GROUP,) + key_terms.shape[1:], jnp.float32)
     key_total = return_group(zero_rows.at[mate_rows].add(key_terms))
     value_total = return_group(zero_rows.at[mate_rows].add(value_terms))

time: 122 us -> 141 us (1.16)
  starting transfers between devices: 39.4 us -> 52.6 us
  other arithmetic: 13.6 us -> 18.5 us
  Pallas kernels: 43.9 us -> 47.9 us
  waiting for transfers between devices: 19.3 us -> 16.2 us
    ppermute x7 -> x14, starting transfers between devices: 14.4 us -> 26.1 us  [head_sum(): total = total + lax.ppermute(row_part, 'head', route)]
    pallas_call x1 -> x2, Pallas kernels: 24.7 us -> 30.1 us  [attention_backward(): pl.pallas_call(backward_kernel, grid_spec=pltpu.PrefetchScalarGridSpec(nu...]
    reduce_sum x1 -> x2, other arithmetic: 1.87 us -> 3.73 us  [body(): jnp.sum(attention_flat * attention_flat, -1)]
    ppermute x7 -> x14, waiting for transfers between devices: 1.73 us -> 0.04 us  [head_sum(): total = total + lax.ppermute(row_part, 'head', route)]
    ppermute x12, starting transfers between devices: 25 us -> 26.5 us  [exchange(): return lax.ppermute(block, axis, route)]
    broadcast_in_dim x0 -> x1, other arithmetic: none -> 1.49 us  [body(): normed_out = jnp.concatenate(normed_parts, 0)[None]]
    pallas_call x1 -> x2, Pallas kernels: 19.2 us -> 17.8 us  [attention_forward(): pl.pallas_call(forward_kernel, grid_spec=pltpu.PrefetchScalarGridSpec(num...]
  transfers between devices with their start and end apart: 19 -> 26, of which waited for: 10 -> 8; matrix products, arithmetic and copies ran while one was open for 6% -> 8% of each run, Pallas kernels for 0% -> 17%
where the time goes in v6:
time: 141 us
  starting transfers between devices  52.6 us (37%)
  Pallas kernels  47.9 us (34%)
  other arithmetic  18.5 us (13%)
  waiting for transfers between devices  16.2 us (11%)
  local copies, waits for them, and re-layouts  3.63 us (3%)
  between operations  1.68 us (1%)
    pallas_call x2, Pallas kernels, attention_backward(): pl.pallas_call(backward_kernel, grid_spec=pltpu.PrefetchScalarGridSpec(nu...  30.1 us
    ppermute x12, starting transfers between devices, exchange(): return lax.ppermute(block, axis, route)  26.5 us
    ppermute x14, starting transfers between devices, head_sum(): total = total + lax.ppermute(row_part, 'head', route)  26.1 us
    pallas_call x2, Pallas kernels, attention_forward(): pl.pallas_call(forward_kernel, grid_spec=pltpu.PrefetchScalarGridSpec(num...  17.8 us
    ppermute x12, waiting for transfers between devices, exchange(): return lax.ppermute(block, axis, route)  16.2 us
    reduce_sum x2, other arithmetic, body(): jnp.sum(attention_flat * attention_flat, -1)  3.73 us
    concatenate x6, other arithmetic, gather_group(): block = jnp.concatenate([block, exchange(block, 'resp', bit)], 0)  3.08 us
  transfers between devices with their start and end apart: 26, of which 8 were waited for; matrix products, arithmetic and copies ran while one was open for 8% of the time, Pallas kernels for 17%

profile of v6, /device:TPU:1, one launch (start us, length us, event | category | flops | bytes accessed | tf_op | source)
XLA Modules:
  0.0 140.5 jit_solution(3268899557552562464)
XLA Ops:
  0.6 0.0 copy-start.5
  0.6 0.0 copy-start.6
  0.7 3.7 %collective-permute-start = (bf16[1,512,128]{2,1,0:T(8,128)(2,1)}, bf16[1,512,128]{2,1,0:T(8,128)(2,1)S(1)}, u32[]{:S(2)}, u32[]{:S(2)}) collective-permute-start(bf16[1,512,128]{2,1,0:T(8,128)(2,1)} %param.10), channel_id=1, source_target_pairs={{0,32},{8,40},{16,48},{24,56},{32,0},{40,8},{48,16},{56,24},{64,96... | collective-permute-start | bytes 393224 | tf_op jit(solution)/shard_map/ppermute | solution.py:128
  4.3 0.1 collective-permute-start.3
  4.4 2.5 %collective-permute-done = bf16[1,512,128]{2,1,0:T(8,128)(2,1)S(1)} collective-permute-done((bf16[1,512,128]{2,1,0:T(8,128)(2,1)}, bf16[1,512,128]{2,1,0:T(8,128)(2,1)S(1)}, u32[]{:S(2)}, u32[]{:S(2)}) %collective-permute-start) | collective-permute-done | bytes 131104 | tf_op jit(solution)/shard_map/ppermute | solution.py:128
  6.9 0.9 pad_maximum_fusion.4
  7.8 2.1 %collective-permute-start.1 = (bf16[2,512,128]{2,1,0:T(8,128)(2,1)S(1)}, bf16[2,512,128]{2,1,0:T(8,128)(2,1)S(1)}, u32[]{:S(2)}, u32[]{:S(2)}) collective-permute-start(bf16[2,512,128]{2,1,0:T(8,128)(2,1)S(1)} %pad_maximum_fusion.4), channel_id=1, source_target_pairs={{0,16},{8,24},{16,0},{24,8},{32,48},{40,56},{48,32},{56,40},{64,80... | collective-permute-start | bytes 786440 | tf_op jit(solution)/shard_map/ppermute | solution.py:128
  9.9 1.5 %collective-permute-done.3 = bf16[1,512,128]{2,1,0:T(8,128)(2,1)S(1)} collective-permute-done((bf16[1,512,128]{2,1,0:T(8,128)(2,1)}, bf16[1,512,128]{2,1,0:T(8,128)(2,1)S(1)}, u32[]{:S(2)}, u32[]{:S(2)}) %collective-permute-start.3) | collective-permute-done | bytes 131104 | tf_op jit(solution)/shard_map/ppermute | solution.py:128
  11.4 0.9 pad_maximum_fusion.5
  12.3 0.5 collective-permute-start.4
  12.8 0.7 fusion.24
  13.5 0.7 collective-permute-done.1
  14.2 1.0 pad_maximum_fusion.2
  15.2 7.0 %collective-permute-start.2 = (bf16[4,512,128]{2,1,0:T(8,128)(2,1)S(1)}, bf16[4,512,128]{2,1,0:T(8,128)(2,1)S(1)}, u32[]{:S(2)}, u32[]{:S(2)}) collective-permute-start(bf16[4,512,128]{2,1,0:T(8,128)(2,1)S(1)} %pad_maximum_fusion.2), channel_id=1, source_target_pairs={{0,8},{8,0},{16,24},{24,16},{32,40},{40,32},{48,56},{56,48},{64,72... | collective-permute-start | bytes 1572872 | tf_op jit(solution)/shard_map/ppermute | solution.py:128
  22.2 0.1 pad_maximum_fusion.3
  22.3 1.8 %collective-permute-start.5 = (bf16[4,512,128]{2,1,0:T(8,128)(2,1)S(1)}, bf16[4,512,128]{2,1,0:T(8,128)(2,1)S(1)}, u32[]{:S(2)}, u32[]{:S(2)}) collective-permute-start(bf16[4,512,128]{2,1,0:T(8,128)(2,1)S(1)} %pad_maximum_fusion.3), channel_id=1, source_target_pairs={{0,8},{8,0},{16,24},{24,16},{32,40},{40,32},{48,56},{56,48},{64,72... | collective-permute-start | bytes 1572872 | tf_op jit(solution)/shard_map/ppermute | solution.py:128
  24.8 0.1 pad_maximum_fusion
  24.9 0.6 gather_fusion
  25.6 0.1 collective-permute-done.5
  25.6 0.1 pad_maximum_fusion.1
  25.8 0.6 gather_fusion.1
  26.4 1.0 broadcast_select_fusion
  27.5 8.9 %shard_map.102 = (bf16[256,1024]{1,0:T(8,128)(2,1)}, f32[256,1024]{1,0:T(8,128)}) custom-call(s32[1]{0:T(128)S(6)} %copy.13.count_ref, bf16[512,1024]{1,0:T(8,128)(2,1)} %bitcast.29, bf16[3,512,128]{2,1,0:T(8,128)(2,1)} %get-tuple-element.48.k_ref, bf16[3,512,128]{2,1,0:T(8,128)(2,1)} %get-tuple-element.47.v_ref), custom_call_target="tpu_custom_call" | custom-call | tf_op jit(solution)/shard_map/pallas_call | solution.py:84
  36.4 1.4 %fusion = (f32[256]{0:T(256)S(1)}, f32[256]{0:T(256)S(1)}) fusion(bf16[256,1024]{1,0:T(8,128)(2,1)} %get-tuple-element.19.att_ref, f32[1024]{0:T(1024)S(1)} %copy-done.9, bf16[1,512,1024]{2,1,0:T(8,128)(2,1)S(1)} %copy-done.4), kind=kLoop, calls=%fused_computation.12 | loop fusion | flops 1834496 | bytes 1054720 | tf_op jit(solution)/shard_map/reduce_sum | solution.py:174
  37.8 5.0 %collective-permute-start.12 = (f32[2,256]{1,0:T(2,128)S(1)}, f32[2,256]{1,0:T(2,128)S(1)}, u32[]{:S(2)}, u32[]{:S(2)}) collective-permute-start(f32[2,256]{1,0:T(2,128)S(1)} %pad_maximum_fusion.6), channel_id=1, source_target_pairs={{0,7},{1,6},{2,5},{3,4},{4,3},{5,2},{6,1},{7,0},{8,15},{9,14},{10,... | collective-permute-start | bytes 6152 | tf_op jit(solution)/shard_map/ppermute | solution.py:154
  42.8 0.5 collective-permute-start.11
  43.4 3.5 %collective-permute-start.10 = (f32[2,256]{1,0:T(2,128)S(1)}, f32[2,256]{1,0:T(2,128)S(1)}, u32[]{:S(2)}, u32[]{:S(2)}) collective-permute-start(f32[2,256]{1,0:T(2,128)S(1)} %pad_maximum_fusion.6), channel_id=1, source_target_pairs={{0,5},{1,4},{2,7},{3,6},{4,1},{5,0},{6,3},{7,2},{8,13},{9,12},{10,... | collective-permute-start | bytes 6152 | tf_op jit(solution)/shard_map/ppermute | solution.py:154
  46.8 1.8 %collective-permute-start.9 = (f32[2,256]{1,0:T(2,128)S(1)}, f32[2,256]{1,0:T(2,128)S(1)}, u32[]{:S(2)}, u32[]{:S(2)}) collective-permute-start(f32[2,256]{1,0:T(2,128)S(1)} %pad_maximum_fusion.6), channel_id=1, source_target_pairs={{0,4},{1,5},{2,6},{3,7},{4,0},{5,1},{6,2},{7,3},{8,12},{9,13},{10,... | collective-permute-start | bytes 6152 | tf_op jit(solution)/shard_map/ppermute | solution.py:154
  48.7 1.6 %collective-permute-start.8 = (f32[2,256]{1,0:T(2,128)S(1)}, f32[2,256]{1,0:T(2,128)S(1)}, u32[]{:S(2)}, u32[]{:S(2)}) collective-permute-start(f32[2,256]{1,0:T(2,128)S(1)} %pad_maximum_fusion.6), channel_id=1, source_target_pairs={{0,3},{1,2},{2,1},{3,0},{4,7},{5,6},{6,5},{7,4},{8,11},{9,10},{10,... | collective-permute-start | bytes 6152 | tf_op jit(solution)/shard_map/ppermute | solution.py:154
  50.3 1.9 %collective-permute-start.6 = (f32[2,256]{1,0:T(2,128)S(1)}, f32[2,256]{1,0:T(2,128)S(1)}, u32[]{:S(2)}, u32[]{:S(2)}) collective-permute-start(f32[2,256]{1,0:T(2,128)S(1)} %pad_maximum_fusion.6), channel_id=1, source_target_pairs={{0,1},{1,0},{2,3},{3,2},{4,5},{5,4},{6,7},{7,6},{8,9},{9,8},{10,11... | collective-permute-start | bytes 6152 | tf_op jit(solution)/shard_map/ppermute | solution.py:154
  52.2 8.9 %shard_map.103 = (bf16[256,1024]{1,0:T(8,128)(2,1)}, f32[256,1024]{1,0:T(8,128)}) custom-call(s32[1]{0:T(128)S(6)} %copy.13.count_ref, bf16[512,1024]{1,0:T(8,128)(2,1)} %bitcast.30, bf16[3,512,128]{2,1,0:T(8,128)(2,1)} %get-tuple-element.48.k_ref, bf16[3,512,128]{2,1,0:T(8,128)(2,1)} %get-tuple-element.47.v_ref), custom_call_target="tpu_custom_call" | custom-call | tf_op jit(solution)/shard_map/pallas_call | solution.py:84
  61.2 2.3 %fusion.6 = (f32[256]{0:T(256)S(1)}, f32[256]{0:T(256)S(1)}, bf16[256,1024]{1,0:T(8,128)(2,1)}) fusion(bf16[256,1024]{1,0:T(8,128)(2,1)} %get-tuple-element.22.att_ref, f32[1024]{0:T(1024)S(1)} %copy-done.9, bf16[1,512,1024]{2,1,0:T(8,128)(2,1)S(1)} %copy-done.4, f32[256]{0:T(256)S(1)} %fusion.17, bf16[256,1024]{1,0:T(8,128)(2,1)S(1)} %copy-done.1, ...), kind=kLoop, calls=%fused_computation.18 | loop fusion | flops 3669504 | bytes 2629632 | tf_op jit(solution)/shard_map/reduce_sum | solution.py:174
  63.6 2.3 %collective-permute-start.19 = (f32[2,256]{1,0:T(2,128)S(1)}, f32[2,256]{1,0:T(2,128)S(1)}, u32[]{:S(2)}, u32[]{:S(2)}) collective-permute-start(f32[2,256]{1,0:T(2,128)S(1)} %pad_maximum_fusion.7), channel_id=1, source_target_pairs={{0,7},{1,6},{2,5},{3,4},{4,3},{5,2},{6,1},{7,0},{8,15},{9,14},{10,... | collective-permute-start | bytes 6152 | tf_op jit(solution)/shard_map/ppermute | solution.py:154
  65.9 1.1 collective-permute-start.18
  66.9 2.9 %collective-permute-start.17 = (f32[2,256]{1,0:T(2,128)S(1)}, f32[2,256]{1,0:T(2,128)S(1)}, u32[]{:S(2)}, u32[]{:S(2)}) collective-permute-start(f32[2,256]{1,0:T(2,128)S(1)} %pad_maximum_fusion.7), channel_id=1, source_target_pairs={{0,5},{1,4},{2,7},{3,6},{4,1},{5,0},{6,3},{7,2},{8,13},{9,12},{10,... | collective-permute-start | bytes 6152 | tf_op jit(solution)/shard_map/ppermute | solution.py:154
  69.9 1.8 %collective-permute-start.16 = (f32[2,256]{1,0:T(2,128)S(1)}, f32[2,256]{1,0:T(2,128)S(1)}, u32[]{:S(2)}, u32[]{:S(2)}) collective-permute-start(f32[2,256]{1,0:T(2,128)S(1)} %pad_maximum_fusion.7), channel_id=1, source_target_pairs={{0,4},{1,5},{2,6},{3,7},{4,0},{5,1},{6,2},{7,3},{8,12},{9,13},{10,... | collective-permute-start | bytes 6152 | tf_op jit(solution)/shard_map/ppermute | solution.py:154
  71.7 1.6 %collective-permute-start.15 = (f32[2,256]{1,0:T(2,128)S(1)}, f32[2,256]{1,0:T(2,128)S(1)}, u32[]{:S(2)}, u32[]{:S(2)}) collective-permute-start(f32[2,256]{1,0:T(2,128)S(1)} %pad_maximum_fusion.7), channel_id=1, source_target_pairs={{0,3},{1,2},{2,1},{3,0},{4,7},{5,6},{6,5},{7,4},{8,11},{9,10},{10,... | collective-permute-start | bytes 6152 | tf_op jit(solution)/shard_map/ppermute | solution.py:154
  73.3 0.5 collective-permute-start.14
  73.8 1.5 %collective-permute-start.13 = (f32[2,256]{1,0:T(2,128)S(1)}, f32[2,256]{1,0:T(2,128)S(1)}, u32[]{:S(2)}, u32[]{:S(2)}) collective-permute-start(f32[2,256]{1,0:T(2,128)S(1)} %pad_maximum_fusion.7), channel_id=1, source_target_pairs={{0,1},{1,0},{2,3},{3,2},{4,5},{5,4},{6,7},{7,6},{8,9},{9,8},{10,11... | collective-permute-start | bytes 6152 | tf_op jit(solution)/shard_map/ppermute | solution.py:154
  75.3 0.9 broadcast_17_dk_in_dv_in.2.dk_in.dv_in
  76.2 15.1 %shard_map.104 = (bf16[256,1024]{1,0:T(8,128)(2,1)}, f32[3,512,128]{2,1,0:T(8,128)}, f32[3,512,128]{2,1,0:T(8,128)}) custom-call(s32[1]{0:T(128)S(6)} %copy.13.count_ref, bf16[512,1024]{1,0:T(8,128)(2,1)} %bitcast.31, bf16[3,512,128]{2,1,0:T(8,128)(2,1)} %get-tuple-element.48.k_ref, bf16[3,512,128]{2,1,0:T(8,128)(2,1)} %get-tuple-element.47.v_ref, ...), custom_call_target="tpu_custom_call" | custom-call | tf_op jit(solution)/shard_map/pallas_call | solution.py:108
  91.4 1.2 fusion.11
  92.7 15.0 %shard_map.105 = (bf16[256,1024]{1,0:T(8,128)(2,1)}, f32[3,512,128]{2,1,0:T(8,128)}, f32[3,512,128]{2,1,0:T(8,128)}) custom-call(s32[1]{0:T(128)S(6)} %copy.13.count_ref, bf16[512,1024]{1,0:T(8,128)(2,1)} %bitcast.32, bf16[3,512,128]{2,1,0:T(8,128)(2,1)} %get-tuple-element.48.k_ref, bf16[3,512,128]{2,1,0:T(8,128)(2,1)} %get-tuple-element.47.v_ref, ...), custom_call_target="tpu_custom_call" | custom-call | tf_op jit(solution)/shard_map/pallas_call | solution.py:108
  107.7 0.1 broadcast_in_dim.17.clone
  107.8 2.1 %scatter_fusion = f32[8,512,128]{2,1,0:T(8,128)S(1)} fusion(f32[8,512,128]{2,1,0:T(8,128)S(1)} %broadcast_in_dim.17.clone, s32[3]{0:T(128)S(1)} %get-tuple-element.37, f32[3,512,128]{2,1,0:T(8,128)} %get-tuple-element.31), kind=kCustom, calls=%fused_computation.2 | custom fusion | flops 196608 | bytes 2359308 | tf_op jit(solution)/shard_map/scatter-add | solution.py:209
  109.9 0.9 slice.129
  110.9 4.0 %collective-permute-start.20 = (bf16[4,512,128]{2,1,0:T(8,128)(2,1)}, bf16[4,512,128]{2,1,0:T(8,128)(2,1)}, u32[]{:S(2)}, u32[]{:S(2)}) collective-permute-start(bf16[4,512,128]{2,1,0:T(8,128)(2,1)} %slice.129), channel_id=1, source_target_pairs={{0,8},{8,0},{16,24},{24,16},{32,40},{40,32},{48,56},{56,48},{64,72... | collective-permute-start | bytes 1572872 | tf_op jit(solution)/shard_map/ppermute | solution.py:128
  114.9 0.1 broadcast_in_dim.17.clone.1
  115.0 2.1 %scatter_fusion.1 = f32[8,512,128]{2,1,0:T(8,128)S(1)} fusion(f32[8,512,128]{2,1,0:T(8,128)S(1)} %broadcast_in_dim.17.clone.1, s32[3]{0:T(128)S(1)} %get-tuple-element.37, f32[3,512,128]{2,1,0:T(8,128)} %get-tuple-element.32), kind=kCustom, calls=%fused_computation.3 | custom fusion | flops 196608 | bytes 2359308 | tf_op jit(solution)/shard_map/scatter-add | solution.py:210
  117.1 0.1 slice.128
  117.2 0.6 collective-permute-start.23
  117.8 1.4 %slice_add_fusion.1 = f32[4,512,128]{2,1,0:T(8,128)S(1)} fusion(f32[8,512,128]{2,1,0:T(8,128)} %copy-done, bf16[4,512,128]{2,1,0:T(8,128)(2,1)} %collective-permute-done.20), kind=kLoop, calls=%fused_computation.27 | loop fusion | flops 524288 | bytes 2621440 | tf_op jit(solution)/shard_map/add | solution.py:145
  119.3 1.2 collective-permute-start.21
  120.6 0.1 slice_add_fusion
  120.7 0.4 collective-permute-start.24
  121.1 1.5 %maximum_bitcast_fusion = (bf16[1,512,1024]{2,1,0:T(8,128)(2,1)}, bf16[1,512,1024]{2,1,0:T(8,128)(2,1)}) fusion(bf16[256,1024]{1,0:T(8,128)(2,1)S(1)} %get-tuple-element.41, bf16[256,1024]{1,0:T(8,128)(2,1)S(1)} %get-tuple-element.42, bf16[256,1024]{1,0:T(8,128)(2,1)S(1)} %copy-done.8, bf16[256,1024]{1,0:T(8,128)(2,1)S(1)} %copy-done.7), kind=kLoop, calls=%fused_computation.30 | loop fusion | flops 4194304 | bytes 4194304 | tf_op jit(solution)/shard_map/broadcast_in_dim | solution.py:194
  122.6 4.7 %collective-permute-done.21 = bf16[2,512,128]{2,1,0:T(8,128)(2,1)S(1)} collective-permute-done((bf16[2,512,128]{2,1,0:T(8,128)(2,1)S(1)}, bf16[2,512,128]{2,1,0:T(8,128)(2,1)S(1)}, u32[]{:S(2)}, u32[]{:S(2)}) %collective-permute-start.21) | collective-permute-done | bytes 262176 | tf_op jit(solution)/shard_map/ppermute | solution.py:128
  127.4 2.5 %collective-permute-start.22 = (bf16[1,512,128]{2,1,0:T(8,128)(2,1)S(1)}, bf16[1,512,128]{2,1,0:T(8,128)(2,1)S(1)}, u32[]{:S(2)}, u32[]{:S(2)}) collective-permute-start(bf16[1,512,128]{2,1,0:T(8,128)(2,1)S(1)} %slice.133), channel_id=1, source_target_pairs={{0,32},{8,40},{16,48},{24,56},{32,0},{40,8},{48,16},{56,24},{64,96... | collective-permute-start | bytes 393224 | tf_op jit(solution)/shard_map/ppermute | solution.py:128
  129.9 3.0 %collective-permute-done.24 = bf16[2,512,128]{2,1,0:T(8,128)(2,1)S(1)} collective-permute-done((bf16[2,512,128]{2,1,0:T(8,128)(2,1)S(1)}, bf16[2,512,128]{2,1,0:T(8,128)(2,1)S(1)}, u32[]{:S(2)}, u32[]{:S(2)}) %collective-permute-start.24) | collective-permute-done | bytes 262176 | tf_op jit(solution)/shard_map/ppermute | solution.py:128
  133.0 2.5 %collective-permute-start.25 = (bf16[1,512,128]{2,1,0:T(8,128)(2,1)S(1)}, bf16[1,512,128]{2,1,0:T(8,128)(2,1)S(1)}, u32[]{:S(2)}, u32[]{:S(2)}) collective-permute-start(bf16[1,512,128]{2,1,0:T(8,128)(2,1)S(1)} %slice.132), channel_id=1, source_target_pairs={{0,32},{8,40},{16,48},{24,56},{32,0},{40,8},{48,16},{56,24},{64,96... | collective-permute-start | bytes 393224 | tf_op jit(solution)/shard_map/ppermute | solution.py:128
  135.5 2.1 %collective-permute-done.22 = bf16[1,512,128]{2,1,0:T(8,128)(2,1)S(1)} collective-permute-done((bf16[1,512,128]{2,1,0:T(8,128)(2,1)S(1)}, bf16[1,512,128]{2,1,0:T(8,128)(2,1)S(1)}, u32[]{:S(2)}, u32[]{:S(2)}) %collective-permute-start.22) | collective-permute-done | bytes 131104 | tf_op jit(solution)/shard_map/ppermute | solution.py:128
  137.6 0.7 fusion.15
  138.3 1.5 %collective-permute-done.25 = bf16[1,512,128]{2,1,0:T(8,128)(2,1)S(1)} collective-permute-done((bf16[1,512,128]{2,1,0:T(8,128)(2,1)S(1)}, bf16[1,512,128]{2,1,0:T(8,128)(2,1)S(1)}, u32[]{:S(2)}, u32[]{:S(2)}) %collective-permute-start.25) | collective-permute-done | bytes 131104 | tf_op jit(solution)/shard_map/ppermute | solution.py:128
  139.9 0.7 fusion.14
  (54 shorter events, 0.4 us)
Async XLA Ops:
  0.6 24.2 %copy-start.5 = (bf16[1,512,128]{2,1,0:T(8,128)(2,1)S(1)}, bf16[1,512,128]{2,1,0:T(8,128)(2,1)}, u32[]{:S(2)}) copy-start(bf16[1,512,128]{2,1,0:T(8,128)(2,1)} %param.10) | copy-start | bytes 393220
  0.6 21.6 %copy-start.6 = (bf16[1,512,128]{2,1,0:T(8,128)(2,1)S(1)}, bf16[1,512,128]{2,1,0:T(8,128)(2,1)}, u32[]{:S(2)}) copy-start(bf16[1,512,128]{2,1,0:T(8,128)(2,1)} %param.11) | copy-start | bytes 393220
  0.7 6.2 %collective-permute-start = (bf16[1,512,128]{2,1,0:T(8,128)(2,1)}, bf16[1,512,128]{2,1,0:T(8,128)(2,1)S(1)}, u32[]{:S(2)}, u32[]{:S(2)}) collective-permute-start(bf16[1,512,128]{2,1,0:T(8,128)(2,1)} %param.10), channel_id=1, source_target_pairs={{0,32},{8,40},{16,48},{24,56},{32,0},{40,8},{48,16},{56,24},{64,96... | collective-permute-start | bytes 393224 | tf_op jit(solution)/shard_map/ppermute | solution.py:128
  4.3 7.1 %collective-permute-start.3 = (bf16[1,512,128]{2,1,0:T(8,128)(2,1)}, bf16[1,512,128]{2,1,0:T(8,128)(2,1)S(1)}, u32[]{:S(2)}, u32[]{:S(2)}) collective-permute-start(bf16[1,512,128]{2,1,0:T(8,128)(2,1)} %param.11), channel_id=1, source_target_pairs={{0,32},{8,40},{16,48},{24,56},{32,0},{40,8},{48,16},{56,24},{64,96... | collective-permute-start | bytes 393224 | tf_op jit(solution)/shard_map/ppermute | solution.py:128
  7.8 6.4 %collective-permute-start.1 = (bf16[2,512,128]{2,1,0:T(8,128)(2,1)S(1)}, bf16[2,512,128]{2,1,0:T(8,128)(2,1)S(1)}, u32[]{:S(2)}, u32[]{:S(2)}) collective-permute-start(bf16[2,512,128]{2,1,0:T(8,128)(2,1)S(1)} %pad_maximum_fusion.4), channel_id=1, source_target_pairs={{0,16},{8,24},{16,0},{24,8},{32,48},{40,56},{48,32},{56,40},{64,80... | collective-permute-start | bytes 786440 | tf_op jit(solution)/shard_map/ppermute | solution.py:128
  12.3 9.9 %collective-permute-start.4 = (bf16[2,512,128]{2,1,0:T(8,128)(2,1)S(1)}, bf16[2,512,128]{2,1,0:T(8,128)(2,1)S(1)}, u32[]{:S(2)}, u32[]{:S(2)}) collective-permute-start(bf16[2,512,128]{2,1,0:T(8,128)(2,1)S(1)} %pad_maximum_fusion.5), channel_id=1, source_target_pairs={{0,16},{8,24},{16,0},{24,8},{32,48},{40,56},{48,32},{56,40},{64,80... | collective-permute-start | bytes 786440 | tf_op jit(solution)/shard_map/ppermute | solution.py:128
  15.2 9.6 %collective-permute-start.2 = (bf16[4,512,128]{2,1,0:T(8,128)(2,1)S(1)}, bf16[4,512,128]{2,1,0:T(8,128)(2,1)S(1)}, u32[]{:S(2)}, u32[]{:S(2)}) collective-permute-start(bf16[4,512,128]{2,1,0:T(8,128)(2,1)S(1)} %pad_maximum_fusion.2), channel_id=1, source_target_pairs={{0,8},{8,0},{16,24},{24,16},{32,40},{40,32},{48,56},{56,48},{64,72... | collective-permute-start | bytes 1572872 | tf_op jit(solution)/shard_map/ppermute | solution.py:128
  22.3 3.4 %collective-permute-start.5 = (bf16[4,512,128]{2,1,0:T(8,128)(2,1)S(1)}, bf16[4,512,128]{2,1,0:T(8,128)(2,1)S(1)}, u32[]{:S(2)}, u32[]{:S(2)}) collective-permute-start(bf16[4,512,128]{2,1,0:T(8,128)(2,1)S(1)} %pad_maximum_fusion.3), channel_id=1, source_target_pairs={{0,8},{8,0},{16,24},{24,16},{32,40},{40,32},{48,56},{56,48},{64,72... | collective-permute-start | bytes 1572872 | tf_op jit(solution)/shard_map/ppermute | solution.py:128
  25.8 10.6 %copy-start.4 = (bf16[1,512,1024]{2,1,0:T(8,128)(2,1)S(1)}, bf16[1,512,1024]{2,1,0:T(8,128)(2,1)}, u32[]{:S(2)}) copy-start(bf16[1,512,1024]{2,1,0:T(8,128)(2,1)} %param.15) | copy-start | bytes 3145732
  25.8 10.6 %copy-start.9 = (f32[1024]{0:T(1024)S(1)}, f32[1024]{0:T(1024)}, u32[]{:S(2)}) copy-start(f32[1024]{0:T(1024)} %param.14) | copy-start | bytes 12292
  36.4 24.9 %copy-start.1 = (bf16[256,1024]{1,0:T(8,128)(2,1)S(1)}, bf16[256,1024]{1,0:T(8,128)(2,1)}, u32[]{:S(2)}) copy-start(bf16[256,1024]{1,0:T(8,128)(2,1)} %get-tuple-element.19.att_ref) | copy-start | bytes 1572868
  37.8 12.5 %collective-permute-start.12 = (f32[2,256]{1,0:T(2,128)S(1)}, f32[2,256]{1,0:T(2,128)S(1)}, u32[]{:S(2)}, u32[]{:S(2)}) collective-permute-start(f32[2,256]{1,0:T(2,128)S(1)} %pad_maximum_fusion.6), channel_id=1, source_target_pairs={{0,7},{1,6},{2,5},{3,4},{4,3},{5,2},{6,1},{7,0},{8,15},{9,14},{10,... | collective-permute-start | bytes 6152 | tf_op jit(solution)/shard_map/ppermute | solution.py:154
  42.8 7.5 %collective-permute-start.11 = (f32[2,256]{1,0:T(2,128)S(1)}, f32[2,256]{1,0:T(2,128)S(1)}, u32[]{:S(2)}, u32[]{:S(2)}) collective-permute-start(f32[2,256]{1,0:T(2,128)S(1)} %pad_maximum_fusion.6), channel_id=1, source_target_pairs={{0,6},{1,7},{2,4},{3,5},{4,2},{5,3},{6,0},{7,1},{8,14},{9,15},{10,... | collective-permute-start | bytes 6152 | tf_op jit(solution)/shard_map/ppermute | solution.py:154
  43.4 17.7 %collective-permute-start.10 = (f32[2,256]{1,0:T(2,128)S(1)}, f32[2,256]{1,0:T(2,128)S(1)}, u32[]{:S(2)}, u32[]{:S(2)}) collective-permute-start(f32[2,256]{1,0:T(2,128)S(1)} %pad_maximum_fusion.6), channel_id=1, source_target_pairs={{0,5},{1,4},{2,7},{3,6},{4,1},{5,0},{6,3},{7,2},{8,13},{9,12},{10,... | collective-permute-start | bytes 6152 | tf_op jit(solution)/shard_map/ppermute | solution.py:154
  46.8 14.3 %collective-permute-start.9 = (f32[2,256]{1,0:T(2,128)S(1)}, f32[2,256]{1,0:T(2,128)S(1)}, u32[]{:S(2)}, u32[]{:S(2)}) collective-permute-start(f32[2,256]{1,0:T(2,128)S(1)} %pad_maximum_fusion.6), channel_id=1, source_target_pairs={{0,4},{1,5},{2,6},{3,7},{4,0},{5,1},{6,2},{7,3},{8,12},{9,13},{10,... | collective-permute-start | bytes 6152 | tf_op jit(solution)/shard_map/ppermute | solution.py:154
  48.7 12.5 %collective-permute-start.8 = (f32[2,256]{1,0:T(2,128)S(1)}, f32[2,256]{1,0:T(2,128)S(1)}, u32[]{:S(2)}, u32[]{:S(2)}) collective-permute-start(f32[2,256]{1,0:T(2,128)S(1)} %pad_maximum_fusion.6), channel_id=1, source_target_pairs={{0,3},{1,2},{2,1},{3,0},{4,7},{5,6},{6,5},{7,4},{8,11},{9,10},{10,... | collective-permute-start | bytes 6152 | tf_op jit(solution)/shard_map/ppermute | solution.py:154
  50.3 10.9 %collective-permute-start.7 = (f32[2,256]{1,0:T(2,128)S(1)}, f32[2,256]{1,0:T(2,128)S(1)}, u32[]{:S(2)}, u32[]{:S(2)}) collective-permute-start(f32[2,256]{1,0:T(2,128)S(1)} %pad_maximum_fusion.6), channel_id=1, source_target_pairs={{0,2},{1,3},{2,0},{3,1},{4,6},{5,7},{6,4},{7,5},{8,10},{9,11},{10,... | collective-permute-start | bytes 6152 | tf_op jit(solution)/shard_map/ppermute | solution.py:154
  50.3 10.9 %collective-permute-start.6 = (f32[2,256]{1,0:T(2,128)S(1)}, f32[2,256]{1,0:T(2,128)S(1)}, u32[]{:S(2)}, u32[]{:S(2)}) collective-permute-start(f32[2,256]{1,0:T(2,128)S(1)} %pad_maximum_fusion.6), channel_id=1, source_target_pairs={{0,1},{1,0},{2,3},{3,2},{4,5},{5,4},{6,7},{7,6},{8,9},{9,8},{10,11... | collective-permute-start | bytes 6152 | tf_op jit(solution)/shard_map/ppermute | solution.py:154
  63.6 9.8 %collective-permute-start.19 = (f32[2,256]{1,0:T(2,128)S(1)}, f32[2,256]{1,0:T(2,128)S(1)}, u32[]{:S(2)}, u32[]{:S(2)}) collective-permute-start(f32[2,256]{1,0:T(2,128)S(1)} %pad_maximum_fusion.7), channel_id=1, source_target_pairs={{0,7},{1,6},{2,5},{3,4},{4,3},{5,2},{6,1},{7,0},{8,15},{9,14},{10,... | collective-permute-start | bytes 6152 | tf_op jit(solution)/shard_map/ppermute | solution.py:154
  65.9 7.9 %collective-permute-start.18 = (f32[2,256]{1,0:T(2,128)S(1)}, f32[2,256]{1,0:T(2,128)S(1)}, u32[]{:S(2)}, u32[]{:S(2)}) collective-permute-start(f32[2,256]{1,0:T(2,128)S(1)} %pad_maximum_fusion.7), channel_id=1, source_target_pairs={{0,6},{1,7},{2,4},{3,5},{4,2},{5,3},{6,0},{7,1},{8,14},{9,15},{10,... | collective-permute-start | bytes 6152 | tf_op jit(solution)/shard_map/ppermute | solution.py:154
  66.9 24.4 %collective-permute-start.17 = (f32[2,256]{1,0:T(2,128)S(1)}, f32[2,256]{1,0:T(2,128)S(1)}, u32[]{:S(2)}, u32[]{:S(2)}) collective-permute-start(f32[2,256]{1,0:T(2,128)S(1)} %pad_maximum_fusion.7), channel_id=1, source_target_pairs={{0,5},{1,4},{2,7},{3,6},{4,1},{5,0},{6,3},{7,2},{8,13},{9,12},{10,... | collective-permute-start | bytes 6152 | tf_op jit(solution)/shard_map/ppermute | solution.py:154
  69.9 21.4 %collective-permute-start.16 = (f32[2,256]{1,0:T(2,128)S(1)}, f32[2,256]{1,0:T(2,128)S(1)}, u32[]{:S(2)}, u32[]{:S(2)}) collective-permute-start(f32[2,256]{1,0:T(2,128)S(1)} %pad_maximum_fusion.7), channel_id=1, source_target_pairs={{0,4},{1,5},{2,6},{3,7},{4,0},{5,1},{6,2},{7,3},{8,12},{9,13},{10,... | collective-permute-start | bytes 6152 | tf_op jit(solution)/shard_map/ppermute | solution.py:154
  71.7 19.6 %collective-permute-start.15 = (f32[2,256]{1,0:T(2,128)S(1)}, f32[2,256]{1,0:T(2,128)S(1)}, u32[]{:S(2)}, u32[]{:S(2)}) collective-permute-start(f32[2,256]{1,0:T(2,128)S(1)} %pad_maximum_fusion.7), channel_id=1, source_target_pairs={{0,3},{1,2},{2,1},{3,0},{4,7},{5,6},{6,5},{7,4},{8,11},{9,10},{10,... | collective-permute-start | bytes 6152 | tf_op jit(solution)/shard_map/ppermute | solution.py:154
  73.3 18.0 %collective-permute-start.14 = (f32[2,256]{1,0:T(2,128)S(1)}, f32[2,256]{1,0:T(2,128)S(1)}, u32[]{:S(2)}, u32[]{:S(2)}) collective-permute-start(f32[2,256]{1,0:T(2,128)S(1)} %pad_maximum_fusion.7), channel_id=1, source_target_pairs={{0,2},{1,3},{2,0},{3,1},{4,6},{5,7},{6,4},{7,5},{8,10},{9,11},{10,... | collective-permute-start | bytes 6152 | tf_op jit(solution)/shard_map/ppermute | solution.py:154
  73.8 17.6 %collective-permute-start.13 = (f32[2,256]{1,0:T(2,128)S(1)}, f32[2,256]{1,0:T(2,128)S(1)}, u32[]{:S(2)}, u32[]{:S(2)}) collective-permute-start(f32[2,256]{1,0:T(2,128)S(1)} %pad_maximum_fusion.7), channel_id=1, source_target_pairs={{0,1},{1,0},{2,3},{3,2},{4,5},{5,4},{6,7},{7,6},{8,9},{9,8},{10,11... | collective-permute-start | bytes 6152 | tf_op jit(solution)/shard_map/ppermute | solution.py:154
  76.2 15.2 %copy-start.2 = (bf16[256,1024]{1,0:T(8,128)(2,1)S(1)}, bf16[256,1024]{1,0:T(8,128)(2,1)}, u32[]{:S(2)}) copy-start(bf16[256,1024]{1,0:T(8,128)(2,1)} %get-tuple-element.19.att_ref) | copy-start | bytes 1572868
  76.2 15.2 %copy-start.3 = (bf16[256,1024]{1,0:T(8,128)(2,1)S(1)}, bf16[256,1024]{1,0:T(8,128)(2,1)}, u32[]{:S(2)}) copy-start(bf16[256,1024]{1,0:T(8,128)(2,1)} %get-tuple-element.22.att_ref) | copy-start | bytes 1572868
  109.9 5.0 %copy-start = (f32[8,512,128]{2,1,0:T(8,128)}, f32[8,512,128]{2,1,0:T(8,128)S(1)}, u32[]{:S(2)}) copy-start(f32[8,512,128]{2,1,0:T(8,128)S(1)} %scatter_fusion) | copy-start | bytes 6291460
  110.9 7.0 %collective-permute-start.20 = (bf16[4,512,128]{2,1,0:T(8,128)(2,1)}, bf16[4,512,128]{2,1,0:T(8,128)(2,1)}, u32[]{:S(2)}, u32[]{:S(2)}) collective-permute-start(bf16[4,512,128]{2,1,0:T(8,128)(2,1)} %slice.129), channel_id=1, source_target_pairs={{0,8},{8,0},{16,24},{24,16},{32,40},{40,32},{48,56},{56,48},{64,72... | collective-permute-start | bytes 1572872 | tf_op jit(solution)/shard_map/ppermute | solution.py:128
  117.2 3.4 %collective-permute-start.23 = (bf16[4,512,128]{2,1,0:T(8,128)(2,1)S(1)}, bf16[4,512,128]{2,1,0:T(8,128)(2,1)S(1)}, u32[]{:S(2)}, u32[]{:S(2)}) collective-permute-start(bf16[4,512,128]{2,1,0:T(8,128)(2,1)S(1)} %slice.128), channel_id=1, source_target_pairs={{0,8},{8,0},{16,24},{24,16},{32,40},{40,32},{48,56},{56,48},{64,72... | collective-permute-start | bytes 1572872 | tf_op jit(solution)/shard_map/ppermute | solution.py:128
  119.3 1.8 %copy-start.7 = (bf16[256,1024]{1,0:T(8,128)(2,1)S(1)}, bf16[256,1024]{1,0:T(8,128)(2,1)}, u32[]{:S(2)}) copy-start(bf16[256,1024]{1,0:T(8,128)(2,1)} %get-tuple-element.26) | copy-start | bytes 1572868
  119.3 1.8 %copy-start.8 = (bf16[256,1024]{1,0:T(8,128)(2,1)S(1)}, bf16[256,1024]{1,0:T(8,128)(2,1)}, u32[]{:S(2)}) copy-start(bf16[256,1024]{1,0:T(8,128)(2,1)} %get-tuple-element.30) | copy-start | bytes 1572868
  119.3 8.0 %collective-permute-start.21 = (bf16[2,512,128]{2,1,0:T(8,128)(2,1)S(1)}, bf16[2,512,128]{2,1,0:T(8,128)(2,1)S(1)}, u32[]{:S(2)}, u32[]{:S(2)}) collective-permute-start(bf16[2,512,128]{2,1,0:T(8,128)(2,1)S(1)} %slice.131), channel_id=1, source_target_pairs={{0,16},{8,24},{16,0},{24,8},{32,48},{40,56},{48,32},{56,40},{64,80... | collective-permute-start | bytes 786440 | tf_op jit(solution)/shard_map/ppermute | solution.py:128
  120.7 12.2 %collective-permute-start.24 = (bf16[2,512,128]{2,1,0:T(8,128)(2,1)S(1)}, bf16[2,512,128]{2,1,0:T(8,128)(2,1)S(1)}, u32[]{:S(2)}, u32[]{:S(2)}) collective-permute-start(bf16[2,512,128]{2,1,0:T(8,128)(2,1)S(1)} %slice.130), channel_id=1, source_target_pairs={{0,16},{8,24},{16,0},{24,8},{32,48},{40,56},{48,32},{56,40},{64,80... | collective-permute-start | bytes 786440 | tf_op jit(solution)/shard_map/ppermute | solution.py:128
  127.4 10.2 %collective-permute-start.22 = (bf16[1,512,128]{2,1,0:T(8,128)(2,1)S(1)}, bf16[1,512,128]{2,1,0:T(8,128)(2,1)S(1)}, u32[]{:S(2)}, u32[]{:S(2)}) collective-permute-start(bf16[1,512,128]{2,1,0:T(8,128)(2,1)S(1)} %slice.133), channel_id=1, source_target_pairs={{0,32},{8,40},{16,48},{24,56},{32,0},{40,8},{48,16},{56,24},{64,96... | collective-permute-start | bytes 393224 | tf_op jit(solution)/shard_map/ppermute | solution.py:128
  133.0 6.8 %collective-permute-start.25 = (bf16[1,512,128]{2,1,0:T(8,128)(2,1)S(1)}, bf16[1,512,128]{2,1,0:T(8,128)(2,1)S(1)}, u32[]{:S(2)}, u32[]{:S(2)}) collective-permute-start(bf16[1,512,128]{2,1,0:T(8,128)(2,1)S(1)} %slice.132), channel_id=1, source_target_pairs={{0,32},{8,40},{16,48},{24,56},{32,0},{40,8},{48,16},{56,24},{64,96... | collective-permute-start | bytes 393224 | tf_op jit(solution)/shard_map/ppermute | solution.py:128

commit v7 on v5

--- a/solution.py
+++ b/solution.py
@@ -26,25 +26,27 @@
     return jnp.where(slot < count_ref[0], scores * SCORE_SCALE, NEG_FLOOR)
 
 
-def forward_kernel(count_ref, q_ref, k_ref, v_ref, out_ref, lse_ref):
+def forward_kernel(count_ref, rows_ref, q_ref, *refs):
+    k_refs, v_refs, (out_ref, lse_ref) = refs[:SLOTS], refs[SLOTS : 2 * SLOTS], refs[2 * SLOTS :]
     query_head = q_ref[...]
-    scores = [slot_scores(count_ref, query_head, k_ref[slot], slot) for slot in range(SLOTS)]
+    scores = [slot_scores(count_ref, query_head, k_refs[slot][...], slot) for slot in range(SLOTS)]
     row_max = functools.reduce(
         jnp.maximum, [jnp.max(block, axis=1, keepdims=True) for block in scores]
     )
     exps = [jnp.exp(block - row_max) for block in scores]
     denominator = sum(jnp.sum(block, axis=1, keepdims=True) for block in exps)
     weighted = sum(
-        jnp.dot(exps[slot].astype(jnp.bfloat16), v_ref[slot], preferred_element_type=jnp.float32)
+        jnp.dot(exps[slot].astype(jnp.bfloat16), v_refs[slot][...], preferred_element_type=jnp.float32)
         for slot in range(SLOTS)
     )
     out_ref[...] = (weighted / denominator).astype(out_ref.dtype)
     lse_ref[...] = jnp.broadcast_to(row_max + jnp.log(denominator), lse_ref.shape)
 
 
-def backward_kernel(
-    count_ref, q_ref, k_ref, v_ref, grad_ref, att_ref, lse_ref, dq_ref, dk_ref, dv_ref
-):
+def backward_kernel(count_ref, rows_ref, q_ref, *refs):
+    k_refs, v_refs = refs[:SLOTS], refs[SLOTS : 2 * SLOTS]
+    grad_ref, att_ref, lse_ref, dq_ref, dk_ref, dv_ref = refs[2 * SLOTS :]
+
     @pl.when(pl.program_id(0) == 0)
     def _():
         dk_ref[...] = jnp.zeros_like(dk_ref)
@@ -58,62 +60,74 @@
     log_total = lse_ref[:, :1]
     query_grad = jnp.zeros(dq_ref.shape, jnp.float32)
     for slot in range(SLOTS):
-        mate_keys = k_ref[slot]
+        mate_keys = k_refs[slot][...]
+        mate_row = rows_ref[slot]
         back_probs = jnp.exp(slot_scores(count_ref, query_head, mate_keys, slot) - log_total)
-        dv_ref[slot] += lax.dot_general(
+        dv_ref[mate_row] += lax.dot_general(
             back_probs.astype(jnp.bfloat16), grad_head, TRANS_A, preferred_element_type=jnp.float32
         )
         prob_grad = lax.dot_general(
-            grad_head, v_ref[slot], TRANS_B, preferred_element_type=jnp.float32
+            grad_head, v_refs[slot][...], TRANS_B, preferred_element_type=jnp.float32
         )
         score_grad = (back_probs * (prob_grad - row_delta)).astype(jnp.bfloat16)
         query_grad = query_grad + jnp.dot(score_grad, mate_keys, preferred_element_type=jnp.float32)
-        dk_ref[slot] += SCORE_SCALE * lax.dot_general(
+        dk_ref[mate_row] += SCORE_SCALE * lax.dot_general(
             score_grad, query_head, TRANS_A, preferred_element_type=jnp.float32
         )
     dq_ref[...] = (SCORE_SCALE * query_grad).astype(dq_ref.dtype)
 
 
-def attention_forward(count, queries, mate_keys, mate_values):
+def slot_blocks(seq_len):
+    return [
+        pl.BlockSpec((None, seq_len, HD), lambda h, c, r, slot=slot: (r[slot], 0, 0))
+        for slot in range(SLOTS)
+    ]
+
+
+def attention_forward(count, mate_rows, queries, group_keys, group_values):
     seq_len, width = queries.shape
     heads = width // HD
-    head_block = pl.BlockSpec((seq_len, HD), lambda h, c: (0, h))
-    slot_block = pl.BlockSpec((SLOTS, seq_len, HD), lambda h, c: (0, 0, 0))
+    head_block = pl.BlockSpec((seq_len, HD), lambda h, c, r: (0, h))
     return pl.pallas_call(
         forward_kernel,
         grid_spec=pltpu.PrefetchScalarGridSpec(
-            num_scalar_prefetch=1,
+            num_scalar_prefetch=2,
             grid=(heads,),
-            in_specs=[head_block, slot_block, slot_block],
+            in_specs=[head_block] + slot_blocks(seq_len) * 2,
             out_specs=[head_block, head_block],
         ),
         out_shape=[
             jax.ShapeDtypeStruct((seq_len, width), jnp.bfloat16),
             jax.ShapeDtypeStruct((seq_len, width), jnp.float32),
         ],
-    )(count, queries, mate_keys, mate_values)
-
-
-def attention_backward(count, queries, mate_keys, mate_values, attention_grad, attention, log_total):
+    )(count, mate_rows, queries, *([group_keys] * SLOTS), *([group_values] * SLOTS))
+
+
+def attention_backward(
+    count, mate_rows, queries, group_keys, group_values, attention_grad, attention, log_total
+):
     seq_len, width = queries.shape
     heads = width // HD
-    head_block = pl.BlockSpec((seq_len, HD), lambda h, c: (0, h))
-    slot_block = pl.BlockSpec((SLOTS, seq_len, HD), lambda h, c: (0, 0, 0))
+    head_block = pl.BlockSpec((seq_len, HD), lambda h, c, r: (0, h))
+    group_block = pl.BlockSpec(group_keys.shape, lambda h, c, r: (0, 0, 0))
     return pl.pallas_call(
         backward_kernel,
         grid_spec=pltpu.PrefetchScalarGridSpec(
-            num_scalar_prefetch=1,
+            num_scalar_prefetch=2,
             grid=(heads,),
-            in_specs=[head_block, slot_block, slot_block, head_block, head_block, head_block],
-            out_specs=[head_block, slot_block, slot_block],
+            in_specs=[head_block] + slot_blocks(seq_len) * 2 + [head_block] * 3,
+            out_specs=[head_block, group_block, group_block],
         ),
         out_shape=[
             jax.ShapeDtypeStruct((seq_len, width), jnp.bfloat16),
-            jax.ShapeDtypeStruct((SLOTS, seq_len, HD), jnp.float32),
-            jax.ShapeDtypeStruct((SLOTS, seq_len, HD), jnp.float32),
+            jax.ShapeDtypeStruct(group_keys.shape, jnp.float32),
+            jax.ShapeDtypeStruct(group_keys.shape, jnp.float32),
         ],
         compiler_params=pltpu.CompilerParams(dimension_semantics=("arbitrary",)),
-    )(count, queries, mate_keys, mate_values, attention_grad, attention, log_total)
+    )(
+        count, mate_rows, queries, *([group_keys] * SLOTS), *([group_values] * SLOTS),
+        attention_grad, attention, log_total,
+    )
 
 
 def exchange(block, axis, bit):
@@ -153,10 +167,10 @@
     seq_len = queries.shape[1]
     mate_rows = bit_reversed(jnp.bitwise_xor(partners[0], my_index))
     count = counts.astype(jnp.int32)
-    mate_keys = jnp.take(gather_group(key_states), mate_rows, axis=0)
-    mate_values = jnp.take(gather_group(value_states), mate_rows, axis=0)
-
-    attention, log_total = attention_forward(count, queries[0], mate_keys, mate_values)
+    group_keys = gather_group(key_states)
+    group_values = gather_group(value_states)
+
+    attention, log_total = attention_forward(count, mate_rows, queries[0], group_keys, group_values)
     attention_flat = attention.astype(jnp.float32)
     scaled_grad = out_grad[0].astype(jnp.float32) * norm_gain
     row_sums = jnp.stack(
@@ -172,11 +186,10 @@
     ).astype(jnp.bfloat16)
 
     query_grads, key_terms, value_terms = attention_backward(
-        count, queries[0], mate_keys, mate_values, attention_grad, attention, log_total
-    )
-    zero_rows = jnp.zeros((GROUP,) + key_terms.shape[1:], jnp.float32)
-    key_total = return_group(zero_rows.at[mate_rows].add(key_terms))
-    value_total = return_group(zero_rows.at[mate_rows].add(value_terms))
+        count, mate_rows, queries[0], group_keys, group_values, attention_grad, attention, log_total
+    )
+    key_total = return_group(key_terms)
+    value_total = return_group(value_terms)
     return (
         normed_out,
         query_grads[None],

time: 122 us -> 123 us (level)
  the two profiles are of different devices: /device:TPU:1 before, /device:TPU:56 now
where the time goes in v7:
time: 123 us
  Pallas kernels  46.9 us (38%)
  starting transfers between devices  31 us (25%)
  waiting for transfers between devices  27.6 us (22%)
  other arithmetic  9.58 us (8%)
  local copies, waits for them, and re-layouts  6.16 us (5%)
  between operations  1.56 us (1%)
    pallas_call x1, Pallas kernels, attention_backward(): pl.pallas_call(backward_kernel, grid_spec=pltpu.PrefetchScalarGridSpec(nu...  26.7 us
    ppermute x12, waiting for transfers between devices, exchange(): return lax.ppermute(block, axis, route)  21.5 us
    pallas_call x1, Pallas kernels, attention_forward(): pl.pallas_call(forward_kernel, grid_spec=pltpu.PrefetchScalarGridSpec(num...  20.2 us
    ppermute x12, starting transfers between devices, exchange(): return lax.ppermute(block, axis, route)  16.1 us
    ppermute x7, starting transfers between devices, head_sum(): total = total + lax.ppermute(row_part, 'head', route)  14.9 us
    ppermute x7, waiting for transfers between devices, head_sum(): total = total + lax.ppermute(row_part, 'head', route)  6.06 us
    unnamed x22, local copies, waits for them, and re-layouts  3.03 us
    slice x6, local copies, waits for them, and re-layouts, return_group(): sent = terms[half:].astype(jnp.bfloat16)  2.99 us
  transfers between devices with their start and end apart: 19, of which 10 were waited for; matrix products, arithmetic and copies ran while one was open for 7% of the time, Pallas kernels for 0%

profile of v7, /device:TPU:56, one launch (start us, length us, event | category | flops | bytes accessed | tf_op | source)
XLA Modules:
  0.0 122.8 jit_solution(11203767290946100322)
XLA Ops:
  0.6 0.0 copy-start.6
  0.6 3.1 %collective-permute-start = (bf16[1,512,128]{2,1,0:T(8,128)(2,1)}, bf16[1,512,128]{2,1,0:T(8,128)(2,1)S(1)}, u32[]{:S(2)}, u32[]{:S(2)}) collective-permute-start(bf16[1,512,128]{2,1,0:T(8,128)(2,1)} %param.8), channel_id=1, source_target_pairs={{0,32},{8,40},{16,48},{24,56},{32,0},{40,8},{48,16},{56,24},{64,96... | collective-permute-start | bytes 393224 | tf_op jit(solution)/shard_map/ppermute | solution.py:135
  3.8 0.5 collective-permute-start.3
  4.3 1.2 or_bitcast_fusion.rows_ref
  5.4 2.5 %collective-permute-done = bf16[1,512,128]{2,1,0:T(8,128)(2,1)S(1)} collective-permute-done((bf16[1,512,128]{2,1,0:T(8,128)(2,1)}, bf16[1,512,128]{2,1,0:T(8,128)(2,1)S(1)}, u32[]{:S(2)}, u32[]{:S(2)}) %collective-permute-start) | collective-permute-done | bytes 131104 | tf_op jit(solution)/shard_map/ppermute | solution.py:135
  8.0 0.9 pad_maximum_fusion.2
  8.9 2.3 %collective-permute-start.1 = (bf16[2,512,128]{2,1,0:T(8,128)(2,1)S(1)}, bf16[2,512,128]{2,1,0:T(8,128)(2,1)S(1)}, u32[]{:S(2)}, u32[]{:S(2)}) collective-permute-start(bf16[2,512,128]{2,1,0:T(8,128)(2,1)S(1)} %pad_maximum_fusion.2), channel_id=1, source_target_pairs={{0,16},{8,24},{16,0},{24,8},{32,48},{40,56},{48,32},{56,40},{64,80... | collective-permute-start | bytes 786440 | tf_op jit(solution)/shard_map/ppermute | solution.py:135
  11.2 0.0 collective-permute-done.3
  11.2 0.9 pad_maximum_fusion.3
  12.1 0.9 collective-permute-start.4
  13.0 0.9 constant_dynamic-update-slice_fusion.3
  14.6 0.9 constant_dynamic-update-slice_fusion.7
  15.5 2.9 %collective-permute-done.1 = bf16[2,512,128]{2,1,0:T(8,128)(2,1)S(1)} collective-permute-done((bf16[2,512,128]{2,1,0:T(8,128)(2,1)S(1)}, bf16[2,512,128]{2,1,0:T(8,128)(2,1)S(1)}, u32[]{:S(2)}, u32[]{:S(2)}) %collective-permute-start.1) | collective-permute-done | bytes 262176 | tf_op jit(solution)/shard_map/ppermute | solution.py:135
  18.4 1.0 pad_maximum_fusion
  19.4 0.1 collective-permute-start.2
  19.5 2.3 %collective-permute-done.4 = bf16[2,512,128]{2,1,0:T(8,128)(2,1)S(1)} collective-permute-done((bf16[2,512,128]{2,1,0:T(8,128)(2,1)S(1)}, bf16[2,512,128]{2,1,0:T(8,128)(2,1)S(1)}, u32[]{:S(2)}, u32[]{:S(2)}) %collective-permute-start.4) | collective-permute-done | bytes 262176 | tf_op jit(solution)/shard_map/ppermute | solution.py:135
  21.8 0.0 copy-done.6
  21.8 0.1 pad_maximum_fusion.1
  21.9 0.1 collective-permute-start.5
  22.1 0.0 collective-permute-done.2
  22.1 0.1 constant_dynamic-update-slice_fusion.refs_0_.refs_1_.refs_2_
  22.2 0.0 copy-start.1
  22.2 1.7 %collective-permute-done.5 = bf16[4,512,128]{2,1,0:T(8,128)(2,1)S(1)} collective-permute-done((bf16[4,512,128]{2,1,0:T(8,128)(2,1)S(1)}, bf16[4,512,128]{2,1,0:T(8,128)(2,1)S(1)}, u32[]{:S(2)}, u32[]{:S(2)}) %collective-permute-start.5) | collective-permute-done | bytes 524320 | tf_op jit(solution)/shard_map/ppermute | solution.py:135
  23.9 0.1 constant_dynamic-update-slice_fusion.4.refs_3_.refs_4_.refs_5_
  23.9 0.0 copy-start
  24.0 1.1 copy-done
  25.0 20.2 %shard_map.102 = (bf16[512,1024]{1,0:T(8,128)(2,1)}, f32[512,1024]{1,0:T(8,128)}) custom-call(s32[1]{0:T(128)S(6)} %copy.17.count_ref, s32[3]{0:T(128)} %or_bitcast_fusion.rows_ref, bf16[512,1024]{1,0:T(8,128)(2,1)} %bitcast.14, bf16[8,512,128]{2,1,0:T(8,128)(2,1)} %copy-done.1, bf16[8,512,128]{2,1,0:T(8,128)(2,1)} %copy-done.1, ...), custom_call_target="tpu_custom_call" | custom-call | tf_op jit(solution)/shard_map/pallas_call | solution.py:91
  45.3 0.0 copy-done.7
  45.3 1.9 %fusion = (f32[512]{0:T(512)S(1)}, f32[512]{0:T(512)S(1)}) fusion(bf16[512,1024]{1,0:T(8,128)(2,1)} %get-tuple-element.9.refs_7_, f32[1024]{0:T(1024)S(1)} %copy-done.7, bf16[1,512,1024]{2,1,0:T(8,128)(2,1)S(1)} %copy-done.3), kind=kLoop, calls=%fused_computation.4 | loop fusion | flops 3668992 | bytes 2105344 | tf_op jit(solution)/shard_map/reduce_sum | solution.py:177
  47.2 5.5 %collective-permute-start.11 = (f32[2,512]{1,0:T(2,128)S(1)}, f32[2,512]{1,0:T(2,128)S(1)}, u32[]{:S(2)}, u32[]{:S(2)}) collective-permute-start(f32[2,512]{1,0:T(2,128)S(1)} %pad_maximum_fusion.4), channel_id=1, source_target_pairs={{0,6},{1,7},{2,4},{3,5},{4,2},{5,3},{6,0},{7,1},{8,14},{9,15},{10,... | collective-permute-start | bytes 12296 | tf_op jit(solution)/shard_map/ppermute | solution.py:161
  52.7 0.5 collective-permute-start.10
  53.2 4.9 %collective-permute-start.9 = (f32[2,512]{1,0:T(2,128)S(1)}, f32[2,512]{1,0:T(2,128)S(1)}, u32[]{:S(2)}, u32[]{:S(2)}) collective-permute-start(f32[2,512]{1,0:T(2,128)S(1)} %pad_maximum_fusion.4), channel_id=1, source_target_pairs={{0,4},{1,5},{2,6},{3,7},{4,0},{5,1},{6,2},{7,3},{8,12},{9,13},{10,... | collective-permute-start | bytes 12296 | tf_op jit(solution)/shard_map/ppermute | solution.py:161
  58.1 1.0 collective-permute-start.8
  59.1 2.4 %collective-permute-start.7 = (f32[2,512]{1,0:T(2,128)S(1)}, f32[2,512]{1,0:T(2,128)S(1)}, u32[]{:S(2)}, u32[]{:S(2)}) collective-permute-start(f32[2,512]{1,0:T(2,128)S(1)} %pad_maximum_fusion.4), channel_id=1, source_target_pairs={{0,2},{1,3},{2,0},{3,1},{4,6},{5,7},{6,4},{7,5},{8,10},{9,11},{10,... | collective-permute-start | bytes 12296 | tf_op jit(solution)/shard_map/ppermute | solution.py:161
  61.5 0.0 collective-permute-done.11
  61.5 0.5 collective-permute-start.12
  62.1 0.0 collective-permute-done.10
  62.1 0.0 collective-permute-start.6
  62.1 0.0 collective-permute-done.9
  62.1 0.0 collective-permute-done.8
  62.1 1.6 %collective-permute-done.7 = f32[2,512]{1,0:T(2,128)S(1)} collective-permute-done((f32[2,512]{1,0:T(2,128)S(1)}, f32[2,512]{1,0:T(2,128)S(1)}, u32[]{:S(2)}, u32[]{:S(2)}) %collective-permute-start.7) | collective-permute-done | bytes 4128 | tf_op jit(solution)/shard_map/ppermute | solution.py:161
  63.7 4.5 %collective-permute-done.12 = f32[2,512]{1,0:T(2,128)S(1)} collective-permute-done((f32[2,512]{1,0:T(2,128)S(1)}, f32[2,512]{1,0:T(2,128)S(1)}, u32[]{:S(2)}, u32[]{:S(2)}) %collective-permute-start.12) | collective-permute-done | bytes 4128 | tf_op jit(solution)/shard_map/ppermute | solution.py:161
  68.1 0.0 collective-permute-done.6
  68.2 2.0 %fusion.5 = (bf16[512,1024]{1,0:T(8,128)(2,1)}, bf16[1,512,1024]{2,1,0:T(8,128)(2,1)}) fusion(bf16[512,1024]{1,0:T(8,128)(2,1)S(1)} %copy-done.2, bf16[1,512,1024]{2,1,0:T(8,128)(2,1)S(1)} %copy-done.3, f32[512]{0:T(512)S(1)} %fusion.11, f32[512]{0:T(512)S(1)} %bitcast.17, f32[1024]{0:T(1024)S(1)} %copy-done.7), kind=kLoop, calls=%fused_computation.9 | loop fusion | flops 5242880 | bytes 4202496 | tf_op jit(solution)/shard_map/convert_element_type | solution.py:186
  70.2 26.7 %shard_map.103 = (bf16[512,1024]{1,0:T(8,128)(2,1)}, f32[8,512,128]{2,1,0:T(8,128)}, f32[8,512,128]{2,1,0:T(8,128)}) custom-call(s32[1]{0:T(128)S(6)} %copy.17.count_ref, s32[3]{0:T(128)} %or_bitcast_fusion.rows_ref, bf16[512,1024]{1,0:T(8,128)(2,1)} %bitcast.15, bf16[8,512,128]{2,1,0:T(8,128)(2,1)} %copy-done.1, bf16[8,512,128]{2,1,0:T(8,128)(2,1)} %copy-done.1, ...), custom_call_target="tpu_custom_call" | custom-call | tf_op jit(solution)/shard_map/pallas_call | solution.py:113
  96.9 0.0 copy-start.5
  96.9 1.4 %slice.95 = bf16[4,512,128]{2,1,0:T(8,128)(2,1)S(1)} slice(f32[8,512,128]{2,1,0:T(8,128)} %get-tuple-element.13), slice={[4:8], [0:512], [0:128]} | slice | bytes 1048576 | tf_op jit(solution)/shard_map/slice | solution.py:151
  98.3 0.1 collective-permute-start.16
  98.5 1.4 %slice.96 = bf16[4,512,128]{2,1,0:T(8,128)(2,1)S(1)} slice(f32[8,512,128]{2,1,0:T(8,128)} %get-tuple-element.12), slice={[4:8], [0:512], [0:128]} | slice | bytes 1048576 | tf_op jit(solution)/shard_map/slice | solution.py:151
  99.9 0.6 collective-permute-start.13
  100.5 0.0 collective-permute-done.16
  100.5 0.1 convert_add_fusion
  100.6 1.5 %collective-permute-start.17 = (bf16[2,512,128]{2,1,0:T(8,128)(2,1)S(1)}, bf16[2,512,128]{2,1,0:T(8,128)(2,1)S(1)}, u32[]{:S(2)}, u32[]{:S(2)}) collective-permute-start(bf16[2,512,128]{2,1,0:T(8,128)(2,1)S(1)} %slice.97), channel_id=1, source_target_pairs={{0,16},{8,24},{16,0},{24,8},{32,48},{40,56},{48,32},{56,40},{64,80... | collective-permute-start | bytes 786440 | tf_op jit(solution)/shard_map/ppermute | solution.py:135
  102.1 0.0 collective-permute-done.13
  102.2 0.1 convert_add_fusion.1
  102.3 1.4 %collective-permute-start.14 = (bf16[2,512,128]{2,1,0:T(8,128)(2,1)S(1)}, bf16[2,512,128]{2,1,0:T(8,128)(2,1)S(1)}, u32[]{:S(2)}, u32[]{:S(2)}) collective-permute-start(bf16[2,512,128]{2,1,0:T(8,128)(2,1)S(1)} %slice.98), channel_id=1, source_target_pairs={{0,16},{8,24},{16,0},{24,8},{32,48},{40,56},{48,32},{56,40},{64,80... | collective-permute-start | bytes 786440 | tf_op jit(solution)/shard_map/ppermute | solution.py:135
  103.7 6.2 %collective-permute-done.17 = bf16[2,512,128]{2,1,0:T(8,128)(2,1)S(1)} collective-permute-done((bf16[2,512,128]{2,1,0:T(8,128)(2,1)S(1)}, bf16[2,512,128]{2,1,0:T(8,128)(2,1)S(1)}, u32[]{:S(2)}, u32[]{:S(2)}) %collective-permute-start.17) | collective-permute-done | bytes 262176 | tf_op jit(solution)/shard_map/ppermute | solution.py:135
  110.0 2.8 %collective-permute-start.18 = (bf16[1,512,128]{2,1,0:T(8,128)(2,1)S(1)}, bf16[1,512,128]{2,1,0:T(8,128)(2,1)S(1)}, u32[]{:S(2)}, u32[]{:S(2)}) collective-permute-start(bf16[1,512,128]{2,1,0:T(8,128)(2,1)S(1)} %slice.99), channel_id=1, source_target_pairs={{0,32},{8,40},{16,48},{24,56},{32,0},{40,8},{48,16},{56,24},{64,96... | collective-permute-start | bytes 393224 | tf_op jit(solution)/shard_map/ppermute | solution.py:135
  112.7 2.8 %collective-permute-done.14 = bf16[2,512,128]{2,1,0:T(8,128)(2,1)S(1)} collective-permute-done((bf16[2,512,128]{2,1,0:T(8,128)(2,1)S(1)}, bf16[2,512,128]{2,1,0:T(8,128)(2,1)S(1)}, u32[]{:S(2)}, u32[]{:S(2)}) %collective-permute-start.14) | collective-permute-done | bytes 262176 | tf_op jit(solution)/shard_map/ppermute | solution.py:135
  115.6 2.8 %collective-permute-start.15 = (bf16[1,512,128]{2,1,0:T(8,128)(2,1)S(1)}, bf16[1,512,128]{2,1,0:T(8,128)(2,1)S(1)}, u32[]{:S(2)}, u32[]{:S(2)}) collective-permute-start(bf16[1,512,128]{2,1,0:T(8,128)(2,1)S(1)} %slice.100), channel_id=1, source_target_pairs={{0,32},{8,40},{16,48},{24,56},{32,0},{40,8},{48,16},{56,24},{64,96... | collective-permute-start | bytes 393224 | tf_op jit(solution)/shard_map/ppermute | solution.py:135
  118.4 1.8 %collective-permute-done.18 = bf16[1,512,128]{2,1,0:T(8,128)(2,1)S(1)} collective-permute-done((bf16[1,512,128]{2,1,0:T(8,128)(2,1)S(1)}, bf16[1,512,128]{2,1,0:T(8,128)(2,1)S(1)}, u32[]{:S(2)}, u32[]{:S(2)}) %collective-permute-start.18) | collective-permute-done | bytes 131104 | tf_op jit(solution)/shard_map/ppermute | solution.py:135
  120.2 0.7 fusion.8
  120.9 1.3 %collective-permute-done.15 = bf16[1,512,128]{2,1,0:T(8,128)(2,1)S(1)} collective-permute-done((bf16[1,512,128]{2,1,0:T(8,128)(2,1)S(1)}, bf16[1,512,128]{2,1,0:T(8,128)(2,1)S(1)}, u32[]{:S(2)}, u32[]{:S(2)}) %collective-permute-start.15) | collective-permute-done | bytes 131104 | tf_op jit(solution)/shard_map/ppermute | solution.py:135
  122.1 0.7 fusion.9
  (23 shorter events, 0.4 us)
Async XLA Ops:
  0.6 21.2 %copy-start.6 = (bf16[1,512,128]{2,1,0:T(8,128)(2,1)S(1)}, bf16[1,512,128]{2,1,0:T(8,128)(2,1)}, u32[]{:S(2)}) copy-start(bf16[1,512,128]{2,1,0:T(8,128)(2,1)} %param.9) | copy-start | bytes 393220
  0.6 7.3 %collective-permute-start = (bf16[1,512,128]{2,1,0:T(8,128)(2,1)}, bf16[1,512,128]{2,1,0:T(8,128)(2,1)S(1)}, u32[]{:S(2)}, u32[]{:S(2)}) collective-permute-start(bf16[1,512,128]{2,1,0:T(8,128)(2,1)} %param.8), channel_id=1, source_target_pairs={{0,32},{8,40},{16,48},{24,56},{32,0},{40,8},{48,16},{56,24},{64,96... | collective-permute-start | bytes 393224 | tf_op jit(solution)/shard_map/ppermute | solution.py:135
  3.8 7.4 %collective-permute-start.3 = (bf16[1,512,128]{2,1,0:T(8,128)(2,1)}, bf16[1,512,128]{2,1,0:T(8,128)(2,1)S(1)}, u32[]{:S(2)}, u32[]{:S(2)}) collective-permute-start(bf16[1,512,128]{2,1,0:T(8,128)(2,1)} %param.9), channel_id=1, source_target_pairs={{0,32},{8,40},{16,48},{24,56},{32,0},{40,8},{48,16},{56,24},{64,96... | collective-permute-start | bytes 393224 | tf_op jit(solution)/shard_map/ppermute | solution.py:135
  8.9 9.5 %collective-permute-start.1 = (bf16[2,512,128]{2,1,0:T(8,128)(2,1)S(1)}, bf16[2,512,128]{2,1,0:T(8,128)(2,1)S(1)}, u32[]{:S(2)}, u32[]{:S(2)}) collective-permute-start(bf16[2,512,128]{2,1,0:T(8,128)(2,1)S(1)} %pad_maximum_fusion.2), channel_id=1, source_target_pairs={{0,16},{8,24},{16,0},{24,8},{32,48},{40,56},{48,32},{56,40},{64,80... | collective-permute-start | bytes 786440 | tf_op jit(solution)/shard_map/ppermute | solution.py:135
  12.1 9.7 %collective-permute-start.4 = (bf16[2,512,128]{2,1,0:T(8,128)(2,1)S(1)}, bf16[2,512,128]{2,1,0:T(8,128)(2,1)S(1)}, u32[]{:S(2)}, u32[]{:S(2)}) collective-permute-start(bf16[2,512,128]{2,1,0:T(8,128)(2,1)S(1)} %pad_maximum_fusion.3), channel_id=1, source_target_pairs={{0,16},{8,24},{16,0},{24,8},{32,48},{40,56},{48,32},{56,40},{64,80... | collective-permute-start | bytes 786440 | tf_op jit(solution)/shard_map/ppermute | solution.py:135
  19.4 2.7 %collective-permute-start.2 = (bf16[4,512,128]{2,1,0:T(8,128)(2,1)S(1)}, bf16[4,512,128]{2,1,0:T(8,128)(2,1)S(1)}, u32[]{:S(2)}, u32[]{:S(2)}) collective-permute-start(bf16[4,512,128]{2,1,0:T(8,128)(2,1)S(1)} %pad_maximum_fusion), channel_id=1, source_target_pairs={{0,8},{8,0},{16,24},{24,16},{32,40},{40,32},{48,56},{56,48},{64,72... | collective-permute-start | bytes 1572872 | tf_op jit(solution)/shard_map/ppermute | solution.py:135
  21.9 2.0 %collective-permute-start.5 = (bf16[4,512,128]{2,1,0:T(8,128)(2,1)S(1)}, bf16[4,512,128]{2,1,0:T(8,128)(2,1)S(1)}, u32[]{:S(2)}, u32[]{:S(2)}) collective-permute-start(bf16[4,512,128]{2,1,0:T(8,128)(2,1)S(1)} %pad_maximum_fusion.1), channel_id=1, source_target_pairs={{0,8},{8,0},{16,24},{24,16},{32,40},{40,32},{48,56},{56,48},{64,72... | collective-permute-start | bytes 1572872 | tf_op jit(solution)/shard_map/ppermute | solution.py:135
  22.2 1.8 %copy-start.1 = (bf16[8,512,128]{2,1,0:T(8,128)(2,1)}, bf16[8,512,128]{2,1,0:T(8,128)(2,1)S(1)}, u32[]{:S(2)}) copy-start(bf16[8,512,128]{2,1,0:T(8,128)(2,1)S(1)} %constant_dynamic-update-slice_fusion.refs_0_.refs_1_.refs_2_) | copy-start | bytes 3145732
  23.9 1.1 copy-start
  25.0 20.2 %copy-start.3 = (bf16[1,512,1024]{2,1,0:T(8,128)(2,1)S(1)}, bf16[1,512,1024]{2,1,0:T(8,128)(2,1)}, u32[]{:S(2)}) copy-start(bf16[1,512,1024]{2,1,0:T(8,128)(2,1)} %param.13) | copy-start | bytes 3145732
  25.0 20.2 %copy-start.7 = (f32[1024]{0:T(1024)S(1)}, f32[1024]{0:T(1024)}, u32[]{:S(2)}) copy-start(f32[1024]{0:T(1024)} %param.12) | copy-start | bytes 12292
  45.3 22.9 %copy-start.2 = (bf16[512,1024]{1,0:T(8,128)(2,1)S(1)}, bf16[512,1024]{1,0:T(8,128)(2,1)}, u32[]{:S(2)}) copy-start(bf16[512,1024]{1,0:T(8,128)(2,1)} %get-tuple-element.9.refs_7_) | copy-start | bytes 3145732
  47.2 14.4 %collective-permute-start.11 = (f32[2,512]{1,0:T(2,128)S(1)}, f32[2,512]{1,0:T(2,128)S(1)}, u32[]{:S(2)}, u32[]{:S(2)}) collective-permute-start(f32[2,512]{1,0:T(2,128)S(1)} %pad_maximum_fusion.4), channel_id=1, source_target_pairs={{0,6},{1,7},{2,4},{3,5},{4,2},{5,3},{6,0},{7,1},{8,14},{9,15},{10,... | collective-permute-start | bytes 12296 | tf_op jit(solution)/shard_map/ppermute | solution.py:161
  52.7 9.4 %collective-permute-start.10 = (f32[2,512]{1,0:T(2,128)S(1)}, f32[2,512]{1,0:T(2,128)S(1)}, u32[]{:S(2)}, u32[]{:S(2)}) collective-permute-start(f32[2,512]{1,0:T(2,128)S(1)} %pad_maximum_fusion.4), channel_id=1, source_target_pairs={{0,5},{1,4},{2,7},{3,6},{4,1},{5,0},{6,3},{7,2},{8,13},{9,12},{10,... | collective-permute-start | bytes 12296 | tf_op jit(solution)/shard_map/ppermute | solution.py:161
  53.2 8.9 %collective-permute-start.9 = (f32[2,512]{1,0:T(2,128)S(1)}, f32[2,512]{1,0:T(2,128)S(1)}, u32[]{:S(2)}, u32[]{:S(2)}) collective-permute-start(f32[2,512]{1,0:T(2,128)S(1)} %pad_maximum_fusion.4), channel_id=1, source_target_pairs={{0,4},{1,5},{2,6},{3,7},{4,0},{5,1},{6,2},{7,3},{8,12},{9,13},{10,... | collective-permute-start | bytes 12296 | tf_op jit(solution)/shard_map/ppermute | solution.py:161
  58.1 3.9 %collective-permute-start.8 = (f32[2,512]{1,0:T(2,128)S(1)}, f32[2,512]{1,0:T(2,128)S(1)}, u32[]{:S(2)}, u32[]{:S(2)}) collective-permute-start(f32[2,512]{1,0:T(2,128)S(1)} %pad_maximum_fusion.4), channel_id=1, source_target_pairs={{0,3},{1,2},{2,1},{3,0},{4,7},{5,6},{6,5},{7,4},{8,11},{9,10},{10,... | collective-permute-start | bytes 12296 | tf_op jit(solution)/shard_map/ppermute | solution.py:161
  59.1 4.5 %collective-permute-start.7 = (f32[2,512]{1,0:T(2,128)S(1)}, f32[2,512]{1,0:T(2,128)S(1)}, u32[]{:S(2)}, u32[]{:S(2)}) collective-permute-start(f32[2,512]{1,0:T(2,128)S(1)} %pad_maximum_fusion.4), channel_id=1, source_target_pairs={{0,2},{1,3},{2,0},{3,1},{4,6},{5,7},{6,4},{7,5},{8,10},{9,11},{10,... | collective-permute-start | bytes 12296 | tf_op jit(solution)/shard_map/ppermute | solution.py:161
  61.5 6.6 %collective-permute-start.12 = (f32[2,512]{1,0:T(2,128)S(1)}, f32[2,512]{1,0:T(2,128)S(1)}, u32[]{:S(2)}, u32[]{:S(2)}) collective-permute-start(f32[2,512]{1,0:T(2,128)S(1)} %pad_maximum_fusion.4), channel_id=1, source_target_pairs={{0,7},{1,6},{2,5},{3,4},{4,3},{5,2},{6,1},{7,0},{8,15},{9,14},{10,... | collective-permute-start | bytes 12296 | tf_op jit(solution)/shard_map/ppermute | solution.py:161
  62.1 6.1 %collective-permute-start.6 = (f32[2,512]{1,0:T(2,128)S(1)}, f32[2,512]{1,0:T(2,128)S(1)}, u32[]{:S(2)}, u32[]{:S(2)}) collective-permute-start(f32[2,512]{1,0:T(2,128)S(1)} %pad_maximum_fusion.4), channel_id=1, source_target_pairs={{0,1},{1,0},{2,3},{3,2},{4,5},{5,4},{6,7},{7,6},{8,9},{9,8},{10,11... | collective-permute-start | bytes 12296 | tf_op jit(solution)/shard_map/ppermute | solution.py:161
  96.9 3.6 %copy-start.5 = (f32[8,512,128]{2,1,0:T(8,128)S(1)}, f32[8,512,128]{2,1,0:T(8,128)}, u32[]{:S(2)}) copy-start(f32[8,512,128]{2,1,0:T(8,128)} %get-tuple-element.13) | copy-start | bytes 6291460
  98.3 2.1 %collective-permute-start.16 = (bf16[4,512,128]{2,1,0:T(8,128)(2,1)S(1)}, bf16[4,512,128]{2,1,0:T(8,128)(2,1)S(1)}, u32[]{:S(2)}, u32[]{:S(2)}) collective-permute-start(bf16[4,512,128]{2,1,0:T(8,128)(2,1)S(1)} %slice.95), channel_id=1, source_target_pairs={{0,8},{8,0},{16,24},{24,16},{32,40},{40,32},{48,56},{56,48},{64,72... | collective-permute-start | bytes 1572872 | tf_op jit(solution)/shard_map/ppermute | solution.py:135
  98.4 3.7 %copy-start.4 = (f32[8,512,128]{2,1,0:T(8,128)S(1)}, f32[8,512,128]{2,1,0:T(8,128)}, u32[]{:S(2)}) copy-start(f32[8,512,128]{2,1,0:T(8,128)} %get-tuple-element.12) | copy-start | bytes 6291460
  99.9 2.2 %collective-permute-start.13 = (bf16[4,512,128]{2,1,0:T(8,128)(2,1)S(1)}, bf16[4,512,128]{2,1,0:T(8,128)(2,1)S(1)}, u32[]{:S(2)}, u32[]{:S(2)}) collective-permute-start(bf16[4,512,128]{2,1,0:T(8,128)(2,1)S(1)} %slice.96), channel_id=1, source_target_pairs={{0,8},{8,0},{16,24},{24,16},{32,40},{40,32},{48,56},{56,48},{64,72... | collective-permute-start | bytes 1572872 | tf_op jit(solution)/shard_map/ppermute | solution.py:135
  100.6 9.3 %collective-permute-start.17 = (bf16[2,512,128]{2,1,0:T(8,128)(2,1)S(1)}, bf16[2,512,128]{2,1,0:T(8,128)(2,1)S(1)}, u32[]{:S(2)}, u32[]{:S(2)}) collective-permute-start(bf16[2,512,128]{2,1,0:T(8,128)(2,1)S(1)} %slice.97), channel_id=1, source_target_pairs={{0,16},{8,24},{16,0},{24,8},{32,48},{40,56},{48,32},{56,40},{64,80... | collective-permute-start | bytes 786440 | tf_op jit(solution)/shard_map/ppermute | solution.py:135
  102.3 13.2 %collective-permute-start.14 = (bf16[2,512,128]{2,1,0:T(8,128)(2,1)S(1)}, bf16[2,512,128]{2,1,0:T(8,128)(2,1)S(1)}, u32[]{:S(2)}, u32[]{:S(2)}) collective-permute-start(bf16[2,512,128]{2,1,0:T(8,128)(2,1)S(1)} %slice.98), channel_id=1, source_target_pairs={{0,16},{8,24},{16,0},{24,8},{32,48},{40,56},{48,32},{56,40},{64,80... | collective-permute-start | bytes 786440 | tf_op jit(solution)/shard_map/ppermute | solution.py:135
  110.0 10.2 %collective-permute-start.18 = (bf16[1,512,128]{2,1,0:T(8,128)(2,1)S(1)}, bf16[1,512,128]{2,1,0:T(8,128)(2,1)S(1)}, u32[]{:S(2)}, u32[]{:S(2)}) collective-permute-start(bf16[1,512,128]{2,1,0:T(8,128)(2,1)S(1)} %slice.99), channel_id=1, source_target_pairs={{0,32},{8,40},{16,48},{24,56},{32,0},{40,8},{48,16},{56,24},{64,96... | collective-permute-start | bytes 393224 | tf_op jit(solution)/shard_map/ppermute | solution.py:135
  115.6 6.6 %collective-permute-start.15 = (bf16[1,512,128]{2,1,0:T(8,128)(2,1)S(1)}, bf16[1,512,128]{2,1,0:T(8,128)(2,1)S(1)}, u32[]{:S(2)}, u32[]{:S(2)}) collective-permute-start(bf16[1,512,128]{2,1,0:T(8,128)(2,1)S(1)} %slice.100), channel_id=1, source_target_pairs={{0,32},{8,40},{16,48},{24,56},{32,0},{40,8},{48,16},{56,24},{64,96... | collective-permute-start | bytes 393224 | tf_op jit(solution)/shard_map/ppermute | solution.py:135

commit v8 on v5

--- a/solution.py
+++ b/solution.py
@@ -43,7 +43,7 @@
 
 
 def backward_kernel(
-    count_ref, q_ref, k_ref, v_ref, grad_ref, att_ref, lse_ref, dq_ref, dk_ref, dv_ref
+    count_ref, q_ref, k_ref, v_ref, grad_ref, lse_ref, delta_ref, dq_ref, dk_ref, dv_ref
 ):
     @pl.when(pl.program_id(0) == 0)
     def _():
@@ -52,24 +52,24 @@
 
     query_head = q_ref[...]
     grad_head = grad_ref[...]
-    row_delta = jnp.sum(
-        grad_head.astype(jnp.float32) * att_ref[...].astype(jnp.float32), axis=1, keepdims=True
-    )
-    log_total = lse_ref[:, :1]
+    log_total = lse_ref[...]
+    row_delta = delta_ref[...]
     query_grad = jnp.zeros(dq_ref.shape, jnp.float32)
     for slot in range(SLOTS):
         mate_keys = k_ref[slot]
-        back_probs = jnp.exp(slot_scores(count_ref, query_head, mate_keys, slot) - log_total)
-        dv_ref[slot] += lax.dot_general(
-            back_probs.astype(jnp.bfloat16), grad_head, TRANS_A, preferred_element_type=jnp.float32
+        back_probs = jnp.exp(slot_scores(count_ref, mate_keys, query_head, slot) - log_total)
+        dv_ref[slot] += jnp.dot(
+            back_probs.astype(jnp.bfloat16), grad_head, preferred_element_type=jnp.float32
         )
         prob_grad = lax.dot_general(
-            grad_head, v_ref[slot], TRANS_B, preferred_element_type=jnp.float32
+            v_ref[slot], grad_head, TRANS_B, preferred_element_type=jnp.float32
         )
         score_grad = (back_probs * (prob_grad - row_delta)).astype(jnp.bfloat16)
-        query_grad = query_grad + jnp.dot(score_grad, mate_keys, preferred_element_type=jnp.float32)
-        dk_ref[slot] += SCORE_SCALE * lax.dot_general(
-            score_grad, query_head, TRANS_A, preferred_element_type=jnp.float32
+        dk_ref[slot] += SCORE_SCALE * jnp.dot(
+            score_grad, query_head, preferred_element_type=jnp.float32
+        )
+        query_grad = query_grad + lax.dot_general(
+            score_grad, mate_keys, TRANS_A, preferred_element_type=jnp.float32
         )
     dq_ref[...] = (SCORE_SCALE * query_grad).astype(dq_ref.dtype)
 
@@ -94,17 +94,18 @@
     )(count, queries, mate_keys, mate_values)
 
 
-def attention_backward(count, queries, mate_keys, mate_values, attention_grad, attention, log_total):
+def attention_backward(count, queries, mate_keys, mate_values, attention_grad, log_rows, delta_rows):
     seq_len, width = queries.shape
     heads = width // HD
     head_block = pl.BlockSpec((seq_len, HD), lambda h, c: (0, h))
+    row_block = pl.BlockSpec((None, 1, seq_len), lambda h, c: (h, 0, 0))
     slot_block = pl.BlockSpec((SLOTS, seq_len, HD), lambda h, c: (0, 0, 0))
     return pl.pallas_call(
         backward_kernel,
         grid_spec=pltpu.PrefetchScalarGridSpec(
             num_scalar_prefetch=1,
             grid=(heads,),
-            in_specs=[head_block, slot_block, slot_block, head_block, head_block, head_block],
+            in_specs=[head_block, slot_block, slot_block, head_block, row_block, row_block],
             out_specs=[head_block, slot_block, slot_block],
         ),
         out_shape=[
@@ -113,7 +114,7 @@
             jax.ShapeDtypeStruct((SLOTS, seq_len, HD), jnp.float32),
         ],
         compiler_params=pltpu.CompilerParams(dimension_semantics=("arbitrary",)),
-    )(count, queries, mate_keys, mate_values, attention_grad, attention, log_total)
+    )(count, queries, mate_keys, mate_values, attention_grad, log_rows, delta_rows)
 
 
 def exchange(block, axis, bit):
@@ -171,8 +172,13 @@
         - attention_flat * (inverse_rms**3 * dot_sums / D)[:, None]
     ).astype(jnp.bfloat16)
 
+    heads = attention.shape[1] // HD
+    log_rows = log_total[:, ::HD].T.reshape(heads, 1, seq_len)
+    delta_rows = jnp.sum(
+        (attention_grad.astype(jnp.float32) * attention_flat).reshape(seq_len, heads, HD), -1
+    ).T.reshape(heads, 1, seq_len)
     query_grads, key_terms, value_terms = attention_backward(
-        count, queries[0], mate_keys, mate_values, attention_grad, attention, log_total
+        count, queries[0], mate_keys, mate_values, attention_grad, log_rows, delta_rows
     )
     zero_rows = jnp.zeros((GROUP,) + key_terms.shape[1:], jnp.float32)
     key_total = return_group(zero_rows.at[mate_rows].add(key_terms))

time: 122 us -> 124 us (1.016)
  local copies, waits for them, and re-layouts: 3.57 us -> 9.97 us
  Pallas kernels: 43.9 us -> 41.3 us
  waiting for transfers between devices: 19.3 us -> 17.6 us
    pallas_call x0 -> x1, local copies, waits for them, and re-layouts: none -> 2.99 us  [attention_forward(): pl.pallas_call(forward_kernel, grid_spec=pltpu.PrefetchScalarGridSpec(num...]
    pallas_call x1, Pallas kernels: 24.7 us -> 22.1 us  [attention_backward(): pl.pallas_call(backward_kernel, grid_spec=pltpu.PrefetchScalarGridSpec(nu...]
    unnamed x0 -> x1, other arithmetic: none -> 2.04 us
    convert_element_type x1 -> x0, other arithmetic: 1.98 us -> none  [body(): attention_grad = (inverse_rms[:, None] * scaled_grad - attention_flat * (...]
    ppermute x7, waiting for transfers between devices: 1.73 us -> 0.02 us  [head_sum(): total = total + lax.ppermute(row_part, 'head', route)]
    slice x0 -> x1, local copies, waits for them, and re-layouts: none -> 1.6 us  [body(): log_rows = log_total[:, ::HD].T.reshape(heads, 1, seq_len)]
    reshape x0 -> x2, local copies, waits for them, and re-layouts: none -> 1.25 us  [the longest x1 0.63 us: body(): delta_rows = jnp.sum((attention_grad.astype(jnp.float32) * attention_flat...]
  transfers between devices with their start and end apart: 19 -> 19, of which waited for: 10 -> 8; matrix products, arithmetic and copies ran while one was open for 6% -> 10% of each run, Pallas kernels for 0% -> 0%
where the time goes in v8:
time: 124 us
  Pallas kernels  41.3 us (33%)
  starting transfers between devices  39.1 us (32%)
  waiting for transfers between devices  17.6 us (14%)
  other arithmetic  14.1 us (11%)
  local copies, waits for them, and re-layouts  9.97 us (8%)
  between operations  1.6 us (1%)
    ppermute x12, starting transfers between devices, exchange(): return lax.ppermute(block, axis, route)  24.7 us
    pallas_call x1, Pallas kernels, attention_backward(): pl.pallas_call(backward_kernel, grid_spec=pltpu.PrefetchScalarGridSpec(nu...  22.1 us
    pallas_call x1, Pallas kernels, attention_forward(): pl.pallas_call(forward_kernel, grid_spec=pltpu.PrefetchScalarGridSpec(num...  19.2 us
    ppermute x12, waiting for transfers between devices, exchange(): return lax.ppermute(block, axis, route)  17.6 us
    ppermute x7, starting transfers between devices, head_sum(): total = total + lax.ppermute(row_part, 'head', route)  14.4 us
    concatenate x6, other arithmetic, gather_group(): block = jnp.concatenate([block, exchange(block, 'resp', bit)], 0)  3.08 us
    pallas_call x1, local copies, waits for them, and re-layouts, attention_forward(): pl.pallas_call(forward_kernel, grid_spec=pltpu.PrefetchScalarGridSpec(num...  2.99 us
  transfers between devices with their start and end apart: 19, of which 8 were waited for; matrix products, arithmetic and copies ran while one was open for 10% of the time, Pallas kernels for 0%

profile of v8, /device:TPU:1, one launch (start us, length us, event | category | flops | bytes accessed | tf_op | source)
XLA Modules:
  0.0 123.7 jit_solution(10164205345193802596)
XLA Ops:
  0.6 0.0 copy-start.3
  0.6 0.0 copy-start.4
  0.7 3.7 %collective-permute-start.3 = (bf16[1,512,128]{2,1,0:T(8,128)(2,1)}, bf16[1,512,128]{2,1,0:T(8,128)(2,1)S(1)}, u32[]{:S(2)}, u32[]{:S(2)}) collective-permute-start(bf16[1,512,128]{2,1,0:T(8,128)(2,1)} %param.11), channel_id=1, source_target_pairs={{0,32},{8,40},{16,48},{24,56},{32,0},{40,8},{48,16},{56,24},{64,96... | collective-permute-start | bytes 393224 | tf_op jit(solution)/shard_map/ppermute | solution.py:122
  4.3 0.1 collective-permute-start
  4.4 2.5 %collective-permute-done.3 = bf16[1,512,128]{2,1,0:T(8,128)(2,1)S(1)} collective-permute-done((bf16[1,512,128]{2,1,0:T(8,128)(2,1)}, bf16[1,512,128]{2,1,0:T(8,128)(2,1)S(1)}, u32[]{:S(2)}, u32[]{:S(2)}) %collective-permute-start.3) | collective-permute-done | bytes 131104 | tf_op jit(solution)/shard_map/ppermute | solution.py:122
  6.9 0.9 pad_maximum_fusion.5
  7.8 2.1 %collective-permute-start.4 = (bf16[2,512,128]{2,1,0:T(8,128)(2,1)S(1)}, bf16[2,512,128]{2,1,0:T(8,128)(2,1)S(1)}, u32[]{:S(2)}, u32[]{:S(2)}) collective-permute-start(bf16[2,512,128]{2,1,0:T(8,128)(2,1)S(1)} %pad_maximum_fusion.5), channel_id=1, source_target_pairs={{0,16},{8,24},{16,0},{24,8},{32,48},{40,56},{48,32},{56,40},{64,80... | collective-permute-start | bytes 786440 | tf_op jit(solution)/shard_map/ppermute | solution.py:122
  9.9 1.5 %collective-permute-done = bf16[1,512,128]{2,1,0:T(8,128)(2,1)S(1)} collective-permute-done((bf16[1,512,128]{2,1,0:T(8,128)(2,1)}, bf16[1,512,128]{2,1,0:T(8,128)(2,1)S(1)}, u32[]{:S(2)}, u32[]{:S(2)}) %collective-permute-start) | collective-permute-done | bytes 131104 | tf_op jit(solution)/shard_map/ppermute | solution.py:122
  11.4 0.9 pad_maximum_fusion.4
  12.3 0.5 collective-permute-start.1
  12.8 0.7 fusion.15
  13.5 0.7 collective-permute-done.4
  14.2 1.0 pad_maximum_fusion.3
  15.2 7.0 %collective-permute-start.5 = (bf16[4,512,128]{2,1,0:T(8,128)(2,1)S(1)}, bf16[4,512,128]{2,1,0:T(8,128)(2,1)S(1)}, u32[]{:S(2)}, u32[]{:S(2)}) collective-permute-start(bf16[4,512,128]{2,1,0:T(8,128)(2,1)S(1)} %pad_maximum_fusion.3), channel_id=1, source_target_pairs={{0,8},{8,0},{16,24},{24,16},{32,40},{40,32},{48,56},{56,48},{64,72... | collective-permute-start | bytes 1572872 | tf_op jit(solution)/shard_map/ppermute | solution.py:122
  22.2 0.0 collective-permute-done.1
  22.2 0.1 pad_maximum_fusion.2
  22.3 1.8 %collective-permute-start.2 = (bf16[4,512,128]{2,1,0:T(8,128)(2,1)S(1)}, bf16[4,512,128]{2,1,0:T(8,128)(2,1)S(1)}, u32[]{:S(2)}, u32[]{:S(2)}) collective-permute-start(bf16[4,512,128]{2,1,0:T(8,128)(2,1)S(1)} %pad_maximum_fusion.2), channel_id=1, source_target_pairs={{0,8},{8,0},{16,24},{24,16},{32,40},{40,32},{48,56},{56,48},{64,72... | collective-permute-start | bytes 1572872 | tf_op jit(solution)/shard_map/ppermute | solution.py:122
  24.8 0.0 collective-permute-done.5
  24.8 0.1 pad_maximum_fusion.1
  24.9 0.6 gather_fusion.1
  25.6 0.1 collective-permute-done.2
  25.6 0.1 pad_maximum_fusion
  25.8 0.0 copy-start.1
  25.8 0.0 copy-start.7
  25.8 0.6 gather_fusion
  26.4 1.0 broadcast_select_fusion
  27.4 19.2 %shard_map.102 = (bf16[512,1024]{1,0:T(8,128)(2,1)}, f32[512,1024]{1,0:T(8,128)}) custom-call(s32[1]{0:T(128)S(6)} %copy.19.count_ref, bf16[512,1024]{1,0:T(8,128)(2,1)} %bitcast.27, bf16[3,512,128]{2,1,0:T(8,128)(2,1)} %get-tuple-element.25.k_ref, bf16[3,512,128]{2,1,0:T(8,128)(2,1)} %get-tuple-element.24.v_ref), custom_call_target="tpu_custom_call" | custom-call | tf_op jit(solution)/shard_map/pallas_call | solution.py:82
  46.6 1.8 %fusion = (f32[512]{0:T(512)S(1)}, f32[512]{0:T(512)S(1)}) fusion(bf16[512,1024]{1,0:T(8,128)(2,1)} %get-tuple-element.10, f32[1024]{0:T(1024)S(1)} %copy-done.7, bf16[1,512,1024]{2,1,0:T(8,128)(2,1)S(1)} %copy-done.1), kind=kLoop, calls=%fused_computation.9 | loop fusion | flops 3668992 | bytes 2105344 | tf_op jit(solution)/shard_map/reduce_sum | solution.py:164
  48.4 5.0 %collective-permute-start.12 = (f32[2,512]{1,0:T(2,128)S(1)}, f32[2,512]{1,0:T(2,128)S(1)}, u32[]{:S(2)}, u32[]{:S(2)}) collective-permute-start(f32[2,512]{1,0:T(2,128)S(1)} %pad_maximum_fusion.6), channel_id=1, source_target_pairs={{0,7},{1,6},{2,5},{3,4},{4,3},{5,2},{6,1},{7,0},{8,15},{9,14},{10,... | collective-permute-start | bytes 12296 | tf_op jit(solution)/shard_map/ppermute | solution.py:148
  53.5 0.5 collective-permute-start.11
  54.0 3.5 %collective-permute-start.10 = (f32[2,512]{1,0:T(2,128)S(1)}, f32[2,512]{1,0:T(2,128)S(1)}, u32[]{:S(2)}, u32[]{:S(2)}) collective-permute-start(f32[2,512]{1,0:T(2,128)S(1)} %pad_maximum_fusion.6), channel_id=1, source_target_pairs={{0,5},{1,4},{2,7},{3,6},{4,1},{5,0},{6,3},{7,2},{8,13},{9,12},{10,... | collective-permute-start | bytes 12296 | tf_op jit(solution)/shard_map/ppermute | solution.py:148
  57.5 1.8 %collective-permute-start.9 = (f32[2,512]{1,0:T(2,128)S(1)}, f32[2,512]{1,0:T(2,128)S(1)}, u32[]{:S(2)}, u32[]{:S(2)}) collective-permute-start(f32[2,512]{1,0:T(2,128)S(1)} %pad_maximum_fusion.6), channel_id=1, source_target_pairs={{0,4},{1,5},{2,6},{3,7},{4,0},{5,1},{6,2},{7,3},{8,12},{9,13},{10,... | collective-permute-start | bytes 12296 | tf_op jit(solution)/shard_map/ppermute | solution.py:148
  59.3 1.6 %collective-permute-start.8 = (f32[2,512]{1,0:T(2,128)S(1)}, f32[2,512]{1,0:T(2,128)S(1)}, u32[]{:S(2)}, u32[]{:S(2)}) collective-permute-start(f32[2,512]{1,0:T(2,128)S(1)} %pad_maximum_fusion.6), channel_id=1, source_target_pairs={{0,3},{1,2},{2,1},{3,0},{4,7},{5,6},{6,5},{7,4},{8,11},{9,10},{10,... | collective-permute-start | bytes 12296 | tf_op jit(solution)/shard_map/ppermute | solution.py:148
  60.9 1.9 %collective-permute-start.6 = (f32[2,512]{1,0:T(2,128)S(1)}, f32[2,512]{1,0:T(2,128)S(1)}, u32[]{:S(2)}, u32[]{:S(2)}) collective-permute-start(f32[2,512]{1,0:T(2,128)S(1)} %pad_maximum_fusion.6), channel_id=1, source_target_pairs={{0,1},{1,0},{2,3},{3,2},{4,5},{5,4},{6,7},{7,6},{8,9},{9,8},{10,11... | collective-permute-start | bytes 12296 | tf_op jit(solution)/shard_map/ppermute | solution.py:148
  62.8 3.0 %copy.13 = f32[512,1024]{0,1:T(8,128)} copy(f32[512,1024]{1,0:T(8,128)} %get-tuple-element.11) | data formatting | bytes 4194304 | tf_op jit(solution)/shard_map/pallas_call | solution.py:82
  65.8 1.6 %slice.53 = f32[512,8]{0,1:T(8,128)S(1)} slice(f32[512,1024]{0,1:T(8,128)} %copy.13), slice={[0:512:1], [0:1024:128]} | slice | bytes 32768 | tf_op jit(solution)/shard_map/slice | solution.py:176
  67.4 0.6 reshape.114.lse_ref
  68.2 2.0 %fusion.6 = (f32[64,8,8,128]{3,1,2,0:T(8,128)S(1)}, bf16[512,1024]{1,0:T(8,128)(2,1)}, bf16[1,512,1024]{2,1,0:T(8,128)(2,1)}) fusion(bf16[512,1024]{1,0:T(8,128)(2,1)S(1)} %copy-done.2, f32[512]{0:T(512)S(1)} %fusion.12, f32[1024]{0:T(1024)S(1)} %copy-done.7, bf16[1,512,1024]{2,1,0:T(8,128)(2,1)S(1)} %copy-done.1, f32[512]{0:T(512)S(1)} %bitcast.32), kind=kLoop, calls=%fused_computation.15 | loop fusion | flops 6291456 | bytes 6299648
  70.2 0.5 copy.15
  70.7 0.6 reduce_sum.29
  71.3 0.1 copy.14
  71.4 0.6 reshape.116.delta_ref
  72.0 22.1 %shard_map.103 = (bf16[512,1024]{1,0:T(8,128)(2,1)}, f32[3,512,128]{2,1,0:T(8,128)}, f32[3,512,128]{2,1,0:T(8,128)}) custom-call(s32[1]{0:T(128)S(6)} %copy.19.count_ref, bf16[512,1024]{1,0:T(8,128)(2,1)} %bitcast.28, bf16[3,512,128]{2,1,0:T(8,128)(2,1)} %get-tuple-element.25.k_ref, bf16[3,512,128]{2,1,0:T(8,128)(2,1)} %get-tuple-element.24.v_ref, ...), custom_call_target="tpu_custom_call" | custom-call | tf_op jit(solution)/shard_map/pallas_call | solution.py:103
  94.1 0.1 broadcast_in_dim.27.clone
  94.2 1.0 copy-done.6
  95.2 1.0 scatter_fusion
  96.3 0.9 slice.106
  97.1 2.0 %collective-permute-start.13 = (bf16[4,512,128]{2,1,0:T(8,128)(2,1)}, bf16[4,512,128]{2,1,0:T(8,128)(2,1)S(1)}, u32[]{:S(2)}, u32[]{:S(2)}) collective-permute-start(bf16[4,512,128]{2,1,0:T(8,128)(2,1)} %slice.106), channel_id=1, source_target_pairs={{0,8},{8,0},{16,24},{24,16},{32,40},{40,32},{48,56},{56,48},{64,72... | collective-permute-start | bytes 1572872 | tf_op jit(solution)/shard_map/ppermute | solution.py:122
  99.2 0.1 broadcast_in_dim.27.clone.1
  99.3 1.0 scatter_fusion.1
  100.3 0.1 slice.105
  100.4 0.8 collective-permute-start.16
  101.2 1.3 %slice_add_fusion.1 = f32[4,512,128]{2,1,0:T(8,128)S(1)} fusion(f32[8,512,128]{2,1,0:T(8,128)} %copy-done, bf16[4,512,128]{2,1,0:T(8,128)(2,1)S(1)} %collective-permute-done.13), kind=kLoop, calls=%fused_computation.22 | loop fusion | flops 524288 | bytes 2621440 | tf_op jit(solution)/shard_map/add | solution.py:139
  102.5 1.3 %collective-permute-start.14 = (bf16[2,512,128]{2,1,0:T(8,128)(2,1)S(1)}, bf16[2,512,128]{2,1,0:T(8,128)(2,1)S(1)}, u32[]{:S(2)}, u32[]{:S(2)}) collective-permute-start(bf16[2,512,128]{2,1,0:T(8,128)(2,1)S(1)} %slice.108), channel_id=1, source_target_pairs={{0,16},{8,24},{16,0},{24,8},{32,48},{40,56},{48,32},{56,40},{64,80... | collective-permute-start | bytes 786440 | tf_op jit(solution)/shard_map/ppermute | solution.py:122
  103.8 0.1 slice_add_fusion
  103.9 0.4 collective-permute-start.17
  104.3 6.2 %collective-permute-done.14 = bf16[2,512,128]{2,1,0:T(8,128)(2,1)S(1)} collective-permute-done((bf16[2,512,128]{2,1,0:T(8,128)(2,1)S(1)}, bf16[2,512,128]{2,1,0:T(8,128)(2,1)S(1)}, u32[]{:S(2)}, u32[]{:S(2)}) %collective-permute-start.14) | collective-permute-done | bytes 262176 | tf_op jit(solution)/shard_map/ppermute | solution.py:122
  110.6 2.5 %collective-permute-start.15 = (bf16[1,512,128]{2,1,0:T(8,128)(2,1)S(1)}, bf16[1,512,128]{2,1,0:T(8,128)(2,1)S(1)}, u32[]{:S(2)}, u32[]{:S(2)}) collective-permute-start(bf16[1,512,128]{2,1,0:T(8,128)(2,1)S(1)} %slice.110), channel_id=1, source_target_pairs={{0,32},{8,40},{16,48},{24,56},{32,0},{40,8},{48,16},{56,24},{64,96... | collective-permute-start | bytes 393224 | tf_op jit(solution)/shard_map/ppermute | solution.py:122
  113.1 3.0 %collective-permute-done.17 = bf16[2,512,128]{2,1,0:T(8,128)(2,1)S(1)} collective-permute-done((bf16[2,512,128]{2,1,0:T(8,128)(2,1)S(1)}, bf16[2,512,128]{2,1,0:T(8,128)(2,1)S(1)}, u32[]{:S(2)}, u32[]{:S(2)}) %collective-permute-start.17) | collective-permute-done | bytes 262176 | tf_op jit(solution)/shard_map/ppermute | solution.py:122
  116.2 2.5 %collective-permute-start.18 = (bf16[1,512,128]{2,1,0:T(8,128)(2,1)S(1)}, bf16[1,512,128]{2,1,0:T(8,128)(2,1)S(1)}, u32[]{:S(2)}, u32[]{:S(2)}) collective-permute-start(bf16[1,512,128]{2,1,0:T(8,128)(2,1)S(1)} %slice.109), channel_id=1, source_target_pairs={{0,32},{8,40},{16,48},{24,56},{32,0},{40,8},{48,16},{56,24},{64,96... | collective-permute-start | bytes 393224 | tf_op jit(solution)/shard_map/ppermute | solution.py:122
  118.7 2.1 %collective-permute-done.15 = bf16[1,512,128]{2,1,0:T(8,128)(2,1)S(1)} collective-permute-done((bf16[1,512,128]{2,1,0:T(8,128)(2,1)S(1)}, bf16[1,512,128]{2,1,0:T(8,128)(2,1)S(1)}, u32[]{:S(2)}, u32[]{:S(2)}) %collective-permute-start.15) | collective-permute-done | bytes 131104 | tf_op jit(solution)/shard_map/ppermute | solution.py:122
  120.8 0.7 fusion.10
  121.5 1.5 %collective-permute-done.18 = bf16[1,512,128]{2,1,0:T(8,128)(2,1)S(1)} collective-permute-done((bf16[1,512,128]{2,1,0:T(8,128)(2,1)S(1)}, bf16[1,512,128]{2,1,0:T(8,128)(2,1)S(1)}, u32[]{:S(2)}, u32[]{:S(2)}) %collective-permute-start.18) | collective-permute-done | bytes 131104 | tf_op jit(solution)/shard_map/ppermute | solution.py:122
  123.0 0.7 fusion.9
  (34 shorter events, 0.3 us)
Async XLA Ops:
  0.6 24.2 %copy-start.3 = (bf16[1,512,128]{2,1,0:T(8,128)(2,1)S(1)}, bf16[1,512,128]{2,1,0:T(8,128)(2,1)}, u32[]{:S(2)}) copy-start(bf16[1,512,128]{2,1,0:T(8,128)(2,1)} %param.11) | copy-start | bytes 393220
  0.6 21.6 %copy-start.4 = (bf16[1,512,128]{2,1,0:T(8,128)(2,1)S(1)}, bf16[1,512,128]{2,1,0:T(8,128)(2,1)}, u32[]{:S(2)}) copy-start(bf16[1,512,128]{2,1,0:T(8,128)(2,1)} %param.10) | copy-start | bytes 393220
  0.7 6.2 %collective-permute-start.3 = (bf16[1,512,128]{2,1,0:T(8,128)(2,1)}, bf16[1,512,128]{2,1,0:T(8,128)(2,1)S(1)}, u32[]{:S(2)}, u32[]{:S(2)}) collective-permute-start(bf16[1,512,128]{2,1,0:T(8,128)(2,1)} %param.11), channel_id=1, source_target_pairs={{0,32},{8,40},{16,48},{24,56},{32,0},{40,8},{48,16},{56,24},{64,96... | collective-permute-start | bytes 393224 | tf_op jit(solution)/shard_map/ppermute | solution.py:122
  4.3 7.1 %collective-permute-start = (bf16[1,512,128]{2,1,0:T(8,128)(2,1)}, bf16[1,512,128]{2,1,0:T(8,128)(2,1)S(1)}, u32[]{:S(2)}, u32[]{:S(2)}) collective-permute-start(bf16[1,512,128]{2,1,0:T(8,128)(2,1)} %param.10), channel_id=1, source_target_pairs={{0,32},{8,40},{16,48},{24,56},{32,0},{40,8},{48,16},{56,24},{64,96... | collective-permute-start | bytes 393224 | tf_op jit(solution)/shard_map/ppermute | solution.py:122
  7.8 6.4 %collective-permute-start.4 = (bf16[2,512,128]{2,1,0:T(8,128)(2,1)S(1)}, bf16[2,512,128]{2,1,0:T(8,128)(2,1)S(1)}, u32[]{:S(2)}, u32[]{:S(2)}) collective-permute-start(bf16[2,512,128]{2,1,0:T(8,128)(2,1)S(1)} %pad_maximum_fusion.5), channel_id=1, source_target_pairs={{0,16},{8,24},{16,0},{24,8},{32,48},{40,56},{48,32},{56,40},{64,80... | collective-permute-start | bytes 786440 | tf_op jit(solution)/shard_map/ppermute | solution.py:122
  12.3 9.9 %collective-permute-start.1 = (bf16[2,512,128]{2,1,0:T(8,128)(2,1)S(1)}, bf16[2,512,128]{2,1,0:T(8,128)(2,1)S(1)}, u32[]{:S(2)}, u32[]{:S(2)}) collective-permute-start(bf16[2,512,128]{2,1,0:T(8,128)(2,1)S(1)} %pad_maximum_fusion.4), channel_id=1, source_target_pairs={{0,16},{8,24},{16,0},{24,8},{32,48},{40,56},{48,32},{56,40},{64,80... | collective-permute-start | bytes 786440 | tf_op jit(solution)/shard_map/ppermute | solution.py:122
  15.2 9.6 %collective-permute-start.5 = (bf16[4,512,128]{2,1,0:T(8,128)(2,1)S(1)}, bf16[4,512,128]{2,1,0:T(8,128)(2,1)S(1)}, u32[]{:S(2)}, u32[]{:S(2)}) collective-permute-start(bf16[4,512,128]{2,1,0:T(8,128)(2,1)S(1)} %pad_maximum_fusion.3), channel_id=1, source_target_pairs={{0,8},{8,0},{16,24},{24,16},{32,40},{40,32},{48,56},{56,48},{64,72... | collective-permute-start | bytes 1572872 | tf_op jit(solution)/shard_map/ppermute | solution.py:122
  22.3 3.4 %collective-permute-start.2 = (bf16[4,512,128]{2,1,0:T(8,128)(2,1)S(1)}, bf16[4,512,128]{2,1,0:T(8,128)(2,1)S(1)}, u32[]{:S(2)}, u32[]{:S(2)}) collective-permute-start(bf16[4,512,128]{2,1,0:T(8,128)(2,1)S(1)} %pad_maximum_fusion.2), channel_id=1, source_target_pairs={{0,8},{8,0},{16,24},{24,16},{32,40},{40,32},{48,56},{56,48},{64,72... | collective-permute-start | bytes 1572872 | tf_op jit(solution)/shard_map/ppermute | solution.py:122
  25.8 20.9 %copy-start.1 = (bf16[1,512,1024]{2,1,0:T(8,128)(2,1)S(1)}, bf16[1,512,1024]{2,1,0:T(8,128)(2,1)}, u32[]{:S(2)}) copy-start(bf16[1,512,1024]{2,1,0:T(8,128)(2,1)} %param.15) | copy-start | bytes 3145732
  25.8 20.9 %copy-start.7 = (f32[1024]{0:T(1024)S(1)}, f32[1024]{0:T(1024)}, u32[]{:S(2)}) copy-start(f32[1024]{0:T(1024)} %param.14) | copy-start | bytes 12292
  48.4 12.5 %collective-permute-start.12 = (f32[2,512]{1,0:T(2,128)S(1)}, f32[2,512]{1,0:T(2,128)S(1)}, u32[]{:S(2)}, u32[]{:S(2)}) collective-permute-start(f32[2,512]{1,0:T(2,128)S(1)} %pad_maximum_fusion.6), channel_id=1, source_target_pairs={{0,7},{1,6},{2,5},{3,4},{4,3},{5,2},{6,1},{7,0},{8,15},{9,14},{10,... | collective-permute-start | bytes 12296 | tf_op jit(solution)/shard_map/ppermute | solution.py:148
  53.5 7.5 %collective-permute-start.11 = (f32[2,512]{1,0:T(2,128)S(1)}, f32[2,512]{1,0:T(2,128)S(1)}, u32[]{:S(2)}, u32[]{:S(2)}) collective-permute-start(f32[2,512]{1,0:T(2,128)S(1)} %pad_maximum_fusion.6), channel_id=1, source_target_pairs={{0,6},{1,7},{2,4},{3,5},{4,2},{5,3},{6,0},{7,1},{8,14},{9,15},{10,... | collective-permute-start | bytes 12296 | tf_op jit(solution)/shard_map/ppermute | solution.py:148
  54.0 14.1 %collective-permute-start.10 = (f32[2,512]{1,0:T(2,128)S(1)}, f32[2,512]{1,0:T(2,128)S(1)}, u32[]{:S(2)}, u32[]{:S(2)}) collective-permute-start(f32[2,512]{1,0:T(2,128)S(1)} %pad_maximum_fusion.6), channel_id=1, source_target_pairs={{0,5},{1,4},{2,7},{3,6},{4,1},{5,0},{6,3},{7,2},{8,13},{9,12},{10,... | collective-permute-start | bytes 12296 | tf_op jit(solution)/shard_map/ppermute | solution.py:148
  57.5 10.6 %collective-permute-start.9 = (f32[2,512]{1,0:T(2,128)S(1)}, f32[2,512]{1,0:T(2,128)S(1)}, u32[]{:S(2)}, u32[]{:S(2)}) collective-permute-start(f32[2,512]{1,0:T(2,128)S(1)} %pad_maximum_fusion.6), channel_id=1, source_target_pairs={{0,4},{1,5},{2,6},{3,7},{4,0},{5,1},{6,2},{7,3},{8,12},{9,13},{10,... | collective-permute-start | bytes 12296 | tf_op jit(solution)/shard_map/ppermute | solution.py:148
  59.3 8.8 %collective-permute-start.8 = (f32[2,512]{1,0:T(2,128)S(1)}, f32[2,512]{1,0:T(2,128)S(1)}, u32[]{:S(2)}, u32[]{:S(2)}) collective-permute-start(f32[2,512]{1,0:T(2,128)S(1)} %pad_maximum_fusion.6), channel_id=1, source_target_pairs={{0,3},{1,2},{2,1},{3,0},{4,7},{5,6},{6,5},{7,4},{8,11},{9,10},{10,... | collective-permute-start | bytes 12296 | tf_op jit(solution)/shard_map/ppermute | solution.py:148
  60.9 7.2 %collective-permute-start.7 = (f32[2,512]{1,0:T(2,128)S(1)}, f32[2,512]{1,0:T(2,128)S(1)}, u32[]{:S(2)}, u32[]{:S(2)}) collective-permute-start(f32[2,512]{1,0:T(2,128)S(1)} %pad_maximum_fusion.6), channel_id=1, source_target_pairs={{0,2},{1,3},{2,0},{3,1},{4,6},{5,7},{6,4},{7,5},{8,10},{9,11},{10,... | collective-permute-start | bytes 12296 | tf_op jit(solution)/shard_map/ppermute | solution.py:148
  60.9 7.2 %collective-permute-start.6 = (f32[2,512]{1,0:T(2,128)S(1)}, f32[2,512]{1,0:T(2,128)S(1)}, u32[]{:S(2)}, u32[]{:S(2)}) collective-permute-start(f32[2,512]{1,0:T(2,128)S(1)} %pad_maximum_fusion.6), channel_id=1, source_target_pairs={{0,1},{1,0},{2,3},{3,2},{4,5},{5,4},{6,7},{7,6},{8,9},{9,8},{10,11... | collective-permute-start | bytes 12296 | tf_op jit(solution)/shard_map/ppermute | solution.py:148
  62.8 5.3 %copy-start.2 = (bf16[512,1024]{1,0:T(8,128)(2,1)S(1)}, bf16[512,1024]{1,0:T(8,128)(2,1)}, u32[]{:S(2)}) copy-start(bf16[512,1024]{1,0:T(8,128)(2,1)} %get-tuple-element.10) | copy-start | bytes 3145732
  94.1 1.1 copy-start.6
  96.2 2.9 %copy-start = (f32[8,512,128]{2,1,0:T(8,128)}, f32[8,512,128]{2,1,0:T(8,128)S(1)}, u32[]{:S(2)}) copy-start(f32[8,512,128]{2,1,0:T(8,128)S(1)} %scatter_fusion) | copy-start | bytes 6291460
  96.2 3.1 %copy-start.5 = (f32[3,512,128]{2,1,0:T(8,128)S(1)}, f32[3,512,128]{2,1,0:T(8,128)}, u32[]{:S(2)}) copy-start(f32[3,512,128]{2,1,0:T(8,128)} %get-tuple-element.14) | copy-start | bytes 2359300
  97.1 4.1 %collective-permute-start.13 = (bf16[4,512,128]{2,1,0:T(8,128)(2,1)}, bf16[4,512,128]{2,1,0:T(8,128)(2,1)S(1)}, u32[]{:S(2)}, u32[]{:S(2)}) collective-permute-start(bf16[4,512,128]{2,1,0:T(8,128)(2,1)} %slice.106), channel_id=1, source_target_pairs={{0,8},{8,0},{16,24},{24,16},{32,40},{40,32},{48,56},{56,48},{64,72... | collective-permute-start | bytes 1572872 | tf_op jit(solution)/shard_map/ppermute | solution.py:122
  100.4 3.4 %collective-permute-start.16 = (bf16[4,512,128]{2,1,0:T(8,128)(2,1)S(1)}, bf16[4,512,128]{2,1,0:T(8,128)(2,1)S(1)}, u32[]{:S(2)}, u32[]{:S(2)}) collective-permute-start(bf16[4,512,128]{2,1,0:T(8,128)(2,1)S(1)} %slice.105), channel_id=1, source_target_pairs={{0,8},{8,0},{16,24},{24,16},{32,40},{40,32},{48,56},{56,48},{64,72... | collective-permute-start | bytes 1572872 | tf_op jit(solution)/shard_map/ppermute | solution.py:122
  102.5 8.0 %collective-permute-start.14 = (bf16[2,512,128]{2,1,0:T(8,128)(2,1)S(1)}, bf16[2,512,128]{2,1,0:T(8,128)(2,1)S(1)}, u32[]{:S(2)}, u32[]{:S(2)}) collective-permute-start(bf16[2,512,128]{2,1,0:T(8,128)(2,1)S(1)} %slice.108), channel_id=1, source_target_pairs={{0,16},{8,24},{16,0},{24,8},{32,48},{40,56},{48,32},{56,40},{64,80... | collective-permute-start | bytes 786440 | tf_op jit(solution)/shard_map/ppermute | solution.py:122
  103.9 12.2 %collective-permute-start.17 = (bf16[2,512,128]{2,1,0:T(8,128)(2,1)S(1)}, bf16[2,512,128]{2,1,0:T(8,128)(2,1)S(1)}, u32[]{:S(2)}, u32[]{:S(2)}) collective-permute-start(bf16[2,512,128]{2,1,0:T(8,128)(2,1)S(1)} %slice.107), channel_id=1, source_target_pairs={{0,16},{8,24},{16,0},{24,8},{32,48},{40,56},{48,32},{56,40},{64,80... | collective-permute-start | bytes 786440 | tf_op jit(solution)/shard_map/ppermute | solution.py:122
  110.6 10.2 %collective-permute-start.15 = (bf16[1,512,128]{2,1,0:T(8,128)(2,1)S(1)}, bf16[1,512,128]{2,1,0:T(8,128)(2,1)S(1)}, u32[]{:S(2)}, u32[]{:S(2)}) collective-permute-start(bf16[1,512,128]{2,1,0:T(8,128)(2,1)S(1)} %slice.110), channel_id=1, source_target_pairs={{0,32},{8,40},{16,48},{24,56},{32,0},{40,8},{48,16},{56,24},{64,96... | collective-permute-start | bytes 393224 | tf_op jit(solution)/shard_map/ppermute | solution.py:122
  116.2 6.8 %collective-permute-start.18 = (bf16[1,512,128]{2,1,0:T(8,128)(2,1)S(1)}, bf16[1,512,128]{2,1,0:T(8,128)(2,1)S(1)}, u32[]{:S(2)}, u32[]{:S(2)}) collective-permute-start(bf16[1,512,128]{2,1,0:T(8,128)(2,1)S(1)} %slice.109), channel_id=1, source_target_pairs={{0,32},{8,40},{16,48},{24,56},{32,0},{40,8},{48,16},{56,24},{64,96... | collective-permute-start | bytes 393224 | tf_op jit(solution)/shard_map/ppermute | solution.py:122

commit v9 on v8

--- a/solution.py
+++ b/solution.py
@@ -26,6 +26,10 @@
     return jnp.where(slot < count_ref[0], scores * SCORE_SCALE, NEG_FLOOR)
 
 
+def as_lane_row(column):
+    return jnp.transpose(jnp.broadcast_to(column, (column.shape[0], HD)))[:1]
+
+
 def forward_kernel(count_ref, q_ref, k_ref, v_ref, out_ref, lse_ref):
     query_head = q_ref[...]
     scores = [slot_scores(count_ref, query_head, k_ref[slot], slot) for slot in range(SLOTS)]
@@ -39,11 +43,11 @@
         for slot in range(SLOTS)
     )
     out_ref[...] = (weighted / denominator).astype(out_ref.dtype)
-    lse_ref[...] = jnp.broadcast_to(row_max + jnp.log(denominator), lse_ref.shape)
+    lse_ref[...] = as_lane_row(row_max + jnp.log(denominator))
 
 
 def backward_kernel(
-    count_ref, q_ref, k_ref, v_ref, grad_ref, lse_ref, delta_ref, dq_ref, dk_ref, dv_ref
+    count_ref, q_ref, k_ref, v_ref, grad_ref, att_ref, lse_ref, dq_ref, dk_ref, dv_ref
 ):
     @pl.when(pl.program_id(0) == 0)
     def _():
@@ -53,7 +57,9 @@
     query_head = q_ref[...]
     grad_head = grad_ref[...]
     log_total = lse_ref[...]
-    row_delta = delta_ref[...]
+    row_delta = as_lane_row(
+        jnp.sum(grad_head.astype(jnp.float32) * att_ref[...].astype(jnp.float32), axis=1, keepdims=True)
+    )
     query_grad = jnp.zeros(dq_ref.shape, jnp.float32)
     for slot in range(SLOTS):
         mate_keys = k_ref[slot]
@@ -85,16 +91,16 @@
             num_scalar_prefetch=1,
             grid=(heads,),
             in_specs=[head_block, slot_block, slot_block],
-            out_specs=[head_block, head_block],
+            out_specs=[head_block, pl.BlockSpec((None, 1, seq_len), lambda h, c: (h, 0, 0))],
         ),
         out_shape=[
             jax.ShapeDtypeStruct((seq_len, width), jnp.bfloat16),
-            jax.ShapeDtypeStruct((seq_len, width), jnp.float32),
+            jax.ShapeDtypeStruct((heads, 1, seq_len), jnp.float32),
         ],
     )(count, queries, mate_keys, mate_values)
 
 
-def attention_backward(count, queries, mate_keys, mate_values, attention_grad, log_rows, delta_rows):
+def attention_backward(count, queries, mate_keys, mate_values, attention_grad, attention, log_rows):
     seq_len, width = queries.shape
     heads = width // HD
     head_block = pl.BlockSpec((seq_len, HD), lambda h, c: (0, h))
@@ -105,7 +111,7 @@
         grid_spec=pltpu.PrefetchScalarGridSpec(
             num_scalar_prefetch=1,
             grid=(heads,),
-            in_specs=[head_block, slot_block, slot_block, head_block, row_block, row_block],
+            in_specs=[head_block, slot_block, slot_block, head_block, head_block, row_block],
             out_specs=[head_block, slot_block, slot_block],
         ),
         out_shape=[
@@ -114,7 +120,7 @@
             jax.ShapeDtypeStruct((SLOTS, seq_len, HD), jnp.float32),
         ],
         compiler_params=pltpu.CompilerParams(dimension_semantics=("arbitrary",)),
-    )(count, queries, mate_keys, mate_values, attention_grad, log_rows, delta_rows)
+    )(count, queries, mate_keys, mate_values, attention_grad, attention, log_rows)
 
 
 def exchange(block, axis, bit):
@@ -172,13 +178,8 @@
         - attention_flat * (inverse_rms**3 * dot_sums / D)[:, None]
     ).astype(jnp.bfloat16)
 
-    heads = attention.shape[1] // HD
-    log_rows = log_total[:, ::HD].T.reshape(heads, 1, seq_len)
-    delta_rows = jnp.sum(
-        (attention_grad.astype(jnp.float32) * attention_flat).reshape(seq_len, heads, HD), -1
-    ).T.reshape(heads, 1, seq_len)
     query_grads, key_terms, value_terms = attention_backward(
-        count, queries[0], mate_keys, mate_values, attention_grad, log_rows, delta_rows
+        count, queries[0], mate_keys, mate_values, attention_grad, attention, log_total
     )
     zero_rows = jnp.zeros((GROUP,) + key_terms.shape[1:], jnp.float32)
     key_total = return_group(zero_rows.at[mate_rows].add(key_terms))

time: 124 us -> 121 us (0.976); the launches traced: 124 us -> 119 us
  local copies, waits for them, and re-layouts: 9.97 us -> 3.58 us
  waiting for transfers between devices: 17.6 us -> 19.1 us
    pallas_call x1 -> x0, local copies, waits for them, and re-layouts: 2.99 us -> none  [attention_forward(): pl.pallas_call(forward_kernel, grid_spec=pltpu.PrefetchScalarGridSpec(num...]
    unnamed x1 -> x0, other arithmetic: 2.04 us -> none
    convert_element_type x0 -> x1, other arithmetic: none -> 1.98 us  [body(): attention_grad = (inverse_rms[:, None] * scaled_grad - attention_flat * (...]
    slice x1 -> x0, local copies, waits for them, and re-layouts: 1.6 us -> none  [body(): log_rows = log_total[:, ::HD].T.reshape(heads, 1, seq_len)]
    ppermute x7, waiting for transfers between devices: 0.02 us -> 1.49 us  [head_sum(): total = total + lax.ppermute(row_part, 'head', route)]
    reshape x2 -> x0, local copies, waits for them, and re-layouts: 1.25 us -> none  [the longest x1 0.63 us: body(): delta_rows = jnp.sum((attention_grad.astype(jnp.float32) * attention_flat...]
  transfers between devices with their start and end apart: 19 -> 19, of which waited for: 8 -> 11; matrix products, arithmetic and copies ran while one was open for 10% -> 7% of each run, Pallas kernels for 0% -> 0%
where the time goes in v9:
time: 121 us; the launch traced here: 119 us
  Pallas kernels  41.5 us (34%)
  starting transfers between devices  40 us (33%)
  waiting for transfers between devices  19.1 us (16%)
  other arithmetic  13.5 us (11%)
  local copies, waits for them, and re-layouts  3.58 us (3%)
  between operations  1.56 us (1%)
    ppermute x12, starting transfers between devices, exchange(): return lax.ppermute(block, axis, route)  25.6 us
    pallas_call x1, Pallas kernels, attention_backward(): pl.pallas_call(backward_kernel, grid_spec=pltpu.PrefetchScalarGridSpec(nu...  22.3 us
    pallas_call x1, Pallas kernels, attention_forward(): pl.pallas_call(forward_kernel, grid_spec=pltpu.PrefetchScalarGridSpec(num...  19.2 us
    ppermute x12, waiting for transfers between devices, exchange(): return lax.ppermute(block, axis, route)  17.6 us
    ppermute x7, starting transfers between devices, head_sum(): total = total + lax.ppermute(row_part, 'head', route)  14.5 us
    concatenate x6, other arithmetic, gather_group(): block = jnp.concatenate([block, exchange(block, 'resp', bit)], 0)  3.08 us
  transfers between devices with their start and end apart: 19, of which 11 were waited for; matrix products, arithmetic and copies ran while one was open for 7% of the time, Pallas kernels for 0%

profile of v9, /device:TPU:1, one launch (start us, length us, event | category | flops | bytes accessed | tf_op | source)
XLA Modules:
  0.0 119.3 jit_solution(12178021154611736012)
XLA Ops:
  0.6 0.0 copy-start.3
  0.6 0.0 copy-start.4
  0.7 3.7 %collective-permute-start = (bf16[1,512,128]{2,1,0:T(8,128)(2,1)}, bf16[1,512,128]{2,1,0:T(8,128)(2,1)S(1)}, u32[]{:S(2)}, u32[]{:S(2)}) collective-permute-start(bf16[1,512,128]{2,1,0:T(8,128)(2,1)} %param.10), channel_id=1, source_target_pairs={{0,32},{8,40},{16,48},{24,56},{32,0},{40,8},{48,16},{56,24},{64,96... | collective-permute-start | bytes 393224 | tf_op jit(solution)/shard_map/ppermute | solution.py:128
  4.3 0.1 collective-permute-start.3
  4.4 2.5 %collective-permute-done = bf16[1,512,128]{2,1,0:T(8,128)(2,1)S(1)} collective-permute-done((bf16[1,512,128]{2,1,0:T(8,128)(2,1)}, bf16[1,512,128]{2,1,0:T(8,128)(2,1)S(1)}, u32[]{:S(2)}, u32[]{:S(2)}) %collective-permute-start) | collective-permute-done | bytes 131104 | tf_op jit(solution)/shard_map/ppermute | solution.py:128
  6.9 0.9 pad_maximum_fusion.4
  7.8 2.1 %collective-permute-start.1 = (bf16[2,512,128]{2,1,0:T(8,128)(2,1)S(1)}, bf16[2,512,128]{2,1,0:T(8,128)(2,1)S(1)}, u32[]{:S(2)}, u32[]{:S(2)}) collective-permute-start(bf16[2,512,128]{2,1,0:T(8,128)(2,1)S(1)} %pad_maximum_fusion.4), channel_id=1, source_target_pairs={{0,16},{8,24},{16,0},{24,8},{32,48},{40,56},{48,32},{56,40},{64,80... | collective-permute-start | bytes 786440 | tf_op jit(solution)/shard_map/ppermute | solution.py:128
  9.9 1.5 %collective-permute-done.3 = bf16[1,512,128]{2,1,0:T(8,128)(2,1)S(1)} collective-permute-done((bf16[1,512,128]{2,1,0:T(8,128)(2,1)}, bf16[1,512,128]{2,1,0:T(8,128)(2,1)S(1)}, u32[]{:S(2)}, u32[]{:S(2)}) %collective-permute-start.3) | collective-permute-done | bytes 131104 | tf_op jit(solution)/shard_map/ppermute | solution.py:128
  11.4 0.9 pad_maximum_fusion.5
  12.3 0.5 collective-permute-start.4
  12.8 0.7 fusion.14
  13.5 0.7 collective-permute-done.1
  14.2 1.0 pad_maximum_fusion.2
  15.2 7.0 %collective-permute-start.2 = (bf16[4,512,128]{2,1,0:T(8,128)(2,1)S(1)}, bf16[4,512,128]{2,1,0:T(8,128)(2,1)S(1)}, u32[]{:S(2)}, u32[]{:S(2)}) collective-permute-start(bf16[4,512,128]{2,1,0:T(8,128)(2,1)S(1)} %pad_maximum_fusion.2), channel_id=1, source_target_pairs={{0,8},{8,0},{16,24},{24,16},{32,40},{40,32},{48,56},{56,48},{64,72... | collective-permute-start | bytes 1572872 | tf_op jit(solution)/shard_map/ppermute | solution.py:128
  22.2 0.0 collective-permute-done.4
  22.2 0.1 pad_maximum_fusion.3
  22.3 1.8 %collective-permute-start.5 = (bf16[4,512,128]{2,1,0:T(8,128)(2,1)S(1)}, bf16[4,512,128]{2,1,0:T(8,128)(2,1)S(1)}, u32[]{:S(2)}, u32[]{:S(2)}) collective-permute-start(bf16[4,512,128]{2,1,0:T(8,128)(2,1)S(1)} %pad_maximum_fusion.3), channel_id=1, source_target_pairs={{0,8},{8,0},{16,24},{24,16},{32,40},{40,32},{48,56},{56,48},{64,72... | collective-permute-start | bytes 1572872 | tf_op jit(solution)/shard_map/ppermute | solution.py:128
  24.8 0.0 collective-permute-done.2
  24.8 0.1 pad_maximum_fusion
  24.9 0.6 gather_fusion
  25.6 0.1 collective-permute-done.5
  25.6 0.1 pad_maximum_fusion.1
  25.8 0.0 copy-start.2
  25.8 0.0 copy-start.7
  25.8 0.6 gather_fusion.1
  26.4 1.0 broadcast_select_fusion
  27.4 19.2 %shard_map.102 = (bf16[512,1024]{1,0:T(8,128)(2,1)}, f32[8,1,512]{2,1,0:T(1,128)}) custom-call(s32[1]{0:T(128)S(6)} %copy.13.count_ref, bf16[512,1024]{1,0:T(8,128)(2,1)} %bitcast.20, bf16[3,512,128]{2,1,0:T(8,128)(2,1)} %get-tuple-element.24.k_ref, bf16[3,512,128]{2,1,0:T(8,128)(2,1)} %get-tuple-element.23.v_ref), custom_call_target="tpu_custom_call" | custom-call | tf_op jit(solution)/shard_map/pallas_call | solution.py:88
  46.6 1.9 %fusion = (f32[512]{0:T(512)S(1)}, f32[512]{0:T(512)S(1)}) fusion(bf16[512,1024]{1,0:T(8,128)(2,1)} %get-tuple-element.10.att_ref, f32[1024]{0:T(1024)S(1)} %copy-done.7, bf16[1,512,1024]{2,1,0:T(8,128)(2,1)S(1)} %copy-done.2), kind=kLoop, calls=%fused_computation.8 | loop fusion | flops 3668992 | bytes 2105344 | tf_op jit(solution)/shard_map/reduce_sum | solution.py:170
  48.5 5.5 %collective-permute-start.11 = (f32[2,512]{1,0:T(2,128)S(1)}, f32[2,512]{1,0:T(2,128)S(1)}, u32[]{:S(2)}, u32[]{:S(2)}) collective-permute-start(f32[2,512]{1,0:T(2,128)S(1)} %pad_maximum_fusion.6), channel_id=1, source_target_pairs={{0,6},{1,7},{2,4},{3,5},{4,2},{5,3},{6,0},{7,1},{8,14},{9,15},{10,... | collective-permute-start | bytes 12296 | tf_op jit(solution)/shard_map/ppermute | solution.py:154
  54.0 0.7 collective-permute-start.10
  54.7 4.2 %collective-permute-start.9 = (f32[2,512]{1,0:T(2,128)S(1)}, f32[2,512]{1,0:T(2,128)S(1)}, u32[]{:S(2)}, u32[]{:S(2)}) collective-permute-start(f32[2,512]{1,0:T(2,128)S(1)} %pad_maximum_fusion.6), channel_id=1, source_target_pairs={{0,4},{1,5},{2,6},{3,7},{4,0},{5,1},{6,2},{7,3},{8,12},{9,13},{10,... | collective-permute-start | bytes 12296 | tf_op jit(solution)/shard_map/ppermute | solution.py:154
  58.9 1.6 %collective-permute-start.8 = (f32[2,512]{1,0:T(2,128)S(1)}, f32[2,512]{1,0:T(2,128)S(1)}, u32[]{:S(2)}, u32[]{:S(2)}) collective-permute-start(f32[2,512]{1,0:T(2,128)S(1)} %pad_maximum_fusion.6), channel_id=1, source_target_pairs={{0,3},{1,2},{2,1},{3,0},{4,7},{5,6},{6,5},{7,4},{8,11},{9,10},{10,... | collective-permute-start | bytes 12296 | tf_op jit(solution)/shard_map/ppermute | solution.py:154
  60.5 0.3 collective-permute-start.7
  60.8 0.0 collective-permute-done.11
  60.8 2.2 %collective-permute-start.6 = (f32[2,512]{1,0:T(2,128)S(1)}, f32[2,512]{1,0:T(2,128)S(1)}, u32[]{:S(2)}, u32[]{:S(2)}) collective-permute-start(f32[2,512]{1,0:T(2,128)S(1)} %pad_maximum_fusion.6), channel_id=1, source_target_pairs={{0,1},{1,0},{2,3},{3,2},{4,5},{5,4},{6,7},{7,6},{8,9},{9,8},{10,11... | collective-permute-start | bytes 12296 | tf_op jit(solution)/shard_map/ppermute | solution.py:154
  63.0 0.0 collective-permute-done.9
  63.0 0.2 collective-permute-done.8
  63.2 0.7 collective-permute-done.7
  63.9 0.6 collective-permute-done.12
  64.5 0.0 collective-permute-done.6
  64.6 2.0 %fusion.5 = (bf16[512,1024]{1,0:T(8,128)(2,1)}, bf16[1,512,1024]{2,1,0:T(8,128)(2,1)}) fusion(bf16[512,1024]{1,0:T(8,128)(2,1)S(1)} %copy-done.1, bf16[1,512,1024]{2,1,0:T(8,128)(2,1)S(1)} %copy-done.2, f32[512]{0:T(512)S(1)} %fusion.11, f32[512]{0:T(512)S(1)} %bitcast.23, f32[1024]{0:T(1024)S(1)} %copy-done.7), kind=kLoop, calls=%fused_computation.13 | loop fusion | flops 5242880 | bytes 4202496 | tf_op jit(solution)/shard_map/convert_element_type | solution.py:179
  66.6 22.3 %shard_map.103 = (bf16[512,1024]{1,0:T(8,128)(2,1)}, f32[3,512,128]{2,1,0:T(8,128)}, f32[3,512,128]{2,1,0:T(8,128)}) custom-call(s32[1]{0:T(128)S(6)} %copy.13.count_ref, bf16[512,1024]{1,0:T(8,128)(2,1)} %bitcast.21, bf16[3,512,128]{2,1,0:T(8,128)(2,1)} %get-tuple-element.24.k_ref, bf16[3,512,128]{2,1,0:T(8,128)(2,1)} %get-tuple-element.23.v_ref, ...), custom_call_target="tpu_custom_call" | custom-call | tf_op jit(solution)/shard_map/pallas_call | solution.py:109
  88.8 0.1 broadcast_in_dim.27.clone
  89.0 1.0 copy-done.6
  90.0 1.0 scatter_fusion
  91.0 0.9 slice.102
  91.9 2.9 %collective-permute-start.13 = (bf16[4,512,128]{2,1,0:T(8,128)(2,1)}, bf16[4,512,128]{2,1,0:T(8,128)(2,1)S(1)}, u32[]{:S(2)}, u32[]{:S(2)}) collective-permute-start(bf16[4,512,128]{2,1,0:T(8,128)(2,1)} %slice.102), channel_id=1, source_target_pairs={{0,8},{8,0},{16,24},{24,16},{32,40},{40,32},{48,56},{56,48},{64,72... | collective-permute-start | bytes 1572872 | tf_op jit(solution)/shard_map/ppermute | solution.py:128
  94.8 0.1 broadcast_in_dim.27.clone.1
  94.9 1.0 scatter_fusion.1
  95.9 0.1 slice.101
  96.0 0.8 collective-permute-start.16
  96.8 1.3 %slice_add_fusion.1 = f32[4,512,128]{2,1,0:T(8,128)S(1)} fusion(f32[8,512,128]{2,1,0:T(8,128)} %copy-done, bf16[4,512,128]{2,1,0:T(8,128)(2,1)S(1)} %collective-permute-done.13), kind=kLoop, calls=%fused_computation.20 | loop fusion | flops 524288 | bytes 2621440 | tf_op jit(solution)/shard_map/add | solution.py:145
  98.1 1.3 %collective-permute-start.14 = (bf16[2,512,128]{2,1,0:T(8,128)(2,1)S(1)}, bf16[2,512,128]{2,1,0:T(8,128)(2,1)S(1)}, u32[]{:S(2)}, u32[]{:S(2)}) collective-permute-start(bf16[2,512,128]{2,1,0:T(8,128)(2,1)S(1)} %slice.104), channel_id=1, source_target_pairs={{0,16},{8,24},{16,0},{24,8},{32,48},{40,56},{48,32},{56,40},{64,80... | collective-permute-start | bytes 786440 | tf_op jit(solution)/shard_map/ppermute | solution.py:128
  99.4 0.0 collective-permute-done.16
  99.4 0.1 slice_add_fusion
  99.5 0.4 collective-permute-start.17
  99.9 6.2 %collective-permute-done.14 = bf16[2,512,128]{2,1,0:T(8,128)(2,1)S(1)} collective-permute-done((bf16[2,512,128]{2,1,0:T(8,128)(2,1)S(1)}, bf16[2,512,128]{2,1,0:T(8,128)(2,1)S(1)}, u32[]{:S(2)}, u32[]{:S(2)}) %collective-permute-start.14) | collective-permute-done | bytes 262176 | tf_op jit(solution)/shard_map/ppermute | solution.py:128
  106.2 2.5 %collective-permute-start.15 = (bf16[1,512,128]{2,1,0:T(8,128)(2,1)S(1)}, bf16[1,512,128]{2,1,0:T(8,128)(2,1)S(1)}, u32[]{:S(2)}, u32[]{:S(2)}) collective-permute-start(bf16[1,512,128]{2,1,0:T(8,128)(2,1)S(1)} %slice.106), channel_id=1, source_target_pairs={{0,32},{8,40},{16,48},{24,56},{32,0},{40,8},{48,16},{56,24},{64,96... | collective-permute-start | bytes 393224 | tf_op jit(solution)/shard_map/ppermute | solution.py:128
  108.7 3.0 %collective-permute-done.17 = bf16[2,512,128]{2,1,0:T(8,128)(2,1)S(1)} collective-permute-done((bf16[2,512,128]{2,1,0:T(8,128)(2,1)S(1)}, bf16[2,512,128]{2,1,0:T(8,128)(2,1)S(1)}, u32[]{:S(2)}, u32[]{:S(2)}) %collective-permute-start.17) | collective-permute-done | bytes 262176 | tf_op jit(solution)/shard_map/ppermute | solution.py:128
  111.8 2.5 %collective-permute-start.18 = (bf16[1,512,128]{2,1,0:T(8,128)(2,1)S(1)}, bf16[1,512,128]{2,1,0:T(8,128)(2,1)S(1)}, u32[]{:S(2)}, u32[]{:S(2)}) collective-permute-start(bf16[1,512,128]{2,1,0:T(8,128)(2,1)S(1)} %slice.105), channel_id=1, source_target_pairs={{0,32},{8,40},{16,48},{24,56},{32,0},{40,8},{48,16},{56,24},{64,96... | collective-permute-start | bytes 393224 | tf_op jit(solution)/shard_map/ppermute | solution.py:128
  114.3 2.1 %collective-permute-done.15 = bf16[1,512,128]{2,1,0:T(8,128)(2,1)S(1)} collective-permute-done((bf16[1,512,128]{2,1,0:T(8,128)(2,1)S(1)}, bf16[1,512,128]{2,1,0:T(8,128)(2,1)S(1)}, u32[]{:S(2)}, u32[]{:S(2)}) %collective-permute-start.15) | collective-permute-done | bytes 131104 | tf_op jit(solution)/shard_map/ppermute | solution.py:128
  116.4 0.7 fusion.9
  117.1 1.5 %collective-permute-done.18 = bf16[1,512,128]{2,1,0:T(8,128)(2,1)S(1)} collective-permute-done((bf16[1,512,128]{2,1,0:T(8,128)(2,1)S(1)}, bf16[1,512,128]{2,1,0:T(8,128)(2,1)S(1)}, u32[]{:S(2)}, u32[]{:S(2)}) %collective-permute-start.18) | collective-permute-done | bytes 131104 | tf_op jit(solution)/shard_map/ppermute | solution.py:128
  118.6 0.7 fusion.8
  (27 shorter events, 0.3 us)
Async XLA Ops:
  0.6 24.2 %copy-start.3 = (bf16[1,512,128]{2,1,0:T(8,128)(2,1)S(1)}, bf16[1,512,128]{2,1,0:T(8,128)(2,1)}, u32[]{:S(2)}) copy-start(bf16[1,512,128]{2,1,0:T(8,128)(2,1)} %param.10) | copy-start | bytes 393220
  0.6 21.6 %copy-start.4 = (bf16[1,512,128]{2,1,0:T(8,128)(2,1)S(1)}, bf16[1,512,128]{2,1,0:T(8,128)(2,1)}, u32[]{:S(2)}) copy-start(bf16[1,512,128]{2,1,0:T(8,128)(2,1)} %param.11) | copy-start | bytes 393220
  0.7 6.2 %collective-permute-start = (bf16[1,512,128]{2,1,0:T(8,128)(2,1)}, bf16[1,512,128]{2,1,0:T(8,128)(2,1)S(1)}, u32[]{:S(2)}, u32[]{:S(2)}) collective-permute-start(bf16[1,512,128]{2,1,0:T(8,128)(2,1)} %param.10), channel_id=1, source_target_pairs={{0,32},{8,40},{16,48},{24,56},{32,0},{40,8},{48,16},{56,24},{64,96... | collective-permute-start | bytes 393224 | tf_op jit(solution)/shard_map/ppermute | solution.py:128
  4.3 7.1 %collective-permute-start.3 = (bf16[1,512,128]{2,1,0:T(8,128)(2,1)}, bf16[1,512,128]{2,1,0:T(8,128)(2,1)S(1)}, u32[]{:S(2)}, u32[]{:S(2)}) collective-permute-start(bf16[1,512,128]{2,1,0:T(8,128)(2,1)} %param.11), channel_id=1, source_target_pairs={{0,32},{8,40},{16,48},{24,56},{32,0},{40,8},{48,16},{56,24},{64,96... | collective-permute-start | bytes 393224 | tf_op jit(solution)/shard_map/ppermute | solution.py:128
  7.8 6.4 %collective-permute-start.1 = (bf16[2,512,128]{2,1,0:T(8,128)(2,1)S(1)}, bf16[2,512,128]{2,1,0:T(8,128)(2,1)S(1)}, u32[]{:S(2)}, u32[]{:S(2)}) collective-permute-start(bf16[2,512,128]{2,1,0:T(8,128)(2,1)S(1)} %pad_maximum_fusion.4), channel_id=1, source_target_pairs={{0,16},{8,24},{16,0},{24,8},{32,48},{40,56},{48,32},{56,40},{64,80... | collective-permute-start | bytes 786440 | tf_op jit(solution)/shard_map/ppermute | solution.py:128
  12.3 9.9 %collective-permute-start.4 = (bf16[2,512,128]{2,1,0:T(8,128)(2,1)S(1)}, bf16[2,512,128]{2,1,0:T(8,128)(2,1)S(1)}, u32[]{:S(2)}, u32[]{:S(2)}) collective-permute-start(bf16[2,512,128]{2,1,0:T(8,128)(2,1)S(1)} %pad_maximum_fusion.5), channel_id=1, source_target_pairs={{0,16},{8,24},{16,0},{24,8},{32,48},{40,56},{48,32},{56,40},{64,80... | collective-permute-start | bytes 786440 | tf_op jit(solution)/shard_map/ppermute | solution.py:128
  15.2 9.6 %collective-permute-start.2 = (bf16[4,512,128]{2,1,0:T(8,128)(2,1)S(1)}, bf16[4,512,128]{2,1,0:T(8,128)(2,1)S(1)}, u32[]{:S(2)}, u32[]{:S(2)}) collective-permute-start(bf16[4,512,128]{2,1,0:T(8,128)(2,1)S(1)} %pad_maximum_fusion.2), channel_id=1, source_target_pairs={{0,8},{8,0},{16,24},{24,16},{32,40},{40,32},{48,56},{56,48},{64,72... | collective-permute-start | bytes 1572872 | tf_op jit(solution)/shard_map/ppermute | solution.py:128
  22.3 3.4 %collective-permute-start.5 = (bf16[4,512,128]{2,1,0:T(8,128)(2,1)S(1)}, bf16[4,512,128]{2,1,0:T(8,128)(2,1)S(1)}, u32[]{:S(2)}, u32[]{:S(2)}) collective-permute-start(bf16[4,512,128]{2,1,0:T(8,128)(2,1)S(1)} %pad_maximum_fusion.3), channel_id=1, source_target_pairs={{0,8},{8,0},{16,24},{24,16},{32,40},{40,32},{48,56},{56,48},{64,72... | collective-permute-start | bytes 1572872 | tf_op jit(solution)/shard_map/ppermute | solution.py:128
  25.8 20.9 %copy-start.2 = (bf16[1,512,1024]{2,1,0:T(8,128)(2,1)S(1)}, bf16[1,512,1024]{2,1,0:T(8,128)(2,1)}, u32[]{:S(2)}) copy-start(bf16[1,512,1024]{2,1,0:T(8,128)(2,1)} %param.15) | copy-start | bytes 3145732
  25.8 20.9 %copy-start.7 = (f32[1024]{0:T(1024)S(1)}, f32[1024]{0:T(1024)}, u32[]{:S(2)}) copy-start(f32[1024]{0:T(1024)} %param.14) | copy-start | bytes 12292
  46.6 17.9 %copy-start.1 = (bf16[512,1024]{1,0:T(8,128)(2,1)S(1)}, bf16[512,1024]{1,0:T(8,128)(2,1)}, u32[]{:S(2)}) copy-start(bf16[512,1024]{1,0:T(8,128)(2,1)} %get-tuple-element.10.att_ref) | copy-start | bytes 3145732
  48.5 12.3 %collective-permute-start.11 = (f32[2,512]{1,0:T(2,128)S(1)}, f32[2,512]{1,0:T(2,128)S(1)}, u32[]{:S(2)}, u32[]{:S(2)}) collective-permute-start(f32[2,512]{1,0:T(2,128)S(1)} %pad_maximum_fusion.6), channel_id=1, source_target_pairs={{0,6},{1,7},{2,4},{3,5},{4,2},{5,3},{6,0},{7,1},{8,14},{9,15},{10,... | collective-permute-start | bytes 12296 | tf_op jit(solution)/shard_map/ppermute | solution.py:154
  54.0 6.8 %collective-permute-start.10 = (f32[2,512]{1,0:T(2,128)S(1)}, f32[2,512]{1,0:T(2,128)S(1)}, u32[]{:S(2)}, u32[]{:S(2)}) collective-permute-start(f32[2,512]{1,0:T(2,128)S(1)} %pad_maximum_fusion.6), channel_id=1, source_target_pairs={{0,5},{1,4},{2,7},{3,6},{4,1},{5,0},{6,3},{7,2},{8,13},{9,12},{10,... | collective-permute-start | bytes 12296 | tf_op jit(solution)/shard_map/ppermute | solution.py:154
  54.7 8.3 %collective-permute-start.9 = (f32[2,512]{1,0:T(2,128)S(1)}, f32[2,512]{1,0:T(2,128)S(1)}, u32[]{:S(2)}, u32[]{:S(2)}) collective-permute-start(f32[2,512]{1,0:T(2,128)S(1)} %pad_maximum_fusion.6), channel_id=1, source_target_pairs={{0,4},{1,5},{2,6},{3,7},{4,0},{5,1},{6,2},{7,3},{8,12},{9,13},{10,... | collective-permute-start | bytes 12296 | tf_op jit(solution)/shard_map/ppermute | solution.py:154
  58.9 4.3 %collective-permute-start.8 = (f32[2,512]{1,0:T(2,128)S(1)}, f32[2,512]{1,0:T(2,128)S(1)}, u32[]{:S(2)}, u32[]{:S(2)}) collective-permute-start(f32[2,512]{1,0:T(2,128)S(1)} %pad_maximum_fusion.6), channel_id=1, source_target_pairs={{0,3},{1,2},{2,1},{3,0},{4,7},{5,6},{6,5},{7,4},{8,11},{9,10},{10,... | collective-permute-start | bytes 12296 | tf_op jit(solution)/shard_map/ppermute | solution.py:154
  60.5 3.4 %collective-permute-start.7 = (f32[2,512]{1,0:T(2,128)S(1)}, f32[2,512]{1,0:T(2,128)S(1)}, u32[]{:S(2)}, u32[]{:S(2)}) collective-permute-start(f32[2,512]{1,0:T(2,128)S(1)} %pad_maximum_fusion.6), channel_id=1, source_target_pairs={{0,2},{1,3},{2,0},{3,1},{4,6},{5,7},{6,4},{7,5},{8,10},{9,11},{10,... | collective-permute-start | bytes 12296 | tf_op jit(solution)/shard_map/ppermute | solution.py:154
  60.8 3.7 %collective-permute-start.12 = (f32[2,512]{1,0:T(2,128)S(1)}, f32[2,512]{1,0:T(2,128)S(1)}, u32[]{:S(2)}, u32[]{:S(2)}) collective-permute-start(f32[2,512]{1,0:T(2,128)S(1)} %pad_maximum_fusion.6), channel_id=1, source_target_pairs={{0,7},{1,6},{2,5},{3,4},{4,3},{5,2},{6,1},{7,0},{8,15},{9,14},{10,... | collective-permute-start | bytes 12296 | tf_op jit(solution)/shard_map/ppermute | solution.py:154
  60.8 3.7 %collective-permute-start.6 = (f32[2,512]{1,0:T(2,128)S(1)}, f32[2,512]{1,0:T(2,128)S(1)}, u32[]{:S(2)}, u32[]{:S(2)}) collective-permute-start(f32[2,512]{1,0:T(2,128)S(1)} %pad_maximum_fusion.6), channel_id=1, source_target_pairs={{0,1},{1,0},{2,3},{3,2},{4,5},{5,4},{6,7},{7,6},{8,9},{9,8},{10,11... | collective-permute-start | bytes 12296 | tf_op jit(solution)/shard_map/ppermute | solution.py:154
  88.8 1.1 copy-start.6
  91.0 3.8 %copy-start = (f32[8,512,128]{2,1,0:T(8,128)}, f32[8,512,128]{2,1,0:T(8,128)S(1)}, u32[]{:S(2)}) copy-start(f32[8,512,128]{2,1,0:T(8,128)S(1)} %scatter_fusion) | copy-start | bytes 6291460
  91.0 3.9 %copy-start.5 = (f32[3,512,128]{2,1,0:T(8,128)S(1)}, f32[3,512,128]{2,1,0:T(8,128)}, u32[]{:S(2)}) copy-start(f32[3,512,128]{2,1,0:T(8,128)} %get-tuple-element.14) | copy-start | bytes 2359300
  91.9 4.9 %collective-permute-start.13 = (bf16[4,512,128]{2,1,0:T(8,128)(2,1)}, bf16[4,512,128]{2,1,0:T(8,128)(2,1)S(1)}, u32[]{:S(2)}, u32[]{:S(2)}) collective-permute-start(bf16[4,512,128]{2,1,0:T(8,128)(2,1)} %slice.102), channel_id=1, source_target_pairs={{0,8},{8,0},{16,24},{24,16},{32,40},{40,32},{48,56},{56,48},{64,72... | collective-permute-start | bytes 1572872 | tf_op jit(solution)/shard_map/ppermute | solution.py:128
  96.0 3.4 %collective-permute-start.16 = (bf16[4,512,128]{2,1,0:T(8,128)(2,1)S(1)}, bf16[4,512,128]{2,1,0:T(8,128)(2,1)S(1)}, u32[]{:S(2)}, u32[]{:S(2)}) collective-permute-start(bf16[4,512,128]{2,1,0:T(8,128)(2,1)S(1)} %slice.101), channel_id=1, source_target_pairs={{0,8},{8,0},{16,24},{24,16},{32,40},{40,32},{48,56},{56,48},{64,72... | collective-permute-start | bytes 1572872 | tf_op jit(solution)/shard_map/ppermute | solution.py:128
  98.1 8.0 %collective-permute-start.14 = (bf16[2,512,128]{2,1,0:T(8,128)(2,1)S(1)}, bf16[2,512,128]{2,1,0:T(8,128)(2,1)S(1)}, u32[]{:S(2)}, u32[]{:S(2)}) collective-permute-start(bf16[2,512,128]{2,1,0:T(8,128)(2,1)S(1)} %slice.104), channel_id=1, source_target_pairs={{0,16},{8,24},{16,0},{24,8},{32,48},{40,56},{48,32},{56,40},{64,80... | collective-permute-start | bytes 786440 | tf_op jit(solution)/shard_map/ppermute | solution.py:128
  99.5 12.2 %collective-permute-start.17 = (bf16[2,512,128]{2,1,0:T(8,128)(2,1)S(1)}, bf16[2,512,128]{2,1,0:T(8,128)(2,1)S(1)}, u32[]{:S(2)}, u32[]{:S(2)}) collective-permute-start(bf16[2,512,128]{2,1,0:T(8,128)(2,1)S(1)} %slice.103), channel_id=1, source_target_pairs={{0,16},{8,24},{16,0},{24,8},{32,48},{40,56},{48,32},{56,40},{64,80... | collective-permute-start | bytes 786440 | tf_op jit(solution)/shard_map/ppermute | solution.py:128
  106.2 10.2 %collective-permute-start.15 = (bf16[1,512,128]{2,1,0:T(8,128)(2,1)S(1)}, bf16[1,512,128]{2,1,0:T(8,128)(2,1)S(1)}, u32[]{:S(2)}, u32[]{:S(2)}) collective-permute-start(bf16[1,512,128]{2,1,0:T(8,128)(2,1)S(1)} %slice.106), channel_id=1, source_target_pairs={{0,32},{8,40},{16,48},{24,56},{32,0},{40,8},{48,16},{56,24},{64,96... | collective-permute-start | bytes 393224 | tf_op jit(solution)/shard_map/ppermute | solution.py:128
  111.8 6.8 %collective-permute-start.18 = (bf16[1,512,128]{2,1,0:T(8,128)(2,1)S(1)}, bf16[1,512,128]{2,1,0:T(8,128)(2,1)S(1)}, u32[]{:S(2)}, u32[]{:S(2)}) collective-permute-start(bf16[1,512,128]{2,1,0:T(8,128)(2,1)S(1)} %slice.105), channel_id=1, source_target_pairs={{0,32},{8,40},{16,48},{24,56},{32,0},{40,8},{48,16},{56,24},{64,96... | collective-permute-start | bytes 393224 | tf_op jit(solution)/shard_map/ppermute | solution.py:128

commit v10 on v9

--- a/solution.py
+++ b/solution.py
@@ -14,16 +14,19 @@
 
 
 EPSILON = 1e-05
-NEG_FLOOR = -1e30
 SCORE_SCALE = HD ** (-0.5)
 
 TRANS_B = (((1,), (1,)), ((), ()))
 TRANS_A = (((0,), (0,)), ((), ()))
 
 
-def slot_scores(count_ref, query_head, mate_keys, slot):
+def slot_scores(query_head, mate_keys):
     scores = lax.dot_general(query_head, mate_keys, TRANS_B, preferred_element_type=jnp.float32)
-    return jnp.where(slot < count_ref[0], scores * SCORE_SCALE, NEG_FLOOR)
+    return scores * SCORE_SCALE
+
+
+def slot_offset(count_ref, slot, offset, dead):
+    return jnp.where(slot < count_ref[0], offset, dead)
 
 
 def as_lane_row(column):
@@ -32,11 +35,18 @@
 
 def forward_kernel(count_ref, q_ref, k_ref, v_ref, out_ref, lse_ref):
     query_head = q_ref[...]
-    scores = [slot_scores(count_ref, query_head, k_ref[slot], slot) for slot in range(SLOTS)]
+    scores = [slot_scores(query_head, k_ref[slot]) for slot in range(SLOTS)]
     row_max = functools.reduce(
-        jnp.maximum, [jnp.max(block, axis=1, keepdims=True) for block in scores]
-    )
-    exps = [jnp.exp(block - row_max) for block in scores]
+        jnp.maximum,
+        [
+            slot_offset(count_ref, slot, jnp.max(block, axis=1, keepdims=True), -jnp.inf)
+            for slot, block in enumerate(scores)
+        ],
+    )
+    exps = [
+        jnp.exp(block - slot_offset(count_ref, slot, row_max, jnp.inf))
+        for slot, block in enumerate(scores)
+    ]
     denominator = sum(jnp.sum(block, axis=1, keepdims=True) for block in exps)
     weighted = sum(
         jnp.dot(exps[slot].astype(jnp.bfloat16), v_ref[slot], preferred_element_type=jnp.float32)
@@ -63,7 +73,9 @@
     query_grad = jnp.zeros(dq_ref.shape, jnp.float32)
     for slot in range(SLOTS):
         mate_keys = k_ref[slot]
-        back_probs = jnp.exp(slot_scores(count_ref, mate_keys, query_head, slot) - log_total)
+        back_probs = jnp.exp(
+            slot_scores(mate_keys, query_head) - slot_offset(count_ref, slot, log_total, jnp.inf)
+        )
         dv_ref[slot] += jnp.dot(
             back_probs.astype(jnp.bfloat16), grad_head, preferred_element_type=jnp.float32
         )
@@ -147,12 +159,9 @@
 
 
 def head_sum(row_part):
-    heads = lax.axis_size("head")
-    total = row_part
-    for distance in range(1, heads):
-        route = [(low, low ^ distance) for low in range(heads)]
-        total = total + lax.ppermute(row_part, "head", route)
-    return total
+    for bit in range(lax.axis_size("head").bit_length() - 1):
+        row_part = row_part + exchange(row_part, "head", bit)
+    return row_part
 
 
 def body(queries, key_states, value_states, partners, counts, norm_gain, out_grad):

time: 121 us -> 118 us (0.975); the launches traced: 119 us -> 118 us
  starting transfers between devices: 40 us -> 36.2 us
  waiting for transfers between devices: 19.1 us -> 21 us
    ppermute x7 -> x0, starting transfers between devices: 14.5 us -> none  [head_sum(): total = total + lax.ppermute(row_part, 'head', route)]
    ppermute x12 -> x15, starting transfers between devices: 25.6 us -> 36.2 us  [exchange(): return lax.ppermute(block, axis, route)]
    ppermute x12 -> x15, waiting for transfers between devices: 17.6 us -> 21 us  [exchange(): return lax.ppermute(block, axis, route)]
    ppermute x7 -> x0, waiting for transfers between devices: 1.49 us -> none  [head_sum(): total = total + lax.ppermute(row_part, 'head', route)]
  transfers between devices with their start and end apart: 19 -> 15, of which waited for: 11 -> 11; matrix products, arithmetic and copies ran while one was open for 7% -> 7% of each run, Pallas kernels for 0% -> 0%
where the time goes in v10:
time: 118 us
  Pallas kernels  41.9 us (36%)
  starting transfers between devices  36.2 us (31%)
  waiting for transfers between devices  21 us (18%)
  other arithmetic  13.6 us (12%)
  local copies, waits for them, and re-layouts  3.58 us (3%)
  between operations  1.54 us (1%)
    ppermute x15, starting transfers between devices, exchange(): return lax.ppermute(block, axis, route)  36.2 us
    pallas_call x1, Pallas kernels, attention_backward(): pl.pallas_call(backward_kernel, grid_spec=pltpu.PrefetchScalarGridSpec(nu...  21.5 us
    ppermute x15, waiting for transfers between devices, exchange(): return lax.ppermute(block, axis, route)  21 us
    pallas_call x1, Pallas kernels, attention_forward(): pl.pallas_call(forward_kernel, grid_spec=pltpu.PrefetchScalarGridSpec(num...  20.3 us
    concatenate x6, other arithmetic, gather_group(): block = jnp.concatenate([block, exchange(block, 'resp', bit)], 0)  3.08 us
  transfers between devices with their start and end apart: 15, of which 11 were waited for; matrix products, arithmetic and copies ran while one was open for 7% of the time, Pallas kernels for 0%

profile of v10, /device:TPU:1, one launch (start us, length us, event | category | flops | bytes accessed | tf_op | source)
XLA Modules:
  0.0 117.7 jit_solution(8455587798265462847)
XLA Ops:
  0.6 0.0 copy-start.3
  0.6 0.0 copy-start.4
  0.7 3.7 %collective-permute-start = (bf16[1,512,128]{2,1,0:T(8,128)(2,1)}, bf16[1,512,128]{2,1,0:T(8,128)(2,1)S(1)}, u32[]{:S(2)}, u32[]{:S(2)}) collective-permute-start(bf16[1,512,128]{2,1,0:T(8,128)(2,1)} %param.10), channel_id=1, source_target_pairs={{0,32},{8,40},{16,48},{24,56},{32,0},{40,8},{48,16},{56,24},{64,96... | collective-permute-start | bytes 393224 | tf_op jit(solution)/shard_map/ppermute | solution.py:140
  4.3 0.1 collective-permute-start.3
  4.4 2.5 %collective-permute-done = bf16[1,512,128]{2,1,0:T(8,128)(2,1)S(1)} collective-permute-done((bf16[1,512,128]{2,1,0:T(8,128)(2,1)}, bf16[1,512,128]{2,1,0:T(8,128)(2,1)S(1)}, u32[]{:S(2)}, u32[]{:S(2)}) %collective-permute-start) | collective-permute-done | bytes 131104 | tf_op jit(solution)/shard_map/ppermute | solution.py:140
  6.9 0.9 pad_maximum_fusion.4
  7.8 2.1 %collective-permute-start.1 = (bf16[2,512,128]{2,1,0:T(8,128)(2,1)S(1)}, bf16[2,512,128]{2,1,0:T(8,128)(2,1)S(1)}, u32[]{:S(2)}, u32[]{:S(2)}) collective-permute-start(bf16[2,512,128]{2,1,0:T(8,128)(2,1)S(1)} %pad_maximum_fusion.4), channel_id=1, source_target_pairs={{0,16},{8,24},{16,0},{24,8},{32,48},{40,56},{48,32},{56,40},{64,80... | collective-permute-start | bytes 786440 | tf_op jit(solution)/shard_map/ppermute | solution.py:140
  9.9 1.5 %collective-permute-done.3 = bf16[1,512,128]{2,1,0:T(8,128)(2,1)S(1)} collective-permute-done((bf16[1,512,128]{2,1,0:T(8,128)(2,1)}, bf16[1,512,128]{2,1,0:T(8,128)(2,1)S(1)}, u32[]{:S(2)}, u32[]{:S(2)}) %collective-permute-start.3) | collective-permute-done | bytes 131104 | tf_op jit(solution)/shard_map/ppermute | solution.py:140
  11.4 0.9 pad_maximum_fusion.5
  12.3 0.5 collective-permute-start.4
  12.8 0.7 fusion.14
  13.5 0.7 collective-permute-done.1
  14.2 1.0 pad_maximum_fusion.2
  15.2 7.0 %collective-permute-start.2 = (bf16[4,512,128]{2,1,0:T(8,128)(2,1)S(1)}, bf16[4,512,128]{2,1,0:T(8,128)(2,1)S(1)}, u32[]{:S(2)}, u32[]{:S(2)}) collective-permute-start(bf16[4,512,128]{2,1,0:T(8,128)(2,1)S(1)} %pad_maximum_fusion.2), channel_id=1, source_target_pairs={{0,8},{8,0},{16,24},{24,16},{32,40},{40,32},{48,56},{56,48},{64,72... | collective-permute-start | bytes 1572872 | tf_op jit(solution)/shard_map/ppermute | solution.py:140
  22.2 0.0 collective-permute-done.4
  22.2 0.0 copy-done.4
  22.2 0.1 pad_maximum_fusion.3
  22.3 1.8 %collective-permute-start.5 = (bf16[4,512,128]{2,1,0:T(8,128)(2,1)S(1)}, bf16[4,512,128]{2,1,0:T(8,128)(2,1)S(1)}, u32[]{:S(2)}, u32[]{:S(2)}) collective-permute-start(bf16[4,512,128]{2,1,0:T(8,128)(2,1)S(1)} %pad_maximum_fusion.3), channel_id=1, source_target_pairs={{0,8},{8,0},{16,24},{24,16},{32,40},{40,32},{48,56},{56,48},{64,72... | collective-permute-start | bytes 1572872 | tf_op jit(solution)/shard_map/ppermute | solution.py:140
  24.8 0.0 collective-permute-done.2
  24.8 0.0 copy-done.3
  24.8 0.1 pad_maximum_fusion
  24.9 0.6 gather_fusion
  25.6 0.1 collective-permute-done.5
  25.6 0.1 pad_maximum_fusion.1
  25.8 0.0 copy-start.2
  25.8 0.0 copy-start.7
  25.8 0.6 gather_fusion.1
  26.4 1.0 broadcast_select_fusion
  27.4 20.3 %shard_map.102 = (bf16[512,1024]{1,0:T(8,128)(2,1)}, f32[8,1,512]{2,1,0:T(1,128)}) custom-call(s32[1]{0:T(128)S(6)} %copy.13.count_ref, bf16[512,1024]{1,0:T(8,128)(2,1)} %bitcast.20, bf16[3,512,128]{2,1,0:T(8,128)(2,1)} %get-tuple-element.24.k_ref, bf16[3,512,128]{2,1,0:T(8,128)(2,1)} %get-tuple-element.23.v_ref), custom_call_target="tpu_custom_call" | custom-call | tf_op jit(solution)/shard_map/pallas_call | solution.py:100
  47.8 0.0 copy-done.2
  47.8 0.0 copy-done.7
  47.8 1.9 %fusion = (f32[512]{0:T(512)S(1)}, f32[512]{0:T(512)S(1)}) fusion(bf16[512,1024]{1,0:T(8,128)(2,1)} %get-tuple-element.10.att_ref, f32[1024]{0:T(1024)S(1)} %copy-done.7, bf16[1,512,1024]{2,1,0:T(8,128)(2,1)S(1)} %copy-done.2), kind=kLoop, calls=%fused_computation.8 | loop fusion | flops 3668992 | bytes 2105344 | tf_op jit(solution)/shard_map/reduce_sum | solution.py:179
  49.7 1.1 collective-permute-start.6
  50.8 1.5 %collective-permute-done.6 = f32[2,512]{1,0:T(2,128)S(1)} collective-permute-done((f32[2,512]{1,0:T(2,128)S(1)}, f32[2,512]{1,0:T(2,128)S(1)}, u32[]{:S(2)}, u32[]{:S(2)}) %collective-permute-start.6) | collective-permute-done | bytes 4128 | tf_op jit(solution)/shard_map/ppermute | solution.py:140
  52.2 2.6 %collective-permute-start.7 = (f32[2,512]{1,0:T(2,128)S(1)}, f32[2,512]{1,0:T(2,128)S(1)}, u32[]{:S(2)}, u32[]{:S(2)}) collective-permute-start(f32[2,512]{1,0:T(2,128)S(1)} %fusion.15), channel_id=1, source_target_pairs={{0,2},{1,3},{2,0},{3,1},{4,6},{5,7},{6,4},{7,5},{8,10},{9,11},{10,... | collective-permute-start | bytes 12296 | tf_op jit(solution)/shard_map/ppermute | solution.py:140
  54.9 1.0 collective-permute-done.7
  55.9 6.4 %collective-permute-start.8 = (f32[2,512]{1,0:T(2,128)S(1)}, f32[2,512]{1,0:T(2,128)S(1)}, u32[]{:S(2)}, u32[]{:S(2)}) collective-permute-start(f32[2,512]{1,0:T(2,128)S(1)} %fusion.17), channel_id=1, source_target_pairs={{0,4},{1,5},{2,6},{3,7},{4,0},{5,1},{6,2},{7,3},{8,12},{9,13},{10,... | collective-permute-start | bytes 12296 | tf_op jit(solution)/shard_map/ppermute | solution.py:140
  62.2 1.0 collective-permute-done.8
  63.3 0.0 copy-done.1
  63.3 2.0 %fusion.5 = (bf16[512,1024]{1,0:T(8,128)(2,1)}, bf16[1,512,1024]{2,1,0:T(8,128)(2,1)}) fusion(bf16[512,1024]{1,0:T(8,128)(2,1)S(1)} %copy-done.1, bf16[1,512,1024]{2,1,0:T(8,128)(2,1)S(1)} %copy-done.2, f32[512]{0:T(512)S(1)} %fusion.11, f32[512]{0:T(512)S(1)} %bitcast.29, f32[1024]{0:T(1024)S(1)} %copy-done.7), kind=kLoop, calls=%fused_computation.13 | loop fusion | flops 5242880 | bytes 4202496 | tf_op jit(solution)/shard_map/convert_element_type | solution.py:188
  65.3 21.5 %shard_map.103 = (bf16[512,1024]{1,0:T(8,128)(2,1)}, f32[3,512,128]{2,1,0:T(8,128)}, f32[3,512,128]{2,1,0:T(8,128)}) custom-call(s32[1]{0:T(128)S(6)} %copy.13.count_ref, bf16[512,1024]{1,0:T(8,128)(2,1)} %bitcast.21, bf16[3,512,128]{2,1,0:T(8,128)(2,1)} %get-tuple-element.24.k_ref, bf16[3,512,128]{2,1,0:T(8,128)(2,1)} %get-tuple-element.23.v_ref, ...), custom_call_target="tpu_custom_call" | custom-call | tf_op jit(solution)/shard_map/pallas_call | solution.py:121
  86.8 0.1 broadcast_in_dim.27.clone
  86.9 1.0 copy-done.6
  87.9 1.0 scatter_fusion
  88.9 0.9 slice.102
  89.8 3.6 %collective-permute-start.9 = (bf16[4,512,128]{2,1,0:T(8,128)(2,1)}, bf16[4,512,128]{2,1,0:T(8,128)(2,1)S(1)}, u32[]{:S(2)}, u32[]{:S(2)}) collective-permute-start(bf16[4,512,128]{2,1,0:T(8,128)(2,1)} %slice.102), channel_id=1, source_target_pairs={{0,8},{8,0},{16,24},{24,16},{32,40},{40,32},{48,56},{56,48},{64,72... | collective-permute-start | bytes 1572872 | tf_op jit(solution)/shard_map/ppermute | solution.py:140
  93.4 0.1 broadcast_in_dim.27.clone.1
  93.5 1.0 scatter_fusion.1
  94.5 0.1 slice.101
  94.6 0.8 collective-permute-start.12
  95.4 0.0 collective-permute-done.9
  95.4 1.3 %slice_add_fusion.1 = f32[4,512,128]{2,1,0:T(8,128)S(1)} fusion(f32[8,512,128]{2,1,0:T(8,128)} %copy-done, bf16[4,512,128]{2,1,0:T(8,128)(2,1)S(1)} %collective-permute-done.9), kind=kLoop, calls=%fused_computation.20 | loop fusion | flops 524288 | bytes 2621440 | tf_op jit(solution)/shard_map/add | solution.py:157
  96.7 1.2 %collective-permute-start.10 = (bf16[2,512,128]{2,1,0:T(8,128)(2,1)S(1)}, bf16[2,512,128]{2,1,0:T(8,128)(2,1)S(1)}, u32[]{:S(2)}, u32[]{:S(2)}) collective-permute-start(bf16[2,512,128]{2,1,0:T(8,128)(2,1)S(1)} %slice.104), channel_id=1, source_target_pairs={{0,16},{8,24},{16,0},{24,8},{32,48},{40,56},{48,32},{56,40},{64,80... | collective-permute-start | bytes 786440 | tf_op jit(solution)/shard_map/ppermute | solution.py:140
  97.9 0.0 collective-permute-done.12
  98.0 0.1 slice_add_fusion
  98.1 0.4 collective-permute-start.13
  98.5 6.1 %collective-permute-done.10 = bf16[2,512,128]{2,1,0:T(8,128)(2,1)S(1)} collective-permute-done((bf16[2,512,128]{2,1,0:T(8,128)(2,1)S(1)}, bf16[2,512,128]{2,1,0:T(8,128)(2,1)S(1)}, u32[]{:S(2)}, u32[]{:S(2)}) %collective-permute-start.10) | collective-permute-done | bytes 262176 | tf_op jit(solution)/shard_map/ppermute | solution.py:140
  104.7 2.5 %collective-permute-start.11 = (bf16[1,512,128]{2,1,0:T(8,128)(2,1)S(1)}, bf16[1,512,128]{2,1,0:T(8,128)(2,1)S(1)}, u32[]{:S(2)}, u32[]{:S(2)}) collective-permute-start(bf16[1,512,128]{2,1,0:T(8,128)(2,1)S(1)} %slice.106), channel_id=1, source_target_pairs={{0,32},{8,40},{16,48},{24,56},{32,0},{40,8},{48,16},{56,24},{64,96... | collective-permute-start | bytes 393224 | tf_op jit(solution)/shard_map/ppermute | solution.py:140
  107.1 3.1 %collective-permute-done.13 = bf16[2,512,128]{2,1,0:T(8,128)(2,1)S(1)} collective-permute-done((bf16[2,512,128]{2,1,0:T(8,128)(2,1)S(1)}, bf16[2,512,128]{2,1,0:T(8,128)(2,1)S(1)}, u32[]{:S(2)}, u32[]{:S(2)}) %collective-permute-start.13) | collective-permute-done | bytes 262176 | tf_op jit(solution)/shard_map/ppermute | solution.py:140
  110.3 2.5 %collective-permute-start.14 = (bf16[1,512,128]{2,1,0:T(8,128)(2,1)S(1)}, bf16[1,512,128]{2,1,0:T(8,128)(2,1)S(1)}, u32[]{:S(2)}, u32[]{:S(2)}) collective-permute-start(bf16[1,512,128]{2,1,0:T(8,128)(2,1)S(1)} %slice.105), channel_id=1, source_target_pairs={{0,32},{8,40},{16,48},{24,56},{32,0},{40,8},{48,16},{56,24},{64,96... | collective-permute-start | bytes 393224 | tf_op jit(solution)/shard_map/ppermute | solution.py:140
  112.8 2.1 %collective-permute-done.11 = bf16[1,512,128]{2,1,0:T(8,128)(2,1)S(1)} collective-permute-done((bf16[1,512,128]{2,1,0:T(8,128)(2,1)S(1)}, bf16[1,512,128]{2,1,0:T(8,128)(2,1)S(1)}, u32[]{:S(2)}, u32[]{:S(2)}) %collective-permute-start.11) | collective-permute-done | bytes 131104 | tf_op jit(solution)/shard_map/ppermute | solution.py:140
  114.9 0.7 fusion.9
  115.6 1.5 %collective-permute-done.14 = bf16[1,512,128]{2,1,0:T(8,128)(2,1)S(1)} collective-permute-done((bf16[1,512,128]{2,1,0:T(8,128)(2,1)S(1)}, bf16[1,512,128]{2,1,0:T(8,128)(2,1)S(1)}, u32[]{:S(2)}, u32[]{:S(2)}) %collective-permute-start.14) | collective-permute-done | bytes 131104 | tf_op jit(solution)/shard_map/ppermute | solution.py:140
  117.1 0.7 fusion.8
  (21 shorter events, 0.3 us)
Async XLA Ops:
  0.6 24.2 %copy-start.3 = (bf16[1,512,128]{2,1,0:T(8,128)(2,1)S(1)}, bf16[1,512,128]{2,1,0:T(8,128)(2,1)}, u32[]{:S(2)}) copy-start(bf16[1,512,128]{2,1,0:T(8,128)(2,1)} %param.10) | copy-start | bytes 393220
  0.6 21.6 %copy-start.4 = (bf16[1,512,128]{2,1,0:T(8,128)(2,1)S(1)}, bf16[1,512,128]{2,1,0:T(8,128)(2,1)}, u32[]{:S(2)}) copy-start(bf16[1,512,128]{2,1,0:T(8,128)(2,1)} %param.11) | copy-start | bytes 393220
  0.7 6.2 %collective-permute-start = (bf16[1,512,128]{2,1,0:T(8,128)(2,1)}, bf16[1,512,128]{2,1,0:T(8,128)(2,1)S(1)}, u32[]{:S(2)}, u32[]{:S(2)}) collective-permute-start(bf16[1,512,128]{2,1,0:T(8,128)(2,1)} %param.10), channel_id=1, source_target_pairs={{0,32},{8,40},{16,48},{24,56},{32,0},{40,8},{48,16},{56,24},{64,96... | collective-permute-start | bytes 393224 | tf_op jit(solution)/shard_map/ppermute | solution.py:140
  4.3 7.1 %collective-permute-start.3 = (bf16[1,512,128]{2,1,0:T(8,128)(2,1)}, bf16[1,512,128]{2,1,0:T(8,128)(2,1)S(1)}, u32[]{:S(2)}, u32[]{:S(2)}) collective-permute-start(bf16[1,512,128]{2,1,0:T(8,128)(2,1)} %param.11), channel_id=1, source_target_pairs={{0,32},{8,40},{16,48},{24,56},{32,0},{40,8},{48,16},{56,24},{64,96... | collective-permute-start | bytes 393224 | tf_op jit(solution)/shard_map/ppermute | solution.py:140
  7.8 6.4 %collective-permute-start.1 = (bf16[2,512,128]{2,1,0:T(8,128)(2,1)S(1)}, bf16[2,512,128]{2,1,0:T(8,128)(2,1)S(1)}, u32[]{:S(2)}, u32[]{:S(2)}) collective-permute-start(bf16[2,512,128]{2,1,0:T(8,128)(2,1)S(1)} %pad_maximum_fusion.4), channel_id=1, source_target_pairs={{0,16},{8,24},{16,0},{24,8},{32,48},{40,56},{48,32},{56,40},{64,80... | collective-permute-start | bytes 786440 | tf_op jit(solution)/shard_map/ppermute | solution.py:140
  12.3 9.9 %collective-permute-start.4 = (bf16[2,512,128]{2,1,0:T(8,128)(2,1)S(1)}, bf16[2,512,128]{2,1,0:T(8,128)(2,1)S(1)}, u32[]{:S(2)}, u32[]{:S(2)}) collective-permute-start(bf16[2,512,128]{2,1,0:T(8,128)(2,1)S(1)} %pad_maximum_fusion.5), channel_id=1, source_target_pairs={{0,16},{8,24},{16,0},{24,8},{32,48},{40,56},{48,32},{56,40},{64,80... | collective-permute-start | bytes 786440 | tf_op jit(solution)/shard_map/ppermute | solution.py:140
  15.2 9.6 %collective-permute-start.2 = (bf16[4,512,128]{2,1,0:T(8,128)(2,1)S(1)}, bf16[4,512,128]{2,1,0:T(8,128)(2,1)S(1)}, u32[]{:S(2)}, u32[]{:S(2)}) collective-permute-start(bf16[4,512,128]{2,1,0:T(8,128)(2,1)S(1)} %pad_maximum_fusion.2), channel_id=1, source_target_pairs={{0,8},{8,0},{16,24},{24,16},{32,40},{40,32},{48,56},{56,48},{64,72... | collective-permute-start | bytes 1572872 | tf_op jit(solution)/shard_map/ppermute | solution.py:140
  22.3 3.4 %collective-permute-start.5 = (bf16[4,512,128]{2,1,0:T(8,128)(2,1)S(1)}, bf16[4,512,128]{2,1,0:T(8,128)(2,1)S(1)}, u32[]{:S(2)}, u32[]{:S(2)}) collective-permute-start(bf16[4,512,128]{2,1,0:T(8,128)(2,1)S(1)} %pad_maximum_fusion.3), channel_id=1, source_target_pairs={{0,8},{8,0},{16,24},{24,16},{32,40},{40,32},{48,56},{56,48},{64,72... | collective-permute-start | bytes 1572872 | tf_op jit(solution)/shard_map/ppermute | solution.py:140
  25.8 22.0 %copy-start.2 = (bf16[1,512,1024]{2,1,0:T(8,128)(2,1)S(1)}, bf16[1,512,1024]{2,1,0:T(8,128)(2,1)}, u32[]{:S(2)}) copy-start(bf16[1,512,1024]{2,1,0:T(8,128)(2,1)} %param.15) | copy-start | bytes 3145732
  25.8 22.0 %copy-start.7 = (f32[1024]{0:T(1024)S(1)}, f32[1024]{0:T(1024)}, u32[]{:S(2)}) copy-start(f32[1024]{0:T(1024)} %param.14) | copy-start | bytes 12292
  47.8 15.5 %copy-start.1 = (bf16[512,1024]{1,0:T(8,128)(2,1)S(1)}, bf16[512,1024]{1,0:T(8,128)(2,1)}, u32[]{:S(2)}) copy-start(bf16[512,1024]{1,0:T(8,128)(2,1)} %get-tuple-element.10.att_ref) | copy-start | bytes 3145732
  49.7 2.5 %collective-permute-start.6 = (f32[2,512]{1,0:T(2,128)S(1)}, f32[2,512]{1,0:T(2,128)S(1)}, u32[]{:S(2)}, u32[]{:S(2)}) collective-permute-start(f32[2,512]{1,0:T(2,128)S(1)} %pad_maximum_fusion.6), channel_id=1, source_target_pairs={{0,1},{1,0},{2,3},{3,2},{4,5},{5,4},{6,7},{7,6},{8,9},{9,8},{10,11... | collective-permute-start | bytes 12296 | tf_op jit(solution)/shard_map/ppermute | solution.py:140
  52.2 3.6 %collective-permute-start.7 = (f32[2,512]{1,0:T(2,128)S(1)}, f32[2,512]{1,0:T(2,128)S(1)}, u32[]{:S(2)}, u32[]{:S(2)}) collective-permute-start(f32[2,512]{1,0:T(2,128)S(1)} %fusion.15), channel_id=1, source_target_pairs={{0,2},{1,3},{2,0},{3,1},{4,6},{5,7},{6,4},{7,5},{8,10},{9,11},{10,... | collective-permute-start | bytes 12296 | tf_op jit(solution)/shard_map/ppermute | solution.py:140
  55.9 7.4 %collective-permute-start.8 = (f32[2,512]{1,0:T(2,128)S(1)}, f32[2,512]{1,0:T(2,128)S(1)}, u32[]{:S(2)}, u32[]{:S(2)}) collective-permute-start(f32[2,512]{1,0:T(2,128)S(1)} %fusion.17), channel_id=1, source_target_pairs={{0,4},{1,5},{2,6},{3,7},{4,0},{5,1},{6,2},{7,3},{8,12},{9,13},{10,... | collective-permute-start | bytes 12296 | tf_op jit(solution)/shard_map/ppermute | solution.py:140
  86.8 1.1 copy-start.6
  88.9 4.4 %copy-start = (f32[8,512,128]{2,1,0:T(8,128)}, f32[8,512,128]{2,1,0:T(8,128)S(1)}, u32[]{:S(2)}) copy-start(f32[8,512,128]{2,1,0:T(8,128)S(1)} %scatter_fusion) | copy-start | bytes 6291460
  88.9 4.6 %copy-start.5 = (f32[3,512,128]{2,1,0:T(8,128)S(1)}, f32[3,512,128]{2,1,0:T(8,128)}, u32[]{:S(2)}) copy-start(f32[3,512,128]{2,1,0:T(8,128)} %get-tuple-element.14) | copy-start | bytes 2359300
  89.8 5.6 %collective-permute-start.9 = (bf16[4,512,128]{2,1,0:T(8,128)(2,1)}, bf16[4,512,128]{2,1,0:T(8,128)(2,1)S(1)}, u32[]{:S(2)}, u32[]{:S(2)}) collective-permute-start(bf16[4,512,128]{2,1,0:T(8,128)(2,1)} %slice.102), channel_id=1, source_target_pairs={{0,8},{8,0},{16,24},{24,16},{32,40},{40,32},{48,56},{56,48},{64,72... | collective-permute-start | bytes 1572872 | tf_op jit(solution)/shard_map/ppermute | solution.py:140
  94.6 3.3 %collective-permute-start.12 = (bf16[4,512,128]{2,1,0:T(8,128)(2,1)S(1)}, bf16[4,512,128]{2,1,0:T(8,128)(2,1)S(1)}, u32[]{:S(2)}, u32[]{:S(2)}) collective-permute-start(bf16[4,512,128]{2,1,0:T(8,128)(2,1)S(1)} %slice.101), channel_id=1, source_target_pairs={{0,8},{8,0},{16,24},{24,16},{32,40},{40,32},{48,56},{56,48},{64,72... | collective-permute-start | bytes 1572872 | tf_op jit(solution)/shard_map/ppermute | solution.py:140
  96.7 7.9 %collective-permute-start.10 = (bf16[2,512,128]{2,1,0:T(8,128)(2,1)S(1)}, bf16[2,512,128]{2,1,0:T(8,128)(2,1)S(1)}, u32[]{:S(2)}, u32[]{:S(2)}) collective-permute-start(bf16[2,512,128]{2,1,0:T(8,128)(2,1)S(1)} %slice.104), channel_id=1, source_target_pairs={{0,16},{8,24},{16,0},{24,8},{32,48},{40,56},{48,32},{56,40},{64,80... | collective-permute-start | bytes 786440 | tf_op jit(solution)/shard_map/ppermute | solution.py:140
  98.1 12.1 %collective-permute-start.13 = (bf16[2,512,128]{2,1,0:T(8,128)(2,1)S(1)}, bf16[2,512,128]{2,1,0:T(8,128)(2,1)S(1)}, u32[]{:S(2)}, u32[]{:S(2)}) collective-permute-start(bf16[2,512,128]{2,1,0:T(8,128)(2,1)S(1)} %slice.103), channel_id=1, source_target_pairs={{0,16},{8,24},{16,0},{24,8},{32,48},{40,56},{48,32},{56,40},{64,80... | collective-permute-start | bytes 786440 | tf_op jit(solution)/shard_map/ppermute | solution.py:140
  104.7 10.2 %collective-permute-start.11 = (bf16[1,512,128]{2,1,0:T(8,128)(2,1)S(1)}, bf16[1,512,128]{2,1,0:T(8,128)(2,1)S(1)}, u32[]{:S(2)}, u32[]{:S(2)}) collective-permute-start(bf16[1,512,128]{2,1,0:T(8,128)(2,1)S(1)} %slice.106), channel_id=1, source_target_pairs={{0,32},{8,40},{16,48},{24,56},{32,0},{40,8},{48,16},{56,24},{64,96... | collective-permute-start | bytes 393224 | tf_op jit(solution)/shard_map/ppermute | solution.py:140
  110.3 6.8 %collective-permute-start.14 = (bf16[1,512,128]{2,1,0:T(8,128)(2,1)S(1)}, bf16[1,512,128]{2,1,0:T(8,128)(2,1)S(1)}, u32[]{:S(2)}, u32[]{:S(2)}) collective-permute-start(bf16[1,512,128]{2,1,0:T(8,128)(2,1)S(1)} %slice.105), channel_id=1, source_target_pairs={{0,32},{8,40},{16,48},{24,56},{32,0},{40,8},{48,16},{56,24},{64,96... | collective-permute-start | bytes 393224 | tf_op jit(solution)/shard_map/ppermute | solution.py:140

commit v11 on v10

--- a/solution.py
+++ b/solution.py
@@ -144,10 +144,37 @@
     return ((distance & 1) << 2) | (distance & 2) | ((distance >> 2) & 1)
 
 
-def gather_group(block):
-    for bit in reversed(range(GROUP.bit_length() - 1)):
-        block = jnp.concatenate([block, exchange(block, "resp", bit)], 0)
-    return block
+def ring_route(move):
+    route = []
+    for low in range(lax.axis_size("resp")):
+        place = low % GROUP
+        chip, core = divmod(place, 2)
+        to_chip, to_core = move(chip, core)
+        route.append((low, low - place + (to_chip % (GROUP // 2)) * 2 + to_core))
+    return route
+
+
+RING_ROWS = (0, 1, 3, 5, 6, 7, 2, 4)
+
+
+def ring_row(partner, my_index):
+    chip_step = ((partner >> 1) - (my_index >> 1)) % (GROUP // 2)
+    return jnp.asarray(RING_ROWS, jnp.int32)[chip_step * 2 + ((partner ^ my_index) & 1)]
+
+
+def gather_group(block, my_index):
+    from_minus = lax.ppermute(block, "resp", ring_route(lambda x, c: (x + 1, c)))
+    from_plus = lax.ppermute(block, "resp", ring_route(lambda x, c: (x - 1, c)))
+    from_core = lax.ppermute(block, "resp", ring_route(lambda x, c: (x, 1 - c)))
+    relay = jnp.where(my_index % 2 == 0, from_plus, from_minus)
+    far = lax.ppermute(relay, "resp", ring_route(lambda x, c: (x - 1, c) if c == 0 else (x + 1, c)))
+    core_sides = lax.ppermute(
+        jnp.concatenate([from_minus, from_plus], 0), "resp", ring_route(lambda x, c: (x, 1 - c))
+    )
+    far_other = lax.ppermute(far, "resp", ring_route(lambda x, c: (x, 1 - c)))
+    return jnp.concatenate(
+        [block, from_core, from_minus, from_plus, core_sides, far, far_other], 0
+    )
 
 
 def return_group(terms):
@@ -169,8 +196,9 @@
     seq_len = queries.shape[1]
     mate_rows = bit_reversed(jnp.bitwise_xor(partners[0], my_index))
     count = counts.astype(jnp.int32)
-    mate_keys = jnp.take(gather_group(key_states), mate_rows, axis=0)
-    mate_values = jnp.take(gather_group(value_states), mate_rows, axis=0)
+    ring_rows = ring_row(partners[0], my_index)
+    mate_keys = jnp.take(gather_group(key_states, my_index), ring_rows, axis=0)
+    mate_values = jnp.take(gather_group(value_states, my_index), ring_rows, axis=0)
 
     attention, log_total = attention_forward(count, queries[0], mate_keys, mate_values)
     attention_flat = attention.astype(jnp.float32)

time: 118 us -> 116 us (0.983)
  starting transfers between devices: 36.2 us -> 28.8 us
  waiting for transfers between devices: 21 us -> 25.3 us
  local copies, waits for them, and re-layouts: 3.58 us -> 6.93 us
  other arithmetic: 13.6 us -> 10.7 us
    ppermute x15 -> x9, starting transfers between devices: 36.2 us -> 17.7 us  [exchange(): return lax.ppermute(block, axis, route)]
    ppermute x0 -> x12, starting transfers between devices: none -> 11.1 us  [the longest x2 5.53 us: gather_group(): from_plus = lax.ppermute(block, 'resp', ring_route(lambda x, c: (x - 1, c)))]
    ppermute x0 -> x12, waiting for transfers between devices: none -> 6.38 us  [the longest x2 5.92 us: gather_group(): lax.ppermute(relay, 'resp', ring_route(lambda x, c: (x - 1, c) if c == 0...]
    concatenate x6 -> x2, other arithmetic: 3.08 us -> 0.05 us  [gather_group(): jnp.concatenate([from_minus, from_plus], 0)]
    ppermute x15 -> x9, waiting for transfers between devices: 21 us -> 18.9 us  [exchange(): return lax.ppermute(block, axis, route)]
    unnamed x16 -> x22, local copies, waits for them, and re-layouts: 1.03 us -> 3.03 us
    gather x2 -> x3, local copies, waits for them, and re-layouts: 1.24 us -> 2.54 us  [the longest x1 1.3 us: ring_row(): jnp.asarray(RING_ROWS, jnp.int32)]
  transfers between devices with their start and end apart: 15 -> 21, of which waited for: 11 -> 11; matrix products, arithmetic and copies ran while one was open for 7% -> 7% of each run, Pallas kernels for 0% -> 0%
where the time goes in v11:
time: 116 us; the launch traced here: 115 us
  Pallas kernels  41.8 us (36%)
  starting transfers between devices  28.8 us (25%)
  waiting for transfers between devices  25.3 us (22%)
  other arithmetic  10.7 us (9%)
  local copies, waits for them, and re-layouts  6.93 us (6%)
  between operations  1.63 us (1%)
    pallas_call x1, Pallas kernels, attention_backward(): pl.pallas_call(backward_kernel, grid_spec=pltpu.PrefetchScalarGridSpec(nu...  21.5 us
    pallas_call x1, Pallas kernels, attention_forward(): pl.pallas_call(forward_kernel, grid_spec=pltpu.PrefetchScalarGridSpec(num...  20.3 us
    ppermute x9, waiting for transfers between devices, exchange(): return lax.ppermute(block, axis, route)  18.9 us
    ppermute x9, starting transfers between devices, exchange(): return lax.ppermute(block, axis, route)  17.7 us
    ppermute x2, waiting for transfers between devices, gather_group(): lax.ppermute(relay, 'resp', ring_route(lambda x, c: (x - 1, c) if c == 0...  5.92 us
    ppermute x2, starting transfers between devices, gather_group(): from_plus = lax.ppermute(block, 'resp', ring_route(lambda x, c: (x - 1, c)))  5.53 us
    unnamed x22, local copies, waits for them, and re-layouts  3.03 us
  transfers between devices with their start and end apart: 21, of which 11 were waited for; matrix products, arithmetic and copies ran while one was open for 7% of the time, Pallas kernels for 0%

profile of v11, /device:TPU:1, one launch (start us, length us, event | category | flops | bytes accessed | tf_op | source)
XLA Modules:
  0.0 115.2 jit_solution(16541959637879349872)
XLA Ops:
  0.6 2.1 %collective-permute-start.1 = (bf16[1,512,128]{2,1,0:T(8,128)(2,1)}, bf16[1,512,128]{2,1,0:T(8,128)(2,1)S(1)}, u32[]{:S(2)}, u32[]{:S(2)}) collective-permute-start(bf16[1,512,128]{2,1,0:T(8,128)(2,1)} %param.11), channel_id=1, source_target_pairs={{0,16},{8,24},{16,32},{24,40},{32,48},{40,56},{48,0},{56,8},{64,80... | collective-permute-start | bytes 393224 | tf_op jit(solution)/shard_map/ppermute | solution.py:166
  2.7 1.3 %collective-permute-start = (bf16[1,512,128]{2,1,0:T(8,128)(2,1)}, bf16[1,512,128]{2,1,0:T(8,128)(2,1)S(1)}, u32[]{:S(2)}, u32[]{:S(2)}) collective-permute-start(bf16[1,512,128]{2,1,0:T(8,128)(2,1)} %param.11), channel_id=1, source_target_pairs={{0,8},{8,0},{16,24},{24,16},{32,40},{40,32},{48,56},{56,48},{64,72... | collective-permute-start | bytes 393224 | tf_op jit(solution)/shard_map/ppermute | solution.py:168
  4.1 2.9 %collective-permute-start.2 = (bf16[1,512,128]{2,1,0:T(8,128)(2,1)}, bf16[1,512,128]{2,1,0:T(8,128)(2,1)S(1)}, u32[]{:S(2)}, u32[]{:S(2)}) collective-permute-start(bf16[1,512,128]{2,1,0:T(8,128)(2,1)} %param.11), channel_id=1, source_target_pairs={{0,48},{8,56},{16,0},{24,8},{32,16},{40,24},{48,32},{56,40},{64,11... | collective-permute-start | bytes 393224 | tf_op jit(solution)/shard_map/ppermute | solution.py:167
  6.9 0.0 collective-permute-start.7
  6.9 2.7 %collective-permute-start.8 = (bf16[1,512,128]{2,1,0:T(8,128)(2,1)}, bf16[1,512,128]{2,1,0:T(8,128)(2,1)S(1)}, u32[]{:S(2)}, u32[]{:S(2)}) collective-permute-start(bf16[1,512,128]{2,1,0:T(8,128)(2,1)} %param.12), channel_id=1, source_target_pairs={{0,48},{8,56},{16,0},{24,8},{32,16},{40,24},{48,32},{56,40},{64,11... | collective-permute-start | bytes 393224 | tf_op jit(solution)/shard_map/ppermute | solution.py:167
  9.6 0.7 fusion.18
  10.3 1.3 %gather_fusion = s32[3]{0:T(128)S(1)} fusion(s32[8]{0:T(128)} %constant.63.clone, s32[1024]{0:T(1024)S(1)} %pad_clamp_fusion.1), kind=kCustom, calls=%fused_computation.2 | custom fusion | bytes 36 | tf_op jit(solution)/shard_map/gather | solution.py:162
  11.6 0.9 constant_dynamic-update-slice_fusion.6
  12.5 0.9 constant_dynamic-update-slice_fusion.13
  14.1 0.9 collective-permute-start.6
  15.0 0.0 collective-permute-done.2
  15.1 0.1 collective-permute-start.3
  15.2 0.0 collective-permute-done.7
  15.2 0.0 collective-permute-done.8
  15.2 0.6 collective-permute-start.9
  15.8 0.0 collective-permute-done
  15.8 0.1 broadcast_select_fusion.3
  15.9 0.1 collective-permute-start.4
  16.0 0.3 collective-permute-done.6
  16.2 0.1 broadcast_select_fusion.2
  16.3 0.1 collective-permute-start.10
  16.4 4.5 %collective-permute-done.4 = bf16[1,512,128]{2,1,0:T(8,128)(2,1)S(1)} collective-permute-done((bf16[1,512,128]{2,1,0:T(8,128)(2,1)S(1)}, bf16[1,512,128]{2,1,0:T(8,128)(2,1)S(1)}, u32[]{:S(2)}, u32[]{:S(2)}) %collective-permute-start.4) | collective-permute-done | bytes 131104 | tf_op jit(solution)/shard_map/ppermute | solution.py:170
  21.0 0.0 collective-permute-start.5
  21.0 1.4 %collective-permute-done.10 = bf16[1,512,128]{2,1,0:T(8,128)(2,1)S(1)} collective-permute-done((bf16[1,512,128]{2,1,0:T(8,128)(2,1)S(1)}, bf16[1,512,128]{2,1,0:T(8,128)(2,1)S(1)}, u32[]{:S(2)}, u32[]{:S(2)}) %collective-permute-start.10) | collective-permute-done | bytes 131104 | tf_op jit(solution)/shard_map/ppermute | solution.py:170
  22.4 0.4 collective-permute-start.11
  22.8 0.0 collective-permute-done.3
  22.8 0.0 collective-permute-done.9
  22.9 0.6 gather_fusion.1
  23.6 0.2 collective-permute-done.11
  23.8 0.0 copy-start.2
  23.8 0.0 copy-start.5
  23.8 0.6 gather_fusion.2
  24.4 1.0 broadcast_select_fusion
  25.5 20.3 %shard_map.111 = (bf16[512,1024]{1,0:T(8,128)(2,1)}, f32[8,1,512]{2,1,0:T(1,128)}) custom-call(s32[1]{0:T(128)S(6)} %copy.26.count_ref, bf16[512,1024]{1,0:T(8,128)(2,1)} %bitcast.35, bf16[3,512,128]{2,1,0:T(8,128)(2,1)} %get-tuple-element.28.k_ref, bf16[3,512,128]{2,1,0:T(8,128)(2,1)} %get-tuple-element.27.v_ref), custom_call_target="tpu_custom_call" | custom-call | tf_op jit(solution)/shard_map/pallas_call | solution.py:100
  45.8 1.9 %fusion = (f32[512]{0:T(512)S(1)}, f32[512]{0:T(512)S(1)}) fusion(bf16[512,1024]{1,0:T(8,128)(2,1)} %get-tuple-element.10.att_ref, f32[1024]{0:T(1024)S(1)} %copy-done.5, bf16[1,512,1024]{2,1,0:T(8,128)(2,1)S(1)} %copy-done.2), kind=kLoop, calls=%fused_computation.9 | loop fusion | flops 3668992 | bytes 2105344 | tf_op jit(solution)/shard_map/reduce_sum | solution.py:207
  47.7 0.1 collective-permute-start.12
  47.8 2.4 %collective-permute-done.12 = f32[2,512]{1,0:T(2,128)S(1)} collective-permute-done((f32[2,512]{1,0:T(2,128)S(1)}, f32[2,512]{1,0:T(2,128)S(1)}, u32[]{:S(2)}, u32[]{:S(2)}) %collective-permute-start.12) | collective-permute-done | bytes 4128 | tf_op jit(solution)/shard_map/ppermute | solution.py:140
  50.3 1.7 %collective-permute-start.13 = (f32[2,512]{1,0:T(2,128)S(1)}, f32[2,512]{1,0:T(2,128)S(1)}, u32[]{:S(2)}, u32[]{:S(2)}) collective-permute-start(f32[2,512]{1,0:T(2,128)S(1)} %fusion.19), channel_id=1, source_target_pairs={{0,2},{1,3},{2,0},{3,1},{4,6},{5,7},{6,4},{7,5},{8,10},{9,11},{10,... | collective-permute-start | bytes 12296 | tf_op jit(solution)/shard_map/ppermute | solution.py:140
  52.0 1.9 %collective-permute-done.13 = f32[2,512]{1,0:T(2,128)S(1)} collective-permute-done((f32[2,512]{1,0:T(2,128)S(1)}, f32[2,512]{1,0:T(2,128)S(1)}, u32[]{:S(2)}, u32[]{:S(2)}) %collective-permute-start.13) | collective-permute-done | bytes 4128 | tf_op jit(solution)/shard_map/ppermute | solution.py:140
  53.9 5.3 %collective-permute-start.14 = (f32[2,512]{1,0:T(2,128)S(1)}, f32[2,512]{1,0:T(2,128)S(1)}, u32[]{:S(2)}, u32[]{:S(2)}) collective-permute-start(f32[2,512]{1,0:T(2,128)S(1)} %fusion.21), channel_id=1, source_target_pairs={{0,4},{1,5},{2,6},{3,7},{4,0},{5,1},{6,2},{7,3},{8,12},{9,13},{10,... | collective-permute-start | bytes 12296 | tf_op jit(solution)/shard_map/ppermute | solution.py:140
  59.2 1.2 %collective-permute-done.14 = f32[2,512]{1,0:T(2,128)S(1)} collective-permute-done((f32[2,512]{1,0:T(2,128)S(1)}, f32[2,512]{1,0:T(2,128)S(1)}, u32[]{:S(2)}, u32[]{:S(2)}) %collective-permute-start.14) | collective-permute-done | bytes 4128 | tf_op jit(solution)/shard_map/ppermute | solution.py:140
  60.4 2.0 %fusion.5 = (bf16[512,1024]{1,0:T(8,128)(2,1)}, bf16[1,512,1024]{2,1,0:T(8,128)(2,1)}) fusion(bf16[512,1024]{1,0:T(8,128)(2,1)S(1)} %copy-done.1, bf16[1,512,1024]{2,1,0:T(8,128)(2,1)S(1)} %copy-done.2, f32[512]{0:T(512)S(1)} %fusion.11, f32[512]{0:T(512)S(1)} %bitcast.44, f32[1024]{0:T(1024)S(1)} %copy-done.5), kind=kLoop, calls=%fused_computation.14 | loop fusion | flops 5242880 | bytes 4202496 | tf_op jit(solution)/shard_map/convert_element_type | solution.py:216
  62.4 21.5 %shard_map.112 = (bf16[512,1024]{1,0:T(8,128)(2,1)}, f32[3,512,128]{2,1,0:T(8,128)}, f32[3,512,128]{2,1,0:T(8,128)}) custom-call(s32[1]{0:T(128)S(6)} %copy.26.count_ref, bf16[512,1024]{1,0:T(8,128)(2,1)} %bitcast.36, bf16[3,512,128]{2,1,0:T(8,128)(2,1)} %get-tuple-element.28.k_ref, bf16[3,512,128]{2,1,0:T(8,128)(2,1)} %get-tuple-element.27.v_ref, ...), custom_call_target="tpu_custom_call" | custom-call | tf_op jit(solution)/shard_map/pallas_call | solution.py:121
  83.9 0.1 broadcast_in_dim.28.clone
  84.0 1.0 copy-done.4
  85.0 1.0 scatter_fusion
  86.1 0.9 slice.104
  86.9 3.8 %collective-permute-start.15 = (bf16[4,512,128]{2,1,0:T(8,128)(2,1)}, bf16[4,512,128]{2,1,0:T(8,128)(2,1)S(1)}, u32[]{:S(2)}, u32[]{:S(2)}) collective-permute-start(bf16[4,512,128]{2,1,0:T(8,128)(2,1)} %slice.104), channel_id=1, source_target_pairs={{0,8},{8,0},{16,24},{24,16},{32,40},{40,32},{48,56},{56,48},{64,72... | collective-permute-start | bytes 1572872 | tf_op jit(solution)/shard_map/ppermute | solution.py:140
  90.8 0.1 broadcast_in_dim.28.clone.1
  90.9 1.0 scatter_fusion.1
  91.9 0.1 slice.103
  92.0 0.8 collective-permute-start.18
  92.7 1.3 %slice_add_fusion.1 = f32[4,512,128]{2,1,0:T(8,128)S(1)} fusion(f32[8,512,128]{2,1,0:T(8,128)} %copy-done, bf16[4,512,128]{2,1,0:T(8,128)(2,1)S(1)} %collective-permute-done.15), kind=kLoop, calls=%fused_computation.21 | loop fusion | flops 524288 | bytes 2621440 | tf_op jit(solution)/shard_map/add | solution.py:184
  94.1 0.2 collective-permute-start.16
  94.3 0.1 slice_add_fusion
  94.4 1.5 %collective-permute-start.19 = (bf16[2,512,128]{2,1,0:T(8,128)(2,1)S(1)}, bf16[2,512,128]{2,1,0:T(8,128)(2,1)S(1)}, u32[]{:S(2)}, u32[]{:S(2)}) collective-permute-start(bf16[2,512,128]{2,1,0:T(8,128)(2,1)S(1)} %slice.105), channel_id=1, source_target_pairs={{0,16},{8,24},{16,0},{24,8},{32,48},{40,56},{48,32},{56,40},{64,80... | collective-permute-start | bytes 786440 | tf_op jit(solution)/shard_map/ppermute | solution.py:140
  95.9 6.1 %collective-permute-done.16 = bf16[2,512,128]{2,1,0:T(8,128)(2,1)S(1)} collective-permute-done((bf16[2,512,128]{2,1,0:T(8,128)(2,1)S(1)}, bf16[2,512,128]{2,1,0:T(8,128)(2,1)S(1)}, u32[]{:S(2)}, u32[]{:S(2)}) %collective-permute-start.16) | collective-permute-done | bytes 262176 | tf_op jit(solution)/shard_map/ppermute | solution.py:140
  102.0 2.2 %collective-permute-start.17 = (bf16[1,512,128]{2,1,0:T(8,128)(2,1)S(1)}, bf16[1,512,128]{2,1,0:T(8,128)(2,1)S(1)}, u32[]{:S(2)}, u32[]{:S(2)}) collective-permute-start(bf16[1,512,128]{2,1,0:T(8,128)(2,1)S(1)} %slice.108), channel_id=1, source_target_pairs={{0,32},{8,40},{16,48},{24,56},{32,0},{40,8},{48,16},{56,24},{64,96... | collective-permute-start | bytes 393224 | tf_op jit(solution)/shard_map/ppermute | solution.py:140
  104.3 3.3 %collective-permute-done.19 = bf16[2,512,128]{2,1,0:T(8,128)(2,1)S(1)} collective-permute-done((bf16[2,512,128]{2,1,0:T(8,128)(2,1)S(1)}, bf16[2,512,128]{2,1,0:T(8,128)(2,1)S(1)}, u32[]{:S(2)}, u32[]{:S(2)}) %collective-permute-start.19) | collective-permute-done | bytes 262176 | tf_op jit(solution)/shard_map/ppermute | solution.py:140
  107.7 2.2 %collective-permute-start.20 = (bf16[1,512,128]{2,1,0:T(8,128)(2,1)S(1)}, bf16[1,512,128]{2,1,0:T(8,128)(2,1)S(1)}, u32[]{:S(2)}, u32[]{:S(2)}) collective-permute-start(bf16[1,512,128]{2,1,0:T(8,128)(2,1)S(1)} %slice.107), channel_id=1, source_target_pairs={{0,32},{8,40},{16,48},{24,56},{32,0},{40,8},{48,16},{56,24},{64,96... | collective-permute-start | bytes 393224 | tf_op jit(solution)/shard_map/ppermute | solution.py:140
  109.9 2.4 %collective-permute-done.17 = bf16[1,512,128]{2,1,0:T(8,128)(2,1)S(1)} collective-permute-done((bf16[1,512,128]{2,1,0:T(8,128)(2,1)S(1)}, bf16[1,512,128]{2,1,0:T(8,128)(2,1)S(1)}, u32[]{:S(2)}, u32[]{:S(2)}) %collective-permute-start.17) | collective-permute-done | bytes 131104 | tf_op jit(solution)/shard_map/ppermute | solution.py:140
  112.3 0.7 fusion.9
  113.0 1.5 %collective-permute-done.20 = bf16[1,512,128]{2,1,0:T(8,128)(2,1)S(1)} collective-permute-done((bf16[1,512,128]{2,1,0:T(8,128)(2,1)S(1)}, bf16[1,512,128]{2,1,0:T(8,128)(2,1)S(1)}, u32[]{:S(2)}, u32[]{:S(2)}) %collective-permute-start.20) | collective-permute-done | bytes 131104 | tf_op jit(solution)/shard_map/ppermute | solution.py:140
  114.5 0.7 fusion.8
  (41 shorter events, 0.6 us)
Async XLA Ops:
  0.6 13.5 %collective-permute-start.1 = (bf16[1,512,128]{2,1,0:T(8,128)(2,1)}, bf16[1,512,128]{2,1,0:T(8,128)(2,1)S(1)}, u32[]{:S(2)}, u32[]{:S(2)}) collective-permute-start(bf16[1,512,128]{2,1,0:T(8,128)(2,1)} %param.11), channel_id=1, source_target_pairs={{0,16},{8,24},{16,32},{24,40},{32,48},{40,56},{48,0},{56,8},{64,80... | collective-permute-start | bytes 393224 | tf_op jit(solution)/shard_map/ppermute | solution.py:166
  2.7 13.0 %collective-permute-start = (bf16[1,512,128]{2,1,0:T(8,128)(2,1)}, bf16[1,512,128]{2,1,0:T(8,128)(2,1)S(1)}, u32[]{:S(2)}, u32[]{:S(2)}) collective-permute-start(bf16[1,512,128]{2,1,0:T(8,128)(2,1)} %param.11), channel_id=1, source_target_pairs={{0,8},{8,0},{16,24},{24,16},{32,40},{40,32},{48,56},{56,48},{64,72... | collective-permute-start | bytes 393224 | tf_op jit(solution)/shard_map/ppermute | solution.py:168
  4.1 11.0 %collective-permute-start.2 = (bf16[1,512,128]{2,1,0:T(8,128)(2,1)}, bf16[1,512,128]{2,1,0:T(8,128)(2,1)S(1)}, u32[]{:S(2)}, u32[]{:S(2)}) collective-permute-start(bf16[1,512,128]{2,1,0:T(8,128)(2,1)} %param.11), channel_id=1, source_target_pairs={{0,48},{8,56},{16,0},{24,8},{32,16},{40,24},{48,32},{56,40},{64,11... | collective-permute-start | bytes 393224 | tf_op jit(solution)/shard_map/ppermute | solution.py:167
  6.9 8.3 %collective-permute-start.7 = (bf16[1,512,128]{2,1,0:T(8,128)(2,1)}, bf16[1,512,128]{2,1,0:T(8,128)(2,1)S(1)}, u32[]{:S(2)}, u32[]{:S(2)}) collective-permute-start(bf16[1,512,128]{2,1,0:T(8,128)(2,1)} %param.12), channel_id=1, source_target_pairs={{0,16},{8,24},{16,32},{24,40},{32,48},{40,56},{48,0},{56,8},{64,80... | collective-permute-start | bytes 393224 | tf_op jit(solution)/shard_map/ppermute | solution.py:166
  6.9 8.3 %collective-permute-start.8 = (bf16[1,512,128]{2,1,0:T(8,128)(2,1)}, bf16[1,512,128]{2,1,0:T(8,128)(2,1)S(1)}, u32[]{:S(2)}, u32[]{:S(2)}) collective-permute-start(bf16[1,512,128]{2,1,0:T(8,128)(2,1)} %param.12), channel_id=1, source_target_pairs={{0,48},{8,56},{16,0},{24,8},{32,16},{40,24},{48,32},{56,40},{64,11... | collective-permute-start | bytes 393224 | tf_op jit(solution)/shard_map/ppermute | solution.py:167
  14.1 2.1 %collective-permute-start.6 = (bf16[1,512,128]{2,1,0:T(8,128)(2,1)}, bf16[1,512,128]{2,1,0:T(8,128)(2,1)S(1)}, u32[]{:S(2)}, u32[]{:S(2)}) collective-permute-start(bf16[1,512,128]{2,1,0:T(8,128)(2,1)} %param.12), channel_id=1, source_target_pairs={{0,8},{8,0},{16,24},{24,16},{32,40},{40,32},{48,56},{56,48},{64,72... | collective-permute-start | bytes 393224 | tf_op jit(solution)/shard_map/ppermute | solution.py:168
  15.1 7.7 %collective-permute-start.3 = (bf16[2,512,128]{2,1,0:T(8,128)(2,1)S(1)}, bf16[2,512,128]{2,1,0:T(8,128)(2,1)S(1)}, u32[]{:S(2)}, u32[]{:S(2)}) collective-permute-start(bf16[2,512,128]{2,1,0:T(8,128)(2,1)S(1)} %pad_maximum_fusion), channel_id=1, source_target_pairs={{0,8},{8,0},{16,24},{24,16},{32,40},{40,32},{48,56},{56,48},{64,72... | collective-permute-start | bytes 786440 | tf_op jit(solution)/shard_map/ppermute | solution.py:171
  15.2 7.6 %collective-permute-start.9 = (bf16[2,512,128]{2,1,0:T(8,128)(2,1)S(1)}, bf16[2,512,128]{2,1,0:T(8,128)(2,1)S(1)}, u32[]{:S(2)}, u32[]{:S(2)}) collective-permute-start(bf16[2,512,128]{2,1,0:T(8,128)(2,1)S(1)} %pad_maximum_fusion.1), channel_id=1, source_target_pairs={{0,8},{8,0},{16,24},{24,16},{32,40},{40,32},{48,56},{56,48},{64,72... | collective-permute-start | bytes 786440 | tf_op jit(solution)/shard_map/ppermute | solution.py:171
  15.9 5.1 %collective-permute-start.4 = (bf16[1,512,128]{2,1,0:T(8,128)(2,1)S(1)}, bf16[1,512,128]{2,1,0:T(8,128)(2,1)S(1)}, u32[]{:S(2)}, u32[]{:S(2)}) collective-permute-start(bf16[1,512,128]{2,1,0:T(8,128)(2,1)S(1)} %get-tuple-element.21), channel_id=1, source_target_pairs={{0,48},{8,24},{16,0},{24,40},{32,16},{40,56},{48,32},{56,8},{64,11... | collective-permute-start | bytes 393224 | tf_op jit(solution)/shard_map/ppermute | solution.py:170
  16.3 6.1 %collective-permute-start.10 = (bf16[1,512,128]{2,1,0:T(8,128)(2,1)S(1)}, bf16[1,512,128]{2,1,0:T(8,128)(2,1)S(1)}, u32[]{:S(2)}, u32[]{:S(2)}) collective-permute-start(bf16[1,512,128]{2,1,0:T(8,128)(2,1)S(1)} %get-tuple-element.19), channel_id=1, source_target_pairs={{0,48},{8,24},{16,0},{24,40},{32,16},{40,56},{48,32},{56,8},{64,11... | collective-permute-start | bytes 393224 | tf_op jit(solution)/shard_map/ppermute | solution.py:170
  21.0 1.9 %collective-permute-start.5 = (bf16[1,512,128]{2,1,0:T(8,128)(2,1)S(1)}, bf16[1,512,128]{2,1,0:T(8,128)(2,1)S(1)}, u32[]{:S(2)}, u32[]{:S(2)}) collective-permute-start(bf16[1,512,128]{2,1,0:T(8,128)(2,1)S(1)} %collective-permute-done.4), channel_id=1, source_target_pairs={{0,8},{8,0},{16,24},{24,16},{32,40},{40,32},{48,56},{56,48},{64,72... | collective-permute-start | bytes 393224 | tf_op jit(solution)/shard_map/ppermute | solution.py:174
  22.4 1.4 %collective-permute-start.11 = (bf16[1,512,128]{2,1,0:T(8,128)(2,1)S(1)}, bf16[1,512,128]{2,1,0:T(8,128)(2,1)S(1)}, u32[]{:S(2)}, u32[]{:S(2)}) collective-permute-start(bf16[1,512,128]{2,1,0:T(8,128)(2,1)S(1)} %collective-permute-done.10), channel_id=1, source_target_pairs={{0,8},{8,0},{16,24},{24,16},{32,40},{40,32},{48,56},{56,48},{64,72... | collective-permute-start | bytes 393224 | tf_op jit(solution)/shard_map/ppermute | solution.py:174
  23.8 22.0 %copy-start.2 = (bf16[1,512,1024]{2,1,0:T(8,128)(2,1)S(1)}, bf16[1,512,1024]{2,1,0:T(8,128)(2,1)}, u32[]{:S(2)}) copy-start(bf16[1,512,1024]{2,1,0:T(8,128)(2,1)} %param.16) | copy-start | bytes 3145732
  23.8 22.0 %copy-start.5 = (f32[1024]{0:T(1024)S(1)}, f32[1024]{0:T(1024)}, u32[]{:S(2)}) copy-start(f32[1024]{0:T(1024)} %param.15) | copy-start | bytes 12292
  45.8 14.6 %copy-start.1 = (bf16[512,1024]{1,0:T(8,128)(2,1)S(1)}, bf16[512,1024]{1,0:T(8,128)(2,1)}, u32[]{:S(2)}) copy-start(bf16[512,1024]{1,0:T(8,128)(2,1)} %get-tuple-element.10.att_ref) | copy-start | bytes 3145732
  47.7 2.5 %collective-permute-start.12 = (f32[2,512]{1,0:T(2,128)S(1)}, f32[2,512]{1,0:T(2,128)S(1)}, u32[]{:S(2)}, u32[]{:S(2)}) collective-permute-start(f32[2,512]{1,0:T(2,128)S(1)} %pad_maximum_fusion.2), channel_id=1, source_target_pairs={{0,1},{1,0},{2,3},{3,2},{4,5},{5,4},{6,7},{7,6},{8,9},{9,8},{10,11... | collective-permute-start | bytes 12296 | tf_op jit(solution)/shard_map/ppermute | solution.py:140
  50.3 3.6 %collective-permute-start.13 = (f32[2,512]{1,0:T(2,128)S(1)}, f32[2,512]{1,0:T(2,128)S(1)}, u32[]{:S(2)}, u32[]{:S(2)}) collective-permute-start(f32[2,512]{1,0:T(2,128)S(1)} %fusion.19), channel_id=1, source_target_pairs={{0,2},{1,3},{2,0},{3,1},{4,6},{5,7},{6,4},{7,5},{8,10},{9,11},{10,... | collective-permute-start | bytes 12296 | tf_op jit(solution)/shard_map/ppermute | solution.py:140
  53.9 6.5 %collective-permute-start.14 = (f32[2,512]{1,0:T(2,128)S(1)}, f32[2,512]{1,0:T(2,128)S(1)}, u32[]{:S(2)}, u32[]{:S(2)}) collective-permute-start(f32[2,512]{1,0:T(2,128)S(1)} %fusion.21), channel_id=1, source_target_pairs={{0,4},{1,5},{2,6},{3,7},{4,0},{5,1},{6,2},{7,3},{8,12},{9,13},{10,... | collective-permute-start | bytes 12296 | tf_op jit(solution)/shard_map/ppermute | solution.py:140
  83.9 1.1 copy-start.4
  86.0 4.7 %copy-start = (f32[8,512,128]{2,1,0:T(8,128)}, f32[8,512,128]{2,1,0:T(8,128)S(1)}, u32[]{:S(2)}) copy-start(f32[8,512,128]{2,1,0:T(8,128)S(1)} %scatter_fusion) | copy-start | bytes 6291460
  86.0 4.8 %copy-start.3 = (f32[3,512,128]{2,1,0:T(8,128)S(1)}, f32[3,512,128]{2,1,0:T(8,128)}, u32[]{:S(2)}) copy-start(f32[3,512,128]{2,1,0:T(8,128)} %get-tuple-element.14) | copy-start | bytes 2359300
  86.9 5.8 %collective-permute-start.15 = (bf16[4,512,128]{2,1,0:T(8,128)(2,1)}, bf16[4,512,128]{2,1,0:T(8,128)(2,1)S(1)}, u32[]{:S(2)}, u32[]{:S(2)}) collective-permute-start(bf16[4,512,128]{2,1,0:T(8,128)(2,1)} %slice.104), channel_id=1, source_target_pairs={{0,8},{8,0},{16,24},{24,16},{32,40},{40,32},{48,56},{56,48},{64,72... | collective-permute-start | bytes 1572872 | tf_op jit(solution)/shard_map/ppermute | solution.py:140
  92.0 2.3 %collective-permute-start.18 = (bf16[4,512,128]{2,1,0:T(8,128)(2,1)S(1)}, bf16[4,512,128]{2,1,0:T(8,128)(2,1)S(1)}, u32[]{:S(2)}, u32[]{:S(2)}) collective-permute-start(bf16[4,512,128]{2,1,0:T(8,128)(2,1)S(1)} %slice.103), channel_id=1, source_target_pairs={{0,8},{8,0},{16,24},{24,16},{32,40},{40,32},{48,56},{56,48},{64,72... | collective-permute-start | bytes 1572872 | tf_op jit(solution)/shard_map/ppermute | solution.py:140
  94.1 7.9 %collective-permute-start.16 = (bf16[2,512,128]{2,1,0:T(8,128)(2,1)S(1)}, bf16[2,512,128]{2,1,0:T(8,128)(2,1)S(1)}, u32[]{:S(2)}, u32[]{:S(2)}) collective-permute-start(bf16[2,512,128]{2,1,0:T(8,128)(2,1)S(1)} %slice.106), channel_id=1, source_target_pairs={{0,16},{8,24},{16,0},{24,8},{32,48},{40,56},{48,32},{56,40},{64,80... | collective-permute-start | bytes 786440 | tf_op jit(solution)/shard_map/ppermute | solution.py:140
  94.4 13.2 %collective-permute-start.19 = (bf16[2,512,128]{2,1,0:T(8,128)(2,1)S(1)}, bf16[2,512,128]{2,1,0:T(8,128)(2,1)S(1)}, u32[]{:S(2)}, u32[]{:S(2)}) collective-permute-start(bf16[2,512,128]{2,1,0:T(8,128)(2,1)S(1)} %slice.105), channel_id=1, source_target_pairs={{0,16},{8,24},{16,0},{24,8},{32,48},{40,56},{48,32},{56,40},{64,80... | collective-permute-start | bytes 786440 | tf_op jit(solution)/shard_map/ppermute | solution.py:140
  102.0 10.2 %collective-permute-start.17 = (bf16[1,512,128]{2,1,0:T(8,128)(2,1)S(1)}, bf16[1,512,128]{2,1,0:T(8,128)(2,1)S(1)}, u32[]{:S(2)}, u32[]{:S(2)}) collective-permute-start(bf16[1,512,128]{2,1,0:T(8,128)(2,1)S(1)} %slice.108), channel_id=1, source_target_pairs={{0,32},{8,40},{16,48},{24,56},{32,0},{40,8},{48,16},{56,24},{64,96... | collective-permute-start | bytes 393224 | tf_op jit(solution)/shard_map/ppermute | solution.py:140
  107.7 6.8 %collective-permute-start.20 = (bf16[1,512,128]{2,1,0:T(8,128)(2,1)S(1)}, bf16[1,512,128]{2,1,0:T(8,128)(2,1)S(1)}, u32[]{:S(2)}, u32[]{:S(2)}) collective-permute-start(bf16[1,512,128]{2,1,0:T(8,128)(2,1)S(1)} %slice.107), channel_id=1, source_target_pairs={{0,32},{8,40},{16,48},{24,56},{32,0},{40,8},{48,16},{56,24},{64,96... | collective-permute-start | bytes 393224 | tf_op jit(solution)/shard_map/ppermute | solution.py:140

commit v12 on v11

--- a/solution.py
+++ b/solution.py
@@ -140,10 +140,6 @@
     return lax.ppermute(block, axis, route)
 
 
-def bit_reversed(distance):
-    return ((distance & 1) << 2) | (distance & 2) | ((distance >> 2) & 1)
-
-
 def ring_route(move):
     route = []
     for low in range(lax.axis_size("resp")):
@@ -177,12 +173,20 @@
     )
 
 
-def return_group(terms):
-    for bit in range(GROUP.bit_length() - 1):
-        half = terms.shape[0] // 2
-        sent = terms[half:].astype(jnp.bfloat16)
-        terms = terms[:half] + exchange(sent, "resp", bit).astype(jnp.float32)
-    return terms
+def return_group(terms, my_index):
+    def send(block, move):
+        return lax.ppermute(block.astype(jnp.bfloat16), "resp", ring_route(move)).astype(jnp.float32)
+
+    from_core = send(terms[jnp.array([1, 4, 5, 7])], lambda x, c: (x, 1 - c))
+    own = terms[0] + from_core[0]
+    minus = terms[2] + from_core[1]
+    plus = terms[3] + from_core[2]
+    far = terms[6] + from_core[3]
+    far_back = send(far, lambda x, c: (x + 1, c) if c == 0 else (x - 1, c))
+    is_core0 = my_index % 2 == 0
+    plus = plus + jnp.where(is_core0, far_back, 0.0)
+    minus = minus + jnp.where(is_core0, 0.0, far_back)
+    return own + send(minus, lambda x, c: (x - 1, c)) + send(plus, lambda x, c: (x + 1, c))
 
 
 def head_sum(row_part):
@@ -194,7 +198,6 @@
 def body(queries, key_states, value_states, partners, counts, norm_gain, out_grad):
     my_index = lax.axis_index("resp")
     seq_len = queries.shape[1]
-    mate_rows = bit_reversed(jnp.bitwise_xor(partners[0], my_index))
     count = counts.astype(jnp.int32)
     ring_rows = ring_row(partners[0], my_index)
     mate_keys = jnp.take(gather_group(key_states, my_index), ring_rows, axis=0)
@@ -219,8 +222,8 @@
         count, queries[0], mate_keys, mate_values, attention_grad, attention, log_total
     )
     zero_rows = jnp.zeros((GROUP,) + key_terms.shape[1:], jnp.float32)
-    key_total = return_group(zero_rows.at[mate_rows].add(key_terms))
-    value_total = return_group(zero_rows.at[mate_rows].add(value_terms))
+    key_total = return_group(zero_rows.at[ring_rows].add(key_terms), my_index)[None]
+    value_total = return_group(zero_rows.at[ring_rows].add(value_terms), my_index)[None]
     return (
         normed_out,
         query_grads[None],

time: 116 us -> 116 us (level)
  waiting for transfers between devices: 25.3 us -> 16.7 us
  local copies, waits for them, and re-layouts: 6.93 us -> 13.1 us
  other arithmetic: 10.7 us -> 13.9 us
    ppermute x9 -> x3, waiting for transfers between devices: 18.9 us -> 5.56 us  [exchange(): return lax.ppermute(block, axis, route)]
    ppermute x9 -> x3, starting transfers between devices: 17.7 us -> 7.05 us  [exchange(): return lax.ppermute(block, axis, route)]
    ppermute x0 -> x8, starting transfers between devices: none -> 10.5 us  [send(): lax.ppermute(block.astype(jnp.bfloat16), 'resp', ring_route(move))]
    ppermute x0 -> x8, waiting for transfers between devices: none -> 5.59 us  [send(): lax.ppermute(block.astype(jnp.bfloat16), 'resp', ring_route(move))]
    unnamed x22, local copies, waits for them, and re-layouts: 3.03 us -> 6.3 us
    convert_element_type x0 -> x6, other arithmetic: none -> 2.42 us  [the longest x4 2.28 us: send(): block.astype(jnp.bfloat16)]
    gather x0 -> x2, local copies, waits for them, and re-layouts: none -> 2.05 us  [return_group(): from_core = send(terms[jnp.array([1, 4, 5, 7])], lambda x, c: (x, 1 - c))]
    add x4 -> x0, other arithmetic: 1.49 us -> none  [return_group(): terms = terms[:half] + exchange(sent, 'resp', bit).astype(jnp.float32)]
  transfers between devices with their start and end apart: 21 -> 23, of which waited for: 11 -> 8; matrix products, arithmetic and copies ran while one was open for 7% -> 15% of each run, Pallas kernels for 0% -> 0%
where the time goes in v12:
time: 116 us; the launch traced here: 115 us
  Pallas kernels  41.9 us (36%)
  starting transfers between devices  28.2 us (24%)
  waiting for transfers between devices  16.7 us (14%)
  other arithmetic  13.9 us (12%)
  local copies, waits for them, and re-layouts  13.1 us (11%)
  between operations  1.57 us (1%)
    pallas_call x1, Pallas kernels, attention_backward(): pl.pallas_call(backward_kernel, grid_spec=pltpu.PrefetchScalarGridSpec(nu...  21.5 us
    pallas_call x1, Pallas kernels, attention_forward(): pl.pallas_call(forward_kernel, grid_spec=pltpu.PrefetchScalarGridSpec(num...  20.3 us
    ppermute x8, starting transfers between devices, send(): lax.ppermute(block.astype(jnp.bfloat16), 'resp', ring_route(move))  10.5 us
    ppermute x3, starting transfers between devices, exchange(): return lax.ppermute(block, axis, route)  7.05 us
    unnamed x22, local copies, waits for them, and re-layouts  6.3 us
    ppermute x8, waiting for transfers between devices, send(): lax.ppermute(block.astype(jnp.bfloat16), 'resp', ring_route(move))  5.59 us
    ppermute x3, waiting for transfers between devices, exchange(): return lax.ppermute(block, axis, route)  5.56 us
    ppermute x2, waiting for transfers between devices, gather_group(): lax.ppermute(relay, 'resp', ring_route(lambda x, c: (x - 1, c) if c == 0...  5.56 us
  transfers between devices with their start and end apart: 23, of which 8 were waited for; matrix products, arithmetic and copies ran while one was open for 15% of the time, Pallas kernels for 0%

profile of v12, /device:TPU:1, one launch (start us, length us, event | category | flops | bytes accessed | tf_op | source)
XLA Modules:
  0.0 115.3 jit_solution(1052245381153811877)
XLA Ops:
  0.6 2.1 %collective-permute-start.1 = (bf16[1,512,128]{2,1,0:T(8,128)(2,1)}, bf16[1,512,128]{2,1,0:T(8,128)(2,1)S(1)}, u32[]{:S(2)}, u32[]{:S(2)}) collective-permute-start(bf16[1,512,128]{2,1,0:T(8,128)(2,1)} %param.13), channel_id=1, source_target_pairs={{0,16},{8,24},{16,32},{24,40},{32,48},{40,56},{48,0},{56,8},{64,80... | collective-permute-start | bytes 393224 | tf_op jit(solution)/shard_map/ppermute | solution.py:162
  2.7 1.3 %collective-permute-start = (bf16[1,512,128]{2,1,0:T(8,128)(2,1)}, bf16[1,512,128]{2,1,0:T(8,128)(2,1)S(1)}, u32[]{:S(2)}, u32[]{:S(2)}) collective-permute-start(bf16[1,512,128]{2,1,0:T(8,128)(2,1)} %param.13), channel_id=1, source_target_pairs={{0,8},{8,0},{16,24},{24,16},{32,40},{40,32},{48,56},{56,48},{64,72... | collective-permute-start | bytes 393224 | tf_op jit(solution)/shard_map/ppermute | solution.py:164
  4.1 2.9 %collective-permute-start.2 = (bf16[1,512,128]{2,1,0:T(8,128)(2,1)}, bf16[1,512,128]{2,1,0:T(8,128)(2,1)S(1)}, u32[]{:S(2)}, u32[]{:S(2)}) collective-permute-start(bf16[1,512,128]{2,1,0:T(8,128)(2,1)} %param.13), channel_id=1, source_target_pairs={{0,48},{8,56},{16,0},{24,8},{32,16},{40,24},{48,32},{56,40},{64,11... | collective-permute-start | bytes 393224 | tf_op jit(solution)/shard_map/ppermute | solution.py:163
  6.9 0.0 collective-permute-start.7
  6.9 2.7 %collective-permute-start.8 = (bf16[1,512,128]{2,1,0:T(8,128)(2,1)}, bf16[1,512,128]{2,1,0:T(8,128)(2,1)S(1)}, u32[]{:S(2)}, u32[]{:S(2)}) collective-permute-start(bf16[1,512,128]{2,1,0:T(8,128)(2,1)} %param.14), channel_id=1, source_target_pairs={{0,48},{8,56},{16,0},{24,8},{32,16},{40,24},{48,32},{56,40},{64,11... | collective-permute-start | bytes 393224 | tf_op jit(solution)/shard_map/ppermute | solution.py:163
  9.6 0.7 fusion.41
  10.3 0.7 pad_clamp_fusion
  10.9 1.3 %gather_fusion = s32[3]{0:T(128)S(1)} fusion(s32[8]{0:T(128)} %constant.71.clone, s32[1024]{0:T(1024)S(1)} %get-tuple-element.32), kind=kCustom, calls=%fused_computation.2 | custom fusion | bytes 36 | tf_op jit(solution)/shard_map/gather | solution.py:158
  12.2 1.6 %constant_dynamic-update-slice_fusion.6 = bf16[8,512,128]{2,1,0:T(8,128)(2,1)} fusion(bf16[1,512,128]{2,1,0:T(8,128)(2,1)} %param.13), kind=kLoop, calls=%fused_computation.70 | loop fusion | bytes 262144
  13.8 0.9 constant_dynamic-update-slice_fusion.13
  15.4 0.9 collective-permute-start.6
  16.3 0.0 collective-permute-done.2
  16.4 0.1 collective-permute-start.3
  16.5 0.0 collective-permute-done.7
  16.5 0.0 collective-permute-done.8
  16.5 0.6 collective-permute-start.9
  17.1 0.7 constant_dynamic-update-slice_fusion.5
  17.7 0.7 broadcast_select_fusion.3
  18.5 0.1 broadcast_select_fusion.2
  18.5 0.1 collective-permute-start.10
  18.6 0.7 constant_dynamic-update-slice_fusion.3
  19.3 4.2 %collective-permute-done.4 = bf16[1,512,128]{2,1,0:T(8,128)(2,1)S(1)} collective-permute-done((bf16[1,512,128]{2,1,0:T(8,128)(2,1)S(1)}, bf16[1,512,128]{2,1,0:T(8,128)(2,1)S(1)}, u32[]{:S(2)}, u32[]{:S(2)}) %collective-permute-start.4) | collective-permute-done | bytes 131104 | tf_op jit(solution)/shard_map/ppermute | solution.py:166
  23.5 1.4 %collective-permute-done.10 = bf16[1,512,128]{2,1,0:T(8,128)(2,1)S(1)} collective-permute-done((bf16[1,512,128]{2,1,0:T(8,128)(2,1)S(1)}, bf16[1,512,128]{2,1,0:T(8,128)(2,1)S(1)}, u32[]{:S(2)}, u32[]{:S(2)}) %collective-permute-start.10) | collective-permute-done | bytes 131104 | tf_op jit(solution)/shard_map/ppermute | solution.py:166
  24.9 0.7 constant_dynamic-update-slice_fusion.2
  25.6 0.7 constant_dynamic-update-slice_fusion.1
  26.3 0.7 constant_dynamic-update-slice_fusion
  27.0 1.8 %gather_fusion.3 = bf16[3,512,128]{2,1,0:T(8,128)(2,1)S(1)} fusion(bf16[8,512,128]{2,1,0:T(8,128)(2,1)} %constant_dynamic-update-slice_fusion, s32[1024]{0:T(1024)S(1)} %pad_clamp_fusion.1), kind=kCustom, calls=%fused_computation.clone | custom fusion | bytes 786444 | tf_op jit(solution)/shard_map/jit(_take)/gather | solution.py:203
  28.9 0.0 copy-start.2
  28.9 0.0 copy-start.5
  28.9 0.6 gather_fusion.4
  29.5 1.0 broadcast_select_fusion
  30.6 20.3 %shard_map.129 = (bf16[512,1024]{1,0:T(8,128)(2,1)}, f32[8,1,512]{2,1,0:T(1,128)}) custom-call(s32[1]{0:T(128)S(6)} %copy.28.count_ref, bf16[512,1024]{1,0:T(8,128)(2,1)} %bitcast.70, bf16[3,512,128]{2,1,0:T(8,128)(2,1)} %get-tuple-element.30.k_ref, bf16[3,512,128]{2,1,0:T(8,128)(2,1)} %get-tuple-element.29.v_ref), custom_call_target="tpu_custom_call" | custom-call | tf_op jit(solution)/shard_map/pallas_call | solution.py:100
  50.9 1.9 %fusion = (f32[512]{0:T(512)S(1)}, f32[512]{0:T(512)S(1)}) fusion(bf16[512,1024]{1,0:T(8,128)(2,1)} %get-tuple-element.10.att_ref, f32[1024]{0:T(1024)S(1)} %copy-done.5, bf16[1,512,1024]{2,1,0:T(8,128)(2,1)S(1)} %copy-done.2), kind=kLoop, calls=%fused_computation.11 | loop fusion | flops 3668992 | bytes 2105344 | tf_op jit(solution)/shard_map/reduce_sum | solution.py:210
  52.8 0.1 collective-permute-start.12
  52.9 2.4 %collective-permute-done.12 = f32[2,512]{1,0:T(2,128)S(1)} collective-permute-done((f32[2,512]{1,0:T(2,128)S(1)}, f32[2,512]{1,0:T(2,128)S(1)}, u32[]{:S(2)}, u32[]{:S(2)}) %collective-permute-start.12) | collective-permute-done | bytes 4128 | tf_op jit(solution)/shard_map/ppermute | solution.py:140
  55.4 1.7 %collective-permute-start.13 = (f32[2,512]{1,0:T(2,128)S(1)}, f32[2,512]{1,0:T(2,128)S(1)}, u32[]{:S(2)}, u32[]{:S(2)}) collective-permute-start(f32[2,512]{1,0:T(2,128)S(1)} %fusion.43), channel_id=1, source_target_pairs={{0,2},{1,3},{2,0},{3,1},{4,6},{5,7},{6,4},{7,5},{8,10},{9,11},{10,... | collective-permute-start | bytes 12296 | tf_op jit(solution)/shard_map/ppermute | solution.py:140
  57.1 1.9 %collective-permute-done.13 = f32[2,512]{1,0:T(2,128)S(1)} collective-permute-done((f32[2,512]{1,0:T(2,128)S(1)}, f32[2,512]{1,0:T(2,128)S(1)}, u32[]{:S(2)}, u32[]{:S(2)}) %collective-permute-start.13) | collective-permute-done | bytes 4128 | tf_op jit(solution)/shard_map/ppermute | solution.py:140
  59.0 5.3 %collective-permute-start.14 = (f32[2,512]{1,0:T(2,128)S(1)}, f32[2,512]{1,0:T(2,128)S(1)}, u32[]{:S(2)}, u32[]{:S(2)}) collective-permute-start(f32[2,512]{1,0:T(2,128)S(1)} %fusion.45), channel_id=1, source_target_pairs={{0,4},{1,5},{2,6},{3,7},{4,0},{5,1},{6,2},{7,3},{8,12},{9,13},{10,... | collective-permute-start | bytes 12296 | tf_op jit(solution)/shard_map/ppermute | solution.py:140
  64.3 1.2 %collective-permute-done.14 = f32[2,512]{1,0:T(2,128)S(1)} collective-permute-done((f32[2,512]{1,0:T(2,128)S(1)}, f32[2,512]{1,0:T(2,128)S(1)}, u32[]{:S(2)}, u32[]{:S(2)}) %collective-permute-start.14) | collective-permute-done | bytes 4128 | tf_op jit(solution)/shard_map/ppermute | solution.py:140
  65.5 2.0 %fusion.5 = (bf16[512,1024]{1,0:T(8,128)(2,1)}, bf16[1,512,1024]{2,1,0:T(8,128)(2,1)}) fusion(bf16[512,1024]{1,0:T(8,128)(2,1)S(1)} %copy-done.1, bf16[1,512,1024]{2,1,0:T(8,128)(2,1)S(1)} %copy-done.2, f32[512]{0:T(512)S(1)} %fusion.35, f32[512]{0:T(512)S(1)} %bitcast.79, f32[1024]{0:T(1024)S(1)} %copy-done.5), kind=kLoop, calls=%fused_computation.16 | loop fusion | flops 5242880 | bytes 4202496 | tf_op jit(solution)/shard_map/convert_element_type | solution.py:219
  67.5 21.5 %shard_map.130 = (bf16[512,1024]{1,0:T(8,128)(2,1)}, f32[3,512,128]{2,1,0:T(8,128)}, f32[3,512,128]{2,1,0:T(8,128)}) custom-call(s32[1]{0:T(128)S(6)} %copy.28.count_ref, bf16[512,1024]{1,0:T(8,128)(2,1)} %bitcast.71, bf16[3,512,128]{2,1,0:T(8,128)(2,1)} %get-tuple-element.30.k_ref, bf16[3,512,128]{2,1,0:T(8,128)(2,1)} %get-tuple-element.29.v_ref, ...), custom_call_target="tpu_custom_call" | custom-call | tf_op jit(solution)/shard_map/pallas_call | solution.py:121
  89.0 0.1 broadcast_in_dim.44.clone
  89.2 1.0 copy-done.4
  90.2 1.0 scatter_fusion
  91.2 1.4 %gather_fusion.1 = bf16[4,512,128]{2,1,0:T(8,128)(2,1)} fusion(f32[8,512,128]{2,1,0:T(8,128)S(1)} %scatter_fusion, s32[1024]{0:T(1024)S(1)} %get-tuple-element.31), kind=kCustom, calls=%fused_computation.3 | custom fusion | bytes 1048592 | tf_op jit(solution)/shard_map/gather | solution.py:180
  92.6 3.9 %collective-permute-start.15 = (bf16[4,512,128]{2,1,0:T(8,128)(2,1)}, bf16[4,512,128]{2,1,0:T(8,128)(2,1)S(1)}, u32[]{:S(2)}, u32[]{:S(2)}) collective-permute-start(bf16[4,512,128]{2,1,0:T(8,128)(2,1)} %gather_fusion.1), channel_id=1, source_target_pairs={{0,8},{8,0},{16,24},{24,16},{32,40},{40,32},{48,56},{56,48},{64,72... | collective-permute-start | bytes 1572872 | tf_op jit(solution)/shard_map/ppermute | solution.py:178
  96.5 0.1 broadcast_in_dim.44.clone.1
  96.7 1.0 scatter_fusion.1
  97.7 0.6 gather_fusion.2
  98.3 0.2 collective-permute-start.19
  98.6 0.1 convert_element_type.87
  98.6 1.0 fusion.31
  99.6 0.8 collective-permute-start.16
  100.5 0.1 convert_element_type.98
  100.6 0.7 collective-permute-start.20
  101.3 2.2 %collective-permute-done.16 = bf16[512,128]{1,0:T(8,128)(2,1)S(1)} collective-permute-done((bf16[512,128]{1,0:T(8,128)(2,1)S(1)}, bf16[512,128]{1,0:T(8,128)(2,1)S(1)}, u32[]{:S(2)}, u32[]{:S(2)}) %collective-permute-start.16) | collective-permute-done | bytes 131104 | tf_op jit(solution)/shard_map/ppermute | solution.py:178
  103.5 1.1 fusion.9
  104.7 2.0 %collective-permute-start.17 = (bf16[512,128]{1,0:T(8,128)(2,1)S(1)}, bf16[512,128]{1,0:T(8,128)(2,1)S(1)}, u32[]{:S(2)}, u32[]{:S(2)}) collective-permute-start(bf16[512,128]{1,0:T(8,128)(2,1)S(1)} %get-tuple-element.19), channel_id=1, source_target_pairs={{0,48},{8,56},{16,0},{24,8},{32,16},{40,24},{48,32},{56,40},{64,11... | collective-permute-start | bytes 393224 | tf_op jit(solution)/shard_map/ppermute | solution.py:178
  106.7 0.1 fusion.13
  106.8 2.8 %collective-permute-start.21 = (bf16[512,128]{1,0:T(8,128)(2,1)S(1)}, bf16[512,128]{1,0:T(8,128)(2,1)S(1)}, u32[]{:S(2)}, u32[]{:S(2)}) collective-permute-start(bf16[512,128]{1,0:T(8,128)(2,1)S(1)} %get-tuple-element.17), channel_id=1, source_target_pairs={{0,48},{8,56},{16,0},{24,8},{32,16},{40,24},{48,32},{56,40},{64,11... | collective-permute-start | bytes 393224 | tf_op jit(solution)/shard_map/ppermute | solution.py:178
  109.6 2.5 %collective-permute-done.18 = bf16[512,128]{1,0:T(8,128)(2,1)S(1)} collective-permute-done((bf16[512,128]{1,0:T(8,128)(2,1)S(1)}, bf16[512,128]{1,0:T(8,128)(2,1)S(1)}, u32[]{:S(2)}, u32[]{:S(2)}) %collective-permute-start.18) | collective-permute-done | bytes 131104 | tf_op jit(solution)/shard_map/ppermute | solution.py:178
  112.1 1.7 %fusion.30 = bf16[1,512,128]{2,1,0:T(8,128)(2,1)} fusion(bf16[512,128]{1,0:T(8,128)(2,1)S(1)} %collective-permute-done.18, bf16[512,128]{1,0:T(8,128)(2,1)S(1)} %collective-permute-done.17, f32[4,512,128]{2,1,0:T(8,128)S(1)} %convert_element_type.87, f32[8,512,128]{2,1,0:T(8,128)} %copy-done), kind=kLoop, calls=%fused_computation.58 | loop fusion | flops 393216 | bytes 917504 | tf_op jit(solution)/shard_map/convert_element_type | solution.py:230
  113.7 0.9 collective-permute-done.22
  114.6 0.7 fusion.32
  (44 shorter events, 0.3 us)
Async XLA Ops:
  0.6 14.8 %collective-permute-start.1 = (bf16[1,512,128]{2,1,0:T(8,128)(2,1)}, bf16[1,512,128]{2,1,0:T(8,128)(2,1)S(1)}, u32[]{:S(2)}, u32[]{:S(2)}) collective-permute-start(bf16[1,512,128]{2,1,0:T(8,128)(2,1)} %param.13), channel_id=1, source_target_pairs={{0,16},{8,24},{16,32},{24,40},{32,48},{40,56},{48,0},{56,8},{64,80... | collective-permute-start | bytes 393224 | tf_op jit(solution)/shard_map/ppermute | solution.py:162
  2.7 14.3 %collective-permute-start = (bf16[1,512,128]{2,1,0:T(8,128)(2,1)}, bf16[1,512,128]{2,1,0:T(8,128)(2,1)S(1)}, u32[]{:S(2)}, u32[]{:S(2)}) collective-permute-start(bf16[1,512,128]{2,1,0:T(8,128)(2,1)} %param.13), channel_id=1, source_target_pairs={{0,8},{8,0},{16,24},{24,16},{32,40},{40,32},{48,56},{56,48},{64,72... | collective-permute-start | bytes 393224 | tf_op jit(solution)/shard_map/ppermute | solution.py:164
  4.1 12.3 %collective-permute-start.2 = (bf16[1,512,128]{2,1,0:T(8,128)(2,1)}, bf16[1,512,128]{2,1,0:T(8,128)(2,1)S(1)}, u32[]{:S(2)}, u32[]{:S(2)}) collective-permute-start(bf16[1,512,128]{2,1,0:T(8,128)(2,1)} %param.13), channel_id=1, source_target_pairs={{0,48},{8,56},{16,0},{24,8},{32,16},{40,24},{48,32},{56,40},{64,11... | collective-permute-start | bytes 393224 | tf_op jit(solution)/shard_map/ppermute | solution.py:163
  6.9 9.6 %collective-permute-start.7 = (bf16[1,512,128]{2,1,0:T(8,128)(2,1)}, bf16[1,512,128]{2,1,0:T(8,128)(2,1)S(1)}, u32[]{:S(2)}, u32[]{:S(2)}) collective-permute-start(bf16[1,512,128]{2,1,0:T(8,128)(2,1)} %param.14), channel_id=1, source_target_pairs={{0,16},{8,24},{16,32},{24,40},{32,48},{40,56},{48,0},{56,8},{64,80... | collective-permute-start | bytes 393224 | tf_op jit(solution)/shard_map/ppermute | solution.py:162
  6.9 9.6 %collective-permute-start.8 = (bf16[1,512,128]{2,1,0:T(8,128)(2,1)}, bf16[1,512,128]{2,1,0:T(8,128)(2,1)S(1)}, u32[]{:S(2)}, u32[]{:S(2)}) collective-permute-start(bf16[1,512,128]{2,1,0:T(8,128)(2,1)} %param.14), channel_id=1, source_target_pairs={{0,48},{8,56},{16,0},{24,8},{32,16},{40,24},{48,32},{56,40},{64,11... | collective-permute-start | bytes 393224 | tf_op jit(solution)/shard_map/ppermute | solution.py:163
  15.4 3.0 %collective-permute-start.6 = (bf16[1,512,128]{2,1,0:T(8,128)(2,1)}, bf16[1,512,128]{2,1,0:T(8,128)(2,1)S(1)}, u32[]{:S(2)}, u32[]{:S(2)}) collective-permute-start(bf16[1,512,128]{2,1,0:T(8,128)(2,1)} %param.14), channel_id=1, source_target_pairs={{0,8},{8,0},{16,24},{24,16},{32,40},{40,32},{48,56},{56,48},{64,72... | collective-permute-start | bytes 393224 | tf_op jit(solution)/shard_map/ppermute | solution.py:164
  16.4 8.5 %collective-permute-start.3 = (bf16[2,512,128]{2,1,0:T(8,128)(2,1)S(1)}, bf16[2,512,128]{2,1,0:T(8,128)(2,1)S(1)}, u32[]{:S(2)}, u32[]{:S(2)}) collective-permute-start(bf16[2,512,128]{2,1,0:T(8,128)(2,1)S(1)} %pad_maximum_fusion), channel_id=1, source_target_pairs={{0,8},{8,0},{16,24},{24,16},{32,40},{40,32},{48,56},{56,48},{64,72... | collective-permute-start | bytes 786440 | tf_op jit(solution)/shard_map/ppermute | solution.py:167
  16.5 9.7 %collective-permute-start.9 = (bf16[2,512,128]{2,1,0:T(8,128)(2,1)S(1)}, bf16[2,512,128]{2,1,0:T(8,128)(2,1)S(1)}, u32[]{:S(2)}, u32[]{:S(2)}) collective-permute-start(bf16[2,512,128]{2,1,0:T(8,128)(2,1)S(1)} %pad_maximum_fusion.1), channel_id=1, source_target_pairs={{0,8},{8,0},{16,24},{24,16},{32,40},{40,32},{48,56},{56,48},{64,72... | collective-permute-start | bytes 786440 | tf_op jit(solution)/shard_map/ppermute | solution.py:167
  18.4 5.0 %collective-permute-start.4 = (bf16[1,512,128]{2,1,0:T(8,128)(2,1)S(1)}, bf16[1,512,128]{2,1,0:T(8,128)(2,1)S(1)}, u32[]{:S(2)}, u32[]{:S(2)}) collective-permute-start(bf16[1,512,128]{2,1,0:T(8,128)(2,1)S(1)} %get-tuple-element.25), channel_id=1, source_target_pairs={{0,48},{8,24},{16,0},{24,40},{32,16},{40,56},{48,32},{56,8},{64,11... | collective-permute-start | bytes 393224 | tf_op jit(solution)/shard_map/ppermute | solution.py:166
  18.5 6.3 %collective-permute-start.10 = (bf16[1,512,128]{2,1,0:T(8,128)(2,1)S(1)}, bf16[1,512,128]{2,1,0:T(8,128)(2,1)S(1)}, u32[]{:S(2)}, u32[]{:S(2)}) collective-permute-start(bf16[1,512,128]{2,1,0:T(8,128)(2,1)S(1)} %get-tuple-element.23), channel_id=1, source_target_pairs={{0,48},{8,24},{16,0},{24,40},{32,16},{40,56},{48,32},{56,8},{64,11... | collective-permute-start | bytes 393224 | tf_op jit(solution)/shard_map/ppermute | solution.py:166
  23.5 2.8 %collective-permute-start.5 = (bf16[1,512,128]{2,1,0:T(8,128)(2,1)S(1)}, bf16[1,512,128]{2,1,0:T(8,128)(2,1)S(1)}, u32[]{:S(2)}, u32[]{:S(2)}) collective-permute-start(bf16[1,512,128]{2,1,0:T(8,128)(2,1)S(1)} %collective-permute-done.4), channel_id=1, source_target_pairs={{0,8},{8,0},{16,24},{24,16},{32,40},{40,32},{48,56},{56,48},{64,72... | collective-permute-start | bytes 393224 | tf_op jit(solution)/shard_map/ppermute | solution.py:170
  24.9 4.0 %collective-permute-start.11 = (bf16[1,512,128]{2,1,0:T(8,128)(2,1)S(1)}, bf16[1,512,128]{2,1,0:T(8,128)(2,1)S(1)}, u32[]{:S(2)}, u32[]{:S(2)}) collective-permute-start(bf16[1,512,128]{2,1,0:T(8,128)(2,1)S(1)} %collective-permute-done.10), channel_id=1, source_target_pairs={{0,8},{8,0},{16,24},{24,16},{32,40},{40,32},{48,56},{56,48},{64,72... | collective-permute-start | bytes 393224 | tf_op jit(solution)/shard_map/ppermute | solution.py:170
  28.9 22.0 %copy-start.2 = (bf16[1,512,1024]{2,1,0:T(8,128)(2,1)S(1)}, bf16[1,512,1024]{2,1,0:T(8,128)(2,1)}, u32[]{:S(2)}) copy-start(bf16[1,512,1024]{2,1,0:T(8,128)(2,1)} %param.18) | copy-start | bytes 3145732
  28.9 22.0 %copy-start.5 = (f32[1024]{0:T(1024)S(1)}, f32[1024]{0:T(1024)}, u32[]{:S(2)}) copy-start(f32[1024]{0:T(1024)} %param.17) | copy-start | bytes 12292
  50.9 14.6 %copy-start.1 = (bf16[512,1024]{1,0:T(8,128)(2,1)S(1)}, bf16[512,1024]{1,0:T(8,128)(2,1)}, u32[]{:S(2)}) copy-start(bf16[512,1024]{1,0:T(8,128)(2,1)} %get-tuple-element.10.att_ref) | copy-start | bytes 3145732
  52.8 2.5 %collective-permute-start.12 = (f32[2,512]{1,0:T(2,128)S(1)}, f32[2,512]{1,0:T(2,128)S(1)}, u32[]{:S(2)}, u32[]{:S(2)}) collective-permute-start(f32[2,512]{1,0:T(2,128)S(1)} %pad_maximum_fusion.2), channel_id=1, source_target_pairs={{0,1},{1,0},{2,3},{3,2},{4,5},{5,4},{6,7},{7,6},{8,9},{9,8},{10,11... | collective-permute-start | bytes 12296 | tf_op jit(solution)/shard_map/ppermute | solution.py:140
  55.4 3.6 %collective-permute-start.13 = (f32[2,512]{1,0:T(2,128)S(1)}, f32[2,512]{1,0:T(2,128)S(1)}, u32[]{:S(2)}, u32[]{:S(2)}) collective-permute-start(f32[2,512]{1,0:T(2,128)S(1)} %fusion.43), channel_id=1, source_target_pairs={{0,2},{1,3},{2,0},{3,1},{4,6},{5,7},{6,4},{7,5},{8,10},{9,11},{10,... | collective-permute-start | bytes 12296 | tf_op jit(solution)/shard_map/ppermute | solution.py:140
  59.0 6.5 %collective-permute-start.14 = (f32[2,512]{1,0:T(2,128)S(1)}, f32[2,512]{1,0:T(2,128)S(1)}, u32[]{:S(2)}, u32[]{:S(2)}) collective-permute-start(f32[2,512]{1,0:T(2,128)S(1)} %fusion.45), channel_id=1, source_target_pairs={{0,4},{1,5},{2,6},{3,7},{4,0},{5,1},{6,2},{7,3},{8,12},{9,13},{10,... | collective-permute-start | bytes 12296 | tf_op jit(solution)/shard_map/ppermute | solution.py:140
  89.0 1.1 copy-start.4
  91.2 5.4 %copy-start = (f32[8,512,128]{2,1,0:T(8,128)}, f32[8,512,128]{2,1,0:T(8,128)S(1)}, u32[]{:S(2)}) copy-start(f32[8,512,128]{2,1,0:T(8,128)S(1)} %scatter_fusion) | copy-start | bytes 6291460
  91.2 5.5 %copy-start.3 = (f32[3,512,128]{2,1,0:T(8,128)S(1)}, f32[3,512,128]{2,1,0:T(8,128)}, u32[]{:S(2)}) copy-start(f32[3,512,128]{2,1,0:T(8,128)} %get-tuple-element.14) | copy-start | bytes 2359300
  92.6 5.9 %collective-permute-start.15 = (bf16[4,512,128]{2,1,0:T(8,128)(2,1)}, bf16[4,512,128]{2,1,0:T(8,128)(2,1)S(1)}, u32[]{:S(2)}, u32[]{:S(2)}) collective-permute-start(bf16[4,512,128]{2,1,0:T(8,128)(2,1)} %gather_fusion.1), channel_id=1, source_target_pairs={{0,8},{8,0},{16,24},{24,16},{32,40},{40,32},{48,56},{56,48},{64,72... | collective-permute-start | bytes 1572872 | tf_op jit(solution)/shard_map/ppermute | solution.py:178
  98.3 2.1 %collective-permute-start.19 = (bf16[4,512,128]{2,1,0:T(8,128)(2,1)S(1)}, bf16[4,512,128]{2,1,0:T(8,128)(2,1)S(1)}, u32[]{:S(2)}, u32[]{:S(2)}) collective-permute-start(bf16[4,512,128]{2,1,0:T(8,128)(2,1)S(1)} %gather_fusion.2), channel_id=1, source_target_pairs={{0,8},{8,0},{16,24},{24,16},{32,40},{40,32},{48,56},{56,48},{64,72... | collective-permute-start | bytes 1572872 | tf_op jit(solution)/shard_map/ppermute | solution.py:178
  99.6 3.9 %collective-permute-start.16 = (bf16[512,128]{1,0:T(8,128)(2,1)S(1)}, bf16[512,128]{1,0:T(8,128)(2,1)S(1)}, u32[]{:S(2)}, u32[]{:S(2)}) collective-permute-start(bf16[512,128]{1,0:T(8,128)(2,1)S(1)} %fusion.31), channel_id=1, source_target_pairs={{0,16},{8,56},{16,32},{24,8},{32,48},{40,24},{48,0},{56,40},{64,80... | collective-permute-start | bytes 393224 | tf_op jit(solution)/shard_map/ppermute | solution.py:178
  100.6 6.1 %collective-permute-start.20 = (bf16[512,128]{1,0:T(8,128)(2,1)S(1)}, bf16[512,128]{1,0:T(8,128)(2,1)S(1)}, u32[]{:S(2)}, u32[]{:S(2)}) collective-permute-start(bf16[512,128]{1,0:T(8,128)(2,1)S(1)} %fusion.33), channel_id=1, source_target_pairs={{0,16},{8,56},{16,32},{24,8},{32,48},{40,24},{48,0},{56,40},{64,80... | collective-permute-start | bytes 393224 | tf_op jit(solution)/shard_map/ppermute | solution.py:178
  104.7 4.9 %collective-permute-start.17 = (bf16[512,128]{1,0:T(8,128)(2,1)S(1)}, bf16[512,128]{1,0:T(8,128)(2,1)S(1)}, u32[]{:S(2)}, u32[]{:S(2)}) collective-permute-start(bf16[512,128]{1,0:T(8,128)(2,1)S(1)} %get-tuple-element.19), channel_id=1, source_target_pairs={{0,48},{8,56},{16,0},{24,8},{32,16},{40,24},{48,32},{56,40},{64,11... | collective-permute-start | bytes 393224 | tf_op jit(solution)/shard_map/ppermute | solution.py:178
  106.7 5.4 %collective-permute-start.18 = (bf16[512,128]{1,0:T(8,128)(2,1)S(1)}, bf16[512,128]{1,0:T(8,128)(2,1)S(1)}, u32[]{:S(2)}, u32[]{:S(2)}) collective-permute-start(bf16[512,128]{1,0:T(8,128)(2,1)S(1)} %get-tuple-element.20), channel_id=1, source_target_pairs={{0,16},{8,24},{16,32},{24,40},{32,48},{40,56},{48,0},{56,8},{64,80... | collective-permute-start | bytes 393224 | tf_op jit(solution)/shard_map/ppermute | solution.py:178
  106.8 6.9 %collective-permute-start.21 = (bf16[512,128]{1,0:T(8,128)(2,1)S(1)}, bf16[512,128]{1,0:T(8,128)(2,1)S(1)}, u32[]{:S(2)}, u32[]{:S(2)}) collective-permute-start(bf16[512,128]{1,0:T(8,128)(2,1)S(1)} %get-tuple-element.17), channel_id=1, source_target_pairs={{0,48},{8,56},{16,0},{24,8},{32,16},{40,24},{48,32},{56,40},{64,11... | collective-permute-start | bytes 393224 | tf_op jit(solution)/shard_map/ppermute | solution.py:178
  109.6 5.0 %collective-permute-start.22 = (bf16[512,128]{1,0:T(8,128)(2,1)S(1)}, bf16[512,128]{1,0:T(8,128)(2,1)S(1)}, u32[]{:S(2)}, u32[]{:S(2)}) collective-permute-start(bf16[512,128]{1,0:T(8,128)(2,1)S(1)} %get-tuple-element.18), channel_id=1, source_target_pairs={{0,16},{8,24},{16,32},{24,40},{32,48},{40,56},{48,0},{56,8},{64,80... | collective-permute-start | bytes 393224 | tf_op jit(solution)/shard_map/ppermute | solution.py:178

commit v13 on v12

--- a/solution.py
+++ b/solution.py
@@ -33,9 +33,10 @@
     return jnp.transpose(jnp.broadcast_to(column, (column.shape[0], HD)))[:1]
 
 
-def forward_kernel(count_ref, q_ref, k_ref, v_ref, out_ref, lse_ref):
+def forward_kernel(count_ref, rows_ref, q_ref, *refs):
+    k_ref, v_ref, (out_ref, lse_ref) = refs[:SLOTS], refs[SLOTS : 2 * SLOTS], refs[2 * SLOTS :]
     query_head = q_ref[...]
-    scores = [slot_scores(query_head, k_ref[slot]) for slot in range(SLOTS)]
+    scores = [slot_scores(query_head, k_ref[slot][...]) for slot in range(SLOTS)]
     row_max = functools.reduce(
         jnp.maximum,
         [
@@ -49,16 +50,17 @@
     ]
     denominator = sum(jnp.sum(block, axis=1, keepdims=True) for block in exps)
     weighted = sum(
-        jnp.dot(exps[slot].astype(jnp.bfloat16), v_ref[slot], preferred_element_type=jnp.float32)
+        jnp.dot(exps[slot].astype(jnp.bfloat16), v_ref[slot][...], preferred_element_type=jnp.float32)
         for slot in range(SLOTS)
     )
     out_ref[...] = (weighted / denominator).astype(out_ref.dtype)
     lse_ref[...] = as_lane_row(row_max + jnp.log(denominator))
 
 
-def backward_kernel(
-    count_ref, q_ref, k_ref, v_ref, grad_ref, att_ref, lse_ref, dq_ref, dk_ref, dv_ref
-):
+def backward_kernel(count_ref, rows_ref, q_ref, *refs):
+    k_ref, v_ref = refs[:SLOTS], refs[SLOTS : 2 * SLOTS]
+    grad_ref, att_ref, lse_ref, dq_ref, dk_ref, dv_ref = refs[2 * SLOTS :]
+
     @pl.when(pl.program_id(0) == 0)
     def _():
         dk_ref[...] = jnp.zeros_like(dk_ref)
@@ -72,7 +74,7 @@
     )
     query_grad = jnp.zeros(dq_ref.shape, jnp.float32)
     for slot in range(SLOTS):
-        mate_keys = k_ref[slot]
+        mate_keys = k_ref[slot][...]
         back_probs = jnp.exp(
             slot_scores(mate_keys, query_head) - slot_offset(count_ref, slot, log_total, jnp.inf)
         )
@@ -80,7 +82,7 @@
             back_probs.astype(jnp.bfloat16), grad_head, preferred_element_type=jnp.float32
         )
         prob_grad = lax.dot_general(
-            v_ref[slot], grad_head, TRANS_B, preferred_element_type=jnp.float32
+            v_ref[slot][...], grad_head, TRANS_B, preferred_element_type=jnp.float32
         )
         score_grad = (back_probs * (prob_grad - row_delta)).astype(jnp.bfloat16)
         dk_ref[slot] += SCORE_SCALE * jnp.dot(
@@ -92,38 +94,46 @@
     dq_ref[...] = (SCORE_SCALE * query_grad).astype(dq_ref.dtype)
 
 
-def attention_forward(count, queries, mate_keys, mate_values):
+def slot_blocks(seq_len):
+    return [
+        pl.BlockSpec((None, seq_len, HD), lambda h, c, r, slot=slot: (r[slot], 0, 0))
+        for slot in range(SLOTS)
+    ]
+
+
+def attention_forward(count, mate_rows, queries, group_keys, group_values):
     seq_len, width = queries.shape
     heads = width // HD
-    head_block = pl.BlockSpec((seq_len, HD), lambda h, c: (0, h))
-    slot_block = pl.BlockSpec((SLOTS, seq_len, HD), lambda h, c: (0, 0, 0))
+    head_block = pl.BlockSpec((seq_len, HD), lambda h, c, r: (0, h))
     return pl.pallas_call(
         forward_kernel,
         grid_spec=pltpu.PrefetchScalarGridSpec(
-            num_scalar_prefetch=1,
+            num_scalar_prefetch=2,
             grid=(heads,),
-            in_specs=[head_block, slot_block, slot_block],
-            out_specs=[head_block, pl.BlockSpec((None, 1, seq_len), lambda h, c: (h, 0, 0))],
+            in_specs=[head_block] + slot_blocks(seq_len) * 2,
+            out_specs=[head_block, pl.BlockSpec((None, 1, seq_len), lambda h, c, r: (h, 0, 0))],
         ),
         out_shape=[
             jax.ShapeDtypeStruct((seq_len, width), jnp.bfloat16),
             jax.ShapeDtypeStruct((heads, 1, seq_len), jnp.float32),
         ],
-    )(count, queries, mate_keys, mate_values)
-
-
-def attention_backward(count, queries, mate_keys, mate_values, attention_grad, attention, log_rows):
+    )(count, mate_rows, queries, *([group_keys] * SLOTS), *([group_values] * SLOTS))
+
+
+def attention_backward(
+    count, mate_rows, queries, group_keys, group_values, attention_grad, attention, log_rows
+):
     seq_len, width = queries.shape
     heads = width // HD
-    head_block = pl.BlockSpec((seq_len, HD), lambda h, c: (0, h))
-    row_block = pl.BlockSpec((None, 1, seq_len), lambda h, c: (h, 0, 0))
-    slot_block = pl.BlockSpec((SLOTS, seq_len, HD), lambda h, c: (0, 0, 0))
+    head_block = pl.BlockSpec((seq_len, HD), lambda h, c, r: (0, h))
+    row_block = pl.BlockSpec((None, 1, seq_len), lambda h, c, r: (h, 0, 0))
+    slot_block = pl.BlockSpec((SLOTS, seq_len, HD), lambda h, c, r: (0, 0, 0))
     return pl.pallas_call(
         backward_kernel,
         grid_spec=pltpu.PrefetchScalarGridSpec(
-            num_scalar_prefetch=1,
+            num_scalar_prefetch=2,
             grid=(heads,),
-            in_specs=[head_block, slot_block, slot_block, head_block, head_block, row_block],
+            in_specs=[head_block] + slot_blocks(seq_len) * 2 + [head_block, head_block, row_block],
             out_specs=[head_block, slot_block, slot_block],
         ),
         out_shape=[
@@ -132,7 +142,10 @@
             jax.ShapeDtypeStruct((SLOTS, seq_len, HD), jnp.float32),
         ],
         compiler_params=pltpu.CompilerParams(dimension_semantics=("arbitrary",)),
-    )(count, queries, mate_keys, mate_values, attention_grad, attention, log_rows)
+    )(
+        count, mate_rows, queries, *([group_keys] * SLOTS), *([group_values] * SLOTS),
+        attention_grad, attention, log_rows,
+    )
 
 
 def exchange(block, axis, bit):
@@ -200,10 +213,10 @@
     seq_len = queries.shape[1]
     count = counts.astype(jnp.int32)
     ring_rows = ring_row(partners[0], my_index)
-    mate_keys = jnp.take(gather_group(key_states, my_index), ring_rows, axis=0)
-    mate_values = jnp.take(gather_group(value_states, my_index), ring_rows, axis=0)
-
-    attention, log_total = attention_forward(count, queries[0], mate_keys, mate_values)
+    group_keys = gather_group(key_states, my_index)
+    group_values = gather_group(value_states, my_index)
+
+    attention, log_total = attention_forward(count, ring_rows, queries[0], group_keys, group_values)
     attention_flat = attention.astype(jnp.float32)
     scaled_grad = out_grad[0].astype(jnp.float32) * norm_gain
     row_sums = jnp.stack(
@@ -219,7 +232,7 @@
     ).astype(jnp.bfloat16)
 
     query_grads, key_terms, value_terms = attention_backward(
-        count, queries[0], mate_keys, mate_values, attention_grad, attention, log_total
+        count, ring_rows, queries[0], group_keys, group_values, attention_grad, attention, log_total
     )
     zero_rows = jnp.zeros((GROUP,) + key_terms.shape[1:], jnp.float32)
     key_total = return_group(zero_rows.at[ring_rows].add(key_terms), my_index)[None]

time: 116 us -> 114 us (0.983)
  starting transfers between devices: 28.2 us -> 35.4 us
  local copies, waits for them, and re-layouts: 13.1 us -> 8.13 us
  waiting for transfers between devices: 16.7 us -> 11.9 us
  other arithmetic: 13.9 us -> 11.6 us
  Pallas kernels: 41.9 us -> 43.8 us
    ppermute x3, starting transfers between devices: 7.05 us -> 11.2 us  [exchange(): return lax.ppermute(block, axis, route)]
    ppermute x2, starting transfers between devices: 0.68 us -> 3.48 us  [gather_group(): lax.ppermute(jnp.concatenate([from_minus, from_plus], 0), 'resp', ring_ro...]
    ppermute x3, waiting for transfers between devices: 5.56 us -> 2.97 us  [exchange(): return lax.ppermute(block, axis, route)]
    gather x2 -> x0, local copies, waits for them, and re-layouts: 2.47 us -> none  [the longest x1 1.84 us: body(): mate_keys = jnp.take(gather_group(key_states, my_index), ring_rows, axis=0)]
    unnamed x22 -> x30, local copies, waits for them, and re-layouts: 6.3 us -> 3.98 us
    ppermute x8, waiting for transfers between devices: 5.59 us -> 3.34 us  [send(): lax.ppermute(block.astype(jnp.bfloat16), 'resp', ring_route(move))]
    ppermute x2, starting transfers between devices: 2.12 us -> 0.01 us  [gather_group(): lax.ppermute(block, 'resp', ring_route(lambda x, c: (x + 1, c)))]
    ppermute x8, starting transfers between devices: 10.5 us -> 12.1 us  [send(): lax.ppermute(block.astype(jnp.bfloat16), 'resp', ring_route(move))]
  transfers between devices with their start and end apart: 23 -> 23, of which waited for: 8 -> 9; matrix products, arithmetic and copies ran while one was open for 15% -> 9% of each run, Pallas kernels for 0% -> 0%
where the time goes in v13:
time: 114 us; the launch traced here: 112 us
  Pallas kernels  43.8 us (38%)
  starting transfers between devices  35.4 us (31%)
  waiting for transfers between devices  11.9 us (10%)
  other arithmetic  11.6 us (10%)
  local copies, waits for them, and re-layouts  8.13 us (7%)
  between operations  1.64 us (1%)
    pallas_call x1, Pallas kernels, attention_backward(): pl.pallas_call(backward_kernel, grid_spec=pltpu.PrefetchScalarGridSpec(nu...  22.4 us
    pallas_call x1, Pallas kernels, attention_forward(): pl.pallas_call(forward_kernel, grid_spec=pltpu.PrefetchScalarGridSpec(num...  21.4 us
    ppermute x8, starting transfers between devices, send(): lax.ppermute(block.astype(jnp.bfloat16), 'resp', ring_route(move))  12.1 us
    ppermute x3, starting transfers between devices, exchange(): return lax.ppermute(block, axis, route)  11.2 us
    ppermute x2, starting transfers between devices, gather_group(): from_plus = lax.ppermute(block, 'resp', ring_route(lambda x, c: (x - 1, c)))  5.34 us
    ppermute x2, waiting for transfers between devices, gather_group(): lax.ppermute(relay, 'resp', ring_route(lambda x, c: (x - 1, c) if c == 0...  4.03 us
    unnamed x30, local copies, waits for them, and re-layouts  3.98 us
    ppermute x2, starting transfers between devices, gather_group(): lax.ppermute(jnp.concatenate([from_minus, from_plus], 0), 'resp', ring_ro...  3.48 us
  transfers between devices with their start and end apart: 23, of which 9 were waited for; matrix products, arithmetic and copies ran while one was open for 9% of the time, Pallas kernels for 0%

profile of v13, /device:TPU:1, one launch (start us, length us, event | category | flops | bytes accessed | tf_op | source)
XLA Modules:
  0.0 112.5 jit_solution(15585383103656526150)
XLA Ops:
  0.6 3.4 %collective-permute-start.2 = (bf16[1,512,128]{2,1,0:T(8,128)(2,1)}, bf16[1,512,128]{2,1,0:T(8,128)(2,1)S(1)}, u32[]{:S(2)}, u32[]{:S(2)}) collective-permute-start(bf16[1,512,128]{2,1,0:T(8,128)(2,1)} %param.11), channel_id=1, source_target_pairs={{0,48},{8,56},{16,0},{24,8},{32,16},{40,24},{48,32},{56,40},{64,11... | collective-permute-start | bytes 393224 | tf_op jit(solution)/shard_map/ppermute | solution.py:176
  4.0 0.0 collective-permute-start.1
  4.0 2.0 %collective-permute-start = (bf16[1,512,128]{2,1,0:T(8,128)(2,1)}, bf16[1,512,128]{2,1,0:T(8,128)(2,1)S(1)}, u32[]{:S(2)}, u32[]{:S(2)}) collective-permute-start(bf16[1,512,128]{2,1,0:T(8,128)(2,1)} %param.11), channel_id=1, source_target_pairs={{0,8},{8,0},{16,24},{24,16},{32,40},{40,32},{48,56},{56,48},{64,72... | collective-permute-start | bytes 393224 | tf_op jit(solution)/shard_map/ppermute | solution.py:177
  6.0 2.0 %collective-permute-start.8 = (bf16[1,512,128]{2,1,0:T(8,128)(2,1)}, bf16[1,512,128]{2,1,0:T(8,128)(2,1)S(1)}, u32[]{:S(2)}, u32[]{:S(2)}) collective-permute-start(bf16[1,512,128]{2,1,0:T(8,128)(2,1)} %param.12), channel_id=1, source_target_pairs={{0,48},{8,56},{16,0},{24,8},{32,16},{40,24},{48,32},{56,40},{64,11... | collective-permute-start | bytes 393224 | tf_op jit(solution)/shard_map/ppermute | solution.py:176
  7.9 0.0 collective-permute-start.7
  7.9 0.9 constant_dynamic-update-slice_fusion.6
  8.9 0.7 fusion.41
  9.5 0.9 constant_dynamic-update-slice_fusion.13
  11.1 1.8 %gather_fusion = s32[3]{0:T(128)} fusion(s32[8]{0:T(128)} %constant.61.clone, s32[1024]{0:T(1024)S(1)} %pad_clamp_fusion.1), kind=kCustom, calls=%fused_computation | custom fusion | bytes 36 | tf_op jit(solution)/shard_map/gather | solution.py:171
  12.9 0.0 collective-permute-done.2
  12.9 0.3 collective-permute-start.6
  13.2 0.0 collective-permute-done.1
  13.2 0.3 collective-permute-start.3
  13.6 0.0 collective-permute-done
  13.6 0.1 broadcast_select_fusion.1
  13.6 0.1 collective-permute-start.4
  13.7 0.4 collective-permute-done.7
  14.2 3.2 %collective-permute-start.9 = (bf16[2,512,128]{2,1,0:T(8,128)(2,1)S(1)}, bf16[2,512,128]{2,1,0:T(8,128)(2,1)S(1)}, u32[]{:S(2)}, u32[]{:S(2)}) collective-permute-start(bf16[2,512,128]{2,1,0:T(8,128)(2,1)S(1)} %pad_maximum_fusion.1), channel_id=1, source_target_pairs={{0,8},{8,0},{16,24},{24,16},{32,40},{40,32},{48,56},{56,48},{64,72... | collective-permute-start | bytes 786440 | tf_op jit(solution)/shard_map/ppermute | solution.py:180
  17.4 0.0 collective-permute-done.6
  17.4 0.1 broadcast_select_fusion
  17.4 0.1 collective-permute-start.10
  17.6 1.2 %collective-permute-done.4 = bf16[1,512,128]{2,1,0:T(8,128)(2,1)S(1)} collective-permute-done((bf16[1,512,128]{2,1,0:T(8,128)(2,1)S(1)}, bf16[1,512,128]{2,1,0:T(8,128)(2,1)S(1)}, u32[]{:S(2)}, u32[]{:S(2)}) %collective-permute-start.4) | collective-permute-done | bytes 131104 | tf_op jit(solution)/shard_map/ppermute | solution.py:179
  18.8 0.9 collective-permute-start.5
  19.8 2.8 %collective-permute-done.10 = bf16[1,512,128]{2,1,0:T(8,128)(2,1)S(1)} collective-permute-done((bf16[1,512,128]{2,1,0:T(8,128)(2,1)S(1)}, bf16[1,512,128]{2,1,0:T(8,128)(2,1)S(1)}, u32[]{:S(2)}, u32[]{:S(2)}) %collective-permute-start.10) | collective-permute-done | bytes 131104 | tf_op jit(solution)/shard_map/ppermute | solution.py:179
  22.5 0.0 collective-permute-start.11
  22.6 0.0 collective-permute-done.3
  22.6 0.0 collective-permute-done.9
  22.8 1.1 %collective-permute-done.11 = bf16[1,512,128]{2,1,0:T(8,128)(2,1)S(1)} collective-permute-done((bf16[1,512,128]{2,1,0:T(8,128)(2,1)S(1)}, bf16[1,512,128]{2,1,0:T(8,128)(2,1)S(1)}, u32[]{:S(2)}, u32[]{:S(2)}) %collective-permute-start.11) | collective-permute-done | bytes 131104 | tf_op jit(solution)/shard_map/ppermute | solution.py:183
  23.9 0.9 copy-done
  24.9 21.4 %shard_map.129 = (bf16[512,1024]{1,0:T(8,128)(2,1)}, f32[8,1,512]{2,1,0:T(1,128)}) custom-call(s32[1]{0:T(128)S(6)} %copy.28.count_ref, s32[3]{0:T(128)} %gather_fusion, bf16[512,1024]{1,0:T(8,128)(2,1)} %bitcast.70, bf16[8,512,128]{2,1,0:T(8,128)(2,1)} %copy-done.1, bf16[8,512,128]{2,1,0:T(8,128)(2,1)} %copy-done.1, bf16[8,512,128]{2,1,0:T(8,128)(2,1)} %copy-done.1, ...), custom_call_target="tpu_custom_call" | custom-call | tf_op jit(solution)/shard_map/pallas_call | solution.py:108
  46.3 1.9 %fusion = (f32[512]{0:T(512)S(1)}, f32[512]{0:T(512)S(1)}) fusion(bf16[512,1024]{1,0:T(8,128)(2,1)} %get-tuple-element.9.refs_7_, f32[1024]{0:T(1024)S(1)} %copy-done.7, bf16[1,512,1024]{2,1,0:T(8,128)(2,1)S(1)} %copy-done.4), kind=kLoop, calls=%fused_computation.9 | loop fusion | flops 3668992 | bytes 2105344 | tf_op jit(solution)/shard_map/reduce_sum | solution.py:223
  48.2 1.7 %collective-permute-start.12 = (f32[2,512]{1,0:T(2,128)S(1)}, f32[2,512]{1,0:T(2,128)S(1)}, u32[]{:S(2)}, u32[]{:S(2)}) collective-permute-start(f32[2,512]{1,0:T(2,128)S(1)} %pad_maximum_fusion.2), channel_id=1, source_target_pairs={{0,1},{1,0},{2,3},{3,2},{4,5},{5,4},{6,7},{7,6},{8,9},{9,8},{10,11... | collective-permute-start | bytes 12296 | tf_op jit(solution)/shard_map/ppermute | solution.py:153
  50.0 1.0 collective-permute-done.12
  51.0 3.3 %collective-permute-start.13 = (f32[2,512]{1,0:T(2,128)S(1)}, f32[2,512]{1,0:T(2,128)S(1)}, u32[]{:S(2)}, u32[]{:S(2)}) collective-permute-start(f32[2,512]{1,0:T(2,128)S(1)} %fusion.43), channel_id=1, source_target_pairs={{0,2},{1,3},{2,0},{3,1},{4,6},{5,7},{6,4},{7,5},{8,10},{9,11},{10,... | collective-permute-start | bytes 12296 | tf_op jit(solution)/shard_map/ppermute | solution.py:153
  54.2 1.0 collective-permute-done.13
  55.2 6.2 %collective-permute-start.14 = (f32[2,512]{1,0:T(2,128)S(1)}, f32[2,512]{1,0:T(2,128)S(1)}, u32[]{:S(2)}, u32[]{:S(2)}) collective-permute-start(f32[2,512]{1,0:T(2,128)S(1)} %fusion.45), channel_id=1, source_target_pairs={{0,4},{1,5},{2,6},{3,7},{4,0},{5,1},{6,2},{7,3},{8,12},{9,13},{10,... | collective-permute-start | bytes 12296 | tf_op jit(solution)/shard_map/ppermute | solution.py:153
  61.4 1.0 collective-permute-done.14
  62.5 2.0 %fusion.5 = (bf16[512,1024]{1,0:T(8,128)(2,1)}, bf16[1,512,1024]{2,1,0:T(8,128)(2,1)}) fusion(bf16[512,1024]{1,0:T(8,128)(2,1)S(1)} %copy-done.3, bf16[1,512,1024]{2,1,0:T(8,128)(2,1)S(1)} %copy-done.4, f32[512]{0:T(512)S(1)} %fusion.35, f32[512]{0:T(512)S(1)} %bitcast.79, f32[1024]{0:T(1024)S(1)} %copy-done.7), kind=kLoop, calls=%fused_computation.14 | loop fusion | flops 5242880 | bytes 4202496 | tf_op jit(solution)/shard_map/convert_element_type | solution.py:232
  64.5 22.4 %shard_map.130 = (bf16[512,1024]{1,0:T(8,128)(2,1)}, f32[3,512,128]{2,1,0:T(8,128)}, f32[3,512,128]{2,1,0:T(8,128)}) custom-call(s32[1]{0:T(128)S(6)} %copy.28.count_ref, s32[3]{0:T(128)} %gather_fusion, bf16[512,1024]{1,0:T(8,128)(2,1)} %bitcast.71, bf16[8,512,128]{2,1,0:T(8,128)(2,1)} %copy-done.1, bf16[8,512,128]{2,1,0:T(8,128)(2,1)} %copy-done.1, ...), custom_call_target="tpu_custom_call" | custom-call | tf_op jit(solution)/shard_map/pallas_call | solution.py:131
  86.8 0.1 broadcast_in_dim.35.clone
  87.0 1.0 copy-done.6
  88.0 1.0 scatter_fusion
  89.0 1.4 %gather_fusion.1 = bf16[4,512,128]{2,1,0:T(8,128)(2,1)} fusion(f32[8,512,128]{2,1,0:T(8,128)S(1)} %scatter_fusion, s32[1024]{0:T(1024)S(1)} %pad_clamp_fusion), kind=kCustom, calls=%fused_computation.1 | custom fusion | bytes 1048592 | tf_op jit(solution)/shard_map/gather | solution.py:193
  90.4 3.3 %collective-permute-start.15 = (bf16[4,512,128]{2,1,0:T(8,128)(2,1)}, bf16[4,512,128]{2,1,0:T(8,128)(2,1)S(1)}, u32[]{:S(2)}, u32[]{:S(2)}) collective-permute-start(bf16[4,512,128]{2,1,0:T(8,128)(2,1)} %gather_fusion.1), channel_id=1, source_target_pairs={{0,8},{8,0},{16,24},{24,16},{32,40},{40,32},{48,56},{56,48},{64,72... | collective-permute-start | bytes 1572872 | tf_op jit(solution)/shard_map/ppermute | solution.py:191
  93.7 0.1 broadcast_in_dim.35.clone.1
  93.9 1.0 scatter_fusion.1
  94.9 0.6 gather_fusion.2
  95.5 0.2 collective-permute-start.19
  95.7 0.0 collective-permute-done.15
  95.7 0.1 convert_element_type.87
  95.8 1.0 fusion.31
  96.8 1.9 %collective-permute-start.16 = (bf16[512,128]{1,0:T(8,128)(2,1)S(1)}, bf16[512,128]{1,0:T(8,128)(2,1)S(1)}, u32[]{:S(2)}, u32[]{:S(2)}) collective-permute-start(bf16[512,128]{1,0:T(8,128)(2,1)S(1)} %fusion.31), channel_id=1, source_target_pairs={{0,16},{8,56},{16,32},{24,8},{32,48},{40,24},{48,0},{56,40},{64,80... | collective-permute-start | bytes 393224 | tf_op jit(solution)/shard_map/ppermute | solution.py:191
  98.7 0.1 convert_element_type.98
  98.8 0.7 collective-permute-start.20
  99.6 1.2 %collective-permute-done.16 = bf16[512,128]{1,0:T(8,128)(2,1)S(1)} collective-permute-done((bf16[512,128]{1,0:T(8,128)(2,1)S(1)}, bf16[512,128]{1,0:T(8,128)(2,1)S(1)}, u32[]{:S(2)}, u32[]{:S(2)}) %collective-permute-start.16) | collective-permute-done | bytes 131104 | tf_op jit(solution)/shard_map/ppermute | solution.py:191
  100.7 1.1 %fusion.9 = (bf16[512,128]{1,0:T(8,128)(2,1)S(1)}, bf16[512,128]{1,0:T(8,128)(2,1)S(1)}) fusion(bf16[512,128]{1,0:T(8,128)(2,1)S(1)} %collective-permute-done.16, f32[4,512,128]{2,1,0:T(8,128)S(1)} %convert_element_type.87, f32[8,512,128]{2,1,0:T(8,128)} %copy-done.2, pred[]{:T(512)S(6)} %eq.13), kind=kLoop, calls=%fused_computation.23 | loop fusion | flops 589824 | bytes 1441793 | tf_op jit(solution)/shard_map/convert_element_type | solution.py:191
  101.9 0.1 collective-permute-start.18
  102.0 3.1 %collective-permute-start.17 = (bf16[512,128]{1,0:T(8,128)(2,1)S(1)}, bf16[512,128]{1,0:T(8,128)(2,1)S(1)}, u32[]{:S(2)}, u32[]{:S(2)}) collective-permute-start(bf16[512,128]{1,0:T(8,128)(2,1)S(1)} %get-tuple-element.18), channel_id=1, source_target_pairs={{0,48},{8,56},{16,0},{24,8},{32,16},{40,24},{48,32},{56,40},{64,11... | collective-permute-start | bytes 393224 | tf_op jit(solution)/shard_map/ppermute | solution.py:191
  105.1 0.1 fusion.13
  105.2 0.1 collective-permute-start.22
  105.3 2.7 %collective-permute-start.21 = (bf16[512,128]{1,0:T(8,128)(2,1)S(1)}, bf16[512,128]{1,0:T(8,128)(2,1)S(1)}, u32[]{:S(2)}, u32[]{:S(2)}) collective-permute-start(bf16[512,128]{1,0:T(8,128)(2,1)S(1)} %get-tuple-element.16), channel_id=1, source_target_pairs={{0,48},{8,56},{16,0},{24,8},{32,16},{40,24},{48,32},{56,40},{64,11... | collective-permute-start | bytes 393224 | tf_op jit(solution)/shard_map/ppermute | solution.py:191
  107.9 1.7 %fusion.30 = bf16[1,512,128]{2,1,0:T(8,128)(2,1)} fusion(bf16[512,128]{1,0:T(8,128)(2,1)S(1)} %collective-permute-done.18, bf16[512,128]{1,0:T(8,128)(2,1)S(1)} %collective-permute-done.17, f32[4,512,128]{2,1,0:T(8,128)S(1)} %convert_element_type.87, f32[8,512,128]{2,1,0:T(8,128)} %copy-done.2), kind=kLoop, calls=%fused_computation.54 | loop fusion | flops 393216 | bytes 917504 | tf_op jit(solution)/shard_map/convert_element_type | solution.py:243
  109.6 2.2 %collective-permute-done.22 = bf16[512,128]{1,0:T(8,128)(2,1)S(1)} collective-permute-done((bf16[512,128]{1,0:T(8,128)(2,1)S(1)}, bf16[512,128]{1,0:T(8,128)(2,1)S(1)}, u32[]{:S(2)}, u32[]{:S(2)}) %collective-permute-start.22) | collective-permute-done | bytes 131104 | tf_op jit(solution)/shard_map/ppermute | solution.py:191
  111.8 0.7 fusion.32
  (47 shorter events, 0.4 us)
Async XLA Ops:
  0.6 12.3 %collective-permute-start.2 = (bf16[1,512,128]{2,1,0:T(8,128)(2,1)}, bf16[1,512,128]{2,1,0:T(8,128)(2,1)S(1)}, u32[]{:S(2)}, u32[]{:S(2)}) collective-permute-start(bf16[1,512,128]{2,1,0:T(8,128)(2,1)} %param.11), channel_id=1, source_target_pairs={{0,48},{8,56},{16,0},{24,8},{32,16},{40,24},{48,32},{56,40},{64,11... | collective-permute-start | bytes 393224 | tf_op jit(solution)/shard_map/ppermute | solution.py:176
  4.0 9.2 %collective-permute-start.1 = (bf16[1,512,128]{2,1,0:T(8,128)(2,1)}, bf16[1,512,128]{2,1,0:T(8,128)(2,1)S(1)}, u32[]{:S(2)}, u32[]{:S(2)}) collective-permute-start(bf16[1,512,128]{2,1,0:T(8,128)(2,1)} %param.11), channel_id=1, source_target_pairs={{0,16},{8,24},{16,32},{24,40},{32,48},{40,56},{48,0},{56,8},{64,80... | collective-permute-start | bytes 393224 | tf_op jit(solution)/shard_map/ppermute | solution.py:175
  4.0 9.5 %collective-permute-start = (bf16[1,512,128]{2,1,0:T(8,128)(2,1)}, bf16[1,512,128]{2,1,0:T(8,128)(2,1)S(1)}, u32[]{:S(2)}, u32[]{:S(2)}) collective-permute-start(bf16[1,512,128]{2,1,0:T(8,128)(2,1)} %param.11), channel_id=1, source_target_pairs={{0,8},{8,0},{16,24},{24,16},{32,40},{40,32},{48,56},{56,48},{64,72... | collective-permute-start | bytes 393224 | tf_op jit(solution)/shard_map/ppermute | solution.py:177
  6.0 7.8 %collective-permute-start.8 = (bf16[1,512,128]{2,1,0:T(8,128)(2,1)}, bf16[1,512,128]{2,1,0:T(8,128)(2,1)S(1)}, u32[]{:S(2)}, u32[]{:S(2)}) collective-permute-start(bf16[1,512,128]{2,1,0:T(8,128)(2,1)} %param.12), channel_id=1, source_target_pairs={{0,48},{8,56},{16,0},{24,8},{32,16},{40,24},{48,32},{56,40},{64,11... | collective-permute-start | bytes 393224 | tf_op jit(solution)/shard_map/ppermute | solution.py:176
  7.9 6.2 %collective-permute-start.7 = (bf16[1,512,128]{2,1,0:T(8,128)(2,1)}, bf16[1,512,128]{2,1,0:T(8,128)(2,1)S(1)}, u32[]{:S(2)}, u32[]{:S(2)}) collective-permute-start(bf16[1,512,128]{2,1,0:T(8,128)(2,1)} %param.12), channel_id=1, source_target_pairs={{0,16},{8,24},{16,32},{24,40},{32,48},{40,56},{48,0},{56,8},{64,80... | collective-permute-start | bytes 393224 | tf_op jit(solution)/shard_map/ppermute | solution.py:175
  12.9 4.4 %collective-permute-start.6 = (bf16[1,512,128]{2,1,0:T(8,128)(2,1)}, bf16[1,512,128]{2,1,0:T(8,128)(2,1)S(1)}, u32[]{:S(2)}, u32[]{:S(2)}) collective-permute-start(bf16[1,512,128]{2,1,0:T(8,128)(2,1)} %param.12), channel_id=1, source_target_pairs={{0,8},{8,0},{16,24},{24,16},{32,40},{40,32},{48,56},{56,48},{64,72... | collective-permute-start | bytes 393224 | tf_op jit(solution)/shard_map/ppermute | solution.py:177
  13.2 9.3 %collective-permute-start.3 = (bf16[2,512,128]{2,1,0:T(8,128)(2,1)S(1)}, bf16[2,512,128]{2,1,0:T(8,128)(2,1)S(1)}, u32[]{:S(2)}, u32[]{:S(2)}) collective-permute-start(bf16[2,512,128]{2,1,0:T(8,128)(2,1)S(1)} %pad_maximum_fusion), channel_id=1, source_target_pairs={{0,8},{8,0},{16,24},{24,16},{32,40},{40,32},{48,56},{56,48},{64,72... | collective-permute-start | bytes 786440 | tf_op jit(solution)/shard_map/ppermute | solution.py:180
  13.6 5.2 %collective-permute-start.4 = (bf16[1,512,128]{2,1,0:T(8,128)(2,1)S(1)}, bf16[1,512,128]{2,1,0:T(8,128)(2,1)S(1)}, u32[]{:S(2)}, u32[]{:S(2)}) collective-permute-start(bf16[1,512,128]{2,1,0:T(8,128)(2,1)S(1)} %get-tuple-element.24), channel_id=1, source_target_pairs={{0,48},{8,24},{16,0},{24,40},{32,16},{40,56},{48,32},{56,8},{64,11... | collective-permute-start | bytes 393224 | tf_op jit(solution)/shard_map/ppermute | solution.py:179
  14.2 8.4 %collective-permute-start.9 = (bf16[2,512,128]{2,1,0:T(8,128)(2,1)S(1)}, bf16[2,512,128]{2,1,0:T(8,128)(2,1)S(1)}, u32[]{:S(2)}, u32[]{:S(2)}) collective-permute-start(bf16[2,512,128]{2,1,0:T(8,128)(2,1)S(1)} %pad_maximum_fusion.1), channel_id=1, source_target_pairs={{0,8},{8,0},{16,24},{24,16},{32,40},{40,32},{48,56},{56,48},{64,72... | collective-permute-start | bytes 786440 | tf_op jit(solution)/shard_map/ppermute | solution.py:180
  17.4 5.1 %collective-permute-start.10 = (bf16[1,512,128]{2,1,0:T(8,128)(2,1)S(1)}, bf16[1,512,128]{2,1,0:T(8,128)(2,1)S(1)}, u32[]{:S(2)}, u32[]{:S(2)}) collective-permute-start(bf16[1,512,128]{2,1,0:T(8,128)(2,1)S(1)} %get-tuple-element.22), channel_id=1, source_target_pairs={{0,48},{8,24},{16,0},{24,40},{32,16},{40,56},{48,32},{56,8},{64,11... | collective-permute-start | bytes 393224 | tf_op jit(solution)/shard_map/ppermute | solution.py:179
  18.8 3.9 %collective-permute-start.5 = (bf16[1,512,128]{2,1,0:T(8,128)(2,1)S(1)}, bf16[1,512,128]{2,1,0:T(8,128)(2,1)S(1)}, u32[]{:S(2)}, u32[]{:S(2)}) collective-permute-start(bf16[1,512,128]{2,1,0:T(8,128)(2,1)S(1)} %collective-permute-done.4), channel_id=1, source_target_pairs={{0,8},{8,0},{16,24},{24,16},{32,40},{40,32},{48,56},{56,48},{64,72... | collective-permute-start | bytes 393224 | tf_op jit(solution)/shard_map/ppermute | solution.py:183
  22.5 1.3 %collective-permute-start.11 = (bf16[1,512,128]{2,1,0:T(8,128)(2,1)S(1)}, bf16[1,512,128]{2,1,0:T(8,128)(2,1)S(1)}, u32[]{:S(2)}, u32[]{:S(2)}) collective-permute-start(bf16[1,512,128]{2,1,0:T(8,128)(2,1)S(1)} %collective-permute-done.10), channel_id=1, source_target_pairs={{0,8},{8,0},{16,24},{24,16},{32,40},{40,32},{48,56},{56,48},{64,72... | collective-permute-start | bytes 393224 | tf_op jit(solution)/shard_map/ppermute | solution.py:183
  22.7 1.2 %copy-start.1 = (bf16[8,512,128]{2,1,0:T(8,128)(2,1)}, bf16[8,512,128]{2,1,0:T(8,128)(2,1)S(1)}, u32[]{:S(2)}) copy-start(bf16[8,512,128]{2,1,0:T(8,128)(2,1)S(1)} %constant_dynamic-update-slice_fusion.refs_0_.refs_1_.refs_2_) | copy-start | bytes 3145732
  23.9 1.0 copy-start
  24.9 21.4 %copy-start.4 = (bf16[1,512,1024]{2,1,0:T(8,128)(2,1)S(1)}, bf16[1,512,1024]{2,1,0:T(8,128)(2,1)}, u32[]{:S(2)}) copy-start(bf16[1,512,1024]{2,1,0:T(8,128)(2,1)} %param.16) | copy-start | bytes 3145732
  24.9 21.4 %copy-start.7 = (f32[1024]{0:T(1024)S(1)}, f32[1024]{0:T(1024)}, u32[]{:S(2)}) copy-start(f32[1024]{0:T(1024)} %param.15) | copy-start | bytes 12292
  46.3 7.9 %copy-start.8 = (s32[3]{0:T(128)S(1)}, s32[3]{0:T(128)}, u32[]{:S(2)}) copy-start(s32[3]{0:T(128)} %gather_fusion) | copy-start | bytes 40
  46.3 15.1 %copy-start.9 = (s32[4]{0:T(128)S(1)}, s32[4]{0:T(128)}, u32[]{:S(2)}) copy-start(s32[4]{0:T(128)} %constant.73) | copy-start | bytes 52
  46.3 16.1 %copy-start.3 = (bf16[512,1024]{1,0:T(8,128)(2,1)S(1)}, bf16[512,1024]{1,0:T(8,128)(2,1)}, u32[]{:S(2)}) copy-start(bf16[512,1024]{1,0:T(8,128)(2,1)} %get-tuple-element.9.refs_7_) | copy-start | bytes 3145732
  48.2 2.7 %collective-permute-start.12 = (f32[2,512]{1,0:T(2,128)S(1)}, f32[2,512]{1,0:T(2,128)S(1)}, u32[]{:S(2)}, u32[]{:S(2)}) collective-permute-start(f32[2,512]{1,0:T(2,128)S(1)} %pad_maximum_fusion.2), channel_id=1, source_target_pairs={{0,1},{1,0},{2,3},{3,2},{4,5},{5,4},{6,7},{7,6},{8,9},{9,8},{10,11... | collective-permute-start | bytes 12296 | tf_op jit(solution)/shard_map/ppermute | solution.py:153
  51.0 4.3 %collective-permute-start.13 = (f32[2,512]{1,0:T(2,128)S(1)}, f32[2,512]{1,0:T(2,128)S(1)}, u32[]{:S(2)}, u32[]{:S(2)}) collective-permute-start(f32[2,512]{1,0:T(2,128)S(1)} %fusion.43), channel_id=1, source_target_pairs={{0,2},{1,3},{2,0},{3,1},{4,6},{5,7},{6,4},{7,5},{8,10},{9,11},{10,... | collective-permute-start | bytes 12296 | tf_op jit(solution)/shard_map/ppermute | solution.py:153
  55.2 7.2 %collective-permute-start.14 = (f32[2,512]{1,0:T(2,128)S(1)}, f32[2,512]{1,0:T(2,128)S(1)}, u32[]{:S(2)}, u32[]{:S(2)}) collective-permute-start(f32[2,512]{1,0:T(2,128)S(1)} %fusion.45), channel_id=1, source_target_pairs={{0,4},{1,5},{2,6},{3,7},{4,0},{5,1},{6,2},{7,3},{8,12},{9,13},{10,... | collective-permute-start | bytes 12296 | tf_op jit(solution)/shard_map/ppermute | solution.py:153
  86.8 1.1 %copy-start.6 = (f32[3,512,128]{2,1,0:T(8,128)S(1)}, f32[3,512,128]{2,1,0:T(8,128)}, u32[]{:S(2)}) copy-start(f32[3,512,128]{2,1,0:T(8,128)} %get-tuple-element.12) | copy-start | bytes 2359300
  89.0 4.8 %copy-start.2 = (f32[8,512,128]{2,1,0:T(8,128)}, f32[8,512,128]{2,1,0:T(8,128)S(1)}, u32[]{:S(2)}) copy-start(f32[8,512,128]{2,1,0:T(8,128)S(1)} %scatter_fusion) | copy-start | bytes 6291460
  89.0 4.9 %copy-start.5 = (f32[3,512,128]{2,1,0:T(8,128)S(1)}, f32[3,512,128]{2,1,0:T(8,128)}, u32[]{:S(2)}) copy-start(f32[3,512,128]{2,1,0:T(8,128)} %get-tuple-element.13) | copy-start | bytes 2359300
  90.4 5.4 %collective-permute-start.15 = (bf16[4,512,128]{2,1,0:T(8,128)(2,1)}, bf16[4,512,128]{2,1,0:T(8,128)(2,1)S(1)}, u32[]{:S(2)}, u32[]{:S(2)}) collective-permute-start(bf16[4,512,128]{2,1,0:T(8,128)(2,1)} %gather_fusion.1), channel_id=1, source_target_pairs={{0,8},{8,0},{16,24},{24,16},{32,40},{40,32},{48,56},{56,48},{64,72... | collective-permute-start | bytes 1572872 | tf_op jit(solution)/shard_map/ppermute | solution.py:191
  95.5 3.2 %collective-permute-start.19 = (bf16[4,512,128]{2,1,0:T(8,128)(2,1)S(1)}, bf16[4,512,128]{2,1,0:T(8,128)(2,1)S(1)}, u32[]{:S(2)}, u32[]{:S(2)}) collective-permute-start(bf16[4,512,128]{2,1,0:T(8,128)(2,1)S(1)} %gather_fusion.2), channel_id=1, source_target_pairs={{0,8},{8,0},{16,24},{24,16},{32,40},{40,32},{48,56},{56,48},{64,72... | collective-permute-start | bytes 1572872 | tf_op jit(solution)/shard_map/ppermute | solution.py:191
  96.8 3.9 %collective-permute-start.16 = (bf16[512,128]{1,0:T(8,128)(2,1)S(1)}, bf16[512,128]{1,0:T(8,128)(2,1)S(1)}, u32[]{:S(2)}, u32[]{:S(2)}) collective-permute-start(bf16[512,128]{1,0:T(8,128)(2,1)S(1)} %fusion.31), channel_id=1, source_target_pairs={{0,16},{8,56},{16,32},{24,8},{32,48},{40,24},{48,0},{56,40},{64,80... | collective-permute-start | bytes 393224 | tf_op jit(solution)/shard_map/ppermute | solution.py:191
  98.8 6.2 %collective-permute-start.20 = (bf16[512,128]{1,0:T(8,128)(2,1)S(1)}, bf16[512,128]{1,0:T(8,128)(2,1)S(1)}, u32[]{:S(2)}, u32[]{:S(2)}) collective-permute-start(bf16[512,128]{1,0:T(8,128)(2,1)S(1)} %fusion.33), channel_id=1, source_target_pairs={{0,16},{8,56},{16,32},{24,8},{32,48},{40,24},{48,0},{56,40},{64,80... | collective-permute-start | bytes 393224 | tf_op jit(solution)/shard_map/ppermute | solution.py:191
  101.9 6.1 %collective-permute-start.18 = (bf16[512,128]{1,0:T(8,128)(2,1)S(1)}, bf16[512,128]{1,0:T(8,128)(2,1)S(1)}, u32[]{:S(2)}, u32[]{:S(2)}) collective-permute-start(bf16[512,128]{1,0:T(8,128)(2,1)S(1)} %get-tuple-element.19), channel_id=1, source_target_pairs={{0,16},{8,24},{16,32},{24,40},{32,48},{40,56},{48,0},{56,8},{64,80... | collective-permute-start | bytes 393224 | tf_op jit(solution)/shard_map/ppermute | solution.py:191
  102.0 6.0 %collective-permute-start.17 = (bf16[512,128]{1,0:T(8,128)(2,1)S(1)}, bf16[512,128]{1,0:T(8,128)(2,1)S(1)}, u32[]{:S(2)}, u32[]{:S(2)}) collective-permute-start(bf16[512,128]{1,0:T(8,128)(2,1)S(1)} %get-tuple-element.18), channel_id=1, source_target_pairs={{0,48},{8,56},{16,0},{24,8},{32,16},{40,24},{48,32},{56,40},{64,11... | collective-permute-start | bytes 393224 | tf_op jit(solution)/shard_map/ppermute | solution.py:191
  105.2 6.6 %collective-permute-start.22 = (bf16[512,128]{1,0:T(8,128)(2,1)S(1)}, bf16[512,128]{1,0:T(8,128)(2,1)S(1)}, u32[]{:S(2)}, u32[]{:S(2)}) collective-permute-start(bf16[512,128]{1,0:T(8,128)(2,1)S(1)} %get-tuple-element.17), channel_id=1, source_target_pairs={{0,16},{8,24},{16,32},{24,40},{32,48},{40,56},{48,0},{56,8},{64,80... | collective-permute-start | bytes 393224 | tf_op jit(solution)/shard_map/ppermute | solution.py:191
  105.3 6.5 %collective-permute-start.21 = (bf16[512,128]{1,0:T(8,128)(2,1)S(1)}, bf16[512,128]{1,0:T(8,128)(2,1)S(1)}, u32[]{:S(2)}, u32[]{:S(2)}) collective-permute-start(bf16[512,128]{1,0:T(8,128)(2,1)S(1)} %get-tuple-element.16), channel_id=1, source_target_pairs={{0,48},{8,56},{16,0},{24,8},{32,16},{40,24},{48,32},{56,40},{64,11... | collective-permute-start | bytes 393224 | tf_op jit(solution)/shard_map/ppermute | solution.py:191

commit v14 on v13

--- a/solution.py
+++ b/solution.py
@@ -163,12 +163,13 @@
     return route
 
 
-RING_ROWS = (0, 1, 3, 5, 6, 7, 2, 4)
+CHIP_STEP_ROWS = (0, 2, 3, 1)
 
 
 def ring_row(partner, my_index):
     chip_step = ((partner >> 1) - (my_index >> 1)) % (GROUP // 2)
-    return jnp.asarray(RING_ROWS, jnp.int32)[chip_step * 2 + ((partner ^ my_index) & 1)]
+    other_core = (partner ^ my_index) & 1
+    return other_core * 4 + jnp.asarray(CHIP_STEP_ROWS, jnp.int32)[chip_step]
 
 
 def gather_group(block, my_index):
@@ -182,7 +183,7 @@
     )
     far_other = lax.ppermute(far, "resp", ring_route(lambda x, c: (x, 1 - c)))
     return jnp.concatenate(
-        [block, from_core, from_minus, from_plus, core_sides, far, far_other], 0
+        [block, from_minus, from_plus, far, from_core, core_sides, far_other], 0
     )
 
 
@@ -190,11 +191,8 @@
     def send(block, move):
         return lax.ppermute(block.astype(jnp.bfloat16), "resp", ring_route(move)).astype(jnp.float32)
 
-    from_core = send(terms[jnp.array([1, 4, 5, 7])], lambda x, c: (x, 1 - c))
-    own = terms[0] + from_core[0]
-    minus = terms[2] + from_core[1]
-    plus = terms[3] + from_core[2]
-    far = terms[6] + from_core[3]
+    kept = terms[:4] + send(terms[4:], lambda x, c: (x, 1 - c))
+    own, minus, plus, far = kept[0], kept[1], kept[2], kept[3]
     far_back = send(far, lambda x, c: (x + 1, c) if c == 0 else (x - 1, c))
     is_core0 = my_index % 2 == 0
     plus = plus + jnp.where(is_core0, far_back, 0.0)

time: 114 us -> 114 us (level)
  waiting for transfers between devices: 11.9 us -> 14.6 us
  local copies, waits for them, and re-layouts: 8.13 us -> 6.56 us
    ppermute x8, waiting for transfers between devices: 3.34 us -> 5.96 us  [send(): lax.ppermute(block.astype(jnp.bfloat16), 'resp', ring_route(move))]
    add x0 -> x3, other arithmetic: none -> 2.58 us  [the longest x2 1.4 us: return_group(): kept = terms[:4] + send(terms[4:], lambda x, c: (x, 1 - c))]
    gather x3 -> x1, local copies, waits for them, and re-layouts: 3.85 us -> 1.3 us  [ring_row(): return other_core * 4 + jnp.asarray(CHIP_STEP_ROWS, jnp.int32)[chip_step]]
    ppermute x2, starting transfers between devices: 3.48 us -> 1.24 us  [gather_group(): lax.ppermute(jnp.concatenate([from_minus, from_plus], 0), 'resp', ring_ro...]
    convert_element_type x4 -> x2, other arithmetic: 2.28 us -> 0.13 us  [send(): block.astype(jnp.bfloat16)]
    ppermute x2, starting transfers between devices: 0.93 us -> 2.19 us  [gather_group(): far_other = lax.ppermute(far, 'resp', ring_route(lambda x, c: (x, 1 - c)))]
    unnamed x30 -> x28, local copies, waits for them, and re-layouts: 3.98 us -> 3.97 us
  transfers between devices with their start and end apart: 23 -> 23, of which waited for: 9 -> 10; matrix products, arithmetic and copies ran while one was open for 9% -> 8% of each run, Pallas kernels for 0% -> 0%
where the time goes in v14:
time: 114 us; the launch traced here: 113 us
  Pallas kernels  43.8 us (38%)
  starting transfers between devices  35.8 us (31%)
  waiting for transfers between devices  14.6 us (13%)
  other arithmetic  10.9 us (10%)
  local copies, waits for them, and re-layouts  6.56 us (6%)
  between operations  1.63 us (1%)
    pallas_call x1, Pallas kernels, attention_backward(): pl.pallas_call(backward_kernel, grid_spec=pltpu.PrefetchScalarGridSpec(nu...  22.4 us
    pallas_call x1, Pallas kernels, attention_forward(): pl.pallas_call(forward_kernel, grid_spec=pltpu.PrefetchScalarGridSpec(num...  21.4 us
    ppermute x8, starting transfers between devices, send(): lax.ppermute(block.astype(jnp.bfloat16), 'resp', ring_route(move))  12.6 us
    ppermute x3, starting transfers between devices, exchange(): return lax.ppermute(block, axis, route)  11.2 us
    ppermute x8, waiting for transfers between devices, send(): lax.ppermute(block.astype(jnp.bfloat16), 'resp', ring_route(move))  5.96 us
    ppermute x2, starting transfers between devices, gather_group(): from_plus = lax.ppermute(block, 'resp', ring_route(lambda x, c: (x - 1, c)))  5.34 us
    ppermute x2, waiting for transfers between devices, gather_group(): lax.ppermute(relay, 'resp', ring_route(lambda x, c: (x - 1, c) if c == 0...  4.49 us
    unnamed x28, local copies, waits for them, and re-layouts  3.97 us
  transfers between devices with their start and end apart: 23, of which 10 were waited for; matrix products, arithmetic and copies ran while one was open for 8% of the time, Pallas kernels for 0%

profile of v14, /device:TPU:1, one launch (start us, length us, event | category | flops | bytes accessed | tf_op | source)
XLA Modules:
  0.0 113.3 jit_solution(2303254406935649973)
XLA Ops:
  0.6 3.4 %collective-permute-start.1 = (bf16[1,512,128]{2,1,0:T(8,128)(2,1)}, bf16[1,512,128]{2,1,0:T(8,128)(2,1)S(1)}, u32[]{:S(2)}, u32[]{:S(2)}) collective-permute-start(bf16[1,512,128]{2,1,0:T(8,128)(2,1)} %param.9), channel_id=1, source_target_pairs={{0,48},{8,56},{16,0},{24,8},{32,16},{40,24},{48,32},{56,40},{64,11... | collective-permute-start | bytes 393224 | tf_op jit(solution)/shard_map/ppermute | solution.py:177
  4.0 0.0 collective-permute-start
  4.0 2.0 %collective-permute-start.3 = (bf16[1,512,128]{2,1,0:T(8,128)(2,1)}, bf16[1,512,128]{2,1,0:T(8,128)(2,1)S(1)}, u32[]{:S(2)}, u32[]{:S(2)}) collective-permute-start(bf16[1,512,128]{2,1,0:T(8,128)(2,1)} %param.9), channel_id=1, source_target_pairs={{0,8},{8,0},{16,24},{24,16},{32,40},{40,32},{48,56},{56,48},{64,72... | collective-permute-start | bytes 393224 | tf_op jit(solution)/shard_map/ppermute | solution.py:178
  6.0 2.0 %collective-permute-start.7 = (bf16[1,512,128]{2,1,0:T(8,128)(2,1)}, bf16[1,512,128]{2,1,0:T(8,128)(2,1)S(1)}, u32[]{:S(2)}, u32[]{:S(2)}) collective-permute-start(bf16[1,512,128]{2,1,0:T(8,128)(2,1)} %param.10), channel_id=1, source_target_pairs={{0,48},{8,56},{16,0},{24,8},{32,16},{40,24},{48,32},{56,40},{64,11... | collective-permute-start | bytes 393224 | tf_op jit(solution)/shard_map/ppermute | solution.py:177
  7.9 0.0 collective-permute-start.6
  7.9 0.7 fusion.31
  8.6 1.3 %gather_fusion = s32[3]{0:T(128)S(1)} fusion(s32[4]{0:T(128)} %constant.57.clone, s32[1024]{0:T(1024)S(1)} %pad_clamp_fusion), kind=kCustom, calls=%fused_computation | custom fusion | bytes 36 | tf_op jit(solution)/shard_map/gather | solution.py:172
  9.9 1.2 %bitcast_add_fusion.1.rows_ref = s32[3]{0:T(128)} fusion(s32[3]{0:T(128)S(1)} %gather_fusion, s32[1,3]{1,0:T(1,128)} %param.11, s32[]{:T(128)S(6)} %axis_index.15), kind=kLoop, calls=%fused_computation.85 | loop fusion | flops 12 | bytes 40 | tf_op jit(solution)/shard_map/add | solution.py:172
  11.1 0.9 constant_dynamic-update-slice_fusion.6
  12.7 0.9 constant_dynamic-update-slice_fusion.13
  13.6 0.0 collective-permute-done.1
  13.6 0.4 collective-permute-start.9
  14.0 0.0 collective-permute-done
  14.0 0.3 collective-permute-start.4
  14.4 0.0 collective-permute-done.7
  14.4 0.1 collective-permute-start.2
  14.5 0.0 collective-permute-done.6
  14.5 0.1 broadcast_select_fusion
  14.5 0.9 collective-permute-start.8
  15.5 4.0 %collective-permute-done.2 = bf16[1,512,128]{2,1,0:T(8,128)(2,1)S(1)} collective-permute-done((bf16[1,512,128]{2,1,0:T(8,128)(2,1)S(1)}, bf16[1,512,128]{2,1,0:T(8,128)(2,1)S(1)}, u32[]{:S(2)}, u32[]{:S(2)}) %collective-permute-start.2) | collective-permute-done | bytes 131104 | tf_op jit(solution)/shard_map/ppermute | solution.py:180
  19.6 0.9 collective-permute-start.10
  20.5 0.5 collective-permute-done.8
  21.0 2.1 %collective-permute-start.5 = (bf16[1,512,128]{2,1,0:T(8,128)(2,1)S(1)}, bf16[1,512,128]{2,1,0:T(8,128)(2,1)S(1)}, u32[]{:S(2)}, u32[]{:S(2)}) collective-permute-start(bf16[1,512,128]{2,1,0:T(8,128)(2,1)S(1)} %collective-permute-done.2), channel_id=1, source_target_pairs={{0,8},{8,0},{16,24},{24,16},{32,40},{40,32},{48,56},{56,48},{64,72... | collective-permute-start | bytes 393224 | tf_op jit(solution)/shard_map/ppermute | solution.py:184
  23.1 0.0 collective-permute-done.3
  23.1 0.1 collective-permute-start.11
  23.3 0.7 collective-permute-done.5
  24.1 0.4 collective-permute-done.11
  24.6 0.5 copy-done
  25.1 0.4 copy-done.1
  25.5 21.4 %shard_map.111 = (bf16[512,1024]{1,0:T(8,128)(2,1)}, f32[8,1,512]{2,1,0:T(1,128)}) custom-call(s32[1]{0:T(128)S(6)} %copy.26.count_ref, s32[3]{0:T(128)} %bitcast_add_fusion.1.rows_ref, bf16[512,1024]{1,0:T(8,128)(2,1)} %bitcast.70, bf16[8,512,128]{2,1,0:T(8,128)(2,1)} %copy-done, bf16[8,512,128]{2,1,0:T(8,128)(2,1)} %copy-done, ...), custom_call_target="tpu_custom_call" | custom-call | tf_op jit(solution)/shard_map/pallas_call | solution.py:108
  47.0 1.9 %fusion = (f32[512]{0:T(512)S(1)}, f32[512]{0:T(512)S(1)}) fusion(bf16[512,1024]{1,0:T(8,128)(2,1)} %get-tuple-element.9.refs_7_, f32[1024]{0:T(1024)S(1)} %copy-done.7, bf16[1,512,1024]{2,1,0:T(8,128)(2,1)S(1)} %copy-done.4), kind=kLoop, calls=%fused_computation.7 | loop fusion | flops 3668992 | bytes 2105344 | tf_op jit(solution)/shard_map/reduce_sum | solution.py:221
  48.8 1.7 %collective-permute-start.12 = (f32[2,512]{1,0:T(2,128)S(1)}, f32[2,512]{1,0:T(2,128)S(1)}, u32[]{:S(2)}, u32[]{:S(2)}) collective-permute-start(f32[2,512]{1,0:T(2,128)S(1)} %pad_maximum_fusion.2), channel_id=1, source_target_pairs={{0,1},{1,0},{2,3},{3,2},{4,5},{5,4},{6,7},{7,6},{8,9},{9,8},{10,11... | collective-permute-start | bytes 12296 | tf_op jit(solution)/shard_map/ppermute | solution.py:153
  50.6 1.0 collective-permute-done.12
  51.6 3.3 %collective-permute-start.13 = (f32[2,512]{1,0:T(2,128)S(1)}, f32[2,512]{1,0:T(2,128)S(1)}, u32[]{:S(2)}, u32[]{:S(2)}) collective-permute-start(f32[2,512]{1,0:T(2,128)S(1)} %fusion.33), channel_id=1, source_target_pairs={{0,2},{1,3},{2,0},{3,1},{4,6},{5,7},{6,4},{7,5},{8,10},{9,11},{10,... | collective-permute-start | bytes 12296 | tf_op jit(solution)/shard_map/ppermute | solution.py:153
  54.8 1.0 collective-permute-done.13
  55.8 6.2 %collective-permute-start.14 = (f32[2,512]{1,0:T(2,128)S(1)}, f32[2,512]{1,0:T(2,128)S(1)}, u32[]{:S(2)}, u32[]{:S(2)}) collective-permute-start(f32[2,512]{1,0:T(2,128)S(1)} %fusion.35), channel_id=1, source_target_pairs={{0,4},{1,5},{2,6},{3,7},{4,0},{5,1},{6,2},{7,3},{8,12},{9,13},{10,... | collective-permute-start | bytes 12296 | tf_op jit(solution)/shard_map/ppermute | solution.py:153
  62.0 1.0 collective-permute-done.14
  63.1 2.0 %fusion.5 = (bf16[512,1024]{1,0:T(8,128)(2,1)}, bf16[1,512,1024]{2,1,0:T(8,128)(2,1)}) fusion(bf16[512,1024]{1,0:T(8,128)(2,1)S(1)} %copy-done.3, bf16[1,512,1024]{2,1,0:T(8,128)(2,1)S(1)} %copy-done.4, f32[512]{0:T(512)S(1)} %fusion.27, f32[512]{0:T(512)S(1)} %bitcast.79, f32[1024]{0:T(1024)S(1)} %copy-done.7), kind=kLoop, calls=%fused_computation.12 | loop fusion | flops 5242880 | bytes 4202496 | tf_op jit(solution)/shard_map/convert_element_type | solution.py:230
  65.1 22.4 %shard_map.112 = (bf16[512,1024]{1,0:T(8,128)(2,1)}, f32[3,512,128]{2,1,0:T(8,128)}, f32[3,512,128]{2,1,0:T(8,128)}) custom-call(s32[1]{0:T(128)S(6)} %copy.26.count_ref, s32[3]{0:T(128)} %bitcast_add_fusion.1.rows_ref, bf16[512,1024]{1,0:T(8,128)(2,1)} %bitcast.71, bf16[8,512,128]{2,1,0:T(8,128)(2,1)} %copy-done, bf16[8,512,128]{2,1,0:T(8,128)(2,1)} %copy-done, ...), custom_call_target="tpu_custom_call" | custom-call | tf_op jit(solution)/shard_map/pallas_call | solution.py:131
  87.4 0.1 broadcast_in_dim.16.clone
  87.6 1.0 copy-done.6
  88.6 1.0 scatter_fusion
  89.6 0.9 slice.122
  90.5 3.4 %collective-permute-start.15 = (bf16[4,512,128]{2,1,0:T(8,128)(2,1)}, bf16[4,512,128]{2,1,0:T(8,128)(2,1)S(1)}, u32[]{:S(2)}, u32[]{:S(2)}) collective-permute-start(bf16[4,512,128]{2,1,0:T(8,128)(2,1)} %slice.122), channel_id=1, source_target_pairs={{0,8},{8,0},{16,24},{24,16},{32,40},{40,32},{48,56},{56,48},{64,72... | collective-permute-start | bytes 1572872 | tf_op jit(solution)/shard_map/ppermute | solution.py:192
  93.9 0.1 broadcast_in_dim.16.clone.1
  94.1 1.0 scatter_fusion.1
  95.1 0.1 slice.121
  95.1 0.7 collective-permute-start.19
  95.9 1.3 %slice_add_fusion.1 = f32[4,512,128]{2,1,0:T(8,128)S(1)} fusion(f32[8,512,128]{2,1,0:T(8,128)} %copy-done.2, bf16[4,512,128]{2,1,0:T(8,128)(2,1)S(1)} %collective-permute-done.15), kind=kLoop, calls=%fused_computation.19 | loop fusion | flops 524288 | bytes 2621440 | tf_op jit(solution)/shard_map/add | solution.py:194
  97.2 2.3 %collective-permute-start.16 = (bf16[512,128]{1,0:T(8,128)(2,1)S(1)}, bf16[512,128]{1,0:T(8,128)(2,1)S(1)}, u32[]{:S(2)}, u32[]{:S(2)}) collective-permute-start(bf16[512,128]{1,0:T(8,128)(2,1)S(1)} %fusion.23), channel_id=1, source_target_pairs={{0,16},{8,56},{16,32},{24,8},{32,48},{40,24},{48,0},{56,40},{64,80... | collective-permute-start | bytes 393224 | tf_op jit(solution)/shard_map/ppermute | solution.py:192
  99.5 0.0 collective-permute-done.19
  99.5 0.1 slice_add_fusion
  99.6 0.2 collective-permute-start.20
  99.8 1.6 %collective-permute-done.16 = bf16[512,128]{1,0:T(8,128)(2,1)S(1)} collective-permute-done((bf16[512,128]{1,0:T(8,128)(2,1)S(1)}, bf16[512,128]{1,0:T(8,128)(2,1)S(1)}, u32[]{:S(2)}, u32[]{:S(2)}) %collective-permute-start.16) | collective-permute-done | bytes 131104 | tf_op jit(solution)/shard_map/ppermute | solution.py:192
  101.5 0.1 fusion.9
  101.5 3.2 %collective-permute-start.17 = (bf16[512,128]{1,0:T(8,128)(2,1)S(1)}, bf16[512,128]{1,0:T(8,128)(2,1)S(1)}, u32[]{:S(2)}, u32[]{:S(2)}) collective-permute-start(bf16[512,128]{1,0:T(8,128)(2,1)S(1)} %get-tuple-element.18), channel_id=1, source_target_pairs={{0,48},{8,56},{16,0},{24,8},{32,16},{40,24},{48,32},{56,40},{64,11... | collective-permute-start | bytes 393224 | tf_op jit(solution)/shard_map/ppermute | solution.py:192
  104.7 0.1 fusion.13
  104.8 2.8 %collective-permute-start.21 = (bf16[512,128]{1,0:T(8,128)(2,1)S(1)}, bf16[512,128]{1,0:T(8,128)(2,1)S(1)}, u32[]{:S(2)}, u32[]{:S(2)}) collective-permute-start(bf16[512,128]{1,0:T(8,128)(2,1)S(1)} %get-tuple-element.16), channel_id=1, source_target_pairs={{0,48},{8,56},{16,0},{24,8},{32,16},{40,24},{48,32},{56,40},{64,11... | collective-permute-start | bytes 393224 | tf_op jit(solution)/shard_map/ppermute | solution.py:192
  107.5 0.0 collective-permute-done.17
  107.5 3.1 %collective-permute-done.18 = bf16[512,128]{1,0:T(8,128)(2,1)S(1)} collective-permute-done((bf16[512,128]{1,0:T(8,128)(2,1)S(1)}, bf16[512,128]{1,0:T(8,128)(2,1)S(1)}, u32[]{:S(2)}, u32[]{:S(2)}) %collective-permute-start.18) | collective-permute-done | bytes 131104 | tf_op jit(solution)/shard_map/ppermute | solution.py:192
  110.6 0.7 fusion.22
  111.3 0.0 collective-permute-done.21
  111.3 1.2 %collective-permute-done.22 = bf16[512,128]{1,0:T(8,128)(2,1)S(1)} collective-permute-done((bf16[512,128]{1,0:T(8,128)(2,1)S(1)}, bf16[512,128]{1,0:T(8,128)(2,1)S(1)}, u32[]{:S(2)}, u32[]{:S(2)}) %collective-permute-start.22) | collective-permute-done | bytes 131104 | tf_op jit(solution)/shard_map/ppermute | solution.py:192
  112.5 0.7 fusion.24
  (45 shorter events, 0.5 us)
Async XLA Ops:
  0.6 12.9 %collective-permute-start.1 = (bf16[1,512,128]{2,1,0:T(8,128)(2,1)}, bf16[1,512,128]{2,1,0:T(8,128)(2,1)S(1)}, u32[]{:S(2)}, u32[]{:S(2)}) collective-permute-start(bf16[1,512,128]{2,1,0:T(8,128)(2,1)} %param.9), channel_id=1, source_target_pairs={{0,48},{8,56},{16,0},{24,8},{32,16},{40,24},{48,32},{56,40},{64,11... | collective-permute-start | bytes 393224 | tf_op jit(solution)/shard_map/ppermute | solution.py:177
  4.0 9.9 %collective-permute-start = (bf16[1,512,128]{2,1,0:T(8,128)(2,1)}, bf16[1,512,128]{2,1,0:T(8,128)(2,1)S(1)}, u32[]{:S(2)}, u32[]{:S(2)}) collective-permute-start(bf16[1,512,128]{2,1,0:T(8,128)(2,1)} %param.9), channel_id=1, source_target_pairs={{0,16},{8,24},{16,32},{24,40},{32,48},{40,56},{48,0},{56,8},{64,80... | collective-permute-start | bytes 393224 | tf_op jit(solution)/shard_map/ppermute | solution.py:176
  4.0 19.1 %collective-permute-start.3 = (bf16[1,512,128]{2,1,0:T(8,128)(2,1)}, bf16[1,512,128]{2,1,0:T(8,128)(2,1)S(1)}, u32[]{:S(2)}, u32[]{:S(2)}) collective-permute-start(bf16[1,512,128]{2,1,0:T(8,128)(2,1)} %param.9), channel_id=1, source_target_pairs={{0,8},{8,0},{16,24},{24,16},{32,40},{40,32},{48,56},{56,48},{64,72... | collective-permute-start | bytes 393224 | tf_op jit(solution)/shard_map/ppermute | solution.py:178
  6.0 8.4 %collective-permute-start.7 = (bf16[1,512,128]{2,1,0:T(8,128)(2,1)}, bf16[1,512,128]{2,1,0:T(8,128)(2,1)S(1)}, u32[]{:S(2)}, u32[]{:S(2)}) collective-permute-start(bf16[1,512,128]{2,1,0:T(8,128)(2,1)} %param.10), channel_id=1, source_target_pairs={{0,48},{8,56},{16,0},{24,8},{32,16},{40,24},{48,32},{56,40},{64,11... | collective-permute-start | bytes 393224 | tf_op jit(solution)/shard_map/ppermute | solution.py:177
  7.9 6.5 %collective-permute-start.6 = (bf16[1,512,128]{2,1,0:T(8,128)(2,1)}, bf16[1,512,128]{2,1,0:T(8,128)(2,1)S(1)}, u32[]{:S(2)}, u32[]{:S(2)}) collective-permute-start(bf16[1,512,128]{2,1,0:T(8,128)(2,1)} %param.10), channel_id=1, source_target_pairs={{0,16},{8,24},{16,32},{24,40},{32,48},{40,56},{48,0},{56,8},{64,80... | collective-permute-start | bytes 393224 | tf_op jit(solution)/shard_map/ppermute | solution.py:176
  13.6 9.6 %collective-permute-start.9 = (bf16[1,512,128]{2,1,0:T(8,128)(2,1)}, bf16[1,512,128]{2,1,0:T(8,128)(2,1)S(1)}, u32[]{:S(2)}, u32[]{:S(2)}) collective-permute-start(bf16[1,512,128]{2,1,0:T(8,128)(2,1)} %param.10), channel_id=1, source_target_pairs={{0,8},{8,0},{16,24},{24,16},{32,40},{40,32},{48,56},{56,48},{64,72... | collective-permute-start | bytes 393224 | tf_op jit(solution)/shard_map/ppermute | solution.py:178
  14.0 9.3 %collective-permute-start.4 = (bf16[2,512,128]{2,1,0:T(8,128)(2,1)S(1)}, bf16[2,512,128]{2,1,0:T(8,128)(2,1)S(1)}, u32[]{:S(2)}, u32[]{:S(2)}) collective-permute-start(bf16[2,512,128]{2,1,0:T(8,128)(2,1)S(1)} %pad_maximum_fusion), channel_id=1, source_target_pairs={{0,8},{8,0},{16,24},{24,16},{32,40},{40,32},{48,56},{56,48},{64,72... | collective-permute-start | bytes 786440 | tf_op jit(solution)/shard_map/ppermute | solution.py:181
  14.4 5.2 %collective-permute-start.2 = (bf16[1,512,128]{2,1,0:T(8,128)(2,1)S(1)}, bf16[1,512,128]{2,1,0:T(8,128)(2,1)S(1)}, u32[]{:S(2)}, u32[]{:S(2)}) collective-permute-start(bf16[1,512,128]{2,1,0:T(8,128)(2,1)S(1)} %get-tuple-element.24), channel_id=1, source_target_pairs={{0,48},{8,24},{16,0},{24,40},{32,16},{40,56},{48,32},{56,8},{64,11... | collective-permute-start | bytes 393224 | tf_op jit(solution)/shard_map/ppermute | solution.py:180
  14.5 6.4 %collective-permute-start.8 = (bf16[1,512,128]{2,1,0:T(8,128)(2,1)S(1)}, bf16[1,512,128]{2,1,0:T(8,128)(2,1)S(1)}, u32[]{:S(2)}, u32[]{:S(2)}) collective-permute-start(bf16[1,512,128]{2,1,0:T(8,128)(2,1)S(1)} %get-tuple-element.22), channel_id=1, source_target_pairs={{0,48},{8,24},{16,0},{24,40},{32,16},{40,56},{48,32},{56,8},{64,11... | collective-permute-start | bytes 393224 | tf_op jit(solution)/shard_map/ppermute | solution.py:180
  19.6 4.5 %collective-permute-start.10 = (bf16[2,512,128]{2,1,0:T(8,128)(2,1)S(1)}, bf16[2,512,128]{2,1,0:T(8,128)(2,1)S(1)}, u32[]{:S(2)}, u32[]{:S(2)}) collective-permute-start(bf16[2,512,128]{2,1,0:T(8,128)(2,1)S(1)} %pad_maximum_fusion.1), channel_id=1, source_target_pairs={{0,8},{8,0},{16,24},{24,16},{32,40},{40,32},{48,56},{56,48},{64,72... | collective-permute-start | bytes 786440 | tf_op jit(solution)/shard_map/ppermute | solution.py:181
  21.0 3.1 %collective-permute-start.5 = (bf16[1,512,128]{2,1,0:T(8,128)(2,1)S(1)}, bf16[1,512,128]{2,1,0:T(8,128)(2,1)S(1)}, u32[]{:S(2)}, u32[]{:S(2)}) collective-permute-start(bf16[1,512,128]{2,1,0:T(8,128)(2,1)S(1)} %collective-permute-done.2), channel_id=1, source_target_pairs={{0,8},{8,0},{16,24},{24,16},{32,40},{40,32},{48,56},{56,48},{64,72... | collective-permute-start | bytes 393224 | tf_op jit(solution)/shard_map/ppermute | solution.py:184
  23.1 1.4 %collective-permute-start.11 = (bf16[1,512,128]{2,1,0:T(8,128)(2,1)S(1)}, bf16[1,512,128]{2,1,0:T(8,128)(2,1)S(1)}, u32[]{:S(2)}, u32[]{:S(2)}) collective-permute-start(bf16[1,512,128]{2,1,0:T(8,128)(2,1)S(1)} %collective-permute-done.8), channel_id=1, source_target_pairs={{0,8},{8,0},{16,24},{24,16},{32,40},{40,32},{48,56},{56,48},{64,72... | collective-permute-start | bytes 393224 | tf_op jit(solution)/shard_map/ppermute | solution.py:184
  24.1 1.0 copy-start
  24.5 1.0 copy-start.1
  25.5 21.4 %copy-start.4 = (bf16[1,512,1024]{2,1,0:T(8,128)(2,1)S(1)}, bf16[1,512,1024]{2,1,0:T(8,128)(2,1)}, u32[]{:S(2)}) copy-start(bf16[1,512,1024]{2,1,0:T(8,128)(2,1)} %param.14) | copy-start | bytes 3145732
  25.5 21.4 %copy-start.7 = (f32[1024]{0:T(1024)S(1)}, f32[1024]{0:T(1024)}, u32[]{:S(2)}) copy-start(f32[1024]{0:T(1024)} %param.13) | copy-start | bytes 12292
  46.9 15.1 %copy-start.8 = (s32[1,3]{1,0:T(1,128)S(1)}, s32[1,3]{1,0:T(1,128)}, u32[]{:S(2)}) copy-start(s32[1,3]{1,0:T(1,128)} %param.11) | copy-start | bytes 40
  46.9 16.1 %copy-start.3 = (bf16[512,1024]{1,0:T(8,128)(2,1)S(1)}, bf16[512,1024]{1,0:T(8,128)(2,1)}, u32[]{:S(2)}) copy-start(bf16[512,1024]{1,0:T(8,128)(2,1)} %get-tuple-element.9.refs_7_) | copy-start | bytes 3145732
  48.8 2.7 %collective-permute-start.12 = (f32[2,512]{1,0:T(2,128)S(1)}, f32[2,512]{1,0:T(2,128)S(1)}, u32[]{:S(2)}, u32[]{:S(2)}) collective-permute-start(f32[2,512]{1,0:T(2,128)S(1)} %pad_maximum_fusion.2), channel_id=1, source_target_pairs={{0,1},{1,0},{2,3},{3,2},{4,5},{5,4},{6,7},{7,6},{8,9},{9,8},{10,11... | collective-permute-start | bytes 12296 | tf_op jit(solution)/shard_map/ppermute | solution.py:153
  51.6 4.3 %collective-permute-start.13 = (f32[2,512]{1,0:T(2,128)S(1)}, f32[2,512]{1,0:T(2,128)S(1)}, u32[]{:S(2)}, u32[]{:S(2)}) collective-permute-start(f32[2,512]{1,0:T(2,128)S(1)} %fusion.33), channel_id=1, source_target_pairs={{0,2},{1,3},{2,0},{3,1},{4,6},{5,7},{6,4},{7,5},{8,10},{9,11},{10,... | collective-permute-start | bytes 12296 | tf_op jit(solution)/shard_map/ppermute | solution.py:153
  55.8 7.2 %collective-permute-start.14 = (f32[2,512]{1,0:T(2,128)S(1)}, f32[2,512]{1,0:T(2,128)S(1)}, u32[]{:S(2)}, u32[]{:S(2)}) collective-permute-start(f32[2,512]{1,0:T(2,128)S(1)} %fusion.35), channel_id=1, source_target_pairs={{0,4},{1,5},{2,6},{3,7},{4,0},{5,1},{6,2},{7,3},{8,12},{9,13},{10,... | collective-permute-start | bytes 12296 | tf_op jit(solution)/shard_map/ppermute | solution.py:153
  87.4 1.1 %copy-start.6 = (f32[3,512,128]{2,1,0:T(8,128)S(1)}, f32[3,512,128]{2,1,0:T(8,128)}, u32[]{:S(2)}) copy-start(f32[3,512,128]{2,1,0:T(8,128)} %get-tuple-element.12) | copy-start | bytes 2359300
  89.6 4.3 %copy-start.2 = (f32[8,512,128]{2,1,0:T(8,128)}, f32[8,512,128]{2,1,0:T(8,128)S(1)}, u32[]{:S(2)}) copy-start(f32[8,512,128]{2,1,0:T(8,128)S(1)} %scatter_fusion) | copy-start | bytes 6291460
  89.6 4.5 %copy-start.5 = (f32[3,512,128]{2,1,0:T(8,128)S(1)}, f32[3,512,128]{2,1,0:T(8,128)}, u32[]{:S(2)}) copy-start(f32[3,512,128]{2,1,0:T(8,128)} %get-tuple-element.13) | copy-start | bytes 2359300
  90.5 5.4 %collective-permute-start.15 = (bf16[4,512,128]{2,1,0:T(8,128)(2,1)}, bf16[4,512,128]{2,1,0:T(8,128)(2,1)S(1)}, u32[]{:S(2)}, u32[]{:S(2)}) collective-permute-start(bf16[4,512,128]{2,1,0:T(8,128)(2,1)} %slice.122), channel_id=1, source_target_pairs={{0,8},{8,0},{16,24},{24,16},{32,40},{40,32},{48,56},{56,48},{64,72... | collective-permute-start | bytes 1572872 | tf_op jit(solution)/shard_map/ppermute | solution.py:192
  95.1 4.4 %collective-permute-start.19 = (bf16[4,512,128]{2,1,0:T(8,128)(2,1)S(1)}, bf16[4,512,128]{2,1,0:T(8,128)(2,1)S(1)}, u32[]{:S(2)}, u32[]{:S(2)}) collective-permute-start(bf16[4,512,128]{2,1,0:T(8,128)(2,1)S(1)} %slice.121), channel_id=1, source_target_pairs={{0,8},{8,0},{16,24},{24,16},{32,40},{40,32},{48,56},{56,48},{64,72... | collective-permute-start | bytes 1572872 | tf_op jit(solution)/shard_map/ppermute | solution.py:192
  97.2 4.2 %collective-permute-start.16 = (bf16[512,128]{1,0:T(8,128)(2,1)S(1)}, bf16[512,128]{1,0:T(8,128)(2,1)S(1)}, u32[]{:S(2)}, u32[]{:S(2)}) collective-permute-start(bf16[512,128]{1,0:T(8,128)(2,1)S(1)} %fusion.23), channel_id=1, source_target_pairs={{0,16},{8,56},{16,32},{24,8},{32,48},{40,24},{48,0},{56,40},{64,80... | collective-permute-start | bytes 393224 | tf_op jit(solution)/shard_map/ppermute | solution.py:192
  99.6 5.1 %collective-permute-start.20 = (bf16[512,128]{1,0:T(8,128)(2,1)S(1)}, bf16[512,128]{1,0:T(8,128)(2,1)S(1)}, u32[]{:S(2)}, u32[]{:S(2)}) collective-permute-start(bf16[512,128]{1,0:T(8,128)(2,1)S(1)} %fusion.25), channel_id=1, source_target_pairs={{0,16},{8,56},{16,32},{24,8},{32,48},{40,24},{48,0},{56,40},{64,80... | collective-permute-start | bytes 393224 | tf_op jit(solution)/shard_map/ppermute | solution.py:192
  101.5 6.0 %collective-permute-start.17 = (bf16[512,128]{1,0:T(8,128)(2,1)S(1)}, bf16[512,128]{1,0:T(8,128)(2,1)S(1)}, u32[]{:S(2)}, u32[]{:S(2)}) collective-permute-start(bf16[512,128]{1,0:T(8,128)(2,1)S(1)} %get-tuple-element.18), channel_id=1, source_target_pairs={{0,48},{8,56},{16,0},{24,8},{32,16},{40,24},{48,32},{56,40},{64,11... | collective-permute-start | bytes 393224 | tf_op jit(solution)/shard_map/ppermute | solution.py:192
  104.7 5.9 %collective-permute-start.18 = (bf16[512,128]{1,0:T(8,128)(2,1)S(1)}, bf16[512,128]{1,0:T(8,128)(2,1)S(1)}, u32[]{:S(2)}, u32[]{:S(2)}) collective-permute-start(bf16[512,128]{1,0:T(8,128)(2,1)S(1)} %get-tuple-element.19), channel_id=1, source_target_pairs={{0,16},{8,24},{16,32},{24,40},{32,48},{40,56},{48,0},{56,8},{64,80... | collective-permute-start | bytes 393224 | tf_op jit(solution)/shard_map/ppermute | solution.py:192
  104.8 6.6 %collective-permute-start.21 = (bf16[512,128]{1,0:T(8,128)(2,1)S(1)}, bf16[512,128]{1,0:T(8,128)(2,1)S(1)}, u32[]{:S(2)}, u32[]{:S(2)}) collective-permute-start(bf16[512,128]{1,0:T(8,128)(2,1)S(1)} %get-tuple-element.16), channel_id=1, source_target_pairs={{0,48},{8,56},{16,0},{24,8},{32,16},{40,24},{48,32},{56,40},{64,11... | collective-permute-start | bytes 393224 | tf_op jit(solution)/shard_map/ppermute | solution.py:192
  107.5 5.0 %collective-permute-start.22 = (bf16[512,128]{1,0:T(8,128)(2,1)S(1)}, bf16[512,128]{1,0:T(8,128)(2,1)S(1)}, u32[]{:S(2)}, u32[]{:S(2)}) collective-permute-start(bf16[512,128]{1,0:T(8,128)(2,1)S(1)} %get-tuple-element.17), channel_id=1, source_target_pairs={{0,16},{8,24},{16,32},{24,40},{32,48},{40,56},{48,0},{56,8},{64,80... | collective-permute-start | bytes 393224 | tf_op jit(solution)/shard_map/ppermute | solution.py:192

commit v15 on v14

--- a/solution.py
+++ b/solution.py
@@ -201,9 +201,11 @@
 
 
 def head_sum(row_part):
-    for bit in range(lax.axis_size("head").bit_length() - 1):
-        row_part = row_part + exchange(row_part, "head", bit)
-    return row_part
+    heads = lax.axis_size("head")
+    quad = row_part
+    for distance in range(1, 4):
+        quad = quad + lax.ppermute(row_part, "head", [(low, low ^ distance) for low in range(heads)])
+    return quad + lax.ppermute(quad, "head", [(low, low ^ 4) for low in range(heads)])
 
 
 def body(queries, key_states, value_states, partners, counts, norm_gain, out_grad):

time: 114 us -> 113 us (level)
  starting transfers between devices: 35.8 us -> 34 us
    ppermute x3 -> x4, starting transfers between devices: 11.2 us -> 9.91 us  [the longest x1 5.2 us: head_sum(): lax.ppermute(quad, 'head', [(low, low ^ 4) for low in range(heads)])]
    ppermute x3 -> x4, waiting for transfers between devices: 2.98 us -> 3.86 us  [the longest x3 2.62 us: head_sum(): lax.ppermute(row_part, 'head', [(low, low ^ distance) for low in range(he...]
  transfers between devices with their start and end apart: 23 -> 24, of which waited for: 10 -> 9; matrix products, arithmetic and copies ran while one was open for 8% -> 8% of each run, Pallas kernels for 0% -> 0%
where the time goes in v15:
time: 113 us; the launch traced here: 112 us
  Pallas kernels  43.8 us (39%)
  starting transfers between devices  34 us (30%)
  waiting for transfers between devices  15.5 us (14%)
  other arithmetic  10.9 us (10%)
  local copies, waits for them, and re-layouts  6.57 us (6%)
  between operations  1.63 us (1%)
    pallas_call x1, Pallas kernels, attention_backward(): pl.pallas_call(backward_kernel, grid_spec=pltpu.PrefetchScalarGridSpec(nu...  22.4 us
    pallas_call x1, Pallas kernels, attention_forward(): pl.pallas_call(forward_kernel, grid_spec=pltpu.PrefetchScalarGridSpec(num...  21.4 us
    ppermute x8, starting transfers between devices, send(): lax.ppermute(block.astype(jnp.bfloat16), 'resp', ring_route(move))  12 us
    ppermute x8, waiting for transfers between devices, send(): lax.ppermute(block.astype(jnp.bfloat16), 'resp', ring_route(move))  5.96 us
    ppermute x2, starting transfers between devices, gather_group(): from_plus = lax.ppermute(block, 'resp', ring_route(lambda x, c: (x - 1, c)))  5.34 us
    ppermute x1, starting transfers between devices, head_sum(): lax.ppermute(quad, 'head', [(low, low ^ 4) for low in range(heads)])  5.2 us
    ppermute x3, starting transfers between devices, head_sum(): lax.ppermute(row_part, 'head', [(low, low ^ distance) for low in range(he...  4.71 us
    ppermute x2, waiting for transfers between devices, gather_group(): lax.ppermute(relay, 'resp', ring_route(lambda x, c: (x - 1, c) if c == 0...  4.49 us
  transfers between devices with their start and end apart: 24, of which 9 were waited for; matrix products, arithmetic and copies ran while one was open for 8% of the time, Pallas kernels for 0%

profile of v15, /device:TPU:1, one launch (start us, length us, event | category | flops | bytes accessed | tf_op | source)
XLA Modules:
  0.0 112.3 jit_solution(8475015746956042641)
XLA Ops:
  0.6 3.4 %collective-permute-start.1 = (bf16[1,512,128]{2,1,0:T(8,128)(2,1)}, bf16[1,512,128]{2,1,0:T(8,128)(2,1)S(1)}, u32[]{:S(2)}, u32[]{:S(2)}) collective-permute-start(bf16[1,512,128]{2,1,0:T(8,128)(2,1)} %param.9), channel_id=1, source_target_pairs={{0,48},{8,56},{16,0},{24,8},{32,16},{40,24},{48,32},{56,40},{64,11... | collective-permute-start | bytes 393224 | tf_op jit(solution)/shard_map/ppermute | solution.py:177
  4.0 0.0 collective-permute-start
  4.0 2.0 %collective-permute-start.3 = (bf16[1,512,128]{2,1,0:T(8,128)(2,1)}, bf16[1,512,128]{2,1,0:T(8,128)(2,1)S(1)}, u32[]{:S(2)}, u32[]{:S(2)}) collective-permute-start(bf16[1,512,128]{2,1,0:T(8,128)(2,1)} %param.9), channel_id=1, source_target_pairs={{0,8},{8,0},{16,24},{24,16},{32,40},{40,32},{48,56},{56,48},{64,72... | collective-permute-start | bytes 393224 | tf_op jit(solution)/shard_map/ppermute | solution.py:178
  6.0 2.0 %collective-permute-start.7 = (bf16[1,512,128]{2,1,0:T(8,128)(2,1)}, bf16[1,512,128]{2,1,0:T(8,128)(2,1)S(1)}, u32[]{:S(2)}, u32[]{:S(2)}) collective-permute-start(bf16[1,512,128]{2,1,0:T(8,128)(2,1)} %param.10), channel_id=1, source_target_pairs={{0,48},{8,56},{16,0},{24,8},{32,16},{40,24},{48,32},{56,40},{64,11... | collective-permute-start | bytes 393224 | tf_op jit(solution)/shard_map/ppermute | solution.py:177
  7.9 0.0 collective-permute-start.6
  7.9 0.7 fusion.31
  8.6 1.3 %gather_fusion = s32[3]{0:T(128)S(1)} fusion(s32[4]{0:T(128)} %constant.57.clone, s32[1024]{0:T(1024)S(1)} %pad_clamp_fusion), kind=kCustom, calls=%fused_computation | custom fusion | bytes 36 | tf_op jit(solution)/shard_map/gather | solution.py:172
  9.9 1.2 %bitcast_add_fusion.1.rows_ref = s32[3]{0:T(128)} fusion(s32[3]{0:T(128)S(1)} %gather_fusion, s32[1,3]{1,0:T(1,128)} %param.11, s32[]{:T(128)S(6)} %axis_index.15), kind=kLoop, calls=%fused_computation.86 | loop fusion | flops 12 | bytes 40 | tf_op jit(solution)/shard_map/add | solution.py:172
  11.1 0.9 constant_dynamic-update-slice_fusion.6
  12.7 0.9 constant_dynamic-update-slice_fusion.13
  13.6 0.4 collective-permute-start.9
  14.0 0.3 collective-permute-start.4
  14.4 0.0 collective-permute-done.7
  14.4 0.1 collective-permute-start.2
  14.5 0.0 collective-permute-done.6
  14.5 0.1 broadcast_select_fusion
  14.5 0.9 collective-permute-start.8
  15.5 4.0 %collective-permute-done.2 = bf16[1,512,128]{2,1,0:T(8,128)(2,1)S(1)} collective-permute-done((bf16[1,512,128]{2,1,0:T(8,128)(2,1)S(1)}, bf16[1,512,128]{2,1,0:T(8,128)(2,1)S(1)}, u32[]{:S(2)}, u32[]{:S(2)}) %collective-permute-start.2) | collective-permute-done | bytes 131104 | tf_op jit(solution)/shard_map/ppermute | solution.py:180
  19.6 0.9 collective-permute-start.10
  20.5 0.5 collective-permute-done.8
  21.0 2.1 %collective-permute-start.5 = (bf16[1,512,128]{2,1,0:T(8,128)(2,1)S(1)}, bf16[1,512,128]{2,1,0:T(8,128)(2,1)S(1)}, u32[]{:S(2)}, u32[]{:S(2)}) collective-permute-start(bf16[1,512,128]{2,1,0:T(8,128)(2,1)S(1)} %collective-permute-done.2), channel_id=1, source_target_pairs={{0,8},{8,0},{16,24},{24,16},{32,40},{40,32},{48,56},{56,48},{64,72... | collective-permute-start | bytes 393224 | tf_op jit(solution)/shard_map/ppermute | solution.py:184
  23.1 0.0 collective-permute-done.3
  23.1 0.1 collective-permute-start.11
  23.2 0.0 collective-permute-done.9
  23.3 0.0 collective-permute-done.4
  23.3 0.7 collective-permute-done.5
  24.1 0.0 collective-permute-done.10
  24.1 0.4 collective-permute-done.11
  24.6 0.5 copy-done
  25.1 0.5 copy-done.1
  25.5 21.4 %shard_map.111 = (bf16[512,1024]{1,0:T(8,128)(2,1)}, f32[8,1,512]{2,1,0:T(1,128)}) custom-call(s32[1]{0:T(128)S(6)} %copy.26.count_ref, s32[3]{0:T(128)} %bitcast_add_fusion.1.rows_ref, bf16[512,1024]{1,0:T(8,128)(2,1)} %bitcast.70, bf16[8,512,128]{2,1,0:T(8,128)(2,1)} %copy-done, bf16[8,512,128]{2,1,0:T(8,128)(2,1)} %copy-done, ...), custom_call_target="tpu_custom_call" | custom-call | tf_op jit(solution)/shard_map/pallas_call | solution.py:108
  47.0 1.9 %fusion = (f32[512]{0:T(512)S(1)}, f32[512]{0:T(512)S(1)}) fusion(bf16[512,1024]{1,0:T(8,128)(2,1)} %get-tuple-element.9.refs_7_, f32[1024]{0:T(1024)S(1)} %copy-done.7, bf16[1,512,1024]{2,1,0:T(8,128)(2,1)S(1)} %copy-done.4), kind=kLoop, calls=%fused_computation.7 | loop fusion | flops 3668992 | bytes 2105344 | tf_op jit(solution)/shard_map/reduce_sum | solution.py:223
  48.9 3.1 %collective-permute-start.13 = (f32[2,512]{1,0:T(2,128)S(1)}, f32[2,512]{1,0:T(2,128)S(1)}, u32[]{:S(2)}, u32[]{:S(2)}) collective-permute-start(f32[2,512]{1,0:T(2,128)S(1)} %pad_maximum_fusion.2), channel_id=1, source_target_pairs={{0,2},{1,3},{2,0},{3,1},{4,6},{5,7},{6,4},{7,5},{8,10},{9,11},{10,... | collective-permute-start | bytes 12296 | tf_op jit(solution)/shard_map/ppermute | solution.py:207
  51.9 1.6 %collective-permute-start.14 = (f32[2,512]{1,0:T(2,128)S(1)}, f32[2,512]{1,0:T(2,128)S(1)}, u32[]{:S(2)}, u32[]{:S(2)}) collective-permute-start(f32[2,512]{1,0:T(2,128)S(1)} %pad_maximum_fusion.2), channel_id=1, source_target_pairs={{0,3},{1,2},{2,1},{3,0},{4,7},{5,6},{6,5},{7,4},{8,11},{9,10},{10,... | collective-permute-start | bytes 12296 | tf_op jit(solution)/shard_map/ppermute | solution.py:207
  53.6 0.0 collective-permute-start.12
  53.6 0.0 collective-permute-done.13
  53.6 2.6 %collective-permute-done.14 = f32[2,512]{1,0:T(2,128)S(1)} collective-permute-done((f32[2,512]{1,0:T(2,128)S(1)}, f32[2,512]{1,0:T(2,128)S(1)}, u32[]{:S(2)}, u32[]{:S(2)}) %collective-permute-start.14) | collective-permute-done | bytes 4128 | tf_op jit(solution)/shard_map/ppermute | solution.py:207
  56.2 5.2 %collective-permute-start.15 = (f32[2,512]{1,0:T(2,128)S(1)}, f32[2,512]{1,0:T(2,128)S(1)}, u32[]{:S(2)}, u32[]{:S(2)}) collective-permute-start(f32[2,512]{1,0:T(2,128)S(1)} %add_add_fusion), channel_id=1, source_target_pairs={{0,4},{1,5},{2,6},{3,7},{4,0},{5,1},{6,2},{7,3},{8,12},{9,13},{10,... | collective-permute-start | bytes 12296 | tf_op jit(solution)/shard_map/ppermute | solution.py:208
  61.4 1.2 %collective-permute-done.15 = f32[2,512]{1,0:T(2,128)S(1)} collective-permute-done((f32[2,512]{1,0:T(2,128)S(1)}, f32[2,512]{1,0:T(2,128)S(1)}, u32[]{:S(2)}, u32[]{:S(2)}) %collective-permute-start.15) | collective-permute-done | bytes 4128 | tf_op jit(solution)/shard_map/ppermute | solution.py:208
  62.7 2.0 %fusion.5 = (bf16[512,1024]{1,0:T(8,128)(2,1)}, bf16[1,512,1024]{2,1,0:T(8,128)(2,1)}) fusion(bf16[512,1024]{1,0:T(8,128)(2,1)S(1)} %copy-done.3, bf16[1,512,1024]{2,1,0:T(8,128)(2,1)S(1)} %copy-done.4, f32[512]{0:T(512)S(1)} %fusion.27, f32[512]{0:T(512)S(1)} %bitcast.73, f32[1024]{0:T(1024)S(1)} %copy-done.7), kind=kLoop, calls=%fused_computation.12 | loop fusion | flops 5242880 | bytes 4202496 | tf_op jit(solution)/shard_map/convert_element_type | solution.py:232
  64.7 22.4 %shard_map.112 = (bf16[512,1024]{1,0:T(8,128)(2,1)}, f32[3,512,128]{2,1,0:T(8,128)}, f32[3,512,128]{2,1,0:T(8,128)}) custom-call(s32[1]{0:T(128)S(6)} %copy.26.count_ref, s32[3]{0:T(128)} %bitcast_add_fusion.1.rows_ref, bf16[512,1024]{1,0:T(8,128)(2,1)} %bitcast.71, bf16[8,512,128]{2,1,0:T(8,128)(2,1)} %copy-done, bf16[8,512,128]{2,1,0:T(8,128)(2,1)} %copy-done, ...), custom_call_target="tpu_custom_call" | custom-call | tf_op jit(solution)/shard_map/pallas_call | solution.py:131
  87.1 0.1 broadcast_in_dim.16.clone
  87.2 1.0 copy-done.6
  88.2 1.0 scatter_fusion
  89.2 0.9 slice.122
  90.1 2.8 %collective-permute-start.16 = (bf16[4,512,128]{2,1,0:T(8,128)(2,1)}, bf16[4,512,128]{2,1,0:T(8,128)(2,1)S(1)}, u32[]{:S(2)}, u32[]{:S(2)}) collective-permute-start(bf16[4,512,128]{2,1,0:T(8,128)(2,1)} %slice.122), channel_id=1, source_target_pairs={{0,8},{8,0},{16,24},{24,16},{32,40},{40,32},{48,56},{56,48},{64,72... | collective-permute-start | bytes 1572872 | tf_op jit(solution)/shard_map/ppermute | solution.py:192
  92.9 0.1 broadcast_in_dim.16.clone.1
  93.1 1.0 scatter_fusion.1
  94.1 0.1 slice.121
  94.2 0.7 collective-permute-start.20
  94.9 1.3 %slice_add_fusion.1 = f32[4,512,128]{2,1,0:T(8,128)S(1)} fusion(f32[8,512,128]{2,1,0:T(8,128)} %copy-done.2, bf16[4,512,128]{2,1,0:T(8,128)(2,1)S(1)} %collective-permute-done.16), kind=kLoop, calls=%fused_computation.19 | loop fusion | flops 524288 | bytes 2621440 | tf_op jit(solution)/shard_map/add | solution.py:194
  96.3 2.3 %collective-permute-start.17 = (bf16[512,128]{1,0:T(8,128)(2,1)S(1)}, bf16[512,128]{1,0:T(8,128)(2,1)S(1)}, u32[]{:S(2)}, u32[]{:S(2)}) collective-permute-start(bf16[512,128]{1,0:T(8,128)(2,1)S(1)} %fusion.23), channel_id=1, source_target_pairs={{0,16},{8,56},{16,32},{24,8},{32,48},{40,24},{48,0},{56,40},{64,80... | collective-permute-start | bytes 393224 | tf_op jit(solution)/shard_map/ppermute | solution.py:192
  98.5 0.1 slice_add_fusion
  98.7 0.2 collective-permute-start.21
  98.8 1.6 %collective-permute-done.17 = bf16[512,128]{1,0:T(8,128)(2,1)S(1)} collective-permute-done((bf16[512,128]{1,0:T(8,128)(2,1)S(1)}, bf16[512,128]{1,0:T(8,128)(2,1)S(1)}, u32[]{:S(2)}, u32[]{:S(2)}) %collective-permute-start.17) | collective-permute-done | bytes 131104 | tf_op jit(solution)/shard_map/ppermute | solution.py:192
  100.5 0.1 fusion.9
  100.6 3.2 %collective-permute-start.18 = (bf16[512,128]{1,0:T(8,128)(2,1)S(1)}, bf16[512,128]{1,0:T(8,128)(2,1)S(1)}, u32[]{:S(2)}, u32[]{:S(2)}) collective-permute-start(bf16[512,128]{1,0:T(8,128)(2,1)S(1)} %get-tuple-element.18), channel_id=1, source_target_pairs={{0,48},{8,56},{16,0},{24,8},{32,16},{40,24},{48,32},{56,40},{64,11... | collective-permute-start | bytes 393224 | tf_op jit(solution)/shard_map/ppermute | solution.py:192
  103.7 0.1 fusion.13
  103.8 2.8 %collective-permute-start.22 = (bf16[512,128]{1,0:T(8,128)(2,1)S(1)}, bf16[512,128]{1,0:T(8,128)(2,1)S(1)}, u32[]{:S(2)}, u32[]{:S(2)}) collective-permute-start(bf16[512,128]{1,0:T(8,128)(2,1)S(1)} %get-tuple-element.16), channel_id=1, source_target_pairs={{0,48},{8,56},{16,0},{24,8},{32,16},{40,24},{48,32},{56,40},{64,11... | collective-permute-start | bytes 393224 | tf_op jit(solution)/shard_map/ppermute | solution.py:192
  106.6 0.0 collective-permute-done.18
  106.6 3.1 %collective-permute-done.19 = bf16[512,128]{1,0:T(8,128)(2,1)S(1)} collective-permute-done((bf16[512,128]{1,0:T(8,128)(2,1)S(1)}, bf16[512,128]{1,0:T(8,128)(2,1)S(1)}, u32[]{:S(2)}, u32[]{:S(2)}) %collective-permute-start.19) | collective-permute-done | bytes 131104 | tf_op jit(solution)/shard_map/ppermute | solution.py:192
  109.7 0.7 fusion.22
  110.4 1.2 %collective-permute-done.23 = bf16[512,128]{1,0:T(8,128)(2,1)S(1)} collective-permute-done((bf16[512,128]{1,0:T(8,128)(2,1)S(1)}, bf16[512,128]{1,0:T(8,128)(2,1)S(1)}, u32[]{:S(2)}, u32[]{:S(2)}) %collective-permute-start.23) | collective-permute-done | bytes 131104 | tf_op jit(solution)/shard_map/ppermute | solution.py:192
  111.6 0.7 fusion.24
  (46 shorter events, 0.5 us)
Async XLA Ops:
  0.6 12.9 %collective-permute-start.1 = (bf16[1,512,128]{2,1,0:T(8,128)(2,1)}, bf16[1,512,128]{2,1,0:T(8,128)(2,1)S(1)}, u32[]{:S(2)}, u32[]{:S(2)}) collective-permute-start(bf16[1,512,128]{2,1,0:T(8,128)(2,1)} %param.9), channel_id=1, source_target_pairs={{0,48},{8,56},{16,0},{24,8},{32,16},{40,24},{48,32},{56,40},{64,11... | collective-permute-start | bytes 393224 | tf_op jit(solution)/shard_map/ppermute | solution.py:177
  4.0 9.9 %collective-permute-start = (bf16[1,512,128]{2,1,0:T(8,128)(2,1)}, bf16[1,512,128]{2,1,0:T(8,128)(2,1)S(1)}, u32[]{:S(2)}, u32[]{:S(2)}) collective-permute-start(bf16[1,512,128]{2,1,0:T(8,128)(2,1)} %param.9), channel_id=1, source_target_pairs={{0,16},{8,24},{16,32},{24,40},{32,48},{40,56},{48,0},{56,8},{64,80... | collective-permute-start | bytes 393224 | tf_op jit(solution)/shard_map/ppermute | solution.py:176
  4.0 19.1 %collective-permute-start.3 = (bf16[1,512,128]{2,1,0:T(8,128)(2,1)}, bf16[1,512,128]{2,1,0:T(8,128)(2,1)S(1)}, u32[]{:S(2)}, u32[]{:S(2)}) collective-permute-start(bf16[1,512,128]{2,1,0:T(8,128)(2,1)} %param.9), channel_id=1, source_target_pairs={{0,8},{8,0},{16,24},{24,16},{32,40},{40,32},{48,56},{56,48},{64,72... | collective-permute-start | bytes 393224 | tf_op jit(solution)/shard_map/ppermute | solution.py:178
  6.0 8.4 %collective-permute-start.7 = (bf16[1,512,128]{2,1,0:T(8,128)(2,1)}, bf16[1,512,128]{2,1,0:T(8,128)(2,1)S(1)}, u32[]{:S(2)}, u32[]{:S(2)}) collective-permute-start(bf16[1,512,128]{2,1,0:T(8,128)(2,1)} %param.10), channel_id=1, source_target_pairs={{0,48},{8,56},{16,0},{24,8},{32,16},{40,24},{48,32},{56,40},{64,11... | collective-permute-start | bytes 393224 | tf_op jit(solution)/shard_map/ppermute | solution.py:177
  7.9 6.5 %collective-permute-start.6 = (bf16[1,512,128]{2,1,0:T(8,128)(2,1)}, bf16[1,512,128]{2,1,0:T(8,128)(2,1)S(1)}, u32[]{:S(2)}, u32[]{:S(2)}) collective-permute-start(bf16[1,512,128]{2,1,0:T(8,128)(2,1)} %param.10), channel_id=1, source_target_pairs={{0,16},{8,24},{16,32},{24,40},{32,48},{40,56},{48,0},{56,8},{64,80... | collective-permute-start | bytes 393224 | tf_op jit(solution)/shard_map/ppermute | solution.py:176
  13.6 9.6 %collective-permute-start.9 = (bf16[1,512,128]{2,1,0:T(8,128)(2,1)}, bf16[1,512,128]{2,1,0:T(8,128)(2,1)S(1)}, u32[]{:S(2)}, u32[]{:S(2)}) collective-permute-start(bf16[1,512,128]{2,1,0:T(8,128)(2,1)} %param.10), channel_id=1, source_target_pairs={{0,8},{8,0},{16,24},{24,16},{32,40},{40,32},{48,56},{56,48},{64,72... | collective-permute-start | bytes 393224 | tf_op jit(solution)/shard_map/ppermute | solution.py:178
  14.0 9.3 %collective-permute-start.4 = (bf16[2,512,128]{2,1,0:T(8,128)(2,1)S(1)}, bf16[2,512,128]{2,1,0:T(8,128)(2,1)S(1)}, u32[]{:S(2)}, u32[]{:S(2)}) collective-permute-start(bf16[2,512,128]{2,1,0:T(8,128)(2,1)S(1)} %pad_maximum_fusion), channel_id=1, source_target_pairs={{0,8},{8,0},{16,24},{24,16},{32,40},{40,32},{48,56},{56,48},{64,72... | collective-permute-start | bytes 786440 | tf_op jit(solution)/shard_map/ppermute | solution.py:181
  14.4 5.2 %collective-permute-start.2 = (bf16[1,512,128]{2,1,0:T(8,128)(2,1)S(1)}, bf16[1,512,128]{2,1,0:T(8,128)(2,1)S(1)}, u32[]{:S(2)}, u32[]{:S(2)}) collective-permute-start(bf16[1,512,128]{2,1,0:T(8,128)(2,1)S(1)} %get-tuple-element.24), channel_id=1, source_target_pairs={{0,48},{8,24},{16,0},{24,40},{32,16},{40,56},{48,32},{56,8},{64,11... | collective-permute-start | bytes 393224 | tf_op jit(solution)/shard_map/ppermute | solution.py:180
  14.5 6.4 %collective-permute-start.8 = (bf16[1,512,128]{2,1,0:T(8,128)(2,1)S(1)}, bf16[1,512,128]{2,1,0:T(8,128)(2,1)S(1)}, u32[]{:S(2)}, u32[]{:S(2)}) collective-permute-start(bf16[1,512,128]{2,1,0:T(8,128)(2,1)S(1)} %get-tuple-element.22), channel_id=1, source_target_pairs={{0,48},{8,24},{16,0},{24,40},{32,16},{40,56},{48,32},{56,8},{64,11... | collective-permute-start | bytes 393224 | tf_op jit(solution)/shard_map/ppermute | solution.py:180
  19.6 4.5 %collective-permute-start.10 = (bf16[2,512,128]{2,1,0:T(8,128)(2,1)S(1)}, bf16[2,512,128]{2,1,0:T(8,128)(2,1)S(1)}, u32[]{:S(2)}, u32[]{:S(2)}) collective-permute-start(bf16[2,512,128]{2,1,0:T(8,128)(2,1)S(1)} %pad_maximum_fusion.1), channel_id=1, source_target_pairs={{0,8},{8,0},{16,24},{24,16},{32,40},{40,32},{48,56},{56,48},{64,72... | collective-permute-start | bytes 786440 | tf_op jit(solution)/shard_map/ppermute | solution.py:181
  21.0 3.1 %collective-permute-start.5 = (bf16[1,512,128]{2,1,0:T(8,128)(2,1)S(1)}, bf16[1,512,128]{2,1,0:T(8,128)(2,1)S(1)}, u32[]{:S(2)}, u32[]{:S(2)}) collective-permute-start(bf16[1,512,128]{2,1,0:T(8,128)(2,1)S(1)} %collective-permute-done.2), channel_id=1, source_target_pairs={{0,8},{8,0},{16,24},{24,16},{32,40},{40,32},{48,56},{56,48},{64,72... | collective-permute-start | bytes 393224 | tf_op jit(solution)/shard_map/ppermute | solution.py:184
  23.1 1.4 %collective-permute-start.11 = (bf16[1,512,128]{2,1,0:T(8,128)(2,1)S(1)}, bf16[1,512,128]{2,1,0:T(8,128)(2,1)S(1)}, u32[]{:S(2)}, u32[]{:S(2)}) collective-permute-start(bf16[1,512,128]{2,1,0:T(8,128)(2,1)S(1)} %collective-permute-done.8), channel_id=1, source_target_pairs={{0,8},{8,0},{16,24},{24,16},{32,40},{40,32},{48,56},{56,48},{64,72... | collective-permute-start | bytes 393224 | tf_op jit(solution)/shard_map/ppermute | solution.py:184
  24.1 1.0 copy-start
  24.5 1.0 copy-start.1
  25.5 21.4 %copy-start.4 = (bf16[1,512,1024]{2,1,0:T(8,128)(2,1)S(1)}, bf16[1,512,1024]{2,1,0:T(8,128)(2,1)}, u32[]{:S(2)}) copy-start(bf16[1,512,1024]{2,1,0:T(8,128)(2,1)} %param.14) | copy-start | bytes 3145732
  25.5 21.4 %copy-start.7 = (f32[1024]{0:T(1024)S(1)}, f32[1024]{0:T(1024)}, u32[]{:S(2)}) copy-start(f32[1024]{0:T(1024)} %param.13) | copy-start | bytes 12292
  46.9 14.5 %copy-start.8 = (s32[1,3]{1,0:T(1,128)S(1)}, s32[1,3]{1,0:T(1,128)}, u32[]{:S(2)}) copy-start(s32[1,3]{1,0:T(1,128)} %param.11) | copy-start | bytes 40
  46.9 15.8 %copy-start.3 = (bf16[512,1024]{1,0:T(8,128)(2,1)S(1)}, bf16[512,1024]{1,0:T(8,128)(2,1)}, u32[]{:S(2)}) copy-start(bf16[512,1024]{1,0:T(8,128)(2,1)} %get-tuple-element.9.refs_7_) | copy-start | bytes 3145732
  48.9 4.7 %collective-permute-start.13 = (f32[2,512]{1,0:T(2,128)S(1)}, f32[2,512]{1,0:T(2,128)S(1)}, u32[]{:S(2)}, u32[]{:S(2)}) collective-permute-start(f32[2,512]{1,0:T(2,128)S(1)} %pad_maximum_fusion.2), channel_id=1, source_target_pairs={{0,2},{1,3},{2,0},{3,1},{4,6},{5,7},{6,4},{7,5},{8,10},{9,11},{10,... | collective-permute-start | bytes 12296 | tf_op jit(solution)/shard_map/ppermute | solution.py:207
  51.9 4.3 %collective-permute-start.14 = (f32[2,512]{1,0:T(2,128)S(1)}, f32[2,512]{1,0:T(2,128)S(1)}, u32[]{:S(2)}, u32[]{:S(2)}) collective-permute-start(f32[2,512]{1,0:T(2,128)S(1)} %pad_maximum_fusion.2), channel_id=1, source_target_pairs={{0,3},{1,2},{2,1},{3,0},{4,7},{5,6},{6,5},{7,4},{8,11},{9,10},{10,... | collective-permute-start | bytes 12296 | tf_op jit(solution)/shard_map/ppermute | solution.py:207
  53.6 2.6 %collective-permute-start.12 = (f32[2,512]{1,0:T(2,128)S(1)}, f32[2,512]{1,0:T(2,128)S(1)}, u32[]{:S(2)}, u32[]{:S(2)}) collective-permute-start(f32[2,512]{1,0:T(2,128)S(1)} %pad_maximum_fusion.2), channel_id=1, source_target_pairs={{0,1},{1,0},{2,3},{3,2},{4,5},{5,4},{6,7},{7,6},{8,9},{9,8},{10,11... | collective-permute-start | bytes 12296 | tf_op jit(solution)/shard_map/ppermute | solution.py:207
  56.2 6.5 %collective-permute-start.15 = (f32[2,512]{1,0:T(2,128)S(1)}, f32[2,512]{1,0:T(2,128)S(1)}, u32[]{:S(2)}, u32[]{:S(2)}) collective-permute-start(f32[2,512]{1,0:T(2,128)S(1)} %add_add_fusion), channel_id=1, source_target_pairs={{0,4},{1,5},{2,6},{3,7},{4,0},{5,1},{6,2},{7,3},{8,12},{9,13},{10,... | collective-permute-start | bytes 12296 | tf_op jit(solution)/shard_map/ppermute | solution.py:208
  87.0 1.1 %copy-start.6 = (f32[3,512,128]{2,1,0:T(8,128)S(1)}, f32[3,512,128]{2,1,0:T(8,128)}, u32[]{:S(2)}) copy-start(f32[3,512,128]{2,1,0:T(8,128)} %get-tuple-element.12) | copy-start | bytes 2359300
  89.2 3.8 %copy-start.2 = (f32[8,512,128]{2,1,0:T(8,128)}, f32[8,512,128]{2,1,0:T(8,128)S(1)}, u32[]{:S(2)}) copy-start(f32[8,512,128]{2,1,0:T(8,128)S(1)} %scatter_fusion) | copy-start | bytes 6291460
  89.2 3.9 %copy-start.5 = (f32[3,512,128]{2,1,0:T(8,128)S(1)}, f32[3,512,128]{2,1,0:T(8,128)}, u32[]{:S(2)}) copy-start(f32[3,512,128]{2,1,0:T(8,128)} %get-tuple-element.13) | copy-start | bytes 2359300
  90.1 4.8 %collective-permute-start.16 = (bf16[4,512,128]{2,1,0:T(8,128)(2,1)}, bf16[4,512,128]{2,1,0:T(8,128)(2,1)S(1)}, u32[]{:S(2)}, u32[]{:S(2)}) collective-permute-start(bf16[4,512,128]{2,1,0:T(8,128)(2,1)} %slice.122), channel_id=1, source_target_pairs={{0,8},{8,0},{16,24},{24,16},{32,40},{40,32},{48,56},{56,48},{64,72... | collective-permute-start | bytes 1572872 | tf_op jit(solution)/shard_map/ppermute | solution.py:192
  94.2 4.4 %collective-permute-start.20 = (bf16[4,512,128]{2,1,0:T(8,128)(2,1)S(1)}, bf16[4,512,128]{2,1,0:T(8,128)(2,1)S(1)}, u32[]{:S(2)}, u32[]{:S(2)}) collective-permute-start(bf16[4,512,128]{2,1,0:T(8,128)(2,1)S(1)} %slice.121), channel_id=1, source_target_pairs={{0,8},{8,0},{16,24},{24,16},{32,40},{40,32},{48,56},{56,48},{64,72... | collective-permute-start | bytes 1572872 | tf_op jit(solution)/shard_map/ppermute | solution.py:192
  96.3 4.2 %collective-permute-start.17 = (bf16[512,128]{1,0:T(8,128)(2,1)S(1)}, bf16[512,128]{1,0:T(8,128)(2,1)S(1)}, u32[]{:S(2)}, u32[]{:S(2)}) collective-permute-start(bf16[512,128]{1,0:T(8,128)(2,1)S(1)} %fusion.23), channel_id=1, source_target_pairs={{0,16},{8,56},{16,32},{24,8},{32,48},{40,24},{48,0},{56,40},{64,80... | collective-permute-start | bytes 393224 | tf_op jit(solution)/shard_map/ppermute | solution.py:192
  98.7 5.1 %collective-permute-start.21 = (bf16[512,128]{1,0:T(8,128)(2,1)S(1)}, bf16[512,128]{1,0:T(8,128)(2,1)S(1)}, u32[]{:S(2)}, u32[]{:S(2)}) collective-permute-start(bf16[512,128]{1,0:T(8,128)(2,1)S(1)} %fusion.25), channel_id=1, source_target_pairs={{0,16},{8,56},{16,32},{24,8},{32,48},{40,24},{48,0},{56,40},{64,80... | collective-permute-start | bytes 393224 | tf_op jit(solution)/shard_map/ppermute | solution.py:192
  100.6 6.0 %collective-permute-start.18 = (bf16[512,128]{1,0:T(8,128)(2,1)S(1)}, bf16[512,128]{1,0:T(8,128)(2,1)S(1)}, u32[]{:S(2)}, u32[]{:S(2)}) collective-permute-start(bf16[512,128]{1,0:T(8,128)(2,1)S(1)} %get-tuple-element.18), channel_id=1, source_target_pairs={{0,48},{8,56},{16,0},{24,8},{32,16},{40,24},{48,32},{56,40},{64,11... | collective-permute-start | bytes 393224 | tf_op jit(solution)/shard_map/ppermute | solution.py:192
  103.7 5.9 %collective-permute-start.19 = (bf16[512,128]{1,0:T(8,128)(2,1)S(1)}, bf16[512,128]{1,0:T(8,128)(2,1)S(1)}, u32[]{:S(2)}, u32[]{:S(2)}) collective-permute-start(bf16[512,128]{1,0:T(8,128)(2,1)S(1)} %get-tuple-element.19), channel_id=1, source_target_pairs={{0,16},{8,24},{16,32},{24,40},{32,48},{40,56},{48,0},{56,8},{64,80... | collective-permute-start | bytes 393224 | tf_op jit(solution)/shard_map/ppermute | solution.py:192
  103.8 6.6 %collective-permute-start.22 = (bf16[512,128]{1,0:T(8,128)(2,1)S(1)}, bf16[512,128]{1,0:T(8,128)(2,1)S(1)}, u32[]{:S(2)}, u32[]{:S(2)}) collective-permute-start(bf16[512,128]{1,0:T(8,128)(2,1)S(1)} %get-tuple-element.16), channel_id=1, source_target_pairs={{0,48},{8,56},{16,0},{24,8},{32,16},{40,24},{48,32},{56,40},{64,11... | collective-permute-start | bytes 393224 | tf_op jit(solution)/shard_map/ppermute | solution.py:192
  106.6 5.0 %collective-permute-start.23 = (bf16[512,128]{1,0:T(8,128)(2,1)S(1)}, bf16[512,128]{1,0:T(8,128)(2,1)S(1)}, u32[]{:S(2)}, u32[]{:S(2)}) collective-permute-start(bf16[512,128]{1,0:T(8,128)(2,1)S(1)} %get-tuple-element.17), channel_id=1, source_target_pairs={{0,16},{8,24},{16,32},{24,40},{32,48},{40,56},{48,0},{56,8},{64,80... | collective-permute-start | bytes 393224 | tf_op jit(solution)/shard_map/ppermute | solution.py:192

commit v16 on v15

--- a/solution.py
+++ b/solution.py
@@ -163,13 +163,11 @@
     return route
 
 
-CHIP_STEP_ROWS = (0, 2, 3, 1)
-
-
 def ring_row(partner, my_index):
     chip_step = ((partner >> 1) - (my_index >> 1)) % (GROUP // 2)
     other_core = (partner ^ my_index) & 1
-    return other_core * 4 + jnp.asarray(CHIP_STEP_ROWS, jnp.int32)[chip_step]
+    step_row = jnp.where(chip_step == 1, 2, jnp.where(chip_step == 2, 3, jnp.where(chip_step == 3, 1, 0)))
+    return other_core * 4 + step_row
 
 
 def gather_group(block, my_index):

time: 113 us -> 111 us (0.982)
  local copies, waits for them, and re-layouts: 6.57 us -> 5.28 us
  starting transfers between devices: 34 us -> 32.8 us
    ppermute x2, waiting for transfers between devices: 0.01 us -> 1.68 us  [gather_group(): lax.ppermute(block, 'resp', ring_route(lambda x, c: (x + 1, c)))]
    gather x1 -> x0, local copies, waits for them, and re-layouts: 1.3 us -> none  [ring_row(): return other_core * 4 + jnp.asarray(CHIP_STEP_ROWS, jnp.int32)[chip_step]]
  transfers between devices with their start and end apart: 24 -> 24, of which waited for: 9 -> 10; matrix products, arithmetic and copies ran while one was open for 8% -> 6% of each run, Pallas kernels for 0% -> 0%
where the time goes in v16:
time: 111 us; the launch traced here: 110 us
  Pallas kernels  43.8 us (39%)
  starting transfers between devices  32.8 us (30%)
  waiting for transfers between devices  16.6 us (15%)
  other arithmetic  10.2 us (9%)
  local copies, waits for them, and re-layouts  5.28 us (5%)
  between operations  1.63 us (1%)
    pallas_call x1, Pallas kernels, attention_backward(): pl.pallas_call(backward_kernel, grid_spec=pltpu.PrefetchScalarGridSpec(nu...  22.4 us
    pallas_call x1, Pallas kernels, attention_forward(): pl.pallas_call(forward_kernel, grid_spec=pltpu.PrefetchScalarGridSpec(num...  21.4 us
    ppermute x8, starting transfers between devices, send(): lax.ppermute(block.astype(jnp.bfloat16), 'resp', ring_route(move))  12 us
    ppermute x8, waiting for transfers between devices, send(): lax.ppermute(block.astype(jnp.bfloat16), 'resp', ring_route(move))  5.96 us
    ppermute x2, starting transfers between devices, gather_group(): from_plus = lax.ppermute(block, 'resp', ring_route(lambda x, c: (x - 1, c)))  5.34 us
    ppermute x1, starting transfers between devices, head_sum(): lax.ppermute(quad, 'head', [(low, low ^ 4) for low in range(heads)])  5.2 us
    ppermute x3, starting transfers between devices, head_sum(): lax.ppermute(row_part, 'head', [(low, low ^ distance) for low in range(he...  4.72 us
    unnamed x28, local copies, waits for them, and re-layouts  3.98 us
  transfers between devices with their start and end apart: 24, of which 10 were waited for; matrix products, arithmetic and copies ran while one was open for 6% of the time, Pallas kernels for 0%

profile of v16, /device:TPU:1, one launch (start us, length us, event | category | flops | bytes accessed | tf_op | source)
XLA Modules:
  0.0 110.3 jit_solution(18394768528435029680)
XLA Ops:
  0.6 3.4 %collective-permute-start.1 = (bf16[1,512,128]{2,1,0:T(8,128)(2,1)}, bf16[1,512,128]{2,1,0:T(8,128)(2,1)S(1)}, u32[]{:S(2)}, u32[]{:S(2)}) collective-permute-start(bf16[1,512,128]{2,1,0:T(8,128)(2,1)} %param.8), channel_id=1, source_target_pairs={{0,48},{8,56},{16,0},{24,8},{32,16},{40,24},{48,32},{56,40},{64,11... | collective-permute-start | bytes 393224 | tf_op jit(solution)/shard_map/ppermute | solution.py:175
  4.0 0.0 collective-permute-start
  4.0 2.0 %collective-permute-start.3 = (bf16[1,512,128]{2,1,0:T(8,128)(2,1)}, bf16[1,512,128]{2,1,0:T(8,128)(2,1)S(1)}, u32[]{:S(2)}, u32[]{:S(2)}) collective-permute-start(bf16[1,512,128]{2,1,0:T(8,128)(2,1)} %param.8), channel_id=1, source_target_pairs={{0,8},{8,0},{16,24},{24,16},{32,40},{40,32},{48,56},{56,48},{64,72... | collective-permute-start | bytes 393224 | tf_op jit(solution)/shard_map/ppermute | solution.py:176
  6.0 2.0 %collective-permute-start.7 = (bf16[1,512,128]{2,1,0:T(8,128)(2,1)}, bf16[1,512,128]{2,1,0:T(8,128)(2,1)S(1)}, u32[]{:S(2)}, u32[]{:S(2)}) collective-permute-start(bf16[1,512,128]{2,1,0:T(8,128)(2,1)} %param.9), channel_id=1, source_target_pairs={{0,48},{8,56},{16,0},{24,8},{32,16},{40,24},{48,32},{56,40},{64,11... | collective-permute-start | bytes 393224 | tf_op jit(solution)/shard_map/ppermute | solution.py:175
  7.9 0.0 collective-permute-start.6
  7.9 1.2 %fusion.30.rows_ref = s32[3]{0:T(128)} fusion(s32[]{:T(128)S(6)} %shift_right_arithmetic.16, s32[1,3]{1,0:T(1,128)} %param.10, s32[]{:T(128)S(6)} %axis_index.15), kind=kLoop, calls=%fused_computation.88 | loop fusion | flops 69 | bytes 32 | tf_op jit(solution)/shard_map/add | solution.py:170
  9.1 0.9 constant_dynamic-update-slice_fusion.6
  10.7 0.9 constant_dynamic-update-slice_fusion.13
  11.6 0.0 collective-permute-done.1
  11.6 0.4 collective-permute-start.9
  12.0 0.0 collective-permute-done
  12.0 0.3 collective-permute-start.4
  12.4 0.0 collective-permute-done.7
  12.4 0.1 collective-permute-start.2
  12.5 1.7 %collective-permute-done.6 = bf16[1,512,128]{2,1,0:T(8,128)(2,1)S(1)} collective-permute-done((bf16[1,512,128]{2,1,0:T(8,128)(2,1)}, bf16[1,512,128]{2,1,0:T(8,128)(2,1)S(1)}, u32[]{:S(2)}, u32[]{:S(2)}) %collective-permute-start.6) | collective-permute-done | bytes 131104 | tf_op jit(solution)/shard_map/ppermute | solution.py:174
  14.2 0.1 collective-permute-start.8
  14.4 3.2 %collective-permute-done.2 = bf16[1,512,128]{2,1,0:T(8,128)(2,1)S(1)} collective-permute-done((bf16[1,512,128]{2,1,0:T(8,128)(2,1)S(1)}, bf16[1,512,128]{2,1,0:T(8,128)(2,1)S(1)}, u32[]{:S(2)}, u32[]{:S(2)}) %collective-permute-start.2) | collective-permute-done | bytes 131104 | tf_op jit(solution)/shard_map/ppermute | solution.py:178
  17.6 0.9 collective-permute-start.10
  18.5 0.8 collective-permute-done.8
  19.3 1.8 %collective-permute-start.5 = (bf16[1,512,128]{2,1,0:T(8,128)(2,1)S(1)}, bf16[1,512,128]{2,1,0:T(8,128)(2,1)S(1)}, u32[]{:S(2)}, u32[]{:S(2)}) collective-permute-start(bf16[1,512,128]{2,1,0:T(8,128)(2,1)S(1)} %collective-permute-done.2), channel_id=1, source_target_pairs={{0,8},{8,0},{16,24},{24,16},{32,40},{40,32},{48,56},{56,48},{64,72... | collective-permute-start | bytes 393224 | tf_op jit(solution)/shard_map/ppermute | solution.py:182
  21.1 0.1 collective-permute-start.11
  21.3 0.0 collective-permute-done.4
  21.3 0.7 collective-permute-done.5
  22.2 0.4 collective-permute-done.11
  22.6 0.5 copy-done
  23.1 0.5 copy-done.1
  23.6 21.4 %shard_map.102 = (bf16[512,1024]{1,0:T(8,128)(2,1)}, f32[8,1,512]{2,1,0:T(1,128)}) custom-call(s32[1]{0:T(128)S(6)} %copy.25.count_ref, s32[3]{0:T(128)} %fusion.30.rows_ref, bf16[512,1024]{1,0:T(8,128)(2,1)} %bitcast.70, bf16[8,512,128]{2,1,0:T(8,128)(2,1)} %copy-done, bf16[8,512,128]{2,1,0:T(8,128)(2,1)} %copy-done, bf16[8,512,128]{2,1,0:T(8,128)(2,1)} %copy-done, ...), custom_call_target="tpu_custom_call" | custom-call | tf_op jit(solution)/shard_map/pallas_call | solution.py:108
  45.0 1.9 %fusion = (f32[512]{0:T(512)S(1)}, f32[512]{0:T(512)S(1)}) fusion(bf16[512,1024]{1,0:T(8,128)(2,1)} %get-tuple-element.9.refs_7_, f32[1024]{0:T(1024)S(1)} %copy-done.7, bf16[1,512,1024]{2,1,0:T(8,128)(2,1)S(1)} %copy-done.4), kind=kLoop, calls=%fused_computation.6 | loop fusion | flops 3668992 | bytes 2105344 | tf_op jit(solution)/shard_map/reduce_sum | solution.py:221
  46.9 3.1 %collective-permute-start.13 = (f32[2,512]{1,0:T(2,128)S(1)}, f32[2,512]{1,0:T(2,128)S(1)}, u32[]{:S(2)}, u32[]{:S(2)}) collective-permute-start(f32[2,512]{1,0:T(2,128)S(1)} %pad_maximum_fusion.2), channel_id=1, source_target_pairs={{0,2},{1,3},{2,0},{3,1},{4,6},{5,7},{6,4},{7,5},{8,10},{9,11},{10,... | collective-permute-start | bytes 12296 | tf_op jit(solution)/shard_map/ppermute | solution.py:205
  50.0 1.6 %collective-permute-start.14 = (f32[2,512]{1,0:T(2,128)S(1)}, f32[2,512]{1,0:T(2,128)S(1)}, u32[]{:S(2)}, u32[]{:S(2)}) collective-permute-start(f32[2,512]{1,0:T(2,128)S(1)} %pad_maximum_fusion.2), channel_id=1, source_target_pairs={{0,3},{1,2},{2,1},{3,0},{4,7},{5,6},{6,5},{7,4},{8,11},{9,10},{10,... | collective-permute-start | bytes 12296 | tf_op jit(solution)/shard_map/ppermute | solution.py:205
  51.6 0.0 collective-permute-start.12
  51.6 0.0 collective-permute-done.13
  51.6 2.6 %collective-permute-done.14 = f32[2,512]{1,0:T(2,128)S(1)} collective-permute-done((f32[2,512]{1,0:T(2,128)S(1)}, f32[2,512]{1,0:T(2,128)S(1)}, u32[]{:S(2)}, u32[]{:S(2)}) %collective-permute-start.14) | collective-permute-done | bytes 4128 | tf_op jit(solution)/shard_map/ppermute | solution.py:205
  54.2 0.0 collective-permute-done.12
  54.2 5.2 %collective-permute-start.15 = (f32[2,512]{1,0:T(2,128)S(1)}, f32[2,512]{1,0:T(2,128)S(1)}, u32[]{:S(2)}, u32[]{:S(2)}) collective-permute-start(f32[2,512]{1,0:T(2,128)S(1)} %add_add_fusion), channel_id=1, source_target_pairs={{0,4},{1,5},{2,6},{3,7},{4,0},{5,1},{6,2},{7,3},{8,12},{9,13},{10,... | collective-permute-start | bytes 12296 | tf_op jit(solution)/shard_map/ppermute | solution.py:206
  59.5 1.2 %collective-permute-done.15 = f32[2,512]{1,0:T(2,128)S(1)} collective-permute-done((f32[2,512]{1,0:T(2,128)S(1)}, f32[2,512]{1,0:T(2,128)S(1)}, u32[]{:S(2)}, u32[]{:S(2)}) %collective-permute-start.15) | collective-permute-done | bytes 4128 | tf_op jit(solution)/shard_map/ppermute | solution.py:206
  60.7 2.0 %fusion.5 = (bf16[512,1024]{1,0:T(8,128)(2,1)}, bf16[1,512,1024]{2,1,0:T(8,128)(2,1)}) fusion(bf16[512,1024]{1,0:T(8,128)(2,1)S(1)} %copy-done.3, bf16[1,512,1024]{2,1,0:T(8,128)(2,1)S(1)} %copy-done.4, f32[512]{0:T(512)S(1)} %fusion.27, f32[512]{0:T(512)S(1)} %bitcast.73, f32[1024]{0:T(1024)S(1)} %copy-done.7), kind=kLoop, calls=%fused_computation.11 | loop fusion | flops 5242880 | bytes 4202496 | tf_op jit(solution)/shard_map/convert_element_type | solution.py:230
  62.7 22.4 %shard_map.103 = (bf16[512,1024]{1,0:T(8,128)(2,1)}, f32[3,512,128]{2,1,0:T(8,128)}, f32[3,512,128]{2,1,0:T(8,128)}) custom-call(s32[1]{0:T(128)S(6)} %copy.25.count_ref, s32[3]{0:T(128)} %fusion.30.rows_ref, bf16[512,1024]{1,0:T(8,128)(2,1)} %bitcast.71, bf16[8,512,128]{2,1,0:T(8,128)(2,1)} %copy-done, bf16[8,512,128]{2,1,0:T(8,128)(2,1)} %copy-done, ...), custom_call_target="tpu_custom_call" | custom-call | tf_op jit(solution)/shard_map/pallas_call | solution.py:131
  85.1 0.1 broadcast_in_dim.40.clone
  85.2 1.0 copy-done.6
  86.2 1.0 scatter_fusion
  87.2 0.9 slice.120
  88.1 2.8 %collective-permute-start.16 = (bf16[4,512,128]{2,1,0:T(8,128)(2,1)}, bf16[4,512,128]{2,1,0:T(8,128)(2,1)S(1)}, u32[]{:S(2)}, u32[]{:S(2)}) collective-permute-start(bf16[4,512,128]{2,1,0:T(8,128)(2,1)} %slice.120), channel_id=1, source_target_pairs={{0,8},{8,0},{16,24},{24,16},{32,40},{40,32},{48,56},{56,48},{64,72... | collective-permute-start | bytes 1572872 | tf_op jit(solution)/shard_map/ppermute | solution.py:190
  91.0 0.1 broadcast_in_dim.40.clone.1
  91.1 1.0 scatter_fusion.1
  92.1 0.1 slice.119
  92.2 0.7 collective-permute-start.20
  93.0 1.3 %slice_add_fusion.1 = f32[4,512,128]{2,1,0:T(8,128)S(1)} fusion(f32[8,512,128]{2,1,0:T(8,128)} %copy-done.2, bf16[4,512,128]{2,1,0:T(8,128)(2,1)S(1)} %collective-permute-done.16), kind=kLoop, calls=%fused_computation.18 | loop fusion | flops 524288 | bytes 2621440 | tf_op jit(solution)/shard_map/add | solution.py:192
  94.3 2.3 %collective-permute-start.17 = (bf16[512,128]{1,0:T(8,128)(2,1)S(1)}, bf16[512,128]{1,0:T(8,128)(2,1)S(1)}, u32[]{:S(2)}, u32[]{:S(2)}) collective-permute-start(bf16[512,128]{1,0:T(8,128)(2,1)S(1)} %fusion.23), channel_id=1, source_target_pairs={{0,16},{8,56},{16,32},{24,8},{32,48},{40,24},{48,0},{56,40},{64,80... | collective-permute-start | bytes 393224 | tf_op jit(solution)/shard_map/ppermute | solution.py:190
  96.6 0.0 collective-permute-done.20
  96.6 0.1 slice_add_fusion
  96.7 0.2 collective-permute-start.21
  96.9 1.6 %collective-permute-done.17 = bf16[512,128]{1,0:T(8,128)(2,1)S(1)} collective-permute-done((bf16[512,128]{1,0:T(8,128)(2,1)S(1)}, bf16[512,128]{1,0:T(8,128)(2,1)S(1)}, u32[]{:S(2)}, u32[]{:S(2)}) %collective-permute-start.17) | collective-permute-done | bytes 131104 | tf_op jit(solution)/shard_map/ppermute | solution.py:190
  98.5 0.1 fusion.9
  98.6 3.2 %collective-permute-start.18 = (bf16[512,128]{1,0:T(8,128)(2,1)S(1)}, bf16[512,128]{1,0:T(8,128)(2,1)S(1)}, u32[]{:S(2)}, u32[]{:S(2)}) collective-permute-start(bf16[512,128]{1,0:T(8,128)(2,1)S(1)} %get-tuple-element.18), channel_id=1, source_target_pairs={{0,48},{8,56},{16,0},{24,8},{32,16},{40,24},{48,32},{56,40},{64,11... | collective-permute-start | bytes 393224 | tf_op jit(solution)/shard_map/ppermute | solution.py:190
  101.8 0.0 collective-permute-done.21
  101.8 0.1 fusion.13
  101.8 2.8 %collective-permute-start.22 = (bf16[512,128]{1,0:T(8,128)(2,1)S(1)}, bf16[512,128]{1,0:T(8,128)(2,1)S(1)}, u32[]{:S(2)}, u32[]{:S(2)}) collective-permute-start(bf16[512,128]{1,0:T(8,128)(2,1)S(1)} %get-tuple-element.16), channel_id=1, source_target_pairs={{0,48},{8,56},{16,0},{24,8},{32,16},{40,24},{48,32},{56,40},{64,11... | collective-permute-start | bytes 393224 | tf_op jit(solution)/shard_map/ppermute | solution.py:190
  104.6 0.0 collective-permute-start.23
  104.6 0.0 collective-permute-done.18
  104.6 3.1 %collective-permute-done.19 = bf16[512,128]{1,0:T(8,128)(2,1)S(1)} collective-permute-done((bf16[512,128]{1,0:T(8,128)(2,1)S(1)}, bf16[512,128]{1,0:T(8,128)(2,1)S(1)}, u32[]{:S(2)}, u32[]{:S(2)}) %collective-permute-start.19) | collective-permute-done | bytes 131104 | tf_op jit(solution)/shard_map/ppermute | solution.py:190
  107.7 0.7 fusion.22
  108.4 1.2 %collective-permute-done.23 = bf16[512,128]{1,0:T(8,128)(2,1)S(1)} collective-permute-done((bf16[512,128]{1,0:T(8,128)(2,1)S(1)}, bf16[512,128]{1,0:T(8,128)(2,1)S(1)}, u32[]{:S(2)}, u32[]{:S(2)}) %collective-permute-start.23) | collective-permute-done | bytes 131104 | tf_op jit(solution)/shard_map/ppermute | solution.py:190
  109.6 0.7 fusion.24
  (43 shorter events, 0.5 us)
Async XLA Ops:
  0.6 11.0 %collective-permute-start.1 = (bf16[1,512,128]{2,1,0:T(8,128)(2,1)}, bf16[1,512,128]{2,1,0:T(8,128)(2,1)S(1)}, u32[]{:S(2)}, u32[]{:S(2)}) collective-permute-start(bf16[1,512,128]{2,1,0:T(8,128)(2,1)} %param.8), channel_id=1, source_target_pairs={{0,48},{8,56},{16,0},{24,8},{32,16},{40,24},{48,32},{56,40},{64,11... | collective-permute-start | bytes 393224 | tf_op jit(solution)/shard_map/ppermute | solution.py:175
  4.0 8.0 %collective-permute-start = (bf16[1,512,128]{2,1,0:T(8,128)(2,1)}, bf16[1,512,128]{2,1,0:T(8,128)(2,1)S(1)}, u32[]{:S(2)}, u32[]{:S(2)}) collective-permute-start(bf16[1,512,128]{2,1,0:T(8,128)(2,1)} %param.8), channel_id=1, source_target_pairs={{0,16},{8,24},{16,32},{24,40},{32,48},{40,56},{48,0},{56,8},{64,80... | collective-permute-start | bytes 393224 | tf_op jit(solution)/shard_map/ppermute | solution.py:174
  4.0 17.1 %collective-permute-start.3 = (bf16[1,512,128]{2,1,0:T(8,128)(2,1)}, bf16[1,512,128]{2,1,0:T(8,128)(2,1)S(1)}, u32[]{:S(2)}, u32[]{:S(2)}) collective-permute-start(bf16[1,512,128]{2,1,0:T(8,128)(2,1)} %param.8), channel_id=1, source_target_pairs={{0,8},{8,0},{16,24},{24,16},{32,40},{40,32},{48,56},{56,48},{64,72... | collective-permute-start | bytes 393224 | tf_op jit(solution)/shard_map/ppermute | solution.py:176
  6.0 6.4 %collective-permute-start.7 = (bf16[1,512,128]{2,1,0:T(8,128)(2,1)}, bf16[1,512,128]{2,1,0:T(8,128)(2,1)S(1)}, u32[]{:S(2)}, u32[]{:S(2)}) collective-permute-start(bf16[1,512,128]{2,1,0:T(8,128)(2,1)} %param.9), channel_id=1, source_target_pairs={{0,48},{8,56},{16,0},{24,8},{32,16},{40,24},{48,32},{56,40},{64,11... | collective-permute-start | bytes 393224 | tf_op jit(solution)/shard_map/ppermute | solution.py:175
  7.9 6.2 %collective-permute-start.6 = (bf16[1,512,128]{2,1,0:T(8,128)(2,1)}, bf16[1,512,128]{2,1,0:T(8,128)(2,1)S(1)}, u32[]{:S(2)}, u32[]{:S(2)}) collective-permute-start(bf16[1,512,128]{2,1,0:T(8,128)(2,1)} %param.9), channel_id=1, source_target_pairs={{0,16},{8,24},{16,32},{24,40},{32,48},{40,56},{48,0},{56,8},{64,80... | collective-permute-start | bytes 393224 | tf_op jit(solution)/shard_map/ppermute | solution.py:174
  11.6 9.6 %collective-permute-start.9 = (bf16[1,512,128]{2,1,0:T(8,128)(2,1)}, bf16[1,512,128]{2,1,0:T(8,128)(2,1)S(1)}, u32[]{:S(2)}, u32[]{:S(2)}) collective-permute-start(bf16[1,512,128]{2,1,0:T(8,128)(2,1)} %param.9), channel_id=1, source_target_pairs={{0,8},{8,0},{16,24},{24,16},{32,40},{40,32},{48,56},{56,48},{64,72... | collective-permute-start | bytes 393224 | tf_op jit(solution)/shard_map/ppermute | solution.py:176
  12.0 9.3 %collective-permute-start.4 = (bf16[2,512,128]{2,1,0:T(8,128)(2,1)S(1)}, bf16[2,512,128]{2,1,0:T(8,128)(2,1)S(1)}, u32[]{:S(2)}, u32[]{:S(2)}) collective-permute-start(bf16[2,512,128]{2,1,0:T(8,128)(2,1)S(1)} %pad_maximum_fusion), channel_id=1, source_target_pairs={{0,8},{8,0},{16,24},{24,16},{32,40},{40,32},{48,56},{56,48},{64,72... | collective-permute-start | bytes 786440 | tf_op jit(solution)/shard_map/ppermute | solution.py:179
  12.4 5.2 %collective-permute-start.2 = (bf16[1,512,128]{2,1,0:T(8,128)(2,1)S(1)}, bf16[1,512,128]{2,1,0:T(8,128)(2,1)S(1)}, u32[]{:S(2)}, u32[]{:S(2)}) collective-permute-start(bf16[1,512,128]{2,1,0:T(8,128)(2,1)S(1)} %get-tuple-element.24), channel_id=1, source_target_pairs={{0,48},{8,24},{16,0},{24,40},{32,16},{40,56},{48,32},{56,8},{64,11... | collective-permute-start | bytes 393224 | tf_op jit(solution)/shard_map/ppermute | solution.py:178
  14.2 5.1 %collective-permute-start.8 = (bf16[1,512,128]{2,1,0:T(8,128)(2,1)S(1)}, bf16[1,512,128]{2,1,0:T(8,128)(2,1)S(1)}, u32[]{:S(2)}, u32[]{:S(2)}) collective-permute-start(bf16[1,512,128]{2,1,0:T(8,128)(2,1)S(1)} %get-tuple-element.22), channel_id=1, source_target_pairs={{0,48},{8,24},{16,0},{24,40},{32,16},{40,56},{48,32},{56,8},{64,11... | collective-permute-start | bytes 393224 | tf_op jit(solution)/shard_map/ppermute | solution.py:178
  17.6 4.5 %collective-permute-start.10 = (bf16[2,512,128]{2,1,0:T(8,128)(2,1)S(1)}, bf16[2,512,128]{2,1,0:T(8,128)(2,1)S(1)}, u32[]{:S(2)}, u32[]{:S(2)}) collective-permute-start(bf16[2,512,128]{2,1,0:T(8,128)(2,1)S(1)} %pad_maximum_fusion.1), channel_id=1, source_target_pairs={{0,8},{8,0},{16,24},{24,16},{32,40},{40,32},{48,56},{56,48},{64,72... | collective-permute-start | bytes 786440 | tf_op jit(solution)/shard_map/ppermute | solution.py:179
  19.3 2.8 %collective-permute-start.5 = (bf16[1,512,128]{2,1,0:T(8,128)(2,1)S(1)}, bf16[1,512,128]{2,1,0:T(8,128)(2,1)S(1)}, u32[]{:S(2)}, u32[]{:S(2)}) collective-permute-start(bf16[1,512,128]{2,1,0:T(8,128)(2,1)S(1)} %collective-permute-done.2), channel_id=1, source_target_pairs={{0,8},{8,0},{16,24},{24,16},{32,40},{40,32},{48,56},{56,48},{64,72... | collective-permute-start | bytes 393224 | tf_op jit(solution)/shard_map/ppermute | solution.py:182
  21.1 1.4 %collective-permute-start.11 = (bf16[1,512,128]{2,1,0:T(8,128)(2,1)S(1)}, bf16[1,512,128]{2,1,0:T(8,128)(2,1)S(1)}, u32[]{:S(2)}, u32[]{:S(2)}) collective-permute-start(bf16[1,512,128]{2,1,0:T(8,128)(2,1)S(1)} %collective-permute-done.8), channel_id=1, source_target_pairs={{0,8},{8,0},{16,24},{24,16},{32,40},{40,32},{48,56},{56,48},{64,72... | collective-permute-start | bytes 393224 | tf_op jit(solution)/shard_map/ppermute | solution.py:182
  22.1 1.0 copy-start
  22.6 1.0 copy-start.1
  23.6 21.4 %copy-start.4 = (bf16[1,512,1024]{2,1,0:T(8,128)(2,1)S(1)}, bf16[1,512,1024]{2,1,0:T(8,128)(2,1)}, u32[]{:S(2)}) copy-start(bf16[1,512,1024]{2,1,0:T(8,128)(2,1)} %param.13) | copy-start | bytes 3145732
  23.6 21.4 %copy-start.7 = (f32[1024]{0:T(1024)S(1)}, f32[1024]{0:T(1024)}, u32[]{:S(2)}) copy-start(f32[1024]{0:T(1024)} %param.12) | copy-start | bytes 12292
  45.0 14.5 %copy-start.8 = (s32[1,3]{1,0:T(1,128)S(1)}, s32[1,3]{1,0:T(1,128)}, u32[]{:S(2)}) copy-start(s32[1,3]{1,0:T(1,128)} %param.10) | copy-start | bytes 40
  45.0 15.8 %copy-start.3 = (bf16[512,1024]{1,0:T(8,128)(2,1)S(1)}, bf16[512,1024]{1,0:T(8,128)(2,1)}, u32[]{:S(2)}) copy-start(bf16[512,1024]{1,0:T(8,128)(2,1)} %get-tuple-element.9.refs_7_) | copy-start | bytes 3145732
  46.9 4.7 %collective-permute-start.13 = (f32[2,512]{1,0:T(2,128)S(1)}, f32[2,512]{1,0:T(2,128)S(1)}, u32[]{:S(2)}, u32[]{:S(2)}) collective-permute-start(f32[2,512]{1,0:T(2,128)S(1)} %pad_maximum_fusion.2), channel_id=1, source_target_pairs={{0,2},{1,3},{2,0},{3,1},{4,6},{5,7},{6,4},{7,5},{8,10},{9,11},{10,... | collective-permute-start | bytes 12296 | tf_op jit(solution)/shard_map/ppermute | solution.py:205
  50.0 4.3 %collective-permute-start.14 = (f32[2,512]{1,0:T(2,128)S(1)}, f32[2,512]{1,0:T(2,128)S(1)}, u32[]{:S(2)}, u32[]{:S(2)}) collective-permute-start(f32[2,512]{1,0:T(2,128)S(1)} %pad_maximum_fusion.2), channel_id=1, source_target_pairs={{0,3},{1,2},{2,1},{3,0},{4,7},{5,6},{6,5},{7,4},{8,11},{9,10},{10,... | collective-permute-start | bytes 12296 | tf_op jit(solution)/shard_map/ppermute | solution.py:205
  51.6 2.6 %collective-permute-start.12 = (f32[2,512]{1,0:T(2,128)S(1)}, f32[2,512]{1,0:T(2,128)S(1)}, u32[]{:S(2)}, u32[]{:S(2)}) collective-permute-start(f32[2,512]{1,0:T(2,128)S(1)} %pad_maximum_fusion.2), channel_id=1, source_target_pairs={{0,1},{1,0},{2,3},{3,2},{4,5},{5,4},{6,7},{7,6},{8,9},{9,8},{10,11... | collective-permute-start | bytes 12296 | tf_op jit(solution)/shard_map/ppermute | solution.py:205
  54.2 6.5 %collective-permute-start.15 = (f32[2,512]{1,0:T(2,128)S(1)}, f32[2,512]{1,0:T(2,128)S(1)}, u32[]{:S(2)}, u32[]{:S(2)}) collective-permute-start(f32[2,512]{1,0:T(2,128)S(1)} %add_add_fusion), channel_id=1, source_target_pairs={{0,4},{1,5},{2,6},{3,7},{4,0},{5,1},{6,2},{7,3},{8,12},{9,13},{10,... | collective-permute-start | bytes 12296 | tf_op jit(solution)/shard_map/ppermute | solution.py:206
  85.1 1.1 %copy-start.6 = (f32[3,512,128]{2,1,0:T(8,128)S(1)}, f32[3,512,128]{2,1,0:T(8,128)}, u32[]{:S(2)}) copy-start(f32[3,512,128]{2,1,0:T(8,128)} %get-tuple-element.12) | copy-start | bytes 2359300
  87.2 3.8 %copy-start.2 = (f32[8,512,128]{2,1,0:T(8,128)}, f32[8,512,128]{2,1,0:T(8,128)S(1)}, u32[]{:S(2)}) copy-start(f32[8,512,128]{2,1,0:T(8,128)S(1)} %scatter_fusion) | copy-start | bytes 6291460
  87.2 3.9 %copy-start.5 = (f32[3,512,128]{2,1,0:T(8,128)S(1)}, f32[3,512,128]{2,1,0:T(8,128)}, u32[]{:S(2)}) copy-start(f32[3,512,128]{2,1,0:T(8,128)} %get-tuple-element.13) | copy-start | bytes 2359300
  88.1 4.8 %collective-permute-start.16 = (bf16[4,512,128]{2,1,0:T(8,128)(2,1)}, bf16[4,512,128]{2,1,0:T(8,128)(2,1)S(1)}, u32[]{:S(2)}, u32[]{:S(2)}) collective-permute-start(bf16[4,512,128]{2,1,0:T(8,128)(2,1)} %slice.120), channel_id=1, source_target_pairs={{0,8},{8,0},{16,24},{24,16},{32,40},{40,32},{48,56},{56,48},{64,72... | collective-permute-start | bytes 1572872 | tf_op jit(solution)/shard_map/ppermute | solution.py:190
  92.2 4.4 %collective-permute-start.20 = (bf16[4,512,128]{2,1,0:T(8,128)(2,1)S(1)}, bf16[4,512,128]{2,1,0:T(8,128)(2,1)S(1)}, u32[]{:S(2)}, u32[]{:S(2)}) collective-permute-start(bf16[4,512,128]{2,1,0:T(8,128)(2,1)S(1)} %slice.119), channel_id=1, source_target_pairs={{0,8},{8,0},{16,24},{24,16},{32,40},{40,32},{48,56},{56,48},{64,72... | collective-permute-start | bytes 1572872 | tf_op jit(solution)/shard_map/ppermute | solution.py:190
  94.3 4.2 %collective-permute-start.17 = (bf16[512,128]{1,0:T(8,128)(2,1)S(1)}, bf16[512,128]{1,0:T(8,128)(2,1)S(1)}, u32[]{:S(2)}, u32[]{:S(2)}) collective-permute-start(bf16[512,128]{1,0:T(8,128)(2,1)S(1)} %fusion.23), channel_id=1, source_target_pairs={{0,16},{8,56},{16,32},{24,8},{32,48},{40,24},{48,0},{56,40},{64,80... | collective-permute-start | bytes 393224 | tf_op jit(solution)/shard_map/ppermute | solution.py:190
  96.7 5.1 %collective-permute-start.21 = (bf16[512,128]{1,0:T(8,128)(2,1)S(1)}, bf16[512,128]{1,0:T(8,128)(2,1)S(1)}, u32[]{:S(2)}, u32[]{:S(2)}) collective-permute-start(bf16[512,128]{1,0:T(8,128)(2,1)S(1)} %fusion.25), channel_id=1, source_target_pairs={{0,16},{8,56},{16,32},{24,8},{32,48},{40,24},{48,0},{56,40},{64,80... | collective-permute-start | bytes 393224 | tf_op jit(solution)/shard_map/ppermute | solution.py:190
  98.6 6.0 %collective-permute-start.18 = (bf16[512,128]{1,0:T(8,128)(2,1)S(1)}, bf16[512,128]{1,0:T(8,128)(2,1)S(1)}, u32[]{:S(2)}, u32[]{:S(2)}) collective-permute-start(bf16[512,128]{1,0:T(8,128)(2,1)S(1)} %get-tuple-element.18), channel_id=1, source_target_pairs={{0,48},{8,56},{16,0},{24,8},{32,16},{40,24},{48,32},{56,40},{64,11... | collective-permute-start | bytes 393224 | tf_op jit(solution)/shard_map/ppermute | solution.py:190
  101.8 5.9 %collective-permute-start.19 = (bf16[512,128]{1,0:T(8,128)(2,1)S(1)}, bf16[512,128]{1,0:T(8,128)(2,1)S(1)}, u32[]{:S(2)}, u32[]{:S(2)}) collective-permute-start(bf16[512,128]{1,0:T(8,128)(2,1)S(1)} %get-tuple-element.19), channel_id=1, source_target_pairs={{0,16},{8,24},{16,32},{24,40},{32,48},{40,56},{48,0},{56,8},{64,80... | collective-permute-start | bytes 393224 | tf_op jit(solution)/shard_map/ppermute | solution.py:190
  101.8 6.6 %collective-permute-start.22 = (bf16[512,128]{1,0:T(8,128)(2,1)S(1)}, bf16[512,128]{1,0:T(8,128)(2,1)S(1)}, u32[]{:S(2)}, u32[]{:S(2)}) collective-permute-start(bf16[512,128]{1,0:T(8,128)(2,1)S(1)} %get-tuple-element.16), channel_id=1, source_target_pairs={{0,48},{8,56},{16,0},{24,8},{32,16},{40,24},{48,32},{56,40},{64,11... | collective-permute-start | bytes 393224 | tf_op jit(solution)/shard_map/ppermute | solution.py:190
  104.6 5.0 %collective-permute-start.23 = (bf16[512,128]{1,0:T(8,128)(2,1)S(1)}, bf16[512,128]{1,0:T(8,128)(2,1)S(1)}, u32[]{:S(2)}, u32[]{:S(2)}) collective-permute-start(bf16[512,128]{1,0:T(8,128)(2,1)S(1)} %get-tuple-element.17), channel_id=1, source_target_pairs={{0,16},{8,24},{16,32},{24,40},{32,48},{40,56},{48,0},{56,8},{64,80... | collective-permute-start | bytes 393224 | tf_op jit(solution)/shard_map/ppermute | solution.py:190

commit v17 on v16

--- a/solution.py
+++ b/solution.py
@@ -173,16 +173,11 @@
 def gather_group(block, my_index):
     from_minus = lax.ppermute(block, "resp", ring_route(lambda x, c: (x + 1, c)))
     from_plus = lax.ppermute(block, "resp", ring_route(lambda x, c: (x - 1, c)))
-    from_core = lax.ppermute(block, "resp", ring_route(lambda x, c: (x, 1 - c)))
     relay = jnp.where(my_index % 2 == 0, from_plus, from_minus)
     far = lax.ppermute(relay, "resp", ring_route(lambda x, c: (x - 1, c) if c == 0 else (x + 1, c)))
-    core_sides = lax.ppermute(
-        jnp.concatenate([from_minus, from_plus], 0), "resp", ring_route(lambda x, c: (x, 1 - c))
-    )
-    far_other = lax.ppermute(far, "resp", ring_route(lambda x, c: (x, 1 - c)))
-    return jnp.concatenate(
-        [block, from_minus, from_plus, far, from_core, core_sides, far_other], 0
-    )
+    mine = jnp.concatenate([block, from_minus, from_plus, far], 0)
+    other = lax.ppermute(mine, "resp", ring_route(lambda x, c: (x, 1 - c)))
+    return jnp.concatenate([mine, other], 0)
 
 
 def return_group(terms, my_index):

time: 111 us -> 110 us (level)
  starting transfers between devices: 32.8 us -> 31 us
    ppermute x2, waiting for transfers between devices: 3.98 us -> 0.96 us  [gather_group(): lax.ppermute(relay, 'resp', ring_route(lambda x, c: (x - 1, c) if c == 0...]
    ppermute x8, starting transfers between devices: 12 us -> 9.89 us  [send(): lax.ppermute(block.astype(jnp.bfloat16), 'resp', ring_route(move))]
    ppermute x2, waiting for transfers between devices: 1.68 us -> 3.33 us  [gather_group(): lax.ppermute(block, 'resp', ring_route(lambda x, c: (x + 1, c)))]
    ppermute x6 -> x2, starting transfers between devices: 5.43 us -> 4.46 us  [gather_group(): other = lax.ppermute(mine, 'resp', ring_route(lambda x, c: (x, 1 - c)))]
    unnamed x28 -> x26, local copies, waits for them, and re-layouts: 3.98 us -> 3.85 us
  transfers between devices with their start and end apart: 24 -> 20, of which waited for: 10 -> 9; matrix products, arithmetic and copies ran while one was open for 6% -> 7% of each run, Pallas kernels for 0% -> 0%
where the time goes in v17:
time: 110 us; the launch traced here: 109 us
  Pallas kernels  43.8 us (40%)
  starting transfers between devices  31 us (28%)
  waiting for transfers between devices  16.4 us (15%)
  other arithmetic  11.2 us (10%)
  local copies, waits for them, and re-layouts  5.24 us (5%)
  between operations  1.58 us (1%)
    pallas_call x1, Pallas kernels, attention_backward(): pl.pallas_call(backward_kernel, grid_spec=pltpu.PrefetchScalarGridSpec(nu...  22.4 us
    pallas_call x1, Pallas kernels, attention_forward(): pl.pallas_call(forward_kernel, grid_spec=pltpu.PrefetchScalarGridSpec(num...  21.4 us
    ppermute x8, starting transfers between devices, send(): lax.ppermute(block.astype(jnp.bfloat16), 'resp', ring_route(move))  9.89 us
    ppermute x8, waiting for transfers between devices, send(): lax.ppermute(block.astype(jnp.bfloat16), 'resp', ring_route(move))  6.9 us
    ppermute x2, starting transfers between devices, gather_group(): from_plus = lax.ppermute(block, 'resp', ring_route(lambda x, c: (x - 1, c)))  6.06 us
    ppermute x1, starting transfers between devices, head_sum(): lax.ppermute(quad, 'head', [(low, low ^ 4) for low in range(heads)])  5.38 us
    ppermute x3, starting transfers between devices, head_sum(): lax.ppermute(row_part, 'head', [(low, low ^ distance) for low in range(he...  4.71 us
    ppermute x2, starting transfers between devices, gather_group(): other = lax.ppermute(mine, 'resp', ring_route(lambda x, c: (x, 1 - c)))  4.46 us
  transfers between devices with their start and end apart: 20, of which 9 were waited for; matrix products, arithmetic and copies ran while one was open for 7% of the time, Pallas kernels for 0%

profile of v17, /device:TPU:1, one launch (start us, length us, event | category | flops | bytes accessed | tf_op | source)
XLA Modules:
  0.0 109.2 jit_solution(6022712325407404787)
XLA Ops:
  0.6 0.0 copy-start.7
  0.6 3.4 %collective-permute-start.1 = (bf16[1,512,128]{2,1,0:T(8,128)(2,1)}, bf16[1,512,128]{2,1,0:T(8,128)(2,1)S(1)}, u32[]{:S(2)}, u32[]{:S(2)}) collective-permute-start(bf16[1,512,128]{2,1,0:T(8,128)(2,1)} %param.8), channel_id=1, source_target_pairs={{0,48},{8,56},{16,0},{24,8},{32,16},{40,24},{48,32},{56,40},{64,11... | collective-permute-start | bytes 393224 | tf_op jit(solution)/shard_map/ppermute | solution.py:175
  4.0 0.0 collective-permute-start
  4.0 2.7 %collective-permute-start.5 = (bf16[1,512,128]{2,1,0:T(8,128)(2,1)}, bf16[1,512,128]{2,1,0:T(8,128)(2,1)S(1)}, u32[]{:S(2)}, u32[]{:S(2)}) collective-permute-start(bf16[1,512,128]{2,1,0:T(8,128)(2,1)} %param.9), channel_id=1, source_target_pairs={{0,48},{8,56},{16,0},{24,8},{32,16},{40,24},{48,32},{56,40},{64,11... | collective-permute-start | bytes 393224 | tf_op jit(solution)/shard_map/ppermute | solution.py:175
  6.7 0.0 collective-permute-start.4
  6.7 0.9 constant_dynamic-update-slice_fusion.4
  7.6 0.9 constant_dynamic-update-slice_fusion.9
  8.6 0.0 collective-permute-done.1
  8.6 0.7 collective-permute-done
  9.3 0.1 collective-permute-start.2
  9.4 0.0 collective-permute-done.5
  9.5 2.6 %collective-permute-done.4 = bf16[1,512,128]{2,1,0:T(8,128)(2,1)S(1)} collective-permute-done((bf16[1,512,128]{2,1,0:T(8,128)(2,1)}, bf16[1,512,128]{2,1,0:T(8,128)(2,1)S(1)}, u32[]{:S(2)}, u32[]{:S(2)}) %collective-permute-start.4) | collective-permute-done | bytes 131104 | tf_op jit(solution)/shard_map/ppermute | solution.py:174
  12.1 0.4 collective-permute-start.6
  12.5 1.2 %fusion.30.rows_ref = s32[3]{0:T(128)} fusion(s32[]{:T(128)S(6)} %shift_right_arithmetic.16, s32[1,3]{1,0:T(1,128)} %param.10, s32[]{:T(128)S(6)} %axis_index.15), kind=kLoop, calls=%fused_computation.84 | loop fusion | flops 69 | bytes 32 | tf_op jit(solution)/shard_map/add | solution.py:170
  14.4 1.0 collective-permute-done.2
  15.3 1.0 pad_maximum_fusion
  16.3 2.3 %collective-permute-start.3 = (bf16[4,512,128]{2,1,0:T(8,128)(2,1)S(1)}, bf16[4,512,128]{2,1,0:T(8,128)(2,1)S(1)}, u32[]{:S(2)}, u32[]{:S(2)}) collective-permute-start(bf16[4,512,128]{2,1,0:T(8,128)(2,1)S(1)} %pad_maximum_fusion), channel_id=1, source_target_pairs={{0,8},{8,0},{16,24},{24,16},{32,40},{40,32},{48,56},{56,48},{64,72... | collective-permute-start | bytes 1572872 | tf_op jit(solution)/shard_map/ppermute | solution.py:179
  18.6 0.0 collective-permute-done.6
  18.6 0.1 pad_maximum_fusion.1
  18.7 2.1 %collective-permute-start.7 = (bf16[4,512,128]{2,1,0:T(8,128)(2,1)S(1)}, bf16[4,512,128]{2,1,0:T(8,128)(2,1)S(1)}, u32[]{:S(2)}, u32[]{:S(2)}) collective-permute-start(bf16[4,512,128]{2,1,0:T(8,128)(2,1)S(1)} %pad_maximum_fusion.1), channel_id=1, source_target_pairs={{0,8},{8,0},{16,24},{24,16},{32,40},{40,32},{48,56},{56,48},{64,72... | collective-permute-start | bytes 1572872 | tf_op jit(solution)/shard_map/ppermute | solution.py:179
  20.9 0.0 collective-permute-done.3
  20.9 0.1 constant_dynamic-update-slice_fusion.refs_0_.refs_1_.refs_2_
  21.0 1.3 %collective-permute-done.7 = bf16[4,512,128]{2,1,0:T(8,128)(2,1)S(1)} collective-permute-done((bf16[4,512,128]{2,1,0:T(8,128)(2,1)S(1)}, bf16[4,512,128]{2,1,0:T(8,128)(2,1)S(1)}, u32[]{:S(2)}, u32[]{:S(2)}) %collective-permute-start.7) | collective-permute-done | bytes 524320 | tf_op jit(solution)/shard_map/ppermute | solution.py:179
  22.4 0.1 constant_dynamic-update-slice_fusion.5.refs_3_.refs_4_.refs_5_
  22.5 0.9 copy-done.1
  23.4 21.4 %shard_map.102 = (bf16[512,1024]{1,0:T(8,128)(2,1)}, f32[8,1,512]{2,1,0:T(1,128)}) custom-call(s32[1]{0:T(128)S(6)} %copy.21.count_ref, s32[3]{0:T(128)} %fusion.30.rows_ref, bf16[512,1024]{1,0:T(8,128)(2,1)} %bitcast.70, bf16[8,512,128]{2,1,0:T(8,128)(2,1)} %copy-done, bf16[8,512,128]{2,1,0:T(8,128)(2,1)} %copy-done, bf16[8,512,128]{2,1,0:T(8,128)(2,1)} %copy-done, ...), custom_call_target="tpu_custom_call" | custom-call | tf_op jit(solution)/shard_map/pallas_call | solution.py:108
  44.8 1.9 %fusion = (f32[512]{0:T(512)S(1)}, f32[512]{0:T(512)S(1)}) fusion(bf16[512,1024]{1,0:T(8,128)(2,1)} %get-tuple-element.9.refs_7_, f32[1024]{0:T(1024)S(1)} %copy-done.8, bf16[1,512,1024]{2,1,0:T(8,128)(2,1)S(1)} %copy-done.4), kind=kLoop, calls=%fused_computation.6 | loop fusion | flops 3668992 | bytes 2105344 | tf_op jit(solution)/shard_map/reduce_sum | solution.py:216
  46.7 3.1 %collective-permute-start.9 = (f32[2,512]{1,0:T(2,128)S(1)}, f32[2,512]{1,0:T(2,128)S(1)}, u32[]{:S(2)}, u32[]{:S(2)}) collective-permute-start(f32[2,512]{1,0:T(2,128)S(1)} %pad_maximum_fusion.2), channel_id=1, source_target_pairs={{0,2},{1,3},{2,0},{3,1},{4,6},{5,7},{6,4},{7,5},{8,10},{9,11},{10,... | collective-permute-start | bytes 12296 | tf_op jit(solution)/shard_map/ppermute | solution.py:200
  49.8 1.4 %collective-permute-start.10 = (f32[2,512]{1,0:T(2,128)S(1)}, f32[2,512]{1,0:T(2,128)S(1)}, u32[]{:S(2)}, u32[]{:S(2)}) collective-permute-start(f32[2,512]{1,0:T(2,128)S(1)} %pad_maximum_fusion.2), channel_id=1, source_target_pairs={{0,3},{1,2},{2,1},{3,0},{4,7},{5,6},{6,5},{7,4},{8,11},{9,10},{10,... | collective-permute-start | bytes 12296 | tf_op jit(solution)/shard_map/ppermute | solution.py:200
  51.3 0.2 collective-permute-start.8
  51.4 0.0 collective-permute-done.9
  51.5 2.6 %collective-permute-done.10 = f32[2,512]{1,0:T(2,128)S(1)} collective-permute-done((f32[2,512]{1,0:T(2,128)S(1)}, f32[2,512]{1,0:T(2,128)S(1)}, u32[]{:S(2)}, u32[]{:S(2)}) %collective-permute-start.10) | collective-permute-done | bytes 4128 | tf_op jit(solution)/shard_map/ppermute | solution.py:200
  54.1 0.0 collective-permute-done.8
  54.1 5.4 %collective-permute-start.11 = (f32[2,512]{1,0:T(2,128)S(1)}, f32[2,512]{1,0:T(2,128)S(1)}, u32[]{:S(2)}, u32[]{:S(2)}) collective-permute-start(f32[2,512]{1,0:T(2,128)S(1)} %add_add_fusion), channel_id=1, source_target_pairs={{0,4},{1,5},{2,6},{3,7},{4,0},{5,1},{6,2},{7,3},{8,12},{9,13},{10,... | collective-permute-start | bytes 12296 | tf_op jit(solution)/shard_map/ppermute | solution.py:201
  59.5 1.2 %collective-permute-done.11 = f32[2,512]{1,0:T(2,128)S(1)} collective-permute-done((f32[2,512]{1,0:T(2,128)S(1)}, f32[2,512]{1,0:T(2,128)S(1)}, u32[]{:S(2)}, u32[]{:S(2)}) %collective-permute-start.11) | collective-permute-done | bytes 4128 | tf_op jit(solution)/shard_map/ppermute | solution.py:201
  60.8 2.0 %fusion.5 = (bf16[512,1024]{1,0:T(8,128)(2,1)}, bf16[1,512,1024]{2,1,0:T(8,128)(2,1)}) fusion(bf16[512,1024]{1,0:T(8,128)(2,1)S(1)} %copy-done.3, bf16[1,512,1024]{2,1,0:T(8,128)(2,1)S(1)} %copy-done.4, f32[512]{0:T(512)S(1)} %fusion.27, f32[512]{0:T(512)S(1)} %bitcast.73, f32[1024]{0:T(1024)S(1)} %copy-done.8), kind=kLoop, calls=%fused_computation.11 | loop fusion | flops 5242880 | bytes 4202496 | tf_op jit(solution)/shard_map/convert_element_type | solution.py:225
  62.7 22.4 %shard_map.103 = (bf16[512,1024]{1,0:T(8,128)(2,1)}, f32[3,512,128]{2,1,0:T(8,128)}, f32[3,512,128]{2,1,0:T(8,128)}) custom-call(s32[1]{0:T(128)S(6)} %copy.21.count_ref, s32[3]{0:T(128)} %fusion.30.rows_ref, bf16[512,1024]{1,0:T(8,128)(2,1)} %bitcast.71, bf16[8,512,128]{2,1,0:T(8,128)(2,1)} %copy-done, bf16[8,512,128]{2,1,0:T(8,128)(2,1)} %copy-done, ...), custom_call_target="tpu_custom_call" | custom-call | tf_op jit(solution)/shard_map/pallas_call | solution.py:131
  85.1 0.1 broadcast_in_dim.40.clone
  85.3 1.0 copy-done.6
  86.2 1.0 scatter_fusion
  87.3 0.9 slice.120
  88.1 3.0 %collective-permute-start.12 = (bf16[4,512,128]{2,1,0:T(8,128)(2,1)}, bf16[4,512,128]{2,1,0:T(8,128)(2,1)S(1)}, u32[]{:S(2)}, u32[]{:S(2)}) collective-permute-start(bf16[4,512,128]{2,1,0:T(8,128)(2,1)} %slice.120), channel_id=1, source_target_pairs={{0,8},{8,0},{16,24},{24,16},{32,40},{40,32},{48,56},{56,48},{64,72... | collective-permute-start | bytes 1572872 | tf_op jit(solution)/shard_map/ppermute | solution.py:185
  91.1 0.1 broadcast_in_dim.40.clone.1
  91.2 1.0 scatter_fusion.1
  92.3 0.1 slice.119
  92.3 0.8 collective-permute-start.16
  93.1 0.0 collective-permute-done.12
  93.1 1.3 %slice_add_fusion.1 = f32[4,512,128]{2,1,0:T(8,128)S(1)} fusion(f32[8,512,128]{2,1,0:T(8,128)} %copy-done.2, bf16[4,512,128]{2,1,0:T(8,128)(2,1)S(1)} %collective-permute-done.12), kind=kLoop, calls=%fused_computation.18 | loop fusion | flops 524288 | bytes 2621440 | tf_op jit(solution)/shard_map/add | solution.py:187
  94.4 1.0 collective-permute-start.13
  95.4 0.1 slice_add_fusion
  95.6 0.2 collective-permute-start.17
  95.7 2.6 %collective-permute-done.13 = bf16[512,128]{1,0:T(8,128)(2,1)S(1)} collective-permute-done((bf16[512,128]{1,0:T(8,128)(2,1)S(1)}, bf16[512,128]{1,0:T(8,128)(2,1)S(1)}, u32[]{:S(2)}, u32[]{:S(2)}) %collective-permute-start.13) | collective-permute-done | bytes 131104 | tf_op jit(solution)/shard_map/ppermute | solution.py:185
  98.3 0.1 fusion.9
  98.4 2.2 %collective-permute-start.14 = (bf16[512,128]{1,0:T(8,128)(2,1)S(1)}, bf16[512,128]{1,0:T(8,128)(2,1)S(1)}, u32[]{:S(2)}, u32[]{:S(2)}) collective-permute-start(bf16[512,128]{1,0:T(8,128)(2,1)S(1)} %get-tuple-element.18), channel_id=1, source_target_pairs={{0,48},{8,56},{16,0},{24,8},{32,16},{40,24},{48,32},{56,40},{64,11... | collective-permute-start | bytes 393224 | tf_op jit(solution)/shard_map/ppermute | solution.py:185
  100.6 0.0 collective-permute-start.15
  100.6 0.0 collective-permute-done.17
  100.6 0.1 fusion.13
  100.7 2.8 %collective-permute-start.18 = (bf16[512,128]{1,0:T(8,128)(2,1)S(1)}, bf16[512,128]{1,0:T(8,128)(2,1)S(1)}, u32[]{:S(2)}, u32[]{:S(2)}) collective-permute-start(bf16[512,128]{1,0:T(8,128)(2,1)S(1)} %get-tuple-element.16), channel_id=1, source_target_pairs={{0,48},{8,56},{16,0},{24,8},{32,16},{40,24},{48,32},{56,40},{64,11... | collective-permute-start | bytes 393224 | tf_op jit(solution)/shard_map/ppermute | solution.py:185
  103.4 0.0 collective-permute-done.14
  103.5 3.0 %collective-permute-done.15 = bf16[512,128]{1,0:T(8,128)(2,1)S(1)} collective-permute-done((bf16[512,128]{1,0:T(8,128)(2,1)S(1)}, bf16[512,128]{1,0:T(8,128)(2,1)S(1)}, u32[]{:S(2)}, u32[]{:S(2)}) %collective-permute-start.15) | collective-permute-done | bytes 131104 | tf_op jit(solution)/shard_map/ppermute | solution.py:185
  106.5 0.7 fusion.22
  107.2 0.0 collective-permute-done.18
  107.2 1.3 %collective-permute-done.19 = bf16[512,128]{1,0:T(8,128)(2,1)S(1)} collective-permute-done((bf16[512,128]{1,0:T(8,128)(2,1)S(1)}, bf16[512,128]{1,0:T(8,128)(2,1)S(1)}, u32[]{:S(2)}, u32[]{:S(2)}) %collective-permute-start.19) | collective-permute-done | bytes 131104 | tf_op jit(solution)/shard_map/ppermute | solution.py:185
  108.5 0.7 fusion.24
  (33 shorter events, 0.3 us)
Async XLA Ops:
  0.6 18.0 %copy-start.7 = (bf16[1,512,128]{2,1,0:T(8,128)(2,1)S(1)}, bf16[1,512,128]{2,1,0:T(8,128)(2,1)}, u32[]{:S(2)}) copy-start(bf16[1,512,128]{2,1,0:T(8,128)(2,1)} %param.9) | copy-start | bytes 393220
  0.6 7.9 %collective-permute-start.1 = (bf16[1,512,128]{2,1,0:T(8,128)(2,1)}, bf16[1,512,128]{2,1,0:T(8,128)(2,1)S(1)}, u32[]{:S(2)}, u32[]{:S(2)}) collective-permute-start(bf16[1,512,128]{2,1,0:T(8,128)(2,1)} %param.8), channel_id=1, source_target_pairs={{0,48},{8,56},{16,0},{24,8},{32,16},{40,24},{48,32},{56,40},{64,11... | collective-permute-start | bytes 393224 | tf_op jit(solution)/shard_map/ppermute | solution.py:175
  4.0 5.2 %collective-permute-start = (bf16[1,512,128]{2,1,0:T(8,128)(2,1)}, bf16[1,512,128]{2,1,0:T(8,128)(2,1)S(1)}, u32[]{:S(2)}, u32[]{:S(2)}) collective-permute-start(bf16[1,512,128]{2,1,0:T(8,128)(2,1)} %param.8), channel_id=1, source_target_pairs={{0,16},{8,24},{16,32},{24,40},{32,48},{40,56},{48,0},{56,8},{64,80... | collective-permute-start | bytes 393224 | tf_op jit(solution)/shard_map/ppermute | solution.py:174
  4.0 5.4 %collective-permute-start.5 = (bf16[1,512,128]{2,1,0:T(8,128)(2,1)}, bf16[1,512,128]{2,1,0:T(8,128)(2,1)S(1)}, u32[]{:S(2)}, u32[]{:S(2)}) collective-permute-start(bf16[1,512,128]{2,1,0:T(8,128)(2,1)} %param.9), channel_id=1, source_target_pairs={{0,48},{8,56},{16,0},{24,8},{32,16},{40,24},{48,32},{56,40},{64,11... | collective-permute-start | bytes 393224 | tf_op jit(solution)/shard_map/ppermute | solution.py:175
  6.7 5.4 %collective-permute-start.4 = (bf16[1,512,128]{2,1,0:T(8,128)(2,1)}, bf16[1,512,128]{2,1,0:T(8,128)(2,1)S(1)}, u32[]{:S(2)}, u32[]{:S(2)}) collective-permute-start(bf16[1,512,128]{2,1,0:T(8,128)(2,1)} %param.9), channel_id=1, source_target_pairs={{0,16},{8,24},{16,32},{24,40},{32,48},{40,56},{48,0},{56,8},{64,80... | collective-permute-start | bytes 393224 | tf_op jit(solution)/shard_map/ppermute | solution.py:174
  9.3 6.0 %collective-permute-start.2 = (bf16[1,512,128]{2,1,0:T(8,128)(2,1)S(1)}, bf16[1,512,128]{2,1,0:T(8,128)(2,1)S(1)}, u32[]{:S(2)}, u32[]{:S(2)}) collective-permute-start(bf16[1,512,128]{2,1,0:T(8,128)(2,1)S(1)} %get-tuple-element.24), channel_id=1, source_target_pairs={{0,48},{8,24},{16,0},{24,40},{32,16},{40,56},{48,32},{56,8},{64,11... | collective-permute-start | bytes 393224 | tf_op jit(solution)/shard_map/ppermute | solution.py:177
  12.1 6.5 %collective-permute-start.6 = (bf16[1,512,128]{2,1,0:T(8,128)(2,1)S(1)}, bf16[1,512,128]{2,1,0:T(8,128)(2,1)S(1)}, u32[]{:S(2)}, u32[]{:S(2)}) collective-permute-start(bf16[1,512,128]{2,1,0:T(8,128)(2,1)S(1)} %get-tuple-element.22), channel_id=1, source_target_pairs={{0,48},{8,24},{16,0},{24,40},{32,16},{40,56},{48,32},{56,8},{64,11... | collective-permute-start | bytes 393224 | tf_op jit(solution)/shard_map/ppermute | solution.py:177
  16.3 4.6 %collective-permute-start.3 = (bf16[4,512,128]{2,1,0:T(8,128)(2,1)S(1)}, bf16[4,512,128]{2,1,0:T(8,128)(2,1)S(1)}, u32[]{:S(2)}, u32[]{:S(2)}) collective-permute-start(bf16[4,512,128]{2,1,0:T(8,128)(2,1)S(1)} %pad_maximum_fusion), channel_id=1, source_target_pairs={{0,8},{8,0},{16,24},{24,16},{32,40},{40,32},{48,56},{56,48},{64,72... | collective-permute-start | bytes 1572872 | tf_op jit(solution)/shard_map/ppermute | solution.py:179
  18.7 3.7 %collective-permute-start.7 = (bf16[4,512,128]{2,1,0:T(8,128)(2,1)S(1)}, bf16[4,512,128]{2,1,0:T(8,128)(2,1)S(1)}, u32[]{:S(2)}, u32[]{:S(2)}) collective-permute-start(bf16[4,512,128]{2,1,0:T(8,128)(2,1)S(1)} %pad_maximum_fusion.1), channel_id=1, source_target_pairs={{0,8},{8,0},{16,24},{24,16},{32,40},{40,32},{48,56},{56,48},{64,72... | collective-permute-start | bytes 1572872 | tf_op jit(solution)/shard_map/ppermute | solution.py:179
  21.0 1.4 %copy-start = (bf16[8,512,128]{2,1,0:T(8,128)(2,1)}, bf16[8,512,128]{2,1,0:T(8,128)(2,1)S(1)}, u32[]{:S(2)}) copy-start(bf16[8,512,128]{2,1,0:T(8,128)(2,1)S(1)} %constant_dynamic-update-slice_fusion.refs_0_.refs_1_.refs_2_) | copy-start | bytes 3145732
  22.4 0.9 copy-start.1
  23.4 21.4 %copy-start.4 = (bf16[1,512,1024]{2,1,0:T(8,128)(2,1)S(1)}, bf16[1,512,1024]{2,1,0:T(8,128)(2,1)}, u32[]{:S(2)}) copy-start(bf16[1,512,1024]{2,1,0:T(8,128)(2,1)} %param.13) | copy-start | bytes 3145732
  23.4 21.4 %copy-start.8 = (f32[1024]{0:T(1024)S(1)}, f32[1024]{0:T(1024)}, u32[]{:S(2)}) copy-start(f32[1024]{0:T(1024)} %param.12) | copy-start | bytes 12292
  44.8 14.6 %copy-start.9 = (s32[1,3]{1,0:T(1,128)S(1)}, s32[1,3]{1,0:T(1,128)}, u32[]{:S(2)}) copy-start(s32[1,3]{1,0:T(1,128)} %param.10) | copy-start | bytes 40
  44.8 15.9 %copy-start.3 = (bf16[512,1024]{1,0:T(8,128)(2,1)S(1)}, bf16[512,1024]{1,0:T(8,128)(2,1)}, u32[]{:S(2)}) copy-start(bf16[512,1024]{1,0:T(8,128)(2,1)} %get-tuple-element.9.refs_7_) | copy-start | bytes 3145732
  46.7 4.7 %collective-permute-start.9 = (f32[2,512]{1,0:T(2,128)S(1)}, f32[2,512]{1,0:T(2,128)S(1)}, u32[]{:S(2)}, u32[]{:S(2)}) collective-permute-start(f32[2,512]{1,0:T(2,128)S(1)} %pad_maximum_fusion.2), channel_id=1, source_target_pairs={{0,2},{1,3},{2,0},{3,1},{4,6},{5,7},{6,4},{7,5},{8,10},{9,11},{10,... | collective-permute-start | bytes 12296 | tf_op jit(solution)/shard_map/ppermute | solution.py:200
  49.8 4.3 %collective-permute-start.10 = (f32[2,512]{1,0:T(2,128)S(1)}, f32[2,512]{1,0:T(2,128)S(1)}, u32[]{:S(2)}, u32[]{:S(2)}) collective-permute-start(f32[2,512]{1,0:T(2,128)S(1)} %pad_maximum_fusion.2), channel_id=1, source_target_pairs={{0,3},{1,2},{2,1},{3,0},{4,7},{5,6},{6,5},{7,4},{8,11},{9,10},{10,... | collective-permute-start | bytes 12296 | tf_op jit(solution)/shard_map/ppermute | solution.py:200
  51.3 2.8 %collective-permute-start.8 = (f32[2,512]{1,0:T(2,128)S(1)}, f32[2,512]{1,0:T(2,128)S(1)}, u32[]{:S(2)}, u32[]{:S(2)}) collective-permute-start(f32[2,512]{1,0:T(2,128)S(1)} %pad_maximum_fusion.2), channel_id=1, source_target_pairs={{0,1},{1,0},{2,3},{3,2},{4,5},{5,4},{6,7},{7,6},{8,9},{9,8},{10,11... | collective-permute-start | bytes 12296 | tf_op jit(solution)/shard_map/ppermute | solution.py:200
  54.1 6.6 %collective-permute-start.11 = (f32[2,512]{1,0:T(2,128)S(1)}, f32[2,512]{1,0:T(2,128)S(1)}, u32[]{:S(2)}, u32[]{:S(2)}) collective-permute-start(f32[2,512]{1,0:T(2,128)S(1)} %add_add_fusion), channel_id=1, source_target_pairs={{0,4},{1,5},{2,6},{3,7},{4,0},{5,1},{6,2},{7,3},{8,12},{9,13},{10,... | collective-permute-start | bytes 12296 | tf_op jit(solution)/shard_map/ppermute | solution.py:201
  85.1 1.1 %copy-start.6 = (f32[3,512,128]{2,1,0:T(8,128)S(1)}, f32[3,512,128]{2,1,0:T(8,128)}, u32[]{:S(2)}) copy-start(f32[3,512,128]{2,1,0:T(8,128)} %get-tuple-element.12) | copy-start | bytes 2359300
  87.2 3.9 %copy-start.2 = (f32[8,512,128]{2,1,0:T(8,128)}, f32[8,512,128]{2,1,0:T(8,128)S(1)}, u32[]{:S(2)}) copy-start(f32[8,512,128]{2,1,0:T(8,128)S(1)} %scatter_fusion) | copy-start | bytes 6291460
  87.3 4.0 %copy-start.5 = (f32[3,512,128]{2,1,0:T(8,128)S(1)}, f32[3,512,128]{2,1,0:T(8,128)}, u32[]{:S(2)}) copy-start(f32[3,512,128]{2,1,0:T(8,128)} %get-tuple-element.13) | copy-start | bytes 2359300
  88.1 5.0 %collective-permute-start.12 = (bf16[4,512,128]{2,1,0:T(8,128)(2,1)}, bf16[4,512,128]{2,1,0:T(8,128)(2,1)S(1)}, u32[]{:S(2)}, u32[]{:S(2)}) collective-permute-start(bf16[4,512,128]{2,1,0:T(8,128)(2,1)} %slice.120), channel_id=1, source_target_pairs={{0,8},{8,0},{16,24},{24,16},{32,40},{40,32},{48,56},{56,48},{64,72... | collective-permute-start | bytes 1572872 | tf_op jit(solution)/shard_map/ppermute | solution.py:185
  92.3 3.1 %collective-permute-start.16 = (bf16[4,512,128]{2,1,0:T(8,128)(2,1)S(1)}, bf16[4,512,128]{2,1,0:T(8,128)(2,1)S(1)}, u32[]{:S(2)}, u32[]{:S(2)}) collective-permute-start(bf16[4,512,128]{2,1,0:T(8,128)(2,1)S(1)} %slice.119), channel_id=1, source_target_pairs={{0,8},{8,0},{16,24},{24,16},{32,40},{40,32},{48,56},{56,48},{64,72... | collective-permute-start | bytes 1572872 | tf_op jit(solution)/shard_map/ppermute | solution.py:185
  94.4 3.9 %collective-permute-start.13 = (bf16[512,128]{1,0:T(8,128)(2,1)S(1)}, bf16[512,128]{1,0:T(8,128)(2,1)S(1)}, u32[]{:S(2)}, u32[]{:S(2)}) collective-permute-start(bf16[512,128]{1,0:T(8,128)(2,1)S(1)} %fusion.23), channel_id=1, source_target_pairs={{0,16},{8,56},{16,32},{24,8},{32,48},{40,24},{48,0},{56,40},{64,80... | collective-permute-start | bytes 393224 | tf_op jit(solution)/shard_map/ppermute | solution.py:185
  95.6 5.1 %collective-permute-start.17 = (bf16[512,128]{1,0:T(8,128)(2,1)S(1)}, bf16[512,128]{1,0:T(8,128)(2,1)S(1)}, u32[]{:S(2)}, u32[]{:S(2)}) collective-permute-start(bf16[512,128]{1,0:T(8,128)(2,1)S(1)} %fusion.25), channel_id=1, source_target_pairs={{0,16},{8,56},{16,32},{24,8},{32,48},{40,24},{48,0},{56,40},{64,80... | collective-permute-start | bytes 393224 | tf_op jit(solution)/shard_map/ppermute | solution.py:185
  98.4 5.1 %collective-permute-start.14 = (bf16[512,128]{1,0:T(8,128)(2,1)S(1)}, bf16[512,128]{1,0:T(8,128)(2,1)S(1)}, u32[]{:S(2)}, u32[]{:S(2)}) collective-permute-start(bf16[512,128]{1,0:T(8,128)(2,1)S(1)} %get-tuple-element.18), channel_id=1, source_target_pairs={{0,48},{8,56},{16,0},{24,8},{32,16},{40,24},{48,32},{56,40},{64,11... | collective-permute-start | bytes 393224 | tf_op jit(solution)/shard_map/ppermute | solution.py:185
  100.6 5.9 %collective-permute-start.15 = (bf16[512,128]{1,0:T(8,128)(2,1)S(1)}, bf16[512,128]{1,0:T(8,128)(2,1)S(1)}, u32[]{:S(2)}, u32[]{:S(2)}) collective-permute-start(bf16[512,128]{1,0:T(8,128)(2,1)S(1)} %get-tuple-element.19), channel_id=1, source_target_pairs={{0,16},{8,24},{16,32},{24,40},{32,48},{40,56},{48,0},{56,8},{64,80... | collective-permute-start | bytes 393224 | tf_op jit(solution)/shard_map/ppermute | solution.py:185
  100.7 6.5 %collective-permute-start.18 = (bf16[512,128]{1,0:T(8,128)(2,1)S(1)}, bf16[512,128]{1,0:T(8,128)(2,1)S(1)}, u32[]{:S(2)}, u32[]{:S(2)}) collective-permute-start(bf16[512,128]{1,0:T(8,128)(2,1)S(1)} %get-tuple-element.16), channel_id=1, source_target_pairs={{0,48},{8,56},{16,0},{24,8},{32,16},{40,24},{48,32},{56,40},{64,11... | collective-permute-start | bytes 393224 | tf_op jit(solution)/shard_map/ppermute | solution.py:185
  103.4 5.0 %collective-permute-start.19 = (bf16[512,128]{1,0:T(8,128)(2,1)S(1)}, bf16[512,128]{1,0:T(8,128)(2,1)S(1)}, u32[]{:S(2)}, u32[]{:S(2)}) collective-permute-start(bf16[512,128]{1,0:T(8,128)(2,1)S(1)} %get-tuple-element.17), channel_id=1, source_target_pairs={{0,16},{8,24},{16,32},{24,40},{32,48},{40,56},{48,0},{56,8},{64,80... | collective-permute-start | bytes 393224 | tf_op jit(solution)/shard_map/ppermute | solution.py:185
